TPU v7x, 32 devices: a whole 2x2x4 slice. The times are simulated.
32 devices in a mesh: groups: 2 (over y), seq: 16 (over z, x, core).
Axes of the slice: x: 2, y: 2, z: 4, core: 2. Of those that a mesh axis runs over, the one named last changes fastest.
Arguments:
- queries: bfloat16 [12288, 2048], P(('groups', 'seq')), parts along dimension 0, may hold values from -6 to 6
- keys: bfloat16 [12288, 2048], P(('groups', 'seq')), parts along dimension 0, may hold values from -6 to 6
- values: bfloat16 [12288, 2048], P(('groups', 'seq')), parts along dimension 0, may hold values from -40 to 40
- lengths: int32 [8], P('groups'), parts along dimension 0, may hold values from 1 to 4608, 6144 in all
- out_grad: bfloat16 [12288, 2048], P(('groups', 'seq')), parts along dimension 0, may hold values from -6 to 6
Outputs:
- attn_out: bfloat16 [12288, 2048], P(('groups', 'seq')), parts along dimension 0
- grad_queries: bfloat16 [12288, 2048], P(('groups', 'seq')), parts along dimension 0
- grad_keys: bfloat16 [12288, 2048], P(('groups', 'seq')), parts along dimension 0
- grad_values: bfloat16 [12288, 2048], P(('groups', 'seq')), parts along dimension 0
There are 2 independent parts, one for each index of `groups`. A program takes and returns all parts, laid end to end along the dimension named above; each array names one. Nothing has to cross between parts.
Inputs may be any that keep to these rules, and one draw needn't show every extreme that they name: The lengths sum to 6144 and the largest is exactly 4608.
All inputs are finite; a program needn't handle non-finite values.
Results may differ from a plain program's by a relative error of at most 0.0059.
Values sent between devices are 32-bit elements; how exact they have to be, the bound alone decides.
No kernel may reach another device: no remote copies, remote signals or barrier semaphores. Data moves between devices by JAX's collectives and lax.ppermute only.
A program may use at most 128 MiB of HBM per device.

v0:
```python
import jax
import jax.numpy as jnp
from jax import lax
from jax.sharding import PartitionSpec as P

HEAD = 128
SPAN = 12


def passed_along(value, axis, steps):
    count = lax.axis_size(axis)
    first, last = (max(0, -steps), min(count, count - steps))
    return lax.ppermute(value, axis, [(source, source + steps) for source in range(first, last)])


def join_pair(earlier, later_pair):
    return (
        later_pair[0] + (1.0 - later_pair[1]) * earlier[0],
        jnp.maximum(earlier[1], later_pair[1]),
    )


def windowed_prefix(element, direction):
    carried_pair = passed_along((element[0], element[1]), "seq", direction)
    for level_bit in range((SPAN - 1).bit_length()):
        earlier = passed_along(
            (carried_pair[0], carried_pair[1]), "seq", direction * (1 << level_bit)
        )
        carried_pair = join_pair(earlier, carried_pair)
    return carried_pair


def shards(queries, keys, values, lengths, out_grad):
    row_count, feat_width = queries.shape
    head_count = feat_width // HEAD
    first_row = lax.axis_index("seq") * row_count
    position = first_row + lax.iota(jnp.int32, row_count)
    starts = jnp.cumsum(lengths) - lengths
    doc_ids = jnp.sum((starts[None, :] <= position[:, None]).astype(jnp.int32), axis=1)
    keep_mask = (position[None, :] <= position[:, None]) & (doc_ids[None, :] == doc_ids[:, None])
    lead_rows = doc_ids == doc_ids[0]
    tail_rows = doc_ids == doc_ids[row_count - 1]
    continues = jnp.logical_not(jnp.any(starts == first_row))
    has_start = jnp.any((starts >= first_row) & (starts < first_row + row_count))
    stops_back = jnp.logical_or(doc_ids[0] != doc_ids[row_count - 1], jnp.logical_not(continues))
    use_carry = lead_rows & continues
    query_heads = queries.reshape(row_count, head_count, HEAD)
    key_heads = keys.reshape(row_count, head_count, HEAD)
    value_heads = values.reshape(row_count, head_count, HEAD)
    scores = jnp.einsum("thd,shd->hts", query_heads, key_heads, preferred_element_type=jnp.float32)
    weights = jnp.where(keep_mask[None], scores, 0.0).astype(jnp.bfloat16)
    inside = jnp.einsum("hts,she->the", weights, value_heads, preferred_element_type=jnp.float32)
    tail_keys = jnp.where(tail_rows[:, None, None], key_heads, jnp.zeros_like(key_heads))
    state_local = jnp.einsum(
        "shd,she->hde", tail_keys, value_heads, preferred_element_type=jnp.float32
    )
    start_flag = has_start.astype(jnp.float32).reshape(1, 1, 1)
    prefix = windowed_prefix((state_local, start_flag), 1)[0]
    prefix_low = prefix.astype(jnp.bfloat16)
    carried = jnp.einsum(
        "thd,hde->the", query_heads, prefix_low, preferred_element_type=jnp.float32
    )
    mixed = (inside + jnp.where(use_carry[:, None, None], carried, 0.0)).reshape(
        row_count, feat_width
    )
    rms_value = jnp.sqrt(jnp.mean(mixed * mixed, axis=1, keepdims=True) + 1e-05)
    normed = mixed / rms_value
    attn_out = normed.astype(jnp.bfloat16)
    out_cot = out_grad.astype(jnp.float32)
    grad_mix = (out_cot - normed * jnp.mean(out_cot * normed, axis=1, keepdims=True)) / rms_value
    grad_low = grad_mix.astype(jnp.bfloat16).reshape(row_count, head_count, HEAD)
    lead_queries = jnp.where(use_carry[:, None, None], query_heads, jnp.zeros_like(query_heads))
    grad_local = jnp.einsum(
        "thd,the->hde", lead_queries, grad_low, preferred_element_type=jnp.float32
    )
    back_flag = stops_back.astype(jnp.float32).reshape(1, 1, 1)
    suffix = windowed_prefix((grad_local, back_flag), -1)[0]
    grad_scores = jnp.einsum(
        "the,she->hts", grad_low, value_heads, preferred_element_type=jnp.float32
    )
    grad_weights = jnp.where(keep_mask[None], grad_scores, 0.0).astype(jnp.bfloat16)
    suffix_low = suffix.astype(jnp.bfloat16)
    grad_queries = jnp.einsum(
        "hts,shd->thd", grad_weights, key_heads, preferred_element_type=jnp.float32
    )
    query_carry = jnp.einsum(
        "the,hde->thd", grad_low, prefix_low, preferred_element_type=jnp.float32
    )
    grad_queries = grad_queries + jnp.where(use_carry[:, None, None], query_carry, 0.0)
    grad_keys = jnp.einsum(
        "hts,thd->shd", grad_weights, query_heads, preferred_element_type=jnp.float32
    )
    key_carry = jnp.einsum(
        "she,hde->shd", value_heads, suffix_low, preferred_element_type=jnp.float32
    )
    grad_keys = grad_keys + jnp.where(tail_rows[:, None, None], key_carry, 0.0)
    grad_values = jnp.einsum("hts,the->she", weights, grad_low, preferred_element_type=jnp.float32)
    value_carry = jnp.einsum(
        "shd,hde->she", key_heads, suffix_low, preferred_element_type=jnp.float32
    )
    grad_values = grad_values + jnp.where(tail_rows[:, None, None], value_carry, 0.0)
    return (
        attn_out,
        grad_queries.reshape(row_count, feat_width).astype(jnp.bfloat16),
        grad_keys.reshape(row_count, feat_width).astype(jnp.bfloat16),
        grad_values.reshape(row_count, feat_width).astype(jnp.bfloat16),
    )


def solution(mesh):
    return jax.shard_map(
        shards,
        mesh=mesh,
        in_specs=(
            P(("groups", "seq"), None),
            P(("groups", "seq"), None),
            P(("groups", "seq"), None),
            P("groups"),
            P(("groups", "seq"), None),
        ),
        out_specs=(
            P(("groups", "seq"), None),
            P(("groups", "seq"), None),
            P(("groups", "seq"), None),
            P(("groups", "seq"), None),
        ),
        check_vma=False,
    )
```

profile of v0, /device:TPU:1, one launch (start us, length us, event | category | flops | bytes accessed | tf_op | source)
XLA Modules:
  0.0 323.3 jit_solution(3540525058075483763)
XLA Ops:
  4.1 3.0 copy.59
  7.1 2.1 copy.34
  11.0 4.5 %collective-permute-start = (f32[16,128,128]{2,1,0:T(8,128)S(1)}, f32[16,128,128]{2,1,0:T(8,128)}, u32[]{:S(2)}, u32[]{:S(2)}) collective-permute-start(f32[16,128,128]{2,1,0:T(8,128)S(1)} %fusion.9), channel_id=1, source_target_pairs={{0,1},{1,2},{2,3},{3,4},{4,5},{5,6},{6,7},{7,8},{8,9},{9,10},{10,1... | collective-permute-start | bytes 3145736 | tf_op jit(solution)/shard_map/ppermute | solution.py:13
  15.5 11.7 %collective-permute-done = f32[16,128,128]{2,1,0:T(8,128)} collective-permute-done((f32[16,128,128]{2,1,0:T(8,128)S(1)}, f32[16,128,128]{2,1,0:T(8,128)}, u32[]{:S(2)}, u32[]{:S(2)}) %collective-permute-start) | collective-permute-done | bytes 1048608 | tf_op jit(solution)/shard_map/ppermute | solution.py:13
  27.2 4.5 %collective-permute-start.2 = (f32[16,128,128]{2,1,0:T(8,128)}, f32[16,128,128]{2,1,0:T(8,128)S(1)}, u32[]{:S(2)}, u32[]{:S(2)}) collective-permute-start(f32[16,128,128]{2,1,0:T(8,128)} %collective-permute-done), channel_id=1, source_target_pairs={{0,1},{1,2},{2,3},{3,4},{4,5},{5,6},{6,7},{7,8},{8,9},{9,10},{10,1... | collective-permute-start | bytes 3145736 | tf_op jit(solution)/shard_map/ppermute | solution.py:13
  32.4 11.4 %collective-permute-start.1 = (f32[1,1,1]{2,1,0:T(1,128)}, f32[1,1,1]{2,1,0:T(1,128)}, u32[]{:S(2)}, u32[]{:S(2)}) collective-permute-start(f32[1,1,1]{2,1,0:T(1,128)} %bitcast.5), channel_id=1, source_target_pairs={{0,1},{1,2},{2,3},{3,4},{4,5},{5,6},{6,7},{7,8},{8,9},{9,10},{10,1... | collective-permute-start | bytes 20 | tf_op jit(solution)/shard_map/ppermute | solution.py:13
  45.8 4.1 %collective-permute-start.4 = (f32[16,128,128]{2,1,0:T(8,128)S(1)}, f32[16,128,128]{2,1,0:T(8,128)S(1)}, u32[]{:S(2)}, u32[]{:S(2)}) collective-permute-start(f32[16,128,128]{2,1,0:T(8,128)S(1)} %multiply_add_fusion.5), channel_id=1, source_target_pairs={{0,2},{1,3},{2,4},{3,5},{4,6},{5,7},{6,8},{7,9},{8,10},{9,11},{10,... | collective-permute-start | bytes 3145736 | tf_op jit(solution)/shard_map/ppermute | solution.py:13
  49.9 5.4 %collective-permute-start.3 = (f32[1,1,1]{2,1,0:T(1,128)}, f32[1,1,1]{2,1,0:T(1,128)}, u32[]{:S(2)}, u32[]{:S(2)}) collective-permute-start(f32[1,1,1]{2,1,0:T(1,128)} %collective-permute-done.1), channel_id=1, source_target_pairs={{0,1},{1,2},{2,3},{3,4},{4,5},{5,6},{6,7},{7,8},{8,9},{9,10},{10,1... | collective-permute-start | bytes 20 | tf_op jit(solution)/shard_map/ppermute | solution.py:13
  55.4 16.7 %collective-permute-done.3 = f32[1,1,1]{2,1,0:T(1,128)} collective-permute-done((f32[1,1,1]{2,1,0:T(1,128)}, f32[1,1,1]{2,1,0:T(1,128)}, u32[]{:S(2)}, u32[]{:S(2)}) %collective-permute-start.3) | collective-permute-done | bytes 36 | tf_op jit(solution)/shard_map/ppermute | solution.py:13
  74.4 3.9 %collective-permute-start.6 = (f32[16,128,128]{2,1,0:T(8,128)}, f32[16,128,128]{2,1,0:T(8,128)}, u32[]{:S(2)}, u32[]{:S(2)}) collective-permute-start(f32[16,128,128]{2,1,0:T(8,128)} %multiply_add_fusion.4), channel_id=1, source_target_pairs={{0,4},{1,5},{2,6},{3,7},{4,8},{5,9},{6,10},{7,11},{8,12},{9,13},{1... | collective-permute-start | bytes 3145736 | tf_op jit(solution)/shard_map/ppermute | solution.py:13
  78.3 1.9 copy.55
  80.2 3.5 %collective-permute-start.5 = (f32[1,1,1]{2,1,0:T(1,128)}, f32[1,1,1]{2,1,0:T(1,128)}, u32[]{:S(2)}, u32[]{:S(2)}) collective-permute-start(f32[1,1,1]{2,1,0:T(1,128)} %max.18), channel_id=1, source_target_pairs={{0,2},{1,3},{2,4},{3,5},{4,6},{5,7},{6,8},{7,9},{8,10},{9,11},{10,... | collective-permute-start | bytes 20 | tf_op jit(solution)/shard_map/ppermute | solution.py:13
  84.3 14.7 %collective-permute-done.6 = f32[16,128,128]{2,1,0:T(8,128)} collective-permute-done((f32[16,128,128]{2,1,0:T(8,128)}, f32[16,128,128]{2,1,0:T(8,128)}, u32[]{:S(2)}, u32[]{:S(2)}) %collective-permute-start.6) | collective-permute-done | bytes 1048608 | tf_op jit(solution)/shard_map/ppermute | solution.py:13
  99.0 1.8 multiply_add_fusion.3
  100.8 5.5 %collective-permute-start.8 = (f32[16,128,128]{2,1,0:T(8,128)S(1)}, f32[16,128,128]{2,1,0:T(8,128)S(1)}, u32[]{:S(2)}, u32[]{:S(2)}) collective-permute-start(f32[16,128,128]{2,1,0:T(8,128)S(1)} %multiply_add_fusion.3), channel_id=1, source_target_pairs={{0,8},{1,9},{2,10},{3,11},{4,12},{5,13},{6,14},{7,15},{16,24},{17,... | collective-permute-start | bytes 3145736 | tf_op jit(solution)/shard_map/ppermute | solution.py:13
  106.4 1.8 select_convert_fusion.1
  108.2 1.6 fusion.5
  110.4 15.7 %collective-permute-start.7 = (f32[1,1,1]{2,1,0:T(1,128)}, f32[1,1,1]{2,1,0:T(1,128)}, u32[]{:S(2)}, u32[]{:S(2)}) collective-permute-start(f32[1,1,1]{2,1,0:T(1,128)} %max.19), channel_id=1, source_target_pairs={{0,4},{1,5},{2,6},{3,7},{4,8},{5,9},{6,10},{7,11},{8,12},{9,13},{1... | collective-permute-start | bytes 20 | tf_op jit(solution)/shard_map/ppermute | solution.py:13
  126.8 2.3 multiply_reduce_fusion
  129.2 3.6 %copy.38 = f32[384,2048]{1,0:T(8,128)} copy(f32[384,2048]{0,1:T(8,128)} %bitcast.102) | data formatting | bytes 6291456 | tf_op jit(solution)/shard_map/reshape | solution.py:63
  132.8 3.1 fusion
  136.6 2.3 fusion.2
  138.9 2.6 copy.56
  141.5 2.2 fusion.13
  143.7 5.5 %collective-permute-start.9 = (f32[16,128,128]{2,1,0:T(8,128)S(1)}, f32[16,128,128]{2,1,0:T(8,128)S(1)}, u32[]{:S(2)}, u32[]{:S(2)}) collective-permute-start(f32[16,128,128]{2,1,0:T(8,128)S(1)} %fusion.13), channel_id=1, source_target_pairs={{1,0},{2,1},{3,2},{4,3},{5,4},{6,5},{7,6},{8,7},{9,8},{10,9},{11,1... | collective-permute-start | bytes 3145736 | tf_op jit(solution)/shard_map/ppermute | solution.py:13
  149.2 12.3 %collective-permute-done.9 = f32[16,128,128]{2,1,0:T(8,128)S(1)} collective-permute-done((f32[16,128,128]{2,1,0:T(8,128)S(1)}, f32[16,128,128]{2,1,0:T(8,128)S(1)}, u32[]{:S(2)}, u32[]{:S(2)}) %collective-permute-start.9) | collective-permute-done | bytes 1048608 | tf_op jit(solution)/shard_map/ppermute | solution.py:13
  161.5 1.9 collective-permute-start.11
  165.2 2.9 collective-permute-start.10
  168.0 9.7 %collective-permute-done.10 = f32[1,1,1]{2,1,0:T(1,128)} collective-permute-done((f32[1,1,1]{2,1,0:T(1,128)}, f32[1,1,1]{2,1,0:T(1,128)}, u32[]{:S(2)}, u32[]{:S(2)}) %collective-permute-start.10) | collective-permute-done | bytes 36 | tf_op jit(solution)/shard_map/ppermute | solution.py:13
  181.0 1.9 collective-permute-start.12
  182.9 27.1 %collective-permute-done.12 = f32[1,1,1]{2,1,0:T(1,128)} collective-permute-done((f32[1,1,1]{2,1,0:T(1,128)}, f32[1,1,1]{2,1,0:T(1,128)}, u32[]{:S(2)}, u32[]{:S(2)}) %collective-permute-start.12) | collective-permute-done | bytes 36 | tf_op jit(solution)/shard_map/ppermute | solution.py:13
  211.3 8.5 %collective-permute-done.13 = f32[16,128,128]{2,1,0:T(8,128)S(1)} collective-permute-done((f32[16,128,128]{2,1,0:T(8,128)S(1)}, f32[16,128,128]{2,1,0:T(8,128)S(1)}, u32[]{:S(2)}, u32[]{:S(2)}) %collective-permute-start.13) | collective-permute-done | bytes 1048608 | tf_op jit(solution)/shard_map/ppermute | solution.py:13
  220.0 1.4 collective-permute-start.15
  222.7 12.0 %collective-permute-done.14 = f32[1,1,1]{2,1,0:T(1,128)} collective-permute-done((f32[1,1,1]{2,1,0:T(1,128)}, f32[1,1,1]{2,1,0:T(1,128)}, u32[]{:S(2)}, u32[]{:S(2)}) %collective-permute-start.14) | collective-permute-done | bytes 36 | tf_op jit(solution)/shard_map/ppermute | solution.py:13
  235.3 1.5 collective-permute-start.16
  236.8 21.9 %collective-permute-done.16 = f32[1,1,1]{2,1,0:T(1,128)} collective-permute-done((f32[1,1,1]{2,1,0:T(1,128)}, f32[1,1,1]{2,1,0:T(1,128)}, u32[]{:S(2)}, u32[]{:S(2)}) %collective-permute-start.16) | collective-permute-done | bytes 36 | tf_op jit(solution)/shard_map/ppermute | solution.py:13
  259.4 1.7 select_convert_fusion
  261.2 1.6 fusion.30
  263.4 1.4 collective-permute-start.17
  264.9 1.7 fusion.4
  266.6 2.6 copy.50
  269.2 4.2 %fusion.31 = f32[16,128,384]{2,1,0:T(8,128)S(1)} fusion(bf16[384,16,128]{0,2,1:T(8,128)(2,1)} %bitcast.99, bf16[16,384,384]{2,1,0:T(8,128)(2,1)} %copy-done.2), kind=kOutput, calls=%fused_computation.59 | convolution fusion | flops 603979776 | bytes 9437184 | tf_op jit(solution)/shard_map/hts,the->she/dot_general | solution.py:97
  273.7 2.9 fusion.32
  276.6 38.4 %collective-permute-done.17 = f32[16,128,128]{2,1,0:T(8,128)} collective-permute-done((f32[16,128,128]{2,1,0:T(8,128)S(1)}, f32[16,128,128]{2,1,0:T(8,128)}, u32[]{:S(2)}, u32[]{:S(2)}) %collective-permute-start.17) | collective-permute-done | bytes 1048608 | tf_op jit(solution)/shard_map/ppermute | solution.py:13
  315.0 1.3 add_convert_fusion.1
  317.2 1.6 copy.52
  318.9 2.9 fusion.3
  321.7 1.6 copy.51
  (62 shorter events, 14.5 us)
Async XLA Ops:
  0.6 9.8 %copy-start = (bf16[384,2048]{1,0:T(8,128)(2,1)S(1)}, bf16[384,2048]{1,0:T(8,128)(2,1)}, u32[]{:S(2)}) copy-start(bf16[384,2048]{1,0:T(8,128)(2,1)} %param.7) | copy-start | bytes 4718596
  9.2 1.8 copy-start.8
  11.0 16.2 %collective-permute-start = (f32[16,128,128]{2,1,0:T(8,128)S(1)}, f32[16,128,128]{2,1,0:T(8,128)}, u32[]{:S(2)}, u32[]{:S(2)}) collective-permute-start(f32[16,128,128]{2,1,0:T(8,128)S(1)} %fusion.9), channel_id=1, source_target_pairs={{0,1},{1,2},{2,3},{3,4},{4,5},{5,6},{6,7},{7,8},{8,9},{9,10},{10,1... | collective-permute-start | bytes 3145736 | tf_op jit(solution)/shard_map/ppermute | solution.py:13
  27.2 17.2 %collective-permute-start.2 = (f32[16,128,128]{2,1,0:T(8,128)}, f32[16,128,128]{2,1,0:T(8,128)S(1)}, u32[]{:S(2)}, u32[]{:S(2)}) collective-permute-start(f32[16,128,128]{2,1,0:T(8,128)} %collective-permute-done), channel_id=1, source_target_pairs={{0,1},{1,2},{2,3},{3,4},{4,5},{5,6},{6,7},{7,8},{8,9},{9,10},{10,1... | collective-permute-start | bytes 3145736 | tf_op jit(solution)/shard_map/ppermute | solution.py:13
  32.4 11.4 %collective-permute-start.1 = (f32[1,1,1]{2,1,0:T(1,128)}, f32[1,1,1]{2,1,0:T(1,128)}, u32[]{:S(2)}, u32[]{:S(2)}) collective-permute-start(f32[1,1,1]{2,1,0:T(1,128)} %bitcast.5), channel_id=1, source_target_pairs={{0,1},{1,2},{2,3},{3,4},{4,5},{5,6},{6,7},{7,8},{8,9},{9,10},{10,1... | collective-permute-start | bytes 20 | tf_op jit(solution)/shard_map/ppermute | solution.py:13
  45.8 27.5 %collective-permute-start.4 = (f32[16,128,128]{2,1,0:T(8,128)S(1)}, f32[16,128,128]{2,1,0:T(8,128)S(1)}, u32[]{:S(2)}, u32[]{:S(2)}) collective-permute-start(f32[16,128,128]{2,1,0:T(8,128)S(1)} %multiply_add_fusion.5), channel_id=1, source_target_pairs={{0,2},{1,3},{2,4},{3,5},{4,6},{5,7},{6,8},{7,9},{8,10},{9,11},{10,... | collective-permute-start | bytes 3145736 | tf_op jit(solution)/shard_map/ppermute | solution.py:13
  49.9 22.1 %collective-permute-start.3 = (f32[1,1,1]{2,1,0:T(1,128)}, f32[1,1,1]{2,1,0:T(1,128)}, u32[]{:S(2)}, u32[]{:S(2)}) collective-permute-start(f32[1,1,1]{2,1,0:T(1,128)} %collective-permute-done.1), channel_id=1, source_target_pairs={{0,1},{1,2},{2,3},{3,4},{4,5},{5,6},{6,7},{7,8},{8,9},{9,10},{10,1... | collective-permute-start | bytes 20 | tf_op jit(solution)/shard_map/ppermute | solution.py:13
  74.4 24.6 %collective-permute-start.6 = (f32[16,128,128]{2,1,0:T(8,128)}, f32[16,128,128]{2,1,0:T(8,128)}, u32[]{:S(2)}, u32[]{:S(2)}) collective-permute-start(f32[16,128,128]{2,1,0:T(8,128)} %multiply_add_fusion.4), channel_id=1, source_target_pairs={{0,4},{1,5},{2,6},{3,7},{4,8},{5,9},{6,10},{7,11},{8,12},{9,13},{1... | collective-permute-start | bytes 3145736 | tf_op jit(solution)/shard_map/ppermute | solution.py:13
  80.1 61.4 %copy-start.4 = (bf16[384,2048]{0,1:T(8,128)(2,1)}, bf16[384,2048]{0,1:T(8,128)(2,1)S(1)}, u32[]{:S(2)}) copy-start(bf16[384,2048]{0,1:T(8,128)(2,1)S(1)} %copy.55) | copy-start | bytes 4718596
  80.2 3.5 %collective-permute-start.5 = (f32[1,1,1]{2,1,0:T(1,128)}, f32[1,1,1]{2,1,0:T(1,128)}, u32[]{:S(2)}, u32[]{:S(2)}) collective-permute-start(f32[1,1,1]{2,1,0:T(1,128)} %max.18), channel_id=1, source_target_pairs={{0,2},{1,3},{2,4},{3,5},{4,6},{5,7},{6,8},{7,9},{8,10},{9,11},{10,... | collective-permute-start | bytes 20 | tf_op jit(solution)/shard_map/ppermute | solution.py:13
  99.0 7.5 %copy-start.10 = (bf16[384,2048]{1,0:T(8,128)(2,1)S(1)}, bf16[384,2048]{1,0:T(8,128)(2,1)}, u32[]{:S(2)}) copy-start(bf16[384,2048]{1,0:T(8,128)(2,1)} %param.6) | copy-start | bytes 4718596
  100.8 25.9 %collective-permute-start.8 = (f32[16,128,128]{2,1,0:T(8,128)S(1)}, f32[16,128,128]{2,1,0:T(8,128)S(1)}, u32[]{:S(2)}, u32[]{:S(2)}) collective-permute-start(f32[16,128,128]{2,1,0:T(8,128)S(1)} %multiply_add_fusion.3), channel_id=1, source_target_pairs={{0,8},{1,9},{2,10},{3,11},{4,12},{5,13},{6,14},{7,15},{16,24},{17,... | collective-permute-start | bytes 3145736 | tf_op jit(solution)/shard_map/ppermute | solution.py:13
  108.2 2.1 copy-start.2
  110.4 15.7 %collective-permute-start.7 = (f32[1,1,1]{2,1,0:T(1,128)}, f32[1,1,1]{2,1,0:T(1,128)}, u32[]{:S(2)}, u32[]{:S(2)}) collective-permute-start(f32[1,1,1]{2,1,0:T(1,128)} %max.19), channel_id=1, source_target_pairs={{0,4},{1,5},{2,6},{3,7},{4,8},{5,9},{6,10},{7,11},{8,12},{9,13},{1... | collective-permute-start | bytes 20 | tf_op jit(solution)/shard_map/ppermute | solution.py:13
  126.8 2.4 copy-start.12
  132.8 3.3 %copy-start.1 = (f32[384,2048]{1,0:T(8,128)S(1)}, f32[384,2048]{1,0:T(8,128)}, u32[]{:S(2)}) copy-start(f32[384,2048]{1,0:T(8,128)} %copy.38) | copy-start | bytes 9437188
  132.8 3.8 %copy-start.7 = (bf16[384,2048]{1,0:T(8,128)(2,1)S(1)}, bf16[384,2048]{1,0:T(8,128)(2,1)}, u32[]{:S(2)}) copy-start(bf16[384,2048]{1,0:T(8,128)(2,1)} %param.9) | copy-start | bytes 4718596
  143.7 17.8 %collective-permute-start.9 = (f32[16,128,128]{2,1,0:T(8,128)S(1)}, f32[16,128,128]{2,1,0:T(8,128)S(1)}, u32[]{:S(2)}, u32[]{:S(2)}) collective-permute-start(f32[16,128,128]{2,1,0:T(8,128)S(1)} %fusion.13), channel_id=1, source_target_pairs={{1,0},{2,1},{3,2},{4,3},{5,4},{6,5},{7,6},{8,7},{9,8},{10,9},{11,1... | collective-permute-start | bytes 3145736 | tf_op jit(solution)/shard_map/ppermute | solution.py:13
  161.5 16.8 %collective-permute-start.11 = (f32[16,128,128]{2,1,0:T(8,128)S(1)}, f32[16,128,128]{2,1,0:T(8,128)}, u32[]{:S(2)}, u32[]{:S(2)}) collective-permute-start(f32[16,128,128]{2,1,0:T(8,128)S(1)} %collective-permute-done.9), channel_id=1, source_target_pairs={{1,0},{2,1},{3,2},{4,3},{5,4},{6,5},{7,6},{8,7},{9,8},{10,9},{11,1... | collective-permute-start | bytes 3145736 | tf_op jit(solution)/shard_map/ppermute | solution.py:13
  165.2 12.6 %collective-permute-start.10 = (f32[1,1,1]{2,1,0:T(1,128)}, f32[1,1,1]{2,1,0:T(1,128)}, u32[]{:S(2)}, u32[]{:S(2)}) collective-permute-start(f32[1,1,1]{2,1,0:T(1,128)} %bitcast.16), channel_id=1, source_target_pairs={{1,0},{2,1},{3,2},{4,3},{5,4},{6,5},{7,6},{8,7},{9,8},{10,9},{11,1... | collective-permute-start | bytes 20 | tf_op jit(solution)/shard_map/ppermute | solution.py:13
  179.7 40.1 %collective-permute-start.13 = (f32[16,128,128]{2,1,0:T(8,128)S(1)}, f32[16,128,128]{2,1,0:T(8,128)S(1)}, u32[]{:S(2)}, u32[]{:S(2)}) collective-permute-start(f32[16,128,128]{2,1,0:T(8,128)S(1)} %multiply_add_fusion.2), channel_id=1, source_target_pairs={{2,0},{3,1},{4,2},{5,3},{6,4},{7,5},{8,6},{9,7},{10,8},{11,9},{12,... | collective-permute-start | bytes 3145736 | tf_op jit(solution)/shard_map/ppermute | solution.py:13
  181.0 29.0 %collective-permute-start.12 = (f32[1,1,1]{2,1,0:T(1,128)}, f32[1,1,1]{2,1,0:T(1,128)}, u32[]{:S(2)}, u32[]{:S(2)}) collective-permute-start(f32[1,1,1]{2,1,0:T(1,128)} %collective-permute-done.10), channel_id=1, source_target_pairs={{1,0},{2,1},{3,2},{4,3},{5,4},{6,5},{7,6},{8,7},{9,8},{10,9},{11,1... | collective-permute-start | bytes 20 | tf_op jit(solution)/shard_map/ppermute | solution.py:13
  219.8 39.6 %copy-start.6 = (bf16[384,2048]{0,1:T(8,128)(2,1)S(1)}, bf16[384,2048]{0,1:T(8,128)(2,1)}, u32[]{:S(2)}) copy-start(bf16[384,2048]{0,1:T(8,128)(2,1)} %copy.56) | copy-start | bytes 4718596
  220.0 43.4 %collective-permute-start.15 = (f32[16,128,128]{2,1,0:T(8,128)S(1)}, f32[16,128,128]{2,1,0:T(8,128)S(1)}, u32[]{:S(2)}, u32[]{:S(2)}) collective-permute-start(f32[16,128,128]{2,1,0:T(8,128)S(1)} %multiply_add_fusion.1), channel_id=1, source_target_pairs={{4,0},{5,1},{6,2},{7,3},{8,4},{9,5},{10,6},{11,7},{12,8},{13,9},{1... | collective-permute-start | bytes 3145736 | tf_op jit(solution)/shard_map/ppermute | solution.py:13
  221.4 13.3 %collective-permute-start.14 = (f32[1,1,1]{2,1,0:T(1,128)}, f32[1,1,1]{2,1,0:T(1,128)}, u32[]{:S(2)}, u32[]{:S(2)}) collective-permute-start(f32[1,1,1]{2,1,0:T(1,128)} %max.21), channel_id=1, source_target_pairs={{2,0},{3,1},{4,2},{5,3},{6,4},{7,5},{8,6},{9,7},{10,8},{11,9},{12,... | collective-permute-start | bytes 20 | tf_op jit(solution)/shard_map/ppermute | solution.py:13
  235.3 23.4 %collective-permute-start.16 = (f32[1,1,1]{2,1,0:T(1,128)}, f32[1,1,1]{2,1,0:T(1,128)}, u32[]{:S(2)}, u32[]{:S(2)}) collective-permute-start(f32[1,1,1]{2,1,0:T(1,128)} %max.22), channel_id=1, source_target_pairs={{4,0},{5,1},{6,2},{7,3},{8,4},{9,5},{10,6},{11,7},{12,8},{13,9},{1... | collective-permute-start | bytes 20 | tf_op jit(solution)/shard_map/ppermute | solution.py:13
  259.4 1.8 copy-start.9
  261.1 2.2 copy-start.3
  263.3 1.6 copy-start.13
  263.4 51.6 %collective-permute-start.17 = (f32[16,128,128]{2,1,0:T(8,128)S(1)}, f32[16,128,128]{2,1,0:T(8,128)}, u32[]{:S(2)}, u32[]{:S(2)}) collective-permute-start(f32[16,128,128]{2,1,0:T(8,128)S(1)} %multiply_add_fusion), channel_id=1, source_target_pairs={{8,0},{9,1},{10,2},{11,3},{12,4},{13,5},{14,6},{15,7},{24,16},{25,... | collective-permute-start | bytes 3145736 | tf_op jit(solution)/shard_map/ppermute | solution.py:13
  266.6 6.8 %slice-start = ((s8[4718592]{0:T(1024)(128)(4,1)}), s8[524288]{0:T(1024)(128)(4,1)S(1)}, s32[]{:S(2)}) async-start(s8[4718592]{0:T(1024)(128)(4,1)} %bitcast.92), calls=%async_computation | async-start | bytes 1048576
  269.2 4.2 %slice-start.1 = ((s8[4718592]{0:T(1024)(128)(4,1)}), s8[4194304]{0:T(1024)(128)(4,1)S(1)}, s32[]{:S(2)}) async-start(s8[4718592]{0:T(1024)(128)(4,1)} %bitcast.92), calls=%async_computation.1 | async-start | bytes 8388608
  269.2 4.5 %copy-start.5 = (bf16[384,2048]{0,1:T(8,128)(2,1)S(1)}, bf16[384,2048]{0,1:T(8,128)(2,1)}, u32[]{:S(2)}) copy-start(bf16[384,2048]{0,1:T(8,128)(2,1)} %copy-done.4) | copy-start | bytes 4718596
  276.6 39.8 %copy-start.11 = (bf16[384,2048]{1,0:T(8,128)(2,1)S(1)}, bf16[384,2048]{1,0:T(8,128)(2,1)}, u32[]{:S(2)}) copy-start(bf16[384,2048]{1,0:T(8,128)(2,1)} %param.6) | copy-start | bytes 4718596
  316.4 0.8 copy-start.14
where the time goes:
time: 326 us; the launch traced here: 323 us
  waiting for transfers between devices  173 us (53%)
  starting transfers between devices  77.6 us (24%)
  matrix products  24.2 us (7%)
  local copies, waits for them, and re-layouts  21.8 us (7%)
  other arithmetic  16.4 us (5%)
  between operations  10.4 us (3%)
    ppermute x18, waiting for transfers between devices, passed_along(): lax.ppermute(value, axis, [(source, source + steps) for source in range(f...  173 us
    ppermute x18, starting transfers between devices, passed_along(): lax.ppermute(value, axis, [(source, source + steps) for source in range(f...  77.6 us
    unnamed x38, local copies, waits for them, and re-layouts  11 us
  transfers between devices with their start and end apart: 18, of which 10 were waited for; matrix products, arithmetic and copies ran while one was open for 6% of the time, Pallas kernels for 0%

commit v1 on v0

--- a/solution.py
+++ b/solution.py
@@ -30,6 +30,68 @@
     return carried_pair
 
 
+GROUP = 4
+
+
+def member_exchange(pieces, axis):
+    count = lax.axis_size(axis)
+    member = lax.axis_index(axis) % GROUP
+    got = [lax.dynamic_index_in_dim(pieces, member, keepdims=False)]
+    for offset in range(1, GROUP):
+        piece = lax.dynamic_index_in_dim(pieces, (member + offset) % GROUP, keepdims=False)
+        pairs = [
+            (row + index, row + (index + offset) % GROUP)
+            for row in range(0, count, GROUP)
+            for index in range(GROUP)
+        ]
+        got.append(lax.ppermute(piece, axis, pairs))
+    return jnp.take(jnp.stack(got), (member - jnp.arange(GROUP)) % GROUP, axis=0)
+
+
+def row_scan(state, keep_row, direction):
+    count = lax.axis_size("seq")
+    heads = state.shape[0]
+    pieces = state.reshape((GROUP, heads // GROUP) + state.shape[1:])
+    mine = member_exchange(pieces, "seq")
+    order = range(GROUP) if direction > 0 else range(GROUP - 1, -1, -1)
+    inner = [None] * GROUP
+    inner_keep = [None] * GROUP
+    total = jnp.zeros_like(mine[0])
+    total_keep = jnp.ones((), jnp.float32)
+    for index in order:
+        inner[index] = total
+        inner_keep[index] = total_keep
+        total = mine[index] + keep_row[index] * total
+        total_keep = total_keep * keep_row[index]
+    shift = GROUP * direction
+    pairs = [(source, source + shift) for source in range(count) if 0 <= source + shift < count]
+    window = total
+    for _ in range(-(-SPAN // GROUP) - 1):
+        window = total + total_keep * lax.ppermute(window, "seq", pairs)
+    entering = lax.ppermute(window, "seq", pairs)
+    scanned = jnp.stack([inner[index] + inner_keep[index] * entering for index in range(GROUP)])
+    return member_exchange(scanned, "seq").reshape(state.shape)
+
+
+def row_flags(starts, row_count):
+    blocks = (lax.axis_index("seq") // GROUP) * GROUP + lax.iota(jnp.int32, GROUP)
+    first = blocks * row_count
+    last = first + row_count - 1
+    doc_first = jnp.sum((starts[None, :] <= first[:, None]).astype(jnp.int32), axis=1)
+    doc_last = jnp.sum((starts[None, :] <= last[:, None]).astype(jnp.int32), axis=1)
+    at_first = jnp.any(starts[None, :] == first[:, None], axis=1)
+    inside = (starts[None, :] >= first[:, None]) & (starts[None, :] <= last[:, None])
+    has_start = jnp.any(inside, axis=1)
+    stops_back = (doc_first != doc_last) | at_first
+    return has_start, stops_back
+
+
+def scan_states(state, keep_row, fallback_flag, direction):
+    if lax.axis_size("seq") % GROUP == 0 and state.shape[0] % GROUP == 0:
+        return row_scan(state, keep_row, direction)
+    return windowed_prefix((state, fallback_flag), direction)[0]
+
+
 def shards(queries, keys, values, lengths, out_grad):
     row_count, feat_width = queries.shape
     head_count = feat_width // HEAD
@@ -55,7 +117,9 @@
         "shd,she->hde", tail_keys, value_heads, preferred_element_type=jnp.float32
     )
     start_flag = has_start.astype(jnp.float32).reshape(1, 1, 1)
-    prefix = windowed_prefix((state_local, start_flag), 1)[0]
+    row_start, row_stop = row_flags(starts, row_count)
+    prefix = scan_states(state_local, 1.0 - row_start.astype(jnp.float32), start_flag, 1)
+    prefix = prefix * continues.astype(jnp.float32)
     prefix_low = prefix.astype(jnp.bfloat16)
     carried = jnp.einsum(
         "thd,hde->the", query_heads, prefix_low, preferred_element_type=jnp.float32
@@ -74,7 +138,10 @@
         "thd,the->hde", lead_queries, grad_low, preferred_element_type=jnp.float32
     )
     back_flag = stops_back.astype(jnp.float32).reshape(1, 1, 1)
-    suffix = windowed_prefix((grad_local, back_flag), -1)[0]
+    suffix = scan_states(grad_local, 1.0 - row_stop.astype(jnp.float32), back_flag, -1)
+    next_first = first_row + row_count
+    next_open = (next_first < lax.axis_size("seq") * row_count) & jnp.logical_not(jnp.any(starts == next_first))
+    suffix = suffix * next_open.astype(jnp.float32)
     grad_scores = jnp.einsum(
         "the,she->hts", grad_low, value_heads, preferred_element_type=jnp.float32
     )

time: 326 us -> 192 us (0.59)
  the two profiles are of different devices: /device:TPU:1 before, /device:TPU:0 now
where the time goes in v1:
time: 192 us; the launch traced here: 190 us
  waiting for transfers between devices  51.5 us (27%)
  local copies, waits for them, and re-layouts  36 us (19%)
  other arithmetic  34.5 us (18%)
  matrix products  34 us (18%)
  starting transfers between devices  25.3 us (13%)
  between operations  8.99 us (5%)
    ppermute x12, waiting for transfers between devices, member_exchange(): got.append(lax.ppermute(piece, axis, pairs))  33.8 us
    ppermute x4, waiting for transfers between devices, row_scan(): window = total + total_keep * lax.ppermute(window, 'seq', pairs)  14.2 us
    unnamed x72, local copies, waits for them, and re-layouts  13.2 us
    ppermute x4, starting transfers between devices, row_scan(): window = total + total_keep * lax.ppermute(window, 'seq', pairs)  11.7 us
    gather x4, local copies, waits for them, and re-layouts, member_exchange(): jnp.take(jnp.stack(got), (member - jnp.arange(GROUP)) % GROUP, axis=0)  9.4 us
    ppermute x12, starting transfers between devices, member_exchange(): got.append(lax.ppermute(piece, axis, pairs))  7.98 us
    dot_general x1, matrix products, shards(): jnp.einsum('hts,thd->shd', grad_weights, query_heads, preferred_element_t...  5.68 us
    ppermute x2, starting transfers between devices, row_scan(): entering = lax.ppermute(window, 'seq', pairs)  5.68 us
  transfers between devices with their start and end apart: 18, of which 14 were waited for; matrix products, arithmetic and copies ran while one was open for 14% of the time, Pallas kernels for 0%

profile of v1, /device:TPU:0, one launch (start us, length us, event | category | flops | bytes accessed | tf_op | source)
XLA Modules:
  0.0 190.3 jit_solution(1185236238741750362)
XLA Ops:
  4.3 3.0 %copy.63 = bf16[48,8,16,128]{3,2,1,0:T(8,128)(2,1)} copy(bf16[48,8,16,128]{3,1,2,0:T(8,128)(2,1)} %bitcast.204) | data formatting | bytes 3145728
  7.3 2.1 %copy.35 = bf16[384,16,128]{0,2,1:T(8,128)(2,1)S(1)} copy(bf16[384,16,128]{2,1,0:T(8,128)(2,1)} %bitcast.203) | data formatting | bytes 3145728 | tf_op jit(solution)/shard_map/reshape | solution.py:110
  9.4 1.8 compare_and_fusion.3
  12.0 2.5 %collective-permute-start.2 = (f32[4,128,128]{2,1,0:T(8,128)S(1)}, f32[4,128,128]{2,1,0:T(8,128)S(1)}, u32[]{:S(2)}, u32[]{:S(2)}) collective-permute-start(f32[4,128,128]{2,1,0:T(8,128)S(1)} %get-tuple-element.43), channel_id=1, source_target_pairs={{0,3},{1,0},{2,1},{3,2},{4,7},{5,4},{6,5},{7,6},{8,11},{9,8},{10,9... | collective-permute-start | bytes 786440 | tf_op jit(solution)/shard_map/ppermute | solution.py:47
  17.4 3.6 %collective-permute-done.2 = f32[4,128,128]{2,1,0:T(8,128)S(1)} collective-permute-done((f32[4,128,128]{2,1,0:T(8,128)S(1)}, f32[4,128,128]{2,1,0:T(8,128)S(1)}, u32[]{:S(2)}, u32[]{:S(2)}) %collective-permute-start.2) | collective-permute-done | bytes 262176 | tf_op jit(solution)/shard_map/ppermute | solution.py:47
  21.1 6.5 %collective-permute-done.1 = f32[4,128,128]{2,1,0:T(8,128)S(1)} collective-permute-done((f32[4,128,128]{2,1,0:T(8,128)S(1)}, f32[4,128,128]{2,1,0:T(8,128)S(1)}, u32[]{:S(2)}, u32[]{:S(2)}) %collective-permute-start.1) | collective-permute-done | bytes 262176 | tf_op jit(solution)/shard_map/ppermute | solution.py:47
  28.6 1.8 gather_fusion
  31.7 2.7 %fusion.36 = (f32[4,128,128]{2,1,0:T(8,128)S(1)}, f32[4,128,128]{2,1,0:T(8,128)}) fusion(f32[4,4,128,128]{3,2,1,0:T(8,128)S(1)} %broadcast_select_fusion.1, f32[]{:T(128)} %bitcast.13, f32[]{:T(128)} %bitcast.15, f32[]{:T(128)S(6)} %mul.173, f32[]{:T(128)} %bitcast.17), kind=kLoop, calls=%fused_computation.69 | loop fusion | flops 458752 | bytes 1572880 | tf_op jit(solution)/shard_map/add | solution.py:64
  34.4 3.7 %collective-permute-start.3 = (f32[4,128,128]{2,1,0:T(8,128)S(1)}, f32[4,128,128]{2,1,0:T(8,128)S(1)}, u32[]{:S(2)}, u32[]{:S(2)}) collective-permute-start(f32[4,128,128]{2,1,0:T(8,128)S(1)} %get-tuple-element.22), channel_id=1, source_target_pairs={{0,4},{1,5},{2,6},{3,7},{4,8},{5,9},{6,10},{7,11},{8,12},{9,13},{1... | collective-permute-start | bytes 786440 | tf_op jit(solution)/shard_map/ppermute | solution.py:70
  40.7 2.2 %collective-permute-done.3 = f32[4,128,128]{2,1,0:T(8,128)S(1)} collective-permute-done((f32[4,128,128]{2,1,0:T(8,128)S(1)}, f32[4,128,128]{2,1,0:T(8,128)S(1)}, u32[]{:S(2)}, u32[]{:S(2)}) %collective-permute-start.3) | collective-permute-done | bytes 262176 | tf_op jit(solution)/shard_map/ppermute | solution.py:70
  43.6 5.1 %collective-permute-start.4 = (f32[4,128,128]{2,1,0:T(8,128)}, f32[4,128,128]{2,1,0:T(8,128)}, u32[]{:S(2)}, u32[]{:S(2)}) collective-permute-start(f32[4,128,128]{2,1,0:T(8,128)} %multiply_add_fusion.3), channel_id=1, source_target_pairs={{0,4},{1,5},{2,6},{3,7},{4,8},{5,9},{6,10},{7,11},{8,12},{9,13},{1... | collective-permute-start | bytes 786440 | tf_op jit(solution)/shard_map/ppermute | solution.py:70
  48.7 1.9 copy.59
  53.3 4.4 %collective-permute-start.5 = (f32[4,128,128]{2,1,0:T(8,128)S(1)}, f32[4,128,128]{2,1,0:T(8,128)S(1)}, u32[]{:S(2)}, u32[]{:S(2)}) collective-permute-start(f32[4,128,128]{2,1,0:T(8,128)S(1)} %multiply_add_fusion.2), channel_id=1, source_target_pairs={{0,4},{1,5},{2,6},{3,7},{4,8},{5,9},{6,10},{7,11},{8,12},{9,13},{1... | collective-permute-start | bytes 786440 | tf_op jit(solution)/shard_map/ppermute | solution.py:71
  57.8 3.2 %select_convert_fusion.1 = bf16[16,384,384]{2,1,0:T(8,128)(2,1)S(1)} fusion(pred[384,384]{1,0:T(8,128)(4,1)S(1)} %compare_and_fusion, bf16[384,16,128]{0,2,1:T(8,128)(2,1)S(1)} %bitcast.198, bf16[384,2048]{1,0:T(8,128)(2,1)} %param.8), kind=kOutput, calls=%fused_computation.5 | convolution fusion | flops 608698368 | bytes 8011776 | tf_op jit(solution)/shard_map/thd,shd->hts/dot_general | solution.py:112
  64.7 3.3 %fusion.5 = f32[16,384,128]{1,2,0:T(8,128)} fusion(bf16[16,384,384]{2,1,0:T(8,128)(2,1)S(1)} %select_convert_fusion.1, bf16[384,2048]{1,0:T(8,128)(2,1)S(1)} %copy-done), kind=kOutput, calls=%fused_computation.18 | convolution fusion | flops 603979776 | bytes 9437184 | tf_op jit(solution)/shard_map/hts,she->the/dot_general | solution.py:114
  68.6 1.5 fusion.37
  71.1 5.6 %collective-permute-done.7 = f32[4,128,128]{2,1,0:T(8,128)} collective-permute-done((f32[4,128,128]{2,1,0:T(8,128)}, f32[4,128,128]{2,1,0:T(8,128)}, u32[]{:S(2)}, u32[]{:S(2)}) %collective-permute-start.7) | collective-permute-done | bytes 262176 | tf_op jit(solution)/shard_map/ppermute | solution.py:47
  77.6 2.2 %pad_maximum_fusion.2 = f32[4,4,128,128]{3,2,1,0:T(8,128)} fusion(f32[1,4,128,128]{3,2,1,0:T(8,128)} %bitcast.29, f32[1,4,128,128]{3,2,1,0:T(8,128)} %bitcast.27, f32[1,4,128,128]{3,2,1,0:T(8,128)} %bitcast.25, f32[1,4,128,128]{3,2,1,0:T(8,128)S(1)} %get-tuple-element.38), kind=kLoop, calls=%fused_computation.37 | loop fusion | flops 786432 | bytes 2097152 | tf_op jit(solution)/shard_map/stack | solution.py:48
  79.7 2.9 %gather_fusion.1 = f32[4,4,128,128]{3,2,1,0:T(8,128)} fusion(f32[4,4,128,128]{3,2,1,0:T(8,128)} %pad_maximum_fusion.2, s32[1024]{0:T(1024)} %copy-done.19), kind=kCustom, calls=%fused_computation.1.clone | custom fusion | bytes 2097168 | tf_op jit(solution)/shard_map/jit(_take)/gather | solution.py:48
  84.1 4.4 %multiply_reduce_fusion = (f32[384]{0:T(512)S(1)}, f32[384,16,128]{0,2,1:T(8,128)}) fusion(bf16[16,128,128]{2,1,0:T(8,128)(2,1)S(1)} %bitcast.208, bf16[384,16,128]{0,2,1:T(8,128)(2,1)S(1)} %bitcast.199, pred[384]{0:T(512)(128)(4,1)S(1)} %copy-done.27, f32[16,384,128]{1,2,0:T(8,128)} %fusion.5), kind=kOutput, calls=%fused_computation.17 | convolution fusion | flops 204471936 | bytes 8390528 | tf_op jit(solution)/shard_map/thd,hde->the/dot_general | solution.py:124
  88.6 3.7 %copy.39 = f32[384,2048]{1,0:T(8,128)} copy(f32[384,2048]{0,1:T(8,128)} %bitcast.202) | data formatting | bytes 6291456 | tf_op jit(solution)/shard_map/reshape | solution.py:127
  92.3 2.6 %fusion = f32[384]{0:T(512)S(1)} fusion(bf16[384,2048]{1,0:T(8,128)(2,1)S(1)} %copy-done.10, f32[384,2048]{1,0:T(8,128)} %copy.39, f32[384]{0:T(512)S(1)} %add_sqrt_fusion), kind=kLoop, calls=%fused_computation.8 | loop fusion | flops 3145344 | bytes 4721664 | tf_op jit(solution)/shard_map/reduce_sum | solution.py:134
  95.1 2.4 %fusion.2 = (bf16[384,2048]{1,0:T(8,128)(2,1)}, bf16[384,2048]{1,0:T(8,128)(2,1)}) fusion(bf16[384,2048]{1,0:T(8,128)(2,1)S(1)} %copy-done.10, f32[384]{0:T(512)S(1)} %broadcast_multiply_fusion, f32[384]{0:T(512)S(1)} %add_sqrt_fusion, f32[384,2048]{1,0:T(8,128)S(1)} %copy-done.1), kind=kLoop, calls=%fused_computation.10 | loop fusion | flops 5505024 | bytes 7867392 | tf_op jit(solution)/shard_map/convert_element_type | solution.py:135
  97.5 1.9 copy.60
  99.4 2.2 %fusion.14 = f32[16,128,128]{2,1,0:T(8,128)S(1)} fusion(bf16[384,16,128]{0,2,1:T(8,128)(2,1)S(1)} %bitcast.194, bf16[384,16,128]{0,2,1:T(8,128)(2,1)} %bitcast.200, pred[384]{0:T(512)(128)(4,1)S(1)} %copy-done.27), kind=kOutput, calls=%fused_computation.27 | convolution fusion | flops 202113024 | bytes 4194688 | tf_op jit(solution)/shard_map/thd,the->hde/dot_general | solution.py:137
  102.5 1.6 collective-permute-start.10
  108.4 8.8 %collective-permute-done.10 = f32[4,128,128]{2,1,0:T(8,128)} collective-permute-done((f32[4,128,128]{2,1,0:T(8,128)}, f32[4,128,128]{2,1,0:T(8,128)}, u32[]{:S(2)}, u32[]{:S(2)}) %collective-permute-start.10) | collective-permute-done | bytes 262176 | tf_op jit(solution)/shard_map/ppermute | solution.py:47
  117.2 2.2 %pad_maximum_fusion.3 = f32[4,4,128,128]{3,2,1,0:T(8,128)} fusion(f32[1,4,128,128]{3,2,1,0:T(8,128)} %bitcast.43, f32[1,4,128,128]{3,2,1,0:T(8,128)} %bitcast.41, f32[1,4,128,128]{3,2,1,0:T(8,128)} %bitcast.39, f32[1,4,128,128]{3,2,1,0:T(8,128)S(1)} %get-tuple-element.34), kind=kLoop, calls=%fused_computation.38 | loop fusion | flops 786432 | bytes 2097152 | tf_op jit(solution)/shard_map/stack | solution.py:48
  119.4 2.9 %gather_fusion.2 = f32[4,4,128,128]{3,2,1,0:T(8,128)} fusion(f32[4,4,128,128]{3,2,1,0:T(8,128)} %pad_maximum_fusion.3, s32[1024]{0:T(1024)} %copy-done.19), kind=kCustom, calls=%fused_computation.2.clone | custom fusion | bytes 2097168 | tf_op jit(solution)/shard_map/jit(_take)/gather | solution.py:48
  123.7 2.0 %fusion.29 = (f32[4,128,128]{2,1,0:T(8,128)S(1)}, f32[4,128,128]{2,1,0:T(8,128)S(1)}) fusion(f32[4,4,128,128]{3,2,1,0:T(8,128)S(1)} %broadcast_select_fusion, f32[]{:T(128)} %bitcast.51, f32[]{:T(128)} %bitcast.45, f32[]{:T(128)S(6)} %mul.198, f32[]{:T(128)} %bitcast.47), kind=kLoop, calls=%fused_computation.55 | loop fusion | flops 458752 | bytes 1572880 | tf_op jit(solution)/shard_map/add | solution.py:64
  125.7 1.5 collective-permute-start.12
  127.2 1.7 select_convert_fusion
  128.9 5.7 %collective-permute-done.12 = f32[4,128,128]{2,1,0:T(8,128)S(1)} collective-permute-done((f32[4,128,128]{2,1,0:T(8,128)S(1)}, f32[4,128,128]{2,1,0:T(8,128)S(1)}, u32[]{:S(2)}, u32[]{:S(2)}) %collective-permute-start.12) | collective-permute-done | bytes 262176 | tf_op jit(solution)/shard_map/ppermute | solution.py:70
  136.1 1.6 fusion.49
  137.7 5.4 %collective-permute-done.13 = f32[4,128,128]{2,1,0:T(8,128)S(1)} collective-permute-done((f32[4,128,128]{2,1,0:T(8,128)S(1)}, f32[4,128,128]{2,1,0:T(8,128)S(1)}, u32[]{:S(2)}, u32[]{:S(2)}) %collective-permute-start.13) | collective-permute-done | bytes 262176 | tf_op jit(solution)/shard_map/ppermute | solution.py:70
  145.1 1.8 fusion.4
  146.9 2.6 %copy.52 = bf16[384,2048]{1,0:T(8,128)(2,1)} copy(bf16[384,2048]{0,1:T(8,128)(2,1)} %bitcast.205) | data formatting | bytes 3145728
  149.5 2.9 %collective-permute-done.14 = f32[4,128,128]{2,1,0:T(8,128)} collective-permute-done((f32[4,128,128]{2,1,0:T(8,128)}, f32[4,128,128]{2,1,0:T(8,128)}, u32[]{:S(2)}, u32[]{:S(2)}) %collective-permute-start.14) | collective-permute-done | bytes 262176 | tf_op jit(solution)/shard_map/ppermute | solution.py:71
  152.4 2.5 %add_bitcast_fusion.2 = (f32[1,4,128,128]{3,2,1,0:T(8,128)S(1)}, f32[1,4,128,128]{3,2,1,0:T(8,128)S(1)}, f32[1,4,128,128]{3,2,1,0:T(8,128)S(1)}) fusion(f32[4,128,128]{2,1,0:T(8,128)} %collective-permute-done.14, f32[]{:T(128)S(6)} %mul.202, f32[4,128,128]{2,1,0:T(8,128)S(1)} %get-tuple-element.20, f32[]{:T(128)} %bitcast.45, ...), kind=kLoop, calls=%fused_computation.75 | loop fusion | flops 589824 | bytes 1835028 | tf_op jit(solution)/shard_map/stack | solution.py:72
  156.1 2.1 %collective-permute-start.16 = (f32[4,128,128]{2,1,0:T(8,128)S(1)}, f32[4,128,128]{2,1,0:T(8,128)S(1)}, u32[]{:S(2)}, u32[]{:S(2)}) collective-permute-start(f32[4,128,128]{2,1,0:T(8,128)S(1)} %get-tuple-element.32), channel_id=1, source_target_pairs={{0,2},{1,3},{2,0},{3,1},{4,6},{5,7},{6,4},{7,5},{8,10},{9,11},{10,... | collective-permute-start | bytes 786440 | tf_op jit(solution)/shard_map/ppermute | solution.py:47
  158.3 5.3 %fusion.50 = f32[16,128,384]{2,1,0:T(8,128)} fusion(bf16[384,16,128]{0,2,1:T(8,128)(2,1)S(1)} %bitcast.197, bf16[16,384,384]{2,1,0:T(8,128)(2,1)} %copy-done.2), kind=kOutput, calls=%fused_computation.130 | convolution fusion | flops 603979776 | bytes 9437184 | tf_op jit(solution)/shard_map/hts,the->she/dot_general | solution.py:164
  163.6 7.1 %collective-permute-done.16 = f32[4,128,128]{2,1,0:T(8,128)S(1)} collective-permute-done((f32[4,128,128]{2,1,0:T(8,128)S(1)}, f32[4,128,128]{2,1,0:T(8,128)S(1)}, u32[]{:S(2)}, u32[]{:S(2)}) %collective-permute-start.16) | collective-permute-done | bytes 262176 | tf_op jit(solution)/shard_map/ppermute | solution.py:47
  170.8 1.7 gather_fusion.3
  174.0 2.4 %fusion.7 = f32[16,128,384]{2,1,0:T(8,128)} fusion(bf16[16,128,128]{2,1,0:T(8,128)(2,1)S(1)} %bitcast.210, bf16[384,2048]{1,0:T(8,128)(2,1)S(1)} %copy-done), kind=kOutput, calls=%fused_computation.20 | convolution fusion | flops 201326592 | bytes 5242880 | tf_op jit(solution)/shard_map/she,hde->shd/dot_general | solution.py:160
  177.4 1.9 %add_convert_fusion = bf16[16,128,384]{2,1,0:T(8,128)(2,1)} fusion(f32[16,128,384]{2,1,0:T(8,128)S(1)} %copy-done.6, bf16[16,128,128]{2,1,0:T(8,128)(2,1)S(1)} %bitcast.211, pred[384]{0:T(512)(128)(4,1)S(1)} %copy-done.26, bf16[384,2048]{1,0:T(8,128)(2,1)S(1)} %copy-done.13), kind=kOutput, calls=%fused_computation.16 | convolution fusion | flops 203685888 | bytes 6816128 | tf_op jit(solution)/shard_map/shd,hde->she/dot_general | solution.py:165
  179.4 2.7 %copy.54 = bf16[384,2048]{1,0:T(8,128)(2,1)} copy(bf16[384,2048]{0,1:T(8,128)(2,1)} %bitcast.206) | data formatting | bytes 3145728
  182.1 5.7 %fusion.3 = bf16[384,16,128]{0,2,1:T(8,128)(2,1)} fusion(f32[16,128,384]{2,1,0:T(8,128)} %fusion.7, bf16[384,16,128]{0,2,1:T(8,128)(2,1)S(1)} %bitcast.201, bf16[16,384,384]{2,1,0:T(8,128)(2,1)} %copy-done.3, pred[384]{0:T(512)(128)(4,1)S(1)} %copy-done.26), kind=kOutput, calls=%fused_computation.12 | convolution fusion | flops 606339072 | bytes 11010432 | tf_op jit(solution)/shard_map/hts,thd->shd/dot_general | solution.py:157
  187.8 2.6 %copy.53 = bf16[384,2048]{1,0:T(8,128)(2,1)} copy(bf16[384,2048]{0,1:T(8,128)(2,1)} %bitcast.207) | data formatting | bytes 3145728
  (123 shorter events, 29.7 us)
Async XLA Ops:
  0.6 10.6 %copy-start = (bf16[384,2048]{1,0:T(8,128)(2,1)S(1)}, bf16[384,2048]{1,0:T(8,128)(2,1)}, u32[]{:S(2)}) copy-start(bf16[384,2048]{1,0:T(8,128)(2,1)} %param.9) | copy-start | bytes 4718596
  0.7 6.5 %copy-start.18 = (s32[384]{0:T(512)}, s32[384]{0:T(512)S(1)}, u32[]{:S(2)}) copy-start(s32[384]{0:T(512)S(1)} %iota_add_fusion) | copy-start | bytes 4612
  3.0 12.3 %copy-start.24 = (s32[4]{0:T(128)}, s32[4]{0:T(128)S(1)}, u32[]{:S(2)}) copy-start(s32[4]{0:T(128)S(1)} %get-tuple-element.21) | copy-start | bytes 52
  3.7 5.7 %copy-start.17 = (s32[384]{0:T(512)}, s32[384]{0:T(512)S(1)}, u32[]{:S(2)}) copy-start(s32[384]{0:T(512)S(1)} %convert_reduce_fusion) | copy-start | bytes 4612
  9.4 2.5 %copy-start.11 = (bf16[384,16,128]{0,2,1:T(8,128)(2,1)}, bf16[384,16,128]{0,2,1:T(8,128)(2,1)S(1)}, u32[]{:S(2)}) copy-start(bf16[384,16,128]{0,2,1:T(8,128)(2,1)S(1)} %copy.35) | copy-start | bytes 4718596
  12.0 9.1 %collective-permute-start.2 = (f32[4,128,128]{2,1,0:T(8,128)S(1)}, f32[4,128,128]{2,1,0:T(8,128)S(1)}, u32[]{:S(2)}, u32[]{:S(2)}) collective-permute-start(f32[4,128,128]{2,1,0:T(8,128)S(1)} %get-tuple-element.43), channel_id=1, source_target_pairs={{0,3},{1,0},{2,1},{3,2},{4,7},{5,4},{6,5},{7,6},{8,11},{9,8},{10,9... | collective-permute-start | bytes 786440 | tf_op jit(solution)/shard_map/ppermute | solution.py:47
  14.5 13.1 %collective-permute-start.1 = (f32[4,128,128]{2,1,0:T(8,128)S(1)}, f32[4,128,128]{2,1,0:T(8,128)S(1)}, u32[]{:S(2)}, u32[]{:S(2)}) collective-permute-start(f32[4,128,128]{2,1,0:T(8,128)S(1)} %get-tuple-element.44), channel_id=1, source_target_pairs={{0,2},{1,3},{2,0},{3,1},{4,6},{5,7},{6,4},{7,5},{8,10},{9,11},{10,... | collective-permute-start | bytes 786440 | tf_op jit(solution)/shard_map/ppermute | solution.py:47
  15.1 12.5 %collective-permute-start = (f32[4,128,128]{2,1,0:T(8,128)S(1)}, f32[4,128,128]{2,1,0:T(8,128)S(1)}, u32[]{:S(2)}, u32[]{:S(2)}) collective-permute-start(f32[4,128,128]{2,1,0:T(8,128)S(1)} %get-tuple-element.45), channel_id=1, source_target_pairs={{0,1},{1,2},{2,3},{3,0},{4,5},{5,6},{6,7},{7,4},{8,9},{9,10},{10,1... | collective-permute-start | bytes 786440 | tf_op jit(solution)/shard_map/ppermute | solution.py:47
  16.7 13.8 %copy-start.20 = (pred[4]{0:T(512)(128)(4,1)}, pred[4]{0:T(512)(128)(4,1)S(1)}, u32[]{:S(2)}) copy-start(pred[4]{0:T(512)(128)(4,1)S(1)} %compare_and_fusion.2) | copy-start | bytes 16
  17.4 13.1 %copy-start.19 = (s32[1024]{0:T(1024)}, s32[1024]{0:T(1024)S(1)}, u32[]{:S(2)}) copy-start(s32[1024]{0:T(1024)S(1)} %pad_clamp_fusion) | copy-start | bytes 12292
  34.4 8.5 %collective-permute-start.3 = (f32[4,128,128]{2,1,0:T(8,128)S(1)}, f32[4,128,128]{2,1,0:T(8,128)S(1)}, u32[]{:S(2)}, u32[]{:S(2)}) collective-permute-start(f32[4,128,128]{2,1,0:T(8,128)S(1)} %get-tuple-element.22), channel_id=1, source_target_pairs={{0,4},{1,5},{2,6},{3,7},{4,8},{5,9},{6,10},{7,11},{8,12},{9,13},{1... | collective-permute-start | bytes 786440 | tf_op jit(solution)/shard_map/ppermute | solution.py:70
  43.6 8.7 %collective-permute-start.4 = (f32[4,128,128]{2,1,0:T(8,128)}, f32[4,128,128]{2,1,0:T(8,128)}, u32[]{:S(2)}, u32[]{:S(2)}) collective-permute-start(f32[4,128,128]{2,1,0:T(8,128)} %multiply_add_fusion.3), channel_id=1, source_target_pairs={{0,4},{1,5},{2,6},{3,7},{4,8},{5,9},{6,10},{7,11},{8,12},{9,13},{1... | collective-permute-start | bytes 786440 | tf_op jit(solution)/shard_map/ppermute | solution.py:70
  50.6 33.5 %copy-start.4 = (bf16[384,2048]{0,1:T(8,128)(2,1)}, bf16[384,2048]{0,1:T(8,128)(2,1)S(1)}, u32[]{:S(2)}) copy-start(bf16[384,2048]{0,1:T(8,128)(2,1)S(1)} %copy.59) | copy-start | bytes 4718596
  53.3 8.3 %collective-permute-start.5 = (f32[4,128,128]{2,1,0:T(8,128)S(1)}, f32[4,128,128]{2,1,0:T(8,128)S(1)}, u32[]{:S(2)}, u32[]{:S(2)}) collective-permute-start(f32[4,128,128]{2,1,0:T(8,128)S(1)} %multiply_add_fusion.2), channel_id=1, source_target_pairs={{0,4},{1,5},{2,6},{3,7},{4,8},{5,9},{6,10},{7,11},{8,12},{9,13},{1... | collective-permute-start | bytes 786440 | tf_op jit(solution)/shard_map/ppermute | solution.py:71
  57.7 3.9 %copy-start.9 = (f32[4,4,128,128]{3,2,1,0:T(8,128)S(1)}, f32[4,4,128,128]{3,2,1,0:T(8,128)}, u32[]{:S(2)}) copy-start(f32[4,4,128,128]{3,2,1,0:T(8,128)} %copy-done.8) | copy-start | bytes 3145732
  57.8 3.9 %copy-start.16 = (f32[4,128,128]{2,1,0:T(8,128)S(1)}, f32[4,128,128]{2,1,0:T(8,128)}, u32[]{:S(2)}) copy-start(f32[4,128,128]{2,1,0:T(8,128)} %get-tuple-element.23) | copy-start | bytes 786436
  61.0 3.8 %copy-start.2 = (bf16[16,384,384]{2,1,0:T(8,128)(2,1)}, bf16[16,384,384]{2,1,0:T(8,128)(2,1)S(1)}, u32[]{:S(2)}) copy-start(bf16[16,384,384]{2,1,0:T(8,128)(2,1)S(1)} %select_convert_fusion.1) | copy-start | bytes 14155780
  64.1 7.0 %collective-permute-start.8 = (f32[4,128,128]{2,1,0:T(8,128)}, f32[4,128,128]{2,1,0:T(8,128)}, u32[]{:S(2)}, u32[]{:S(2)}) collective-permute-start(f32[4,128,128]{2,1,0:T(8,128)} %get-tuple-element.39), channel_id=1, source_target_pairs={{0,3},{1,0},{2,1},{3,2},{4,7},{5,4},{6,5},{7,6},{8,11},{9,8},{10,9... | collective-permute-start | bytes 786440 | tf_op jit(solution)/shard_map/ppermute | solution.py:47
  64.1 12.6 %collective-permute-start.7 = (f32[4,128,128]{2,1,0:T(8,128)}, f32[4,128,128]{2,1,0:T(8,128)}, u32[]{:S(2)}, u32[]{:S(2)}) collective-permute-start(f32[4,128,128]{2,1,0:T(8,128)} %get-tuple-element.40), channel_id=1, source_target_pairs={{0,2},{1,3},{2,0},{3,1},{4,6},{5,7},{6,4},{7,5},{8,10},{9,11},{10,... | collective-permute-start | bytes 786440 | tf_op jit(solution)/shard_map/ppermute | solution.py:47
  64.5 13.1 %collective-permute-start.6 = (f32[4,128,128]{2,1,0:T(8,128)}, f32[4,128,128]{2,1,0:T(8,128)}, u32[]{:S(2)}, u32[]{:S(2)}) collective-permute-start(f32[4,128,128]{2,1,0:T(8,128)} %get-tuple-element.41), channel_id=1, source_target_pairs={{0,1},{1,2},{2,3},{3,0},{4,5},{5,6},{6,7},{7,4},{8,9},{9,10},{10,1... | collective-permute-start | bytes 786440 | tf_op jit(solution)/shard_map/ppermute | solution.py:47
  79.7 2.9 %copy-start.21 = (pred[4]{0:T(512)(128)(4,1)S(1)}, pred[4]{0:T(512)(128)(4,1)}, u32[]{:S(2)}) copy-start(pred[4]{0:T(512)(128)(4,1)} %copy-done.20) | copy-start | bytes 16
  79.7 4.4 %copy-start.27 = (pred[384]{0:T(512)(128)(4,1)S(1)}, pred[384]{0:T(512)(128)(4,1)}, u32[]{:S(2)}) copy-start(pred[384]{0:T(512)(128)(4,1)} %get-tuple-element.48) | copy-start | bytes 1156
  84.1 4.4 %copy-start.14 = (bf16[4,4,128,128]{3,2,1,0:T(8,128)(2,1)}, bf16[4,4,128,128]{3,2,1,0:T(8,128)(2,1)S(1)}, u32[]{:S(2)}) copy-start(bf16[4,4,128,128]{3,2,1,0:T(8,128)(2,1)S(1)} %fusion.22) | copy-start | bytes 1572868
  88.6 3.7 %copy-start.10 = (bf16[384,2048]{1,0:T(8,128)(2,1)S(1)}, bf16[384,2048]{1,0:T(8,128)(2,1)}, u32[]{:S(2)}) copy-start(bf16[384,2048]{1,0:T(8,128)(2,1)} %param.11) | copy-start | bytes 4718596
  92.3 2.8 %copy-start.1 = (f32[384,2048]{1,0:T(8,128)S(1)}, f32[384,2048]{1,0:T(8,128)}, u32[]{:S(2)}) copy-start(f32[384,2048]{1,0:T(8,128)} %copy.39) | copy-start | bytes 9437188
  101.6 2.7 %copy-start.31 = (pred[4]{0:T(512)(128)(4,1)S(1)}, pred[4]{0:T(512)(128)(4,1)}, u32[]{:S(2)}) copy-start(pred[4]{0:T(512)(128)(4,1)} %get-tuple-element.13) | copy-start | bytes 16
  101.6 2.7 %copy-start.32 = (s32[4]{0:T(128)S(1)}, s32[4]{0:T(128)}, u32[]{:S(2)}) copy-start(s32[4]{0:T(128)} %get-tuple-element.17) | copy-start | bytes 52
  101.6 2.7 %copy-start.33 = (s32[4]{0:T(128)S(1)}, s32[4]{0:T(128)}, u32[]{:S(2)}) copy-start(s32[4]{0:T(128)} %get-tuple-element.18) | copy-start | bytes 52
  102.5 5.9 %collective-permute-start.11 = (f32[4,128,128]{2,1,0:T(8,128)}, f32[4,128,128]{2,1,0:T(8,128)}, u32[]{:S(2)}, u32[]{:S(2)}) collective-permute-start(f32[4,128,128]{2,1,0:T(8,128)} %get-tuple-element.35), channel_id=1, source_target_pairs={{0,3},{1,0},{2,1},{3,2},{4,7},{5,4},{6,5},{7,6},{8,11},{9,8},{10,9... | collective-permute-start | bytes 786440 | tf_op jit(solution)/shard_map/ppermute | solution.py:47
  102.5 14.7 %collective-permute-start.10 = (f32[4,128,128]{2,1,0:T(8,128)}, f32[4,128,128]{2,1,0:T(8,128)}, u32[]{:S(2)}, u32[]{:S(2)}) collective-permute-start(f32[4,128,128]{2,1,0:T(8,128)} %get-tuple-element.36), channel_id=1, source_target_pairs={{0,2},{1,3},{2,0},{3,1},{4,6},{5,7},{6,4},{7,5},{8,10},{9,11},{10,... | collective-permute-start | bytes 786440 | tf_op jit(solution)/shard_map/ppermute | solution.py:47
  104.1 13.1 %collective-permute-start.9 = (f32[4,128,128]{2,1,0:T(8,128)}, f32[4,128,128]{2,1,0:T(8,128)}, u32[]{:S(2)}, u32[]{:S(2)}) collective-permute-start(f32[4,128,128]{2,1,0:T(8,128)} %get-tuple-element.37), channel_id=1, source_target_pairs={{0,1},{1,2},{2,3},{3,0},{4,5},{5,6},{6,7},{7,4},{8,9},{9,10},{10,1... | collective-permute-start | bytes 786440 | tf_op jit(solution)/shard_map/ppermute | solution.py:47
  119.4 2.9 %copy-start.22 = (pred[4]{0:T(512)(128)(4,1)S(1)}, pred[4]{0:T(512)(128)(4,1)}, u32[]{:S(2)}) copy-start(pred[4]{0:T(512)(128)(4,1)} %copy-done.20) | copy-start | bytes 16
  123.7 2.0 %copy-start.7 = (f32[4,4,128,128]{3,2,1,0:T(8,128)}, f32[4,4,128,128]{3,2,1,0:T(8,128)S(1)}, u32[]{:S(2)}) copy-start(f32[4,4,128,128]{3,2,1,0:T(8,128)S(1)} %broadcast_select_fusion) | copy-start | bytes 3145732
  125.7 8.9 %collective-permute-start.12 = (f32[4,128,128]{2,1,0:T(8,128)S(1)}, f32[4,128,128]{2,1,0:T(8,128)S(1)}, u32[]{:S(2)}, u32[]{:S(2)}) collective-permute-start(f32[4,128,128]{2,1,0:T(8,128)S(1)} %get-tuple-element.19), channel_id=1, source_target_pairs={{4,0},{5,1},{6,2},{7,3},{8,4},{9,5},{10,6},{11,7},{12,8},{13,9},{1... | collective-permute-start | bytes 786440 | tf_op jit(solution)/shard_map/ppermute | solution.py:70
  127.2 8.9 %copy-start.12 = (bf16[384,16,128]{0,2,1:T(8,128)(2,1)S(1)}, bf16[384,16,128]{0,2,1:T(8,128)(2,1)}, u32[]{:S(2)}) copy-start(bf16[384,16,128]{0,2,1:T(8,128)(2,1)} %copy-done.11) | copy-start | bytes 4718596
  128.9 8.8 %copy-start.3 = (bf16[16,384,384]{2,1,0:T(8,128)(2,1)}, bf16[16,384,384]{2,1,0:T(8,128)(2,1)S(1)}, u32[]{:S(2)}) copy-start(bf16[16,384,384]{2,1,0:T(8,128)(2,1)S(1)} %select_convert_fusion) | copy-start | bytes 14155780
  134.7 10.5 %copy-start.15 = (bf16[4,4,128,128]{3,2,1,0:T(8,128)(2,1)S(1)}, bf16[4,4,128,128]{3,2,1,0:T(8,128)(2,1)}, u32[]{:S(2)}) copy-start(bf16[4,4,128,128]{3,2,1,0:T(8,128)(2,1)} %copy-done.14) | copy-start | bytes 1572868
  134.7 10.5 %copy-start.28 = (pred[384]{0:T(512)(128)(4,1)S(1)}, pred[384]{0:T(512)(128)(4,1)}, u32[]{:S(2)}) copy-start(pred[384]{0:T(512)(128)(4,1)} %get-tuple-element.48) | copy-start | bytes 1156
  134.7 8.4 %collective-permute-start.13 = (f32[4,128,128]{2,1,0:T(8,128)S(1)}, f32[4,128,128]{2,1,0:T(8,128)S(1)}, u32[]{:S(2)}, u32[]{:S(2)}) collective-permute-start(f32[4,128,128]{2,1,0:T(8,128)S(1)} %multiply_add_fusion.1), channel_id=1, source_target_pairs={{4,0},{5,1},{6,2},{7,3},{8,4},{9,5},{10,6},{11,7},{12,8},{13,9},{1... | collective-permute-start | bytes 786440 | tf_op jit(solution)/shard_map/ppermute | solution.py:70
  143.8 8.6 %collective-permute-start.14 = (f32[4,128,128]{2,1,0:T(8,128)}, f32[4,128,128]{2,1,0:T(8,128)}, u32[]{:S(2)}, u32[]{:S(2)}) collective-permute-start(f32[4,128,128]{2,1,0:T(8,128)} %multiply_add_fusion), channel_id=1, source_target_pairs={{4,0},{5,1},{6,2},{7,3},{8,4},{9,5},{10,6},{11,7},{12,8},{13,9},{1... | collective-permute-start | bytes 786440 | tf_op jit(solution)/shard_map/ppermute | solution.py:71
  156.0 7.6 %collective-permute-start.17 = (f32[4,128,128]{2,1,0:T(8,128)S(1)}, f32[4,128,128]{2,1,0:T(8,128)S(1)}, u32[]{:S(2)}, u32[]{:S(2)}) collective-permute-start(f32[4,128,128]{2,1,0:T(8,128)S(1)} %get-tuple-element.31), channel_id=1, source_target_pairs={{0,3},{1,0},{2,1},{3,2},{4,7},{5,4},{6,5},{7,6},{8,11},{9,8},{10,9... | collective-permute-start | bytes 786440 | tf_op jit(solution)/shard_map/ppermute | solution.py:47
  156.1 14.6 %collective-permute-start.16 = (f32[4,128,128]{2,1,0:T(8,128)S(1)}, f32[4,128,128]{2,1,0:T(8,128)S(1)}, u32[]{:S(2)}, u32[]{:S(2)}) collective-permute-start(f32[4,128,128]{2,1,0:T(8,128)S(1)} %get-tuple-element.32), channel_id=1, source_target_pairs={{0,2},{1,3},{2,0},{3,1},{4,6},{5,7},{6,4},{7,5},{8,10},{9,11},{10,... | collective-permute-start | bytes 786440 | tf_op jit(solution)/shard_map/ppermute | solution.py:47
  158.2 12.5 %collective-permute-start.15 = (f32[4,128,128]{2,1,0:T(8,128)S(1)}, f32[4,128,128]{2,1,0:T(8,128)S(1)}, u32[]{:S(2)}, u32[]{:S(2)}) collective-permute-start(f32[4,128,128]{2,1,0:T(8,128)S(1)} %get-tuple-element.33), channel_id=1, source_target_pairs={{0,1},{1,2},{2,3},{3,0},{4,5},{5,6},{6,7},{7,4},{8,9},{9,10},{10,1... | collective-permute-start | bytes 786440 | tf_op jit(solution)/shard_map/ppermute | solution.py:47
  170.8 1.7 copy-start.23
  173.9 2.5 %copy-start.6 = (f32[16,128,384]{2,1,0:T(8,128)S(1)}, f32[16,128,384]{2,1,0:T(8,128)}, u32[]{:S(2)}) copy-start(f32[16,128,384]{2,1,0:T(8,128)} %fusion.50) | copy-start | bytes 9437188
  174.0 3.5 %copy-start.13 = (bf16[384,2048]{1,0:T(8,128)(2,1)S(1)}, bf16[384,2048]{1,0:T(8,128)(2,1)}, u32[]{:S(2)}) copy-start(bf16[384,2048]{1,0:T(8,128)(2,1)} %param.8) | copy-start | bytes 4718596
  174.0 3.5 %copy-start.26 = (pred[384]{0:T(512)(128)(4,1)S(1)}, pred[384]{0:T(512)(128)(4,1)}, u32[]{:S(2)}) copy-start(pred[384]{0:T(512)(128)(4,1)} %copy-done.25) | copy-start | bytes 1156
  179.4 2.7 %copy-start.5 = (bf16[384,2048]{0,1:T(8,128)(2,1)S(1)}, bf16[384,2048]{0,1:T(8,128)(2,1)}, u32[]{:S(2)}) copy-start(bf16[384,2048]{0,1:T(8,128)(2,1)} %copy-done.4) | copy-start | bytes 4718596
  (4 other events, 3.8 us)

commit v2 on v1

--- a/solution.py
+++ b/solution.py
@@ -33,44 +33,66 @@
 GROUP = 4
 
 
-def member_exchange(pieces, axis):
+def member_send(pick, axis):
     count = lax.axis_size(axis)
     member = lax.axis_index(axis) % GROUP
-    got = [lax.dynamic_index_in_dim(pieces, member, keepdims=False)]
+    got = [pick(member, 0)]
     for offset in range(1, GROUP):
-        piece = lax.dynamic_index_in_dim(pieces, (member + offset) % GROUP, keepdims=False)
         pairs = [
             (row + index, row + (index + offset) % GROUP)
             for row in range(0, count, GROUP)
             for index in range(GROUP)
         ]
-        got.append(lax.ppermute(piece, axis, pairs))
-    return jnp.take(jnp.stack(got), (member - jnp.arange(GROUP)) % GROUP, axis=0)
+        got.append(lax.ppermute(pick((member + offset) % GROUP, offset), axis, pairs))
+    return got
+
+
+def selected(choice, options):
+    picked = options[-1]
+    for index in range(len(options) - 2, -1, -1):
+        picked = jnp.where(choice == index, options[index], picked)
+    return picked
 
 
 def row_scan(state, keep_row, direction):
     count = lax.axis_size("seq")
+    member = lax.axis_index("seq") % GROUP
     heads = state.shape[0]
     pieces = state.reshape((GROUP, heads // GROUP) + state.shape[1:])
-    mine = member_exchange(pieces, "seq")
-    order = range(GROUP) if direction > 0 else range(GROUP - 1, -1, -1)
-    inner = [None] * GROUP
-    inner_keep = [None] * GROUP
-    total = jnp.zeros_like(mine[0])
-    total_keep = jnp.ones((), jnp.float32)
+    near = member_send(lambda target, _: lax.dynamic_index_in_dim(pieces, target, keepdims=False), "seq")
+    order = list(range(GROUP)) if direction > 0 else list(range(GROUP - 1, -1, -1))
+    one = jnp.ones((), jnp.float32)
+    zero = jnp.zeros((), jnp.float32)
+    inner = [[zero] * GROUP for _ in range(GROUP)]
+    inner_keep = [one] * GROUP
+    total = [zero] * GROUP
+    total_keep = one
     for index in order:
-        inner[index] = total
+        inner[index] = list(total)
         inner_keep[index] = total_keep
-        total = mine[index] + keep_row[index] * total
+        total = [keep_row[index] * weight for weight in total]
+        total[index] = one
         total_keep = total_keep * keep_row[index]
+    source = (member - jnp.arange(GROUP)) % GROUP
+    inner_rel = jnp.stack([jnp.stack(row) for row in inner])[:, source]
+    total_rel = jnp.stack(total)[source]
+    row_total = sum(total_rel[offset] * near[offset] for offset in range(GROUP))
     shift = GROUP * direction
-    pairs = [(source, source + shift) for source in range(count) if 0 <= source + shift < count]
-    window = total
+    pairs = [(start, start + shift) for start in range(count) if 0 <= start + shift < count]
+    window = row_total
     for _ in range(-(-SPAN // GROUP) - 1):
-        window = total + total_keep * lax.ppermute(window, "seq", pairs)
+        window = row_total + total_keep * lax.ppermute(window, "seq", pairs)
     entering = lax.ppermute(window, "seq", pairs)
-    scanned = jnp.stack([inner[index] + inner_keep[index] * entering for index in range(GROUP)])
-    return member_exchange(scanned, "seq").reshape(state.shape)
+    inner_keep = jnp.stack(inner_keep)
+
+    def scanned(target, _):
+        weights = inner_rel[target]
+        mixed = sum(weights[offset] * near[offset] for offset in range(GROUP))
+        return mixed + inner_keep[target] * entering
+
+    back = member_send(scanned, "seq")
+    quarters = [selected((member - quarter) % GROUP, back) for quarter in range(GROUP)]
+    return jnp.stack(quarters).reshape(state.shape)
 
 
 def row_flags(starts, row_count):

time: 192 us -> 217 us (1.13)
  the two profiles are of different devices: /device:TPU:0 before, /device:TPU:1 now
where the time goes in v2:
time: 217 us; the launch traced here: 213 us
  other arithmetic  62.9 us (29%)
  local copies, waits for them, and re-layouts  39.8 us (18%)
  matrix products  35.1 us (16%)
  starting transfers between devices  33.7 us (16%)
  waiting for transfers between devices  24.8 us (11%)
  between operations  17 us (8%)
    add x4, other arithmetic, scanned(): return mixed + inner_keep[target] * entering  25.5 us
    ppermute x12, starting transfers between devices, member_send(): lax.ppermute(pick((member + offset) % GROUP, offset), axis, pairs)  17.7 us
    unnamed x48, local copies, waits for them, and re-layouts  13.3 us
    ppermute x12, waiting for transfers between devices, member_send(): lax.ppermute(pick((member + offset) % GROUP, offset), axis, pairs)  12.2 us
    ppermute x4, waiting for transfers between devices, row_scan(): window = row_total + total_keep * lax.ppermute(window, 'seq', pairs)  10.8 us
    another operation x4, other arithmetic, row_scan(): return jnp.stack(quarters).reshape(state.shape)  10.5 us
    ppermute x4, starting transfers between devices, row_scan(): window = row_total + total_keep * lax.ppermute(window, 'seq', pairs)  9.97 us
    add x2, other arithmetic, row_scan(): sum((total_rel[offset] * near[offset] for offset in range(GROUP)))  7.18 us
  transfers between devices with their start and end apart: 18, of which 9 were waited for; matrix products, arithmetic and copies ran while one was open for 30% of the time, Pallas kernels for 0%

profile of v2, /device:TPU:1, one launch (start us, length us, event | category | flops | bytes accessed | tf_op | source)
XLA Modules:
  0.0 213.3 jit_solution(13774000889911037705)
XLA Ops:
  4.3 3.0 %copy.104 = bf16[48,8,16,128]{3,2,1,0:T(8,128)(2,1)} copy(bf16[48,8,16,128]{3,1,2,0:T(8,128)(2,1)} %bitcast.298) | data formatting | bytes 3145728
  7.2 2.1 copy.73
  12.6 2.6 %collective-permute-start = (f32[4,128,128]{2,1,0:T(8,128)}, f32[4,128,128]{2,1,0:T(8,128)S(1)}, u32[]{:S(2)}, u32[]{:S(2)}) collective-permute-start(f32[4,128,128]{2,1,0:T(8,128)} %get-tuple-element.50), channel_id=1, source_target_pairs={{0,1},{1,2},{2,3},{3,0},{4,5},{5,6},{6,7},{7,4},{8,9},{9,10},{10,1... | collective-permute-start | bytes 786440 | tf_op jit(solution)/shard_map/ppermute | solution.py:46
  27.2 1.9 copy.100
  29.1 5.8 %select_convert_fusion.1 = bf16[16,384,384]{2,1,0:T(8,128)(2,1)} fusion(pred[384,384]{1,0:T(8,128)(4,1)} %compare_and_fusion, bf16[384,16,128]{0,2,1:T(8,128)(2,1)S(1)} %bitcast.292, bf16[384,2048]{1,0:T(8,128)(2,1)} %param.6), kind=kOutput, calls=%fused_computation.5 | convolution fusion | flops 608698368 | bytes 8011776 | tf_op jit(solution)/shard_map/thd,shd->hts/dot_general | solution.py:134
  42.5 3.6 %fusion.53 = f32[4,128,128]{2,1,0:T(8,128)S(1)} fusion(f32[4,128,128]{2,1,0:T(8,128)} %collective-permute-done.2, f32[4,128,128]{2,1,0:T(8,128)} %collective-permute-done.1, f32[4,128,128]{2,1,0:T(8,128)S(1)} %collective-permute-done, f32[4,4,128,128]{3,2,1,0:T(8,128)} %bitcast.307, s32[]{:T(128)S(6)} %select_n.302, f32[]{:T(128)} %bitcast.35, f32[]{:T(128)} %bitcast.34, ...), kind=kLoop, calls=%fused_computation.79 | loop fusion | flops 458752 | bytes 1310740 | tf_op jit(solution)/shard_map/add | solution.py:79
  46.2 3.4 %collective-permute-start.3 = (f32[4,128,128]{2,1,0:T(8,128)S(1)}, f32[4,128,128]{2,1,0:T(8,128)S(1)}, u32[]{:S(2)}, u32[]{:S(2)}) collective-permute-start(f32[4,128,128]{2,1,0:T(8,128)S(1)} %fusion.53), channel_id=1, source_target_pairs={{0,4},{1,5},{2,6},{3,7},{4,8},{5,9},{6,10},{7,11},{8,12},{9,13},{1... | collective-permute-start | bytes 786440 | tf_op jit(solution)/shard_map/ppermute | solution.py:84
  49.5 5.5 %fusion.5 = f32[16,384,128]{1,2,0:T(8,128)} fusion(bf16[16,384,384]{2,1,0:T(8,128)(2,1)} %select_convert_fusion.1, bf16[384,2048]{1,0:T(8,128)(2,1)S(1)} %copy-done), kind=kOutput, calls=%fused_computation.18 | convolution fusion | flops 603979776 | bytes 9437184 | tf_op jit(solution)/shard_map/hts,she->the/dot_general | solution.py:136
  55.8 3.9 %collective-permute-start.4 = (f32[4,128,128]{2,1,0:T(8,128)}, f32[4,128,128]{2,1,0:T(8,128)}, u32[]{:S(2)}, u32[]{:S(2)}) collective-permute-start(f32[4,128,128]{2,1,0:T(8,128)} %multiply_add_fusion.3), channel_id=1, source_target_pairs={{0,4},{1,5},{2,6},{3,7},{4,8},{5,9},{6,10},{7,11},{8,12},{9,13},{1... | collective-permute-start | bytes 786440 | tf_op jit(solution)/shard_map/ppermute | solution.py:84
  62.8 1.8 multiply_add_fusion.2
  64.6 4.8 %collective-permute-start.5 = (f32[4,128,128]{2,1,0:T(8,128)}, f32[4,128,128]{2,1,0:T(8,128)}, u32[]{:S(2)}, u32[]{:S(2)}) collective-permute-start(f32[4,128,128]{2,1,0:T(8,128)} %multiply_add_fusion.2), channel_id=1, source_target_pairs={{0,4},{1,5},{2,6},{3,7},{4,8},{5,9},{6,10},{7,11},{8,12},{9,13},{1... | collective-permute-start | bytes 786440 | tf_op jit(solution)/shard_map/ppermute | solution.py:85
  74.0 5.2 %fusion.51 = f32[4,128,128]{2,1,0:T(8,128)} fusion(f32[4,128,128]{2,1,0:T(8,128)} %collective-permute-done.5, f32[4,128,128]{2,1,0:T(8,128)} %collective-permute-done.2, f32[4,128,128]{2,1,0:T(8,128)} %collective-permute-done.1, f32[4,128,128]{2,1,0:T(8,128)S(1)} %collective-permute-done, f32[4,4,128,128]{3,2,1,0:T(8,128)} %bitcast.308, s32[]{:T(128)S(6)} %select_n.302, ...), kind=kLoop, calls=%fused_computation.76 | loop fusion | flops 589824 | bytes 1572888 | tf_op jit(solution)/shard_map/add | solution.py:91
  79.2 4.5 %collective-permute-start.6 = (f32[4,128,128]{2,1,0:T(8,128)}, f32[4,128,128]{2,1,0:T(8,128)}, u32[]{:S(2)}, u32[]{:S(2)}) collective-permute-start(f32[4,128,128]{2,1,0:T(8,128)} %fusion.51), channel_id=1, source_target_pairs={{0,1},{1,2},{2,3},{3,0},{4,5},{5,6},{6,7},{7,4},{8,9},{9,10},{10,1... | collective-permute-start | bytes 786440 | tf_op jit(solution)/shard_map/ppermute | solution.py:46
  83.7 8.5 %fusion.45 = (f32[4,128,128]{2,1,0:T(8,128)}, f32[4,128,128]{2,1,0:T(8,128)}) fusion(f32[4,128,128]{2,1,0:T(8,128)} %collective-permute-done.5, f32[4,128,128]{2,1,0:T(8,128)} %collective-permute-done.2, f32[4,128,128]{2,1,0:T(8,128)} %collective-permute-done.1, f32[4,128,128]{2,1,0:T(8,128)S(1)} %collective-permute-done, f32[4,4,128,128]{3,2,1,0:T(8,128)} %bitcast.309, ...), kind=kLoop, calls=%fused_computation.68 | loop fusion | flops 1179648 | bytes 1835052 | tf_op jit(solution)/shard_map/add | solution.py:91
  96.9 3.7 %collective-permute-done.8 = f32[4,128,128]{2,1,0:T(8,128)} collective-permute-done((f32[4,128,128]{2,1,0:T(8,128)}, f32[4,128,128]{2,1,0:T(8,128)}, u32[]{:S(2)}, u32[]{:S(2)}) %collective-permute-start.8) | collective-permute-done | bytes 262176 | tf_op jit(solution)/shard_map/ppermute | solution.py:46
  100.5 4.6 %select_bitcast_fusion.7 = (f32[1,4,128,128]{3,2,1,0:T(8,128)S(1)}, f32[4,128,128]{2,1,0:T(8,128)S(1)}) fusion(f32[4,128,128]{2,1,0:T(8,128)} %collective-permute-done.6, f32[4,128,128]{2,1,0:T(8,128)} %collective-permute-done.7, f32[4,128,128]{2,1,0:T(8,128)} %collective-permute-done.8, pred[]{:T(512)S(6)} %eq.147, pred[]{:T(512)S(6)} %eq.146, ...), kind=kLoop, calls=%fused_computation.96 | loop fusion | flops 786432 | bytes 2621467 | tf_op jit(solution)/shard_map/stack | solution.py:95
  107.2 2.3 %multiply_reduce_fusion = (f32[384]{0:T(512)S(1)}, f32[384,16,128]{0,2,1:T(8,128)}) fusion(bf16[16,128,128]{2,1,0:T(8,128)(2,1)S(1)} %bitcast.302, bf16[384,16,128]{0,2,1:T(8,128)(2,1)S(1)} %bitcast.293, pred[384]{0:T(512)(128)(4,1)S(1)} %get-tuple-element.55, f32[16,384,128]{1,2,0:T(8,128)S(1)} %copy-done.5), kind=kOutput, calls=%fused_computation.17 | convolution fusion | flops 204471936 | bytes 8390528 | tf_op jit(solution)/shard_map/thd,hde->the/dot_general | solution.py:146
  109.6 3.8 %copy.77 = f32[384,2048]{1,0:T(8,128)} copy(f32[384,2048]{0,1:T(8,128)} %bitcast.296) | data formatting | bytes 6291456 | tf_op jit(solution)/shard_map/reshape | solution.py:149
  113.3 2.6 %fusion = f32[384]{0:T(512)S(1)} fusion(bf16[384,2048]{1,0:T(8,128)(2,1)S(1)} %copy-done.6, f32[384,2048]{1,0:T(8,128)} %copy.77, f32[384]{0:T(512)S(1)} %add_sqrt_fusion), kind=kLoop, calls=%fused_computation.8 | loop fusion | flops 3145344 | bytes 4721664 | tf_op jit(solution)/shard_map/reduce_sum | solution.py:156
  116.2 2.4 %fusion.2 = (bf16[384,2048]{1,0:T(8,128)(2,1)}, bf16[384,2048]{1,0:T(8,128)(2,1)}) fusion(bf16[384,2048]{1,0:T(8,128)(2,1)S(1)} %copy-done.6, f32[384]{0:T(512)S(1)} %broadcast_multiply_fusion, f32[384]{0:T(512)S(1)} %add_sqrt_fusion, f32[384,2048]{1,0:T(8,128)S(1)} %copy-done.1), kind=kLoop, calls=%fused_computation.10 | loop fusion | flops 5505024 | bytes 7867392 | tf_op jit(solution)/shard_map/convert_element_type | solution.py:157
  118.6 1.9 copy.101
  120.5 2.2 %fusion.14 = f32[16,128,128]{2,1,0:T(8,128)S(1)} fusion(bf16[384,16,128]{0,2,1:T(8,128)(2,1)S(1)} %bitcast.288, bf16[384,16,128]{0,2,1:T(8,128)(2,1)} %bitcast.294, pred[384]{0:T(512)(128)(4,1)S(1)} %get-tuple-element.55), kind=kOutput, calls=%fused_computation.27 | convolution fusion | flops 202113024 | bytes 4194688 | tf_op jit(solution)/shard_map/thd,the->hde/dot_general | solution.py:159
  123.9 3.5 %collective-permute-start.9 = (f32[4,128,128]{2,1,0:T(8,128)}, f32[4,128,128]{2,1,0:T(8,128)S(1)}, u32[]{:S(2)}, u32[]{:S(2)}) collective-permute-start(f32[4,128,128]{2,1,0:T(8,128)} %get-tuple-element.44), channel_id=1, source_target_pairs={{0,1},{1,2},{2,3},{3,0},{4,5},{5,6},{6,7},{7,4},{8,9},{9,10},{10,1... | collective-permute-start | bytes 786440 | tf_op jit(solution)/shard_map/ppermute | solution.py:46
  131.1 1.5 fusion.95
  132.6 1.4 fusion.98
  134.1 1.5 fusion.94
  136.3 4.4 %collective-permute-done.10 = f32[4,128,128]{2,1,0:T(8,128)} collective-permute-done((f32[4,128,128]{2,1,0:T(8,128)}, f32[4,128,128]{2,1,0:T(8,128)}, u32[]{:S(2)}, u32[]{:S(2)}) %collective-permute-start.10) | collective-permute-done | bytes 262176 | tf_op jit(solution)/shard_map/ppermute | solution.py:46
  140.7 3.6 %fusion.39 = f32[4,128,128]{2,1,0:T(8,128)S(1)} fusion(f32[4,128,128]{2,1,0:T(8,128)} %collective-permute-done.11, f32[4,128,128]{2,1,0:T(8,128)} %collective-permute-done.10, f32[4,128,128]{2,1,0:T(8,128)S(1)} %collective-permute-done.9, f32[4,4,128,128]{3,2,1,0:T(8,128)} %bitcast.312, s32[]{:T(128)S(6)} %select_n.302, f32[]{:T(128)} %bitcast.95, ...), kind=kLoop, calls=%fused_computation.60 | loop fusion | flops 458752 | bytes 1310740 | tf_op jit(solution)/shard_map/add | solution.py:79
  145.6 1.7 select_convert_fusion
  147.3 5.6 %collective-permute-done.12 = f32[4,128,128]{2,1,0:T(8,128)S(1)} collective-permute-done((f32[4,128,128]{2,1,0:T(8,128)S(1)}, f32[4,128,128]{2,1,0:T(8,128)S(1)}, u32[]{:S(2)}, u32[]{:S(2)}) %collective-permute-start.12) | collective-permute-done | bytes 262176 | tf_op jit(solution)/shard_map/ppermute | solution.py:84
  152.9 1.4 collective-permute-start.13
  154.4 1.6 fusion.108
  155.9 4.9 %collective-permute-done.13 = f32[4,128,128]{2,1,0:T(8,128)S(1)} collective-permute-done((f32[4,128,128]{2,1,0:T(8,128)S(1)}, f32[4,128,128]{2,1,0:T(8,128)S(1)}, u32[]{:S(2)}, u32[]{:S(2)}) %collective-permute-start.13) | collective-permute-done | bytes 262176 | tf_op jit(solution)/shard_map/ppermute | solution.py:84
  162.9 1.8 fusion.4
  164.6 2.6 %copy.93 = bf16[384,2048]{1,0:T(8,128)(2,1)} copy(bf16[384,2048]{0,1:T(8,128)(2,1)} %bitcast.299) | data formatting | bytes 3145728
  167.2 1.8 collective-permute-done.14
  169.0 4.3 %fusion.37 = f32[4,128,128]{2,1,0:T(8,128)S(1)} fusion(f32[4,128,128]{2,1,0:T(8,128)} %collective-permute-done.14, f32[4,128,128]{2,1,0:T(8,128)} %collective-permute-done.11, f32[4,128,128]{2,1,0:T(8,128)} %collective-permute-done.10, f32[4,128,128]{2,1,0:T(8,128)S(1)} %collective-permute-done.9, f32[4,4,128,128]{3,2,1,0:T(8,128)} %bitcast.313, ...), kind=kLoop, calls=%fused_computation.57 | loop fusion | flops 589824 | bytes 1572888 | tf_op jit(solution)/shard_map/add | solution.py:91
  173.3 2.9 %collective-permute-start.15 = (f32[4,128,128]{2,1,0:T(8,128)S(1)}, f32[4,128,128]{2,1,0:T(8,128)S(1)}, u32[]{:S(2)}, u32[]{:S(2)}) collective-permute-start(f32[4,128,128]{2,1,0:T(8,128)S(1)} %fusion.37), channel_id=1, source_target_pairs={{0,1},{1,2},{2,3},{3,0},{4,5},{5,6},{6,7},{7,4},{8,9},{9,10},{10,1... | collective-permute-start | bytes 786440 | tf_op jit(solution)/shard_map/ppermute | solution.py:46
  176.2 7.5 %fusion.31 = (f32[4,128,128]{2,1,0:T(8,128)S(1)}, f32[4,128,128]{2,1,0:T(8,128)S(1)}) fusion(f32[4,128,128]{2,1,0:T(8,128)} %collective-permute-done.14, f32[4,128,128]{2,1,0:T(8,128)} %collective-permute-done.11, f32[4,128,128]{2,1,0:T(8,128)} %collective-permute-done.10, f32[4,128,128]{2,1,0:T(8,128)S(1)} %collective-permute-done.9, ...), kind=kLoop, calls=%fused_computation.49 | loop fusion | flops 1179648 | bytes 1835052 | tf_op jit(solution)/shard_map/add | solution.py:91
  186.3 3.5 %fusion.109 = f32[16,128,384]{2,1,0:T(8,128)S(1)} fusion(bf16[384,16,128]{0,2,1:T(8,128)(2,1)S(1)} %bitcast.291, bf16[16,384,384]{2,1,0:T(8,128)(2,1)} %select_convert_fusion.1), kind=kOutput, calls=%fused_computation.194 | convolution fusion | flops 603979776 | bytes 9437184 | tf_op jit(solution)/shard_map/hts,the->she/dot_general | solution.py:186
  189.9 1.8 collective-permute-done.17
  191.6 1.6 collective-permute-done.16
  193.2 4.5 %select_bitcast_fusion.3 = (f32[1,4,128,128]{3,2,1,0:T(8,128)S(1)}, f32[4,128,128]{2,1,0:T(8,128)S(1)}) fusion(f32[4,128,128]{2,1,0:T(8,128)S(1)} %collective-permute-done.15, f32[4,128,128]{2,1,0:T(8,128)S(1)} %collective-permute-done.16, f32[4,128,128]{2,1,0:T(8,128)S(1)} %collective-permute-done.17, pred[]{:T(512)S(6)} %eq.147, pred[]{:T(512)S(6)} %eq.146, ...), kind=kLoop, calls=%fused_computation.87 | loop fusion | flops 786432 | bytes 2621467 | tf_op jit(solution)/shard_map/stack | solution.py:95
  198.0 2.5 %fusion.7 = f32[16,128,384]{2,1,0:T(8,128)} fusion(bf16[16,128,128]{2,1,0:T(8,128)(2,1)S(1)} %bitcast.304, bf16[384,2048]{1,0:T(8,128)(2,1)S(1)} %copy-done), kind=kOutput, calls=%fused_computation.20 | convolution fusion | flops 201326592 | bytes 5242880 | tf_op jit(solution)/shard_map/she,hde->shd/dot_general | solution.py:182
  200.4 1.9 add_convert_fusion
  202.4 2.7 %copy.95 = bf16[384,2048]{1,0:T(8,128)(2,1)} copy(bf16[384,2048]{0,1:T(8,128)(2,1)} %bitcast.300) | data formatting | bytes 3145728
  205.0 5.7 %fusion.3 = bf16[384,16,128]{0,2,1:T(8,128)(2,1)} fusion(f32[16,128,384]{2,1,0:T(8,128)} %fusion.7, bf16[384,16,128]{0,2,1:T(8,128)(2,1)S(1)} %bitcast.295, bf16[16,384,384]{2,1,0:T(8,128)(2,1)} %copy-done.2, pred[384]{0:T(512)(128)(4,1)S(1)} %copy-done.18), kind=kOutput, calls=%fused_computation.12 | convolution fusion | flops 606339072 | bytes 11010432 | tf_op jit(solution)/shard_map/hts,thd->shd/dot_general | solution.py:179
  210.8 2.6 %copy.94 = bf16[384,2048]{1,0:T(8,128)(2,1)} copy(bf16[384,2048]{0,1:T(8,128)(2,1)} %bitcast.301) | data formatting | bytes 3145728
  (124 shorter events, 38.1 us)
Async XLA Ops:
  0.6 10.1 %copy-start = (bf16[384,2048]{1,0:T(8,128)(2,1)S(1)}, bf16[384,2048]{1,0:T(8,128)(2,1)}, u32[]{:S(2)}) copy-start(bf16[384,2048]{1,0:T(8,128)(2,1)} %param.7) | copy-start | bytes 4718596
  9.4 2.0 copy-start.7
  10.7 0.6 copy-start.17
  10.7 109.7 %copy-start.19 = (pred[384]{0:T(512)(128)(4,1)}, pred[384]{0:T(512)(128)(4,1)S(1)}, u32[]{:S(2)}) copy-start(pred[384]{0:T(512)(128)(4,1)S(1)} %get-tuple-element.55) | copy-start | bytes 1156
  11.4 1.2 copy-start.12
  12.6 29.9 %collective-permute-start = (f32[4,128,128]{2,1,0:T(8,128)}, f32[4,128,128]{2,1,0:T(8,128)S(1)}, u32[]{:S(2)}, u32[]{:S(2)}) collective-permute-start(f32[4,128,128]{2,1,0:T(8,128)} %get-tuple-element.50), channel_id=1, source_target_pairs={{0,1},{1,2},{2,3},{3,0},{4,5},{5,6},{6,7},{7,4},{8,9},{9,10},{10,1... | collective-permute-start | bytes 786440 | tf_op jit(solution)/shard_map/ppermute | solution.py:46
  15.2 27.3 %collective-permute-start.2 = (f32[4,128,128]{2,1,0:T(8,128)}, f32[4,128,128]{2,1,0:T(8,128)}, u32[]{:S(2)}, u32[]{:S(2)}) collective-permute-start(f32[4,128,128]{2,1,0:T(8,128)} %get-tuple-element.51), channel_id=1, source_target_pairs={{0,3},{1,0},{2,1},{3,2},{4,7},{5,4},{6,5},{7,6},{8,11},{9,8},{10,9... | collective-permute-start | bytes 786440 | tf_op jit(solution)/shard_map/ppermute | solution.py:46
  15.2 27.3 %collective-permute-start.1 = (f32[4,128,128]{2,1,0:T(8,128)}, f32[4,128,128]{2,1,0:T(8,128)}, u32[]{:S(2)}, u32[]{:S(2)}) collective-permute-start(f32[4,128,128]{2,1,0:T(8,128)} %get-tuple-element.52), channel_id=1, source_target_pairs={{0,2},{1,3},{2,0},{3,1},{4,6},{5,7},{6,4},{7,5},{8,10},{9,11},{10,... | collective-permute-start | bytes 786440 | tf_op jit(solution)/shard_map/ppermute | solution.py:46
  29.1 77.6 %copy-start.3 = (bf16[384,2048]{0,1:T(8,128)(2,1)}, bf16[384,2048]{0,1:T(8,128)(2,1)S(1)}, u32[]{:S(2)}) copy-start(bf16[384,2048]{0,1:T(8,128)(2,1)S(1)} %copy.100) | copy-start | bytes 4718596
  46.2 8.9 %copy-start.15 = (f32[4,128,128]{2,1,0:T(8,128)}, f32[4,128,128]{2,1,0:T(8,128)S(1)}, u32[]{:S(2)}) copy-start(f32[4,128,128]{2,1,0:T(8,128)S(1)} %fusion.53) | copy-start | bytes 786436
  46.2 8.9 %collective-permute-start.3 = (f32[4,128,128]{2,1,0:T(8,128)S(1)}, f32[4,128,128]{2,1,0:T(8,128)S(1)}, u32[]{:S(2)}, u32[]{:S(2)}) collective-permute-start(f32[4,128,128]{2,1,0:T(8,128)S(1)} %fusion.53), channel_id=1, source_target_pairs={{0,4},{1,5},{2,6},{3,7},{4,8},{5,9},{6,10},{7,11},{8,12},{9,13},{1... | collective-permute-start | bytes 786440 | tf_op jit(solution)/shard_map/ppermute | solution.py:84
  55.8 7.0 %collective-permute-start.4 = (f32[4,128,128]{2,1,0:T(8,128)}, f32[4,128,128]{2,1,0:T(8,128)}, u32[]{:S(2)}, u32[]{:S(2)}) collective-permute-start(f32[4,128,128]{2,1,0:T(8,128)} %multiply_add_fusion.3), channel_id=1, source_target_pairs={{0,4},{1,5},{2,6},{3,7},{4,8},{5,9},{6,10},{7,11},{8,12},{9,13},{1... | collective-permute-start | bytes 786440 | tf_op jit(solution)/shard_map/ppermute | solution.py:84
  64.6 9.5 %collective-permute-start.5 = (f32[4,128,128]{2,1,0:T(8,128)}, f32[4,128,128]{2,1,0:T(8,128)}, u32[]{:S(2)}, u32[]{:S(2)}) collective-permute-start(f32[4,128,128]{2,1,0:T(8,128)} %multiply_add_fusion.2), channel_id=1, source_target_pairs={{0,4},{1,5},{2,6},{3,7},{4,8},{5,9},{6,10},{7,11},{8,12},{9,13},{1... | collective-permute-start | bytes 786440 | tf_op jit(solution)/shard_map/ppermute | solution.py:85
  79.2 17.6 %collective-permute-start.6 = (f32[4,128,128]{2,1,0:T(8,128)}, f32[4,128,128]{2,1,0:T(8,128)}, u32[]{:S(2)}, u32[]{:S(2)}) collective-permute-start(f32[4,128,128]{2,1,0:T(8,128)} %fusion.51), channel_id=1, source_target_pairs={{0,1},{1,2},{2,3},{3,0},{4,5},{5,6},{6,7},{7,4},{8,9},{9,10},{10,1... | collective-permute-start | bytes 786440 | tf_op jit(solution)/shard_map/ppermute | solution.py:46
  92.2 8.4 %collective-permute-start.8 = (f32[4,128,128]{2,1,0:T(8,128)}, f32[4,128,128]{2,1,0:T(8,128)}, u32[]{:S(2)}, u32[]{:S(2)}) collective-permute-start(f32[4,128,128]{2,1,0:T(8,128)} %get-tuple-element.39), channel_id=1, source_target_pairs={{0,3},{1,0},{2,1},{3,2},{4,7},{5,4},{6,5},{7,6},{8,11},{9,8},{10,9... | collective-permute-start | bytes 786440 | tf_op jit(solution)/shard_map/ppermute | solution.py:46
  92.2 8.4 %collective-permute-start.7 = (f32[4,128,128]{2,1,0:T(8,128)}, f32[4,128,128]{2,1,0:T(8,128)}, u32[]{:S(2)}, u32[]{:S(2)}) collective-permute-start(f32[4,128,128]{2,1,0:T(8,128)} %get-tuple-element.40), channel_id=1, source_target_pairs={{0,2},{1,3},{2,0},{3,1},{4,6},{5,7},{6,4},{7,5},{8,10},{9,11},{10,... | collective-permute-start | bytes 786440 | tf_op jit(solution)/shard_map/ppermute | solution.py:46
  105.1 2.1 copy-start.5
  106.6 3.0 %copy-start.10 = (bf16[4,4,128,128]{3,2,1,0:T(8,128)(2,1)}, bf16[4,4,128,128]{3,2,1,0:T(8,128)(2,1)S(1)}, u32[]{:S(2)}) copy-start(bf16[4,4,128,128]{3,2,1,0:T(8,128)(2,1)S(1)} %fusion.21) | copy-start | bytes 1572868
  109.6 3.8 %copy-start.6 = (bf16[384,2048]{1,0:T(8,128)(2,1)S(1)}, bf16[384,2048]{1,0:T(8,128)(2,1)}, u32[]{:S(2)}) copy-start(bf16[384,2048]{1,0:T(8,128)(2,1)} %param.9) | copy-start | bytes 4718596
  113.3 2.8 %copy-start.1 = (f32[384,2048]{1,0:T(8,128)S(1)}, f32[384,2048]{1,0:T(8,128)}, u32[]{:S(2)}) copy-start(f32[384,2048]{1,0:T(8,128)} %copy.77) | copy-start | bytes 9437188
  122.6 1.2 copy-start.13
  122.7 22.9 %copy-start.16 = (pred[384,384]{1,0:T(8,128)(4,1)S(1)}, pred[384,384]{1,0:T(8,128)(4,1)}, u32[]{:S(2)}) copy-start(pred[384,384]{1,0:T(8,128)(4,1)} %compare_and_fusion) | copy-start | bytes 442372
  123.9 11.6 %collective-permute-start.9 = (f32[4,128,128]{2,1,0:T(8,128)}, f32[4,128,128]{2,1,0:T(8,128)S(1)}, u32[]{:S(2)}, u32[]{:S(2)}) collective-permute-start(f32[4,128,128]{2,1,0:T(8,128)} %get-tuple-element.44), channel_id=1, source_target_pairs={{0,1},{1,2},{2,3},{3,0},{4,5},{5,6},{6,7},{7,4},{8,9},{9,10},{10,1... | collective-permute-start | bytes 786440 | tf_op jit(solution)/shard_map/ppermute | solution.py:46
  127.4 8.9 %collective-permute-start.11 = (f32[4,128,128]{2,1,0:T(8,128)}, f32[4,128,128]{2,1,0:T(8,128)}, u32[]{:S(2)}, u32[]{:S(2)}) collective-permute-start(f32[4,128,128]{2,1,0:T(8,128)} %get-tuple-element.45), channel_id=1, source_target_pairs={{0,3},{1,0},{2,1},{3,2},{4,7},{5,4},{6,5},{7,6},{8,11},{9,8},{10,9... | collective-permute-start | bytes 786440 | tf_op jit(solution)/shard_map/ppermute | solution.py:46
  127.4 13.3 %collective-permute-start.10 = (f32[4,128,128]{2,1,0:T(8,128)}, f32[4,128,128]{2,1,0:T(8,128)}, u32[]{:S(2)}, u32[]{:S(2)}) collective-permute-start(f32[4,128,128]{2,1,0:T(8,128)} %get-tuple-element.46), channel_id=1, source_target_pairs={{0,2},{1,3},{2,0},{3,1},{4,6},{5,7},{6,4},{7,5},{8,10},{9,11},{10,... | collective-permute-start | bytes 786440 | tf_op jit(solution)/shard_map/ppermute | solution.py:46
  144.3 8.6 %collective-permute-start.12 = (f32[4,128,128]{2,1,0:T(8,128)S(1)}, f32[4,128,128]{2,1,0:T(8,128)S(1)}, u32[]{:S(2)}, u32[]{:S(2)}) collective-permute-start(f32[4,128,128]{2,1,0:T(8,128)S(1)} %fusion.39), channel_id=1, source_target_pairs={{4,0},{5,1},{6,2},{7,3},{8,4},{9,5},{10,6},{11,7},{12,8},{13,9},{1... | collective-permute-start | bytes 786440 | tf_op jit(solution)/shard_map/ppermute | solution.py:84
  145.6 8.8 %copy-start.8 = (bf16[384,16,128]{0,2,1:T(8,128)(2,1)S(1)}, bf16[384,16,128]{0,2,1:T(8,128)(2,1)}, u32[]{:S(2)}) copy-start(bf16[384,16,128]{0,2,1:T(8,128)(2,1)} %copy-done.7) | copy-start | bytes 4718596
  147.3 8.6 %copy-start.2 = (bf16[16,384,384]{2,1,0:T(8,128)(2,1)}, bf16[16,384,384]{2,1,0:T(8,128)(2,1)S(1)}, u32[]{:S(2)}) copy-start(bf16[16,384,384]{2,1,0:T(8,128)(2,1)S(1)} %select_convert_fusion) | copy-start | bytes 14155780
  152.9 9.9 %copy-start.11 = (bf16[4,4,128,128]{3,2,1,0:T(8,128)(2,1)S(1)}, bf16[4,4,128,128]{3,2,1,0:T(8,128)(2,1)}, u32[]{:S(2)}) copy-start(bf16[4,4,128,128]{3,2,1,0:T(8,128)(2,1)} %copy-done.10) | copy-start | bytes 1572868
  152.9 9.9 %copy-start.20 = (pred[384]{0:T(512)(128)(4,1)S(1)}, pred[384]{0:T(512)(128)(4,1)}, u32[]{:S(2)}) copy-start(pred[384]{0:T(512)(128)(4,1)} %copy-done.19) | copy-start | bytes 1156
  152.9 7.9 %collective-permute-start.13 = (f32[4,128,128]{2,1,0:T(8,128)S(1)}, f32[4,128,128]{2,1,0:T(8,128)S(1)}, u32[]{:S(2)}, u32[]{:S(2)}) collective-permute-start(f32[4,128,128]{2,1,0:T(8,128)S(1)} %multiply_add_fusion.1), channel_id=1, source_target_pairs={{4,0},{5,1},{6,2},{7,3},{8,4},{9,5},{10,6},{11,7},{12,8},{13,9},{1... | collective-permute-start | bytes 786440 | tf_op jit(solution)/shard_map/ppermute | solution.py:84
  161.5 7.4 %collective-permute-start.14 = (f32[4,128,128]{2,1,0:T(8,128)}, f32[4,128,128]{2,1,0:T(8,128)}, u32[]{:S(2)}, u32[]{:S(2)}) collective-permute-start(f32[4,128,128]{2,1,0:T(8,128)} %multiply_add_fusion), channel_id=1, source_target_pairs={{4,0},{5,1},{6,2},{7,3},{8,4},{9,5},{10,6},{11,7},{12,8},{13,9},{1... | collective-permute-start | bytes 786440 | tf_op jit(solution)/shard_map/ppermute | solution.py:85
  167.2 8.9 %copy-start.14 = (f32[16,128,128]{2,1,0:T(8,128)S(1)}, f32[16,128,128]{2,1,0:T(8,128)}, u32[]{:S(2)}) copy-start(f32[16,128,128]{2,1,0:T(8,128)} %copy-done.13) | copy-start | bytes 3145732
  173.3 16.6 %collective-permute-start.15 = (f32[4,128,128]{2,1,0:T(8,128)S(1)}, f32[4,128,128]{2,1,0:T(8,128)S(1)}, u32[]{:S(2)}, u32[]{:S(2)}) collective-permute-start(f32[4,128,128]{2,1,0:T(8,128)S(1)} %fusion.37), channel_id=1, source_target_pairs={{0,1},{1,2},{2,3},{3,0},{4,5},{5,6},{6,7},{7,4},{8,9},{9,10},{10,1... | collective-permute-start | bytes 786440 | tf_op jit(solution)/shard_map/ppermute | solution.py:46
  183.6 8.0 %collective-permute-start.17 = (f32[4,128,128]{2,1,0:T(8,128)S(1)}, f32[4,128,128]{2,1,0:T(8,128)S(1)}, u32[]{:S(2)}, u32[]{:S(2)}) collective-permute-start(f32[4,128,128]{2,1,0:T(8,128)S(1)} %get-tuple-element.37), channel_id=1, source_target_pairs={{0,3},{1,0},{2,1},{3,2},{4,7},{5,4},{6,5},{7,6},{8,11},{9,8},{10,9... | collective-permute-start | bytes 786440 | tf_op jit(solution)/shard_map/ppermute | solution.py:46
  184.9 8.3 %collective-permute-start.16 = (f32[4,128,128]{2,1,0:T(8,128)S(1)}, f32[4,128,128]{2,1,0:T(8,128)S(1)}, u32[]{:S(2)}, u32[]{:S(2)}) collective-permute-start(f32[4,128,128]{2,1,0:T(8,128)S(1)} %get-tuple-element.38), channel_id=1, source_target_pairs={{0,2},{1,3},{2,0},{3,1},{4,6},{5,7},{6,4},{7,5},{8,10},{9,11},{10,... | collective-permute-start | bytes 786440 | tf_op jit(solution)/shard_map/ppermute | solution.py:46
  197.9 2.5 %copy-start.9 = (bf16[384,2048]{1,0:T(8,128)(2,1)S(1)}, bf16[384,2048]{1,0:T(8,128)(2,1)}, u32[]{:S(2)}) copy-start(bf16[384,2048]{1,0:T(8,128)(2,1)} %param.6) | copy-start | bytes 4718596
  197.9 2.5 %copy-start.18 = (pred[384]{0:T(512)(128)(4,1)S(1)}, pred[384]{0:T(512)(128)(4,1)}, u32[]{:S(2)}) copy-start(pred[384]{0:T(512)(128)(4,1)} %copy-done.17) | copy-start | bytes 1156
  202.3 2.7 %copy-start.4 = (bf16[384,2048]{0,1:T(8,128)(2,1)S(1)}, bf16[384,2048]{0,1:T(8,128)(2,1)}, u32[]{:S(2)}) copy-start(bf16[384,2048]{0,1:T(8,128)(2,1)} %copy-done.3) | copy-start | bytes 4718596

commit v3 on v1

--- a/solution.py
+++ b/solution.py
@@ -45,7 +45,10 @@
             for index in range(GROUP)
         ]
         got.append(lax.ppermute(piece, axis, pairs))
-    return jnp.take(jnp.stack(got), (member - jnp.arange(GROUP)) % GROUP, axis=0)
+    placed = jnp.zeros((GROUP,) + got[0].shape, got[0].dtype)
+    for offset, piece in enumerate(got):
+        placed = lax.dynamic_update_index_in_dim(placed, piece, (member - offset) % GROUP, 0)
+    return placed
 
 
 def row_scan(state, keep_row, direction):

time: 192 us -> 177 us (0.922)
  the two profiles are of different devices: /device:TPU:0 before, /device:TPU:1 now
where the time goes in v3:
time: 177 us; the launch traced here: 176 us
  waiting for transfers between devices  43.4 us (25%)
  local copies, waits for them, and re-layouts  37.3 us (21%)
  matrix products  32 us (18%)
  starting transfers between devices  30.4 us (17%)
  other arithmetic  24.6 us (14%)
  between operations  8.75 us (5%)
    ppermute x12, waiting for transfers between devices, member_exchange(): got.append(lax.ppermute(piece, axis, pairs))  24.5 us
    ppermute x12, starting transfers between devices, member_exchange(): got.append(lax.ppermute(piece, axis, pairs))  14.2 us
    unnamed x78, local copies, waits for them, and re-layouts  13.2 us
    ppermute x4, waiting for transfers between devices, row_scan(): window = total + total_keep * lax.ppermute(window, 'seq', pairs)  12.9 us
    ppermute x4, starting transfers between devices, row_scan(): window = total + total_keep * lax.ppermute(window, 'seq', pairs)  10.8 us
    dynamic_update_slice x12, local copies, waits for them, and re-layouts, member_exchange(): lax.dynamic_update_index_in_dim(placed, piece, (member - offset) % GROUP, 0)  7.46 us
    ppermute x2, waiting for transfers between devices, row_scan(): entering = lax.ppermute(window, 'seq', pairs)  5.97 us
    add x2, other arithmetic, row_scan(): total = mine[index] + keep_row[index] * total  5.8 us
  transfers between devices with their start and end apart: 18, of which 13 were waited for; matrix products, arithmetic and copies ran while one was open for 18% of the time, Pallas kernels for 0%

profile of v3, /device:TPU:1, one launch (start us, length us, event | category | flops | bytes accessed | tf_op | source)
XLA Modules:
  0.0 176.5 jit_solution(8103782057276355970)
XLA Ops:
  1.7 1.4 compare_reduce_fusion
  4.4 3.0 %copy.88 = bf16[48,8,16,128]{3,2,1,0:T(8,128)(2,1)} copy(bf16[48,8,16,128]{3,1,2,0:T(8,128)(2,1)} %bitcast.216) | data formatting | bytes 3145728
  7.3 2.1 %copy.60 = bf16[384,16,128]{0,2,1:T(8,128)(2,1)S(1)} copy(bf16[384,16,128]{2,1,0:T(8,128)(2,1)} %bitcast.215) | data formatting | bytes 3145728 | tf_op jit(solution)/shard_map/reshape | solution.py:113
  9.5 1.9 %compare_and_fusion.2 = (pred[384]{0:T(512)(128)(4,1)}, pred[384]{0:T(512)(128)(4,1)S(1)}) fusion(s32[384]{0:T(512)S(1)} %convert_reduce_fusion, s32[]{:T(128)} %bitcast.3, pred[]{:T(512)S(6)} %not.6, s32[]{:T(128)} %bitcast.4), kind=kLoop, calls=%fused_computation.108 | loop fusion | flops 1152 | bytes 2313 | tf_op jit(solution)/shard_map/and | solution.py:111
  13.0 2.7 %collective-permute-start.1 = (f32[4,128,128]{2,1,0:T(8,128)}, f32[4,128,128]{2,1,0:T(8,128)S(1)}, u32[]{:S(2)}, u32[]{:S(2)}) collective-permute-start(f32[4,128,128]{2,1,0:T(8,128)} %get-tuple-element.46), channel_id=1, source_target_pairs={{0,2},{1,3},{2,0},{3,1},{4,6},{5,7},{6,4},{7,5},{8,10},{9,11},{10,... | collective-permute-start | bytes 786440 | tf_op jit(solution)/shard_map/ppermute | solution.py:47
  15.7 1.3 collective-permute-start
  19.1 8.5 %collective-permute-done = f32[4,128,128]{2,1,0:T(8,128)S(1)} collective-permute-done((f32[4,128,128]{2,1,0:T(8,128)}, f32[4,128,128]{2,1,0:T(8,128)S(1)}, u32[]{:S(2)}, u32[]{:S(2)}) %collective-permute-start) | collective-permute-done | bytes 262176 | tf_op jit(solution)/shard_map/ppermute | solution.py:47
  27.8 2.6 %fusion.34 = (f32[4,128,128]{2,1,0:T(8,128)S(1)}, f32[4,128,128]{2,1,0:T(8,128)}) fusion(f32[4,4,128,128]{3,2,1,0:T(8,128)S(1)} %bitcast_dynamic-update-slice_fusion.9, f32[]{:T(128)} %bitcast.13, f32[]{:T(128)} %bitcast.15, f32[]{:T(128)S(6)} %mul.173, f32[]{:T(128)} %bitcast.17), kind=kLoop, calls=%fused_computation.57 | loop fusion | flops 458752 | bytes 1572880 | tf_op jit(solution)/shard_map/add | solution.py:67
  30.4 3.2 %collective-permute-start.3 = (f32[4,128,128]{2,1,0:T(8,128)S(1)}, f32[4,128,128]{2,1,0:T(8,128)S(1)}, u32[]{:S(2)}, u32[]{:S(2)}) collective-permute-start(f32[4,128,128]{2,1,0:T(8,128)S(1)} %get-tuple-element.25), channel_id=1, source_target_pairs={{0,4},{1,5},{2,6},{3,7},{4,8},{5,9},{6,10},{7,11},{8,12},{9,13},{1... | collective-permute-start | bytes 786440 | tf_op jit(solution)/shard_map/ppermute | solution.py:73
  36.0 1.9 %collective-permute-done.3 = f32[4,128,128]{2,1,0:T(8,128)S(1)} collective-permute-done((f32[4,128,128]{2,1,0:T(8,128)S(1)}, f32[4,128,128]{2,1,0:T(8,128)S(1)}, u32[]{:S(2)}, u32[]{:S(2)}) %collective-permute-start.3) | collective-permute-done | bytes 262176 | tf_op jit(solution)/shard_map/ppermute | solution.py:73
  38.6 4.8 %collective-permute-start.4 = (f32[4,128,128]{2,1,0:T(8,128)}, f32[4,128,128]{2,1,0:T(8,128)}, u32[]{:S(2)}, u32[]{:S(2)}) collective-permute-start(f32[4,128,128]{2,1,0:T(8,128)} %multiply_add_fusion.3), channel_id=1, source_target_pairs={{0,4},{1,5},{2,6},{3,7},{4,8},{5,9},{6,10},{7,11},{8,12},{9,13},{1... | collective-permute-start | bytes 786440 | tf_op jit(solution)/shard_map/ppermute | solution.py:73
  43.4 1.9 %copy.84 = bf16[384,2048]{0,1:T(8,128)(2,1)S(1)} copy(bf16[384,2048]{1,0:T(8,128)(2,1)} %param.5) | data formatting | bytes 3145728 | tf_op jit(solution)/shard_map/reshape | solution.py:112
  47.5 4.1 %collective-permute-start.5 = (f32[4,128,128]{2,1,0:T(8,128)S(1)}, f32[4,128,128]{2,1,0:T(8,128)S(1)}, u32[]{:S(2)}, u32[]{:S(2)}) collective-permute-start(f32[4,128,128]{2,1,0:T(8,128)S(1)} %multiply_add_fusion.2), channel_id=1, source_target_pairs={{0,4},{1,5},{2,6},{3,7},{4,8},{5,9},{6,10},{7,11},{8,12},{9,13},{1... | collective-permute-start | bytes 786440 | tf_op jit(solution)/shard_map/ppermute | solution.py:74
  51.7 3.2 %select_convert_fusion.1 = bf16[16,384,384]{2,1,0:T(8,128)(2,1)S(1)} fusion(pred[384,384]{1,0:T(8,128)(4,1)S(1)} %compare_and_fusion, bf16[384,16,128]{0,2,1:T(8,128)(2,1)S(1)} %bitcast.210, bf16[384,2048]{1,0:T(8,128)(2,1)} %param.6), kind=kOutput, calls=%fused_computation.1 | convolution fusion | flops 608698368 | bytes 8011776 | tf_op jit(solution)/shard_map/thd,shd->hts/dot_general | solution.py:115
  58.4 3.8 %collective-permute-start.6 = (f32[4,128,128]{2,1,0:T(8,128)}, f32[4,128,128]{2,1,0:T(8,128)}, u32[]{:S(2)}, u32[]{:S(2)}) collective-permute-start(f32[4,128,128]{2,1,0:T(8,128)} %get-tuple-element.43), channel_id=1, source_target_pairs={{0,1},{1,2},{2,3},{3,0},{4,5},{5,6},{6,7},{7,4},{8,9},{9,10},{10,1... | collective-permute-start | bytes 786440 | tf_op jit(solution)/shard_map/ppermute | solution.py:47
  62.2 3.3 %fusion.5 = f32[16,384,128]{1,2,0:T(8,128)} fusion(bf16[16,384,384]{2,1,0:T(8,128)(2,1)S(1)} %select_convert_fusion.1, bf16[384,2048]{1,0:T(8,128)(2,1)S(1)} %copy-done), kind=kOutput, calls=%fused_computation.14 | convolution fusion | flops 603979776 | bytes 9437184 | tf_op jit(solution)/shard_map/hts,she->the/dot_general | solution.py:117
  65.5 1.4 collective-permute-start.7
  67.7 1.8 %bitcast_dynamic-update-slice_fusion.8 = f32[4,4,128,128]{3,2,1,0:T(8,128)} fusion(f32[4,4,128,128]{3,2,1,0:T(8,128)} %copy-done.18, s32[]{:T(128)S(6)} %select_n.183, f32[4,128,128]{2,1,0:T(8,128)} %collective-permute-done.6), kind=kLoop, calls=%fused_computation.66 | loop fusion | bytes 524292 | tf_op jit(solution)/shard_map/jit(dynamic_update_index_in_dim)/dynamic_update_slice | solution.py:50
  69.5 4.1 %collective-permute-done.7 = f32[4,128,128]{2,1,0:T(8,128)S(1)} collective-permute-done((f32[4,128,128]{2,1,0:T(8,128)}, f32[4,128,128]{2,1,0:T(8,128)S(1)}, u32[]{:S(2)}, u32[]{:S(2)}) %collective-permute-start.7) | collective-permute-done | bytes 262176 | tf_op jit(solution)/shard_map/ppermute | solution.py:47
  74.3 2.3 %collective-permute-done.8 = f32[4,128,128]{2,1,0:T(8,128)S(1)} collective-permute-done((f32[4,128,128]{2,1,0:T(8,128)}, f32[4,128,128]{2,1,0:T(8,128)S(1)}, u32[]{:S(2)}, u32[]{:S(2)}) %collective-permute-start.8) | collective-permute-done | bytes 262176 | tf_op jit(solution)/shard_map/ppermute | solution.py:47
  77.3 1.3 multiply_convert_fusion.1
  78.7 2.4 %multiply_reduce_fusion = (f32[384]{0:T(512)S(1)}, f32[384,16,128]{0,2,1:T(8,128)}) fusion(bf16[16,128,128]{2,1,0:T(8,128)(2,1)S(1)} %bitcast.220, bf16[384,16,128]{0,2,1:T(8,128)(2,1)S(1)} %bitcast.211, pred[384]{0:T(512)(128)(4,1)S(1)} %copy-done.27, f32[16,384,128]{1,2,0:T(8,128)S(1)} %copy-done.7), kind=kOutput, calls=%fused_computation.13 | convolution fusion | flops 204471936 | bytes 8390528 | tf_op jit(solution)/shard_map/thd,hde->the/dot_general | solution.py:127
  81.1 3.7 %copy.64 = f32[384,2048]{1,0:T(8,128)} copy(f32[384,2048]{0,1:T(8,128)} %bitcast.214) | data formatting | bytes 6291456 | tf_op jit(solution)/shard_map/reshape | solution.py:130
  84.8 2.6 %fusion = f32[384]{0:T(512)S(1)} fusion(bf16[384,2048]{1,0:T(8,128)(2,1)S(1)} %copy-done.10, f32[384,2048]{1,0:T(8,128)} %copy.64, f32[384]{0:T(512)S(1)} %add_sqrt_fusion), kind=kLoop, calls=%fused_computation.4 | loop fusion | flops 3145344 | bytes 4721664 | tf_op jit(solution)/shard_map/reduce_sum | solution.py:137
  87.6 2.4 %fusion.2 = (bf16[384,2048]{1,0:T(8,128)(2,1)}, bf16[384,2048]{1,0:T(8,128)(2,1)}) fusion(bf16[384,2048]{1,0:T(8,128)(2,1)S(1)} %copy-done.10, f32[384]{0:T(512)S(1)} %broadcast_multiply_fusion, f32[384]{0:T(512)S(1)} %add_sqrt_fusion, f32[384,2048]{1,0:T(8,128)S(1)} %copy-done.1), kind=kLoop, calls=%fused_computation.6 | loop fusion | flops 5505024 | bytes 7867392 | tf_op jit(solution)/shard_map/convert_element_type | solution.py:138
  90.0 1.9 %copy.85 = bf16[384,2048]{0,1:T(8,128)(2,1)S(1)} copy(bf16[384,2048]{1,0:T(8,128)(2,1)} %get-tuple-element.27) | data formatting | bytes 3145728 | tf_op jit(solution)/shard_map/reshape | solution.py:138
  91.9 2.2 %fusion.14 = f32[16,128,128]{2,1,0:T(8,128)S(1)} fusion(bf16[384,16,128]{0,2,1:T(8,128)(2,1)S(1)} %bitcast.206, bf16[384,16,128]{0,2,1:T(8,128)(2,1)} %bitcast.212, pred[384]{0:T(512)(128)(4,1)S(1)} %copy-done.28), kind=kOutput, calls=%fused_computation.23 | convolution fusion | flops 202113024 | bytes 4194688 | tf_op jit(solution)/shard_map/thd,the->hde/dot_general | solution.py:140
  102.8 4.5 %collective-permute-done.10 = f32[4,128,128]{2,1,0:T(8,128)} collective-permute-done((f32[4,128,128]{2,1,0:T(8,128)}, f32[4,128,128]{2,1,0:T(8,128)}, u32[]{:S(2)}, u32[]{:S(2)}) %collective-permute-start.10) | collective-permute-done | bytes 262176 | tf_op jit(solution)/shard_map/ppermute | solution.py:47
  107.3 1.7 bitcast_dynamic-update-slice_fusion.4
  109.9 3.2 %fusion.27 = (f32[4,128,128]{2,1,0:T(8,128)S(1)}, f32[4,128,128]{2,1,0:T(8,128)S(1)}) fusion(f32[4,4,128,128]{3,2,1,0:T(8,128)} %bitcast_dynamic-update-slice_fusion.3, f32[]{:T(128)} %bitcast.51, f32[]{:T(128)} %bitcast.45, f32[]{:T(128)S(6)} %mul.198, f32[]{:T(128)} %bitcast.47), kind=kLoop, calls=%fused_computation.43 | loop fusion | flops 458752 | bytes 1572880 | tf_op jit(solution)/shard_map/add | solution.py:67
  113.1 1.5 collective-permute-start.12
  114.6 5.2 %fusion.47 = f32[16,128,384]{2,1,0:T(8,128)} fusion(bf16[384,16,128]{0,2,1:T(8,128)(2,1)S(1)} %bitcast.207, bf16[16,384,384]{2,1,0:T(8,128)(2,1)} %copy-done.2), kind=kOutput, calls=%fused_computation.123 | convolution fusion | flops 603979776 | bytes 9437184 | tf_op jit(solution)/shard_map/hts,the->she/dot_general | solution.py:167
  119.8 3.6 %collective-permute-done.12 = f32[4,128,128]{2,1,0:T(8,128)S(1)} collective-permute-done((f32[4,128,128]{2,1,0:T(8,128)S(1)}, f32[4,128,128]{2,1,0:T(8,128)S(1)}, u32[]{:S(2)}, u32[]{:S(2)}) %collective-permute-start.12) | collective-permute-done | bytes 262176 | tf_op jit(solution)/shard_map/ppermute | solution.py:73
  124.7 1.7 select_convert_fusion
  126.4 7.1 %collective-permute-done.13 = f32[4,128,128]{2,1,0:T(8,128)S(1)} collective-permute-done((f32[4,128,128]{2,1,0:T(8,128)S(1)}, f32[4,128,128]{2,1,0:T(8,128)S(1)}, u32[]{:S(2)}, u32[]{:S(2)}) %collective-permute-start.13) | collective-permute-done | bytes 262176 | tf_op jit(solution)/shard_map/ppermute | solution.py:73
  134.9 1.6 fusion.46
  136.5 5.9 %collective-permute-done.14 = f32[4,128,128]{2,1,0:T(8,128)S(1)} collective-permute-done((f32[4,128,128]{2,1,0:T(8,128)S(1)}, f32[4,128,128]{2,1,0:T(8,128)S(1)}, u32[]{:S(2)}, u32[]{:S(2)}) %collective-permute-start.14) | collective-permute-done | bytes 262176 | tf_op jit(solution)/shard_map/ppermute | solution.py:74
  142.4 2.4 %add_bitcast_fusion.2 = (f32[1,4,128,128]{3,2,1,0:T(8,128)S(1)}, f32[1,4,128,128]{3,2,1,0:T(8,128)S(1)}, f32[1,4,128,128]{3,2,1,0:T(8,128)S(1)}) fusion(f32[4,128,128]{2,1,0:T(8,128)S(1)} %collective-permute-done.14, f32[]{:T(128)S(6)} %mul.202, f32[4,128,128]{2,1,0:T(8,128)S(1)} %get-tuple-element.23, f32[]{:T(128)} %bitcast.45, ...), kind=kLoop, calls=%fused_computation.76 | loop fusion | flops 589824 | bytes 1835028 | tf_op jit(solution)/shard_map/stack | solution.py:75
  146.8 2.7 %collective-permute-start.15 = (f32[4,128,128]{2,1,0:T(8,128)}, f32[4,128,128]{2,1,0:T(8,128)}, u32[]{:S(2)}, u32[]{:S(2)}) collective-permute-start(f32[4,128,128]{2,1,0:T(8,128)} %get-tuple-element.35), channel_id=1, source_target_pairs={{0,1},{1,2},{2,3},{3,0},{4,5},{5,6},{6,7},{7,4},{8,9},{9,10},{10,1... | collective-permute-start | bytes 786440 | tf_op jit(solution)/shard_map/ppermute | solution.py:47
  149.5 1.8 %fusion.4 = bf16[384,16,128]{0,2,1:T(8,128)(2,1)} fusion(f32[16,384,128]{1,2,0:T(8,128)S(1)} %fusion.46, bf16[16,128,128]{2,1,0:T(8,128)(2,1)S(1)} %bitcast.221, bf16[384,16,128]{0,2,1:T(8,128)(2,1)S(1)} %bitcast.209, pred[384]{0:T(512)(128)(4,1)S(1)} %copy-done.29), kind=kOutput, calls=%fused_computation.10 | convolution fusion | flops 203685888 | bytes 6816128 | tf_op jit(solution)/shard_map/the,hde->thd/dot_general | solution.py:156
  151.2 2.7 %copy.77 = bf16[384,2048]{1,0:T(8,128)(2,1)} copy(bf16[384,2048]{0,1:T(8,128)(2,1)} %bitcast.217) | data formatting | bytes 3145728
  153.9 2.4 %collective-permute-done.15 = f32[4,128,128]{2,1,0:T(8,128)} collective-permute-done((f32[4,128,128]{2,1,0:T(8,128)}, f32[4,128,128]{2,1,0:T(8,128)}, u32[]{:S(2)}, u32[]{:S(2)}) %collective-permute-start.15) | collective-permute-done | bytes 262176 | tf_op jit(solution)/shard_map/ppermute | solution.py:47
  157.4 2.5 %collective-permute-done.17 = f32[4,128,128]{2,1,0:T(8,128)S(1)} collective-permute-done((f32[4,128,128]{2,1,0:T(8,128)S(1)}, f32[4,128,128]{2,1,0:T(8,128)S(1)}, u32[]{:S(2)}, u32[]{:S(2)}) %collective-permute-start.17) | collective-permute-done | bytes 262176 | tf_op jit(solution)/shard_map/ppermute | solution.py:47
  160.0 2.5 %fusion.7 = f32[16,128,384]{2,1,0:T(8,128)} fusion(bf16[16,128,128]{2,1,0:T(8,128)(2,1)S(1)} %bitcast.222, bf16[384,2048]{1,0:T(8,128)(2,1)S(1)} %copy-done), kind=kOutput, calls=%fused_computation.16 | convolution fusion | flops 201326592 | bytes 5242880 | tf_op jit(solution)/shard_map/she,hde->shd/dot_general | solution.py:163
  163.5 1.9 %add_convert_fusion = bf16[16,128,384]{2,1,0:T(8,128)(2,1)} fusion(f32[16,128,384]{2,1,0:T(8,128)S(1)} %copy-done.6, bf16[16,128,128]{2,1,0:T(8,128)(2,1)S(1)} %bitcast.223, pred[384]{0:T(512)(128)(4,1)S(1)} %copy-done.26, bf16[384,2048]{1,0:T(8,128)(2,1)S(1)} %copy-done.13), kind=kOutput, calls=%fused_computation.12 | convolution fusion | flops 203685888 | bytes 6816128 | tf_op jit(solution)/shard_map/shd,hde->she/dot_general | solution.py:168
  165.4 2.7 %copy.79 = bf16[384,2048]{1,0:T(8,128)(2,1)} copy(bf16[384,2048]{0,1:T(8,128)(2,1)} %bitcast.218) | data formatting | bytes 3145728
  168.1 5.8 %fusion.3 = bf16[384,16,128]{0,2,1:T(8,128)(2,1)} fusion(f32[16,128,384]{2,1,0:T(8,128)} %fusion.7, bf16[384,16,128]{0,2,1:T(8,128)(2,1)S(1)} %bitcast.213, bf16[16,384,384]{2,1,0:T(8,128)(2,1)} %copy-done.3, pred[384]{0:T(512)(128)(4,1)S(1)} %copy-done.26), kind=kOutput, calls=%fused_computation.8 | convolution fusion | flops 606339072 | bytes 11010432 | tf_op jit(solution)/shard_map/hts,thd->shd/dot_general | solution.py:160
  173.9 2.6 %copy.78 = bf16[384,2048]{1,0:T(8,128)(2,1)} copy(bf16[384,2048]{0,1:T(8,128)(2,1)} %bitcast.219) | data formatting | bytes 3145728
  (132 shorter events, 26.2 us)
Async XLA Ops:
  0.6 10.7 %copy-start = (bf16[384,2048]{1,0:T(8,128)(2,1)S(1)}, bf16[384,2048]{1,0:T(8,128)(2,1)}, u32[]{:S(2)}) copy-start(bf16[384,2048]{1,0:T(8,128)(2,1)} %param.7) | copy-start | bytes 4718596
  0.7 6.6 %copy-start.22 = (s32[384]{0:T(512)}, s32[384]{0:T(512)S(1)}, u32[]{:S(2)}) copy-start(s32[384]{0:T(512)S(1)} %iota_add_fusion) | copy-start | bytes 4612
  3.0 14.0 %copy-start.23 = (s32[4]{0:T(128)}, s32[4]{0:T(128)S(1)}, u32[]{:S(2)}) copy-start(s32[4]{0:T(128)S(1)} %get-tuple-element.24) | copy-start | bytes 52
  3.8 5.7 %copy-start.21 = (s32[384]{0:T(512)}, s32[384]{0:T(512)S(1)}, u32[]{:S(2)}) copy-start(s32[384]{0:T(512)S(1)} %convert_reduce_fusion) | copy-start | bytes 4612
  9.5 2.5 %copy-start.11 = (bf16[384,16,128]{0,2,1:T(8,128)(2,1)}, bf16[384,16,128]{0,2,1:T(8,128)(2,1)S(1)}, u32[]{:S(2)}) copy-start(bf16[384,16,128]{0,2,1:T(8,128)(2,1)S(1)} %copy.60) | copy-start | bytes 4718596
  13.0 14.7 %collective-permute-start.2 = (f32[4,128,128]{2,1,0:T(8,128)}, f32[4,128,128]{2,1,0:T(8,128)S(1)}, u32[]{:S(2)}, u32[]{:S(2)}) collective-permute-start(f32[4,128,128]{2,1,0:T(8,128)} %get-tuple-element.45), channel_id=1, source_target_pairs={{0,3},{1,0},{2,1},{3,2},{4,7},{5,4},{6,5},{7,6},{8,11},{9,8},{10,9... | collective-permute-start | bytes 786440 | tf_op jit(solution)/shard_map/ppermute | solution.py:47
  13.0 14.7 %collective-permute-start.1 = (f32[4,128,128]{2,1,0:T(8,128)}, f32[4,128,128]{2,1,0:T(8,128)S(1)}, u32[]{:S(2)}, u32[]{:S(2)}) collective-permute-start(f32[4,128,128]{2,1,0:T(8,128)} %get-tuple-element.46), channel_id=1, source_target_pairs={{0,2},{1,3},{2,0},{3,1},{4,6},{5,7},{6,4},{7,5},{8,10},{9,11},{10,... | collective-permute-start | bytes 786440 | tf_op jit(solution)/shard_map/ppermute | solution.py:47
  15.7 12.0 %collective-permute-start = (f32[4,128,128]{2,1,0:T(8,128)}, f32[4,128,128]{2,1,0:T(8,128)S(1)}, u32[]{:S(2)}, u32[]{:S(2)}) collective-permute-start(f32[4,128,128]{2,1,0:T(8,128)} %get-tuple-element.47), channel_id=1, source_target_pairs={{0,1},{1,2},{2,3},{3,0},{4,5},{5,6},{6,7},{7,4},{8,9},{9,10},{10,1... | collective-permute-start | bytes 786440 | tf_op jit(solution)/shard_map/ppermute | solution.py:47
  27.8 10.9 %copy-start.8 = (f32[4,4,128,128]{3,2,1,0:T(8,128)}, f32[4,4,128,128]{3,2,1,0:T(8,128)S(1)}, u32[]{:S(2)}) copy-start(f32[4,4,128,128]{3,2,1,0:T(8,128)S(1)} %bitcast_dynamic-update-slice_fusion.9) | copy-start | bytes 3145732
  30.4 7.6 %collective-permute-start.3 = (f32[4,128,128]{2,1,0:T(8,128)S(1)}, f32[4,128,128]{2,1,0:T(8,128)S(1)}, u32[]{:S(2)}, u32[]{:S(2)}) collective-permute-start(f32[4,128,128]{2,1,0:T(8,128)S(1)} %get-tuple-element.25), channel_id=1, source_target_pairs={{0,4},{1,5},{2,6},{3,7},{4,8},{5,9},{6,10},{7,11},{8,12},{9,13},{1... | collective-permute-start | bytes 786440 | tf_op jit(solution)/shard_map/ppermute | solution.py:73
  38.6 7.9 %collective-permute-start.4 = (f32[4,128,128]{2,1,0:T(8,128)}, f32[4,128,128]{2,1,0:T(8,128)}, u32[]{:S(2)}, u32[]{:S(2)}) collective-permute-start(f32[4,128,128]{2,1,0:T(8,128)} %multiply_add_fusion.3), channel_id=1, source_target_pairs={{0,4},{1,5},{2,6},{3,7},{4,8},{5,9},{6,10},{7,11},{8,12},{9,13},{1... | collective-permute-start | bytes 786440 | tf_op jit(solution)/shard_map/ppermute | solution.py:73
  45.3 33.3 %copy-start.4 = (bf16[384,2048]{0,1:T(8,128)(2,1)}, bf16[384,2048]{0,1:T(8,128)(2,1)S(1)}, u32[]{:S(2)}) copy-start(bf16[384,2048]{0,1:T(8,128)(2,1)S(1)} %copy.84) | copy-start | bytes 4718596
  47.5 7.4 %collective-permute-start.5 = (f32[4,128,128]{2,1,0:T(8,128)S(1)}, f32[4,128,128]{2,1,0:T(8,128)S(1)}, u32[]{:S(2)}, u32[]{:S(2)}) collective-permute-start(f32[4,128,128]{2,1,0:T(8,128)S(1)} %multiply_add_fusion.2), channel_id=1, source_target_pairs={{0,4},{1,5},{2,6},{3,7},{4,8},{5,9},{6,10},{7,11},{8,12},{9,13},{1... | collective-permute-start | bytes 786440 | tf_op jit(solution)/shard_map/ppermute | solution.py:74
  51.7 3.3 %copy-start.9 = (f32[4,4,128,128]{3,2,1,0:T(8,128)S(1)}, f32[4,4,128,128]{3,2,1,0:T(8,128)}, u32[]{:S(2)}) copy-start(f32[4,4,128,128]{3,2,1,0:T(8,128)} %copy-done.8) | copy-start | bytes 3145732
  51.7 3.3 %copy-start.19 = (f32[4,128,128]{2,1,0:T(8,128)S(1)}, f32[4,128,128]{2,1,0:T(8,128)}, u32[]{:S(2)}) copy-start(f32[4,128,128]{2,1,0:T(8,128)} %get-tuple-element.26) | copy-start | bytes 786436
  54.9 7.4 %copy-start.2 = (bf16[16,384,384]{2,1,0:T(8,128)(2,1)}, bf16[16,384,384]{2,1,0:T(8,128)(2,1)S(1)}, u32[]{:S(2)}) copy-start(bf16[16,384,384]{2,1,0:T(8,128)(2,1)S(1)} %select_convert_fusion.1) | copy-start | bytes 14155780
  58.4 8.5 %copy-start.24 = (s32[4]{0:T(128)S(1)}, s32[4]{0:T(128)}, u32[]{:S(2)}) copy-start(s32[4]{0:T(128)} %copy-done.23) | copy-start | bytes 52
  58.4 8.5 %copy-start.31 = (s32[4]{0:T(128)S(1)}, s32[4]{0:T(128)}, u32[]{:S(2)}) copy-start(s32[4]{0:T(128)} %copy-done.30) | copy-start | bytes 52
  58.4 8.5 %copy-start.33 = (s32[4]{0:T(128)S(1)}, s32[4]{0:T(128)}, u32[]{:S(2)}) copy-start(s32[4]{0:T(128)} %copy-done.32) | copy-start | bytes 52
  58.4 9.2 %collective-permute-start.6 = (f32[4,128,128]{2,1,0:T(8,128)}, f32[4,128,128]{2,1,0:T(8,128)}, u32[]{:S(2)}, u32[]{:S(2)}) collective-permute-start(f32[4,128,128]{2,1,0:T(8,128)} %get-tuple-element.43), channel_id=1, source_target_pairs={{0,1},{1,2},{2,3},{3,0},{4,5},{5,6},{6,7},{7,4},{8,9},{9,10},{10,1... | collective-permute-start | bytes 786440 | tf_op jit(solution)/shard_map/ppermute | solution.py:47
  65.5 8.1 %collective-permute-start.7 = (f32[4,128,128]{2,1,0:T(8,128)}, f32[4,128,128]{2,1,0:T(8,128)S(1)}, u32[]{:S(2)}, u32[]{:S(2)}) collective-permute-start(f32[4,128,128]{2,1,0:T(8,128)} %get-tuple-element.42), channel_id=1, source_target_pairs={{0,2},{1,3},{2,0},{3,1},{4,6},{5,7},{6,4},{7,5},{8,10},{9,11},{10,... | collective-permute-start | bytes 786440 | tf_op jit(solution)/shard_map/ppermute | solution.py:47
  67.6 8.9 %collective-permute-start.8 = (f32[4,128,128]{2,1,0:T(8,128)}, f32[4,128,128]{2,1,0:T(8,128)S(1)}, u32[]{:S(2)}, u32[]{:S(2)}) collective-permute-start(f32[4,128,128]{2,1,0:T(8,128)} %get-tuple-element.41), channel_id=1, source_target_pairs={{0,3},{1,0},{2,1},{3,2},{4,7},{5,4},{6,5},{7,6},{8,11},{9,8},{10,9... | collective-permute-start | bytes 786440 | tf_op jit(solution)/shard_map/ppermute | solution.py:47
  67.6 11.0 %copy-start.7 = (f32[16,384,128]{1,2,0:T(8,128)S(1)}, f32[16,384,128]{1,2,0:T(8,128)}, u32[]{:S(2)}) copy-start(f32[16,384,128]{1,2,0:T(8,128)} %fusion.5) | copy-start | bytes 9437188
  67.6 11.0 %copy-start.27 = (pred[384]{0:T(512)(128)(4,1)S(1)}, pred[384]{0:T(512)(128)(4,1)}, u32[]{:S(2)}) copy-start(pred[384]{0:T(512)(128)(4,1)} %get-tuple-element.51) | copy-start | bytes 1156
  78.6 2.4 %copy-start.14 = (bf16[4,4,128,128]{3,2,1,0:T(8,128)(2,1)}, bf16[4,4,128,128]{3,2,1,0:T(8,128)(2,1)S(1)}, u32[]{:S(2)}) copy-start(bf16[4,4,128,128]{3,2,1,0:T(8,128)(2,1)S(1)} %multiply_convert_fusion.1) | copy-start | bytes 1572868
  81.0 3.7 %copy-start.10 = (bf16[384,2048]{1,0:T(8,128)(2,1)S(1)}, bf16[384,2048]{1,0:T(8,128)(2,1)}, u32[]{:S(2)}) copy-start(bf16[384,2048]{1,0:T(8,128)(2,1)} %param.9) | copy-start | bytes 4718596
  84.8 2.8 %copy-start.1 = (f32[384,2048]{1,0:T(8,128)S(1)}, f32[384,2048]{1,0:T(8,128)}, u32[]{:S(2)}) copy-start(f32[384,2048]{1,0:T(8,128)} %copy.64) | copy-start | bytes 9437188
  94.1 2.1 %copy-start.34 = (pred[4]{0:T(512)(128)(4,1)S(1)}, pred[4]{0:T(512)(128)(4,1)}, u32[]{:S(2)}) copy-start(pred[4]{0:T(512)(128)(4,1)} %get-tuple-element.16) | copy-start | bytes 16
  96.2 5.9 %collective-permute-start.9 = (f32[4,128,128]{2,1,0:T(8,128)}, f32[4,128,128]{2,1,0:T(8,128)S(1)}, u32[]{:S(2)}, u32[]{:S(2)}) collective-permute-start(f32[4,128,128]{2,1,0:T(8,128)} %get-tuple-element.39), channel_id=1, source_target_pairs={{0,1},{1,2},{2,3},{3,0},{4,5},{5,6},{6,7},{7,4},{8,9},{9,10},{10,1... | collective-permute-start | bytes 786440 | tf_op jit(solution)/shard_map/ppermute | solution.py:47
  96.2 11.1 %collective-permute-start.10 = (f32[4,128,128]{2,1,0:T(8,128)}, f32[4,128,128]{2,1,0:T(8,128)}, u32[]{:S(2)}, u32[]{:S(2)}) collective-permute-start(f32[4,128,128]{2,1,0:T(8,128)} %get-tuple-element.38), channel_id=1, source_target_pairs={{0,2},{1,3},{2,0},{3,1},{4,6},{5,7},{6,4},{7,5},{8,10},{9,11},{10,... | collective-permute-start | bytes 786440 | tf_op jit(solution)/shard_map/ppermute | solution.py:47
  101.3 7.9 %collective-permute-start.11 = (f32[4,128,128]{2,1,0:T(8,128)}, f32[4,128,128]{2,1,0:T(8,128)S(1)}, u32[]{:S(2)}, u32[]{:S(2)}) collective-permute-start(f32[4,128,128]{2,1,0:T(8,128)} %get-tuple-element.37), channel_id=1, source_target_pairs={{0,3},{1,0},{2,1},{3,2},{4,7},{5,4},{6,5},{7,6},{8,11},{9,8},{10,9... | collective-permute-start | bytes 786440 | tf_op jit(solution)/shard_map/ppermute | solution.py:47
  113.1 10.3 %collective-permute-start.12 = (f32[4,128,128]{2,1,0:T(8,128)S(1)}, f32[4,128,128]{2,1,0:T(8,128)S(1)}, u32[]{:S(2)}, u32[]{:S(2)}) collective-permute-start(f32[4,128,128]{2,1,0:T(8,128)S(1)} %get-tuple-element.22), channel_id=1, source_target_pairs={{4,0},{5,1},{6,2},{7,3},{8,4},{9,5},{10,6},{11,7},{12,8},{13,9},{1... | collective-permute-start | bytes 786440 | tf_op jit(solution)/shard_map/ppermute | solution.py:73
  123.4 10.1 %collective-permute-start.13 = (f32[4,128,128]{2,1,0:T(8,128)S(1)}, f32[4,128,128]{2,1,0:T(8,128)S(1)}, u32[]{:S(2)}, u32[]{:S(2)}) collective-permute-start(f32[4,128,128]{2,1,0:T(8,128)S(1)} %multiply_add_fusion.1), channel_id=1, source_target_pairs={{4,0},{5,1},{6,2},{7,3},{8,4},{9,5},{10,6},{11,7},{12,8},{13,9},{1... | collective-permute-start | bytes 786440 | tf_op jit(solution)/shard_map/ppermute | solution.py:73
  124.7 10.2 %copy-start.12 = (bf16[384,16,128]{0,2,1:T(8,128)(2,1)S(1)}, bf16[384,16,128]{0,2,1:T(8,128)(2,1)}, u32[]{:S(2)}) copy-start(bf16[384,16,128]{0,2,1:T(8,128)(2,1)} %copy-done.11) | copy-start | bytes 4718596
  126.4 10.0 %copy-start.3 = (bf16[16,384,384]{2,1,0:T(8,128)(2,1)}, bf16[16,384,384]{2,1,0:T(8,128)(2,1)S(1)}, u32[]{:S(2)}) copy-start(bf16[16,384,384]{2,1,0:T(8,128)(2,1)S(1)} %select_convert_fusion) | copy-start | bytes 14155780
  133.6 8.8 %collective-permute-start.14 = (f32[4,128,128]{2,1,0:T(8,128)S(1)}, f32[4,128,128]{2,1,0:T(8,128)S(1)}, u32[]{:S(2)}, u32[]{:S(2)}) collective-permute-start(f32[4,128,128]{2,1,0:T(8,128)S(1)} %multiply_add_fusion), channel_id=1, source_target_pairs={{4,0},{5,1},{6,2},{7,3},{8,4},{9,5},{10,6},{11,7},{12,8},{13,9},{1... | collective-permute-start | bytes 786440 | tf_op jit(solution)/shard_map/ppermute | solution.py:74
  144.9 4.6 %copy-start.15 = (bf16[4,4,128,128]{3,2,1,0:T(8,128)(2,1)S(1)}, bf16[4,4,128,128]{3,2,1,0:T(8,128)(2,1)}, u32[]{:S(2)}) copy-start(bf16[4,4,128,128]{3,2,1,0:T(8,128)(2,1)} %copy-done.14) | copy-start | bytes 1572868
  144.9 4.6 %copy-start.29 = (pred[384]{0:T(512)(128)(4,1)S(1)}, pred[384]{0:T(512)(128)(4,1)}, u32[]{:S(2)}) copy-start(pred[384]{0:T(512)(128)(4,1)} %get-tuple-element.51) | copy-start | bytes 1156
  146.0 5.2 %copy-start.16 = (f32[4,4,128,128]{3,2,1,0:T(8,128)}, f32[4,4,128,128]{3,2,1,0:T(8,128)S(1)}, u32[]{:S(2)}) copy-start(f32[4,4,128,128]{3,2,1,0:T(8,128)S(1)} %get-tuple-element.36) | copy-start | bytes 3145732
  146.0 11.3 %collective-permute-start.16 = (f32[4,128,128]{2,1,0:T(8,128)}, f32[4,128,128]{2,1,0:T(8,128)S(1)}, u32[]{:S(2)}, u32[]{:S(2)}) collective-permute-start(f32[4,128,128]{2,1,0:T(8,128)} %get-tuple-element.34), channel_id=1, source_target_pairs={{0,2},{1,3},{2,0},{3,1},{4,6},{5,7},{6,4},{7,5},{8,10},{9,11},{10,... | collective-permute-start | bytes 786440 | tf_op jit(solution)/shard_map/ppermute | solution.py:47
  146.8 9.6 %collective-permute-start.15 = (f32[4,128,128]{2,1,0:T(8,128)}, f32[4,128,128]{2,1,0:T(8,128)}, u32[]{:S(2)}, u32[]{:S(2)}) collective-permute-start(f32[4,128,128]{2,1,0:T(8,128)} %get-tuple-element.35), channel_id=1, source_target_pairs={{0,1},{1,2},{2,3},{3,0},{4,5},{5,6},{6,7},{7,4},{8,9},{9,10},{10,1... | collective-permute-start | bytes 786440 | tf_op jit(solution)/shard_map/ppermute | solution.py:47
  151.2 2.7 %copy-start.20 = (f32[4,128,128]{2,1,0:T(8,128)S(1)}, f32[4,128,128]{2,1,0:T(8,128)}, u32[]{:S(2)}) copy-start(f32[4,128,128]{2,1,0:T(8,128)} %get-tuple-element.33) | copy-start | bytes 786436
  151.2 5.1 %copy-start.17 = (f32[4,4,128,128]{3,2,1,0:T(8,128)S(1)}, f32[4,4,128,128]{3,2,1,0:T(8,128)}, u32[]{:S(2)}) copy-start(f32[4,4,128,128]{3,2,1,0:T(8,128)} %copy-done.16) | copy-start | bytes 3145732
  153.9 5.9 %collective-permute-start.17 = (f32[4,128,128]{2,1,0:T(8,128)S(1)}, f32[4,128,128]{2,1,0:T(8,128)S(1)}, u32[]{:S(2)}, u32[]{:S(2)}) collective-permute-start(f32[4,128,128]{2,1,0:T(8,128)S(1)} %copy-done.20), channel_id=1, source_target_pairs={{0,3},{1,0},{2,1},{3,2},{4,7},{5,4},{6,5},{7,6},{8,11},{9,8},{10,9... | collective-permute-start | bytes 786440 | tf_op jit(solution)/shard_map/ppermute | solution.py:47
  160.0 2.6 %copy-start.6 = (f32[16,128,384]{2,1,0:T(8,128)S(1)}, f32[16,128,384]{2,1,0:T(8,128)}, u32[]{:S(2)}) copy-start(f32[16,128,384]{2,1,0:T(8,128)} %fusion.47) | copy-start | bytes 9437188
  160.0 3.5 %copy-start.13 = (bf16[384,2048]{1,0:T(8,128)(2,1)S(1)}, bf16[384,2048]{1,0:T(8,128)(2,1)}, u32[]{:S(2)}) copy-start(bf16[384,2048]{1,0:T(8,128)(2,1)} %param.6) | copy-start | bytes 4718596
  160.0 3.5 %copy-start.26 = (pred[384]{0:T(512)(128)(4,1)S(1)}, pred[384]{0:T(512)(128)(4,1)}, u32[]{:S(2)}) copy-start(pred[384]{0:T(512)(128)(4,1)} %copy-done.25) | copy-start | bytes 1156
  165.4 2.7 %copy-start.5 = (bf16[384,2048]{0,1:T(8,128)(2,1)S(1)}, bf16[384,2048]{0,1:T(8,128)(2,1)}, u32[]{:S(2)}) copy-start(bf16[384,2048]{0,1:T(8,128)(2,1)} %copy-done.4) | copy-start | bytes 4718596
  (7 other events, 9.2 us)

commit v4 on v3

--- a/solution.py
+++ b/solution.py
@@ -2,6 +2,7 @@
 import jax.numpy as jnp
 from jax import lax
 from jax.sharding import PartitionSpec as P
+from jax.experimental import pallas as pl
 
 HEAD = 128
 SPAN = 12
@@ -95,6 +96,96 @@
     return windowed_prefix((state, fallback_flag), direction)[0]
 
 
+HEAD_STEP = 4
+INTERPRET = False
+NN = ((1,), (0,))
+NT = ((1,), (1,))
+TN = ((0,), (0,))
+
+
+def mm(left, right, contract):
+    return lax.dot_general(left, right, (contract, ((), ())), preferred_element_type=jnp.float32)
+
+
+def head_call(body, inputs, outputs):
+    rows = inputs[0].shape[0]
+
+    def spec(shape):
+        if len(shape) == 3:
+            return pl.BlockSpec((HEAD_STEP,) + shape[1:], lambda g: (g, 0, 0))
+        if shape[1] == rows or shape[1] == 1:
+            return pl.BlockSpec(shape, lambda g: (0, 0))
+        return pl.BlockSpec((shape[0], HEAD_STEP * HEAD), lambda g: (0, g))
+
+    heads = inputs[0].shape[1] // HEAD
+    return pl.pallas_call(
+        body,
+        grid=(heads // HEAD_STEP,),
+        in_specs=[spec(x.shape) for x in inputs],
+        out_specs=[spec(o.shape) for o in outputs],
+        out_shape=outputs,
+        interpret=INTERPRET,
+    )(*inputs)
+
+
+def columns(index):
+    return slice(index * HEAD, (index + 1) * HEAD)
+
+
+def zeroed(mask, value):
+    return jnp.where(mask, value, jnp.zeros_like(value))
+
+
+def state_body(key_ref, value_ref, tail_ref, state_ref):
+    tail = tail_ref[...] > 0
+    for i in range(HEAD_STEP):
+        state_ref[i] = mm(zeroed(tail, key_ref[:, columns(i)]), value_ref[:, columns(i)], TN)
+
+
+def inside_body(query_ref, key_ref, value_ref, keep_ref, weight_ref, inside_ref):
+    keep = keep_ref[...] > 0
+    for i in range(HEAD_STEP):
+        scores = mm(query_ref[:, columns(i)], key_ref[:, columns(i)], NT)
+        weights = zeroed(keep, scores).astype(jnp.bfloat16)
+        weight_ref[i] = weights
+        inside_ref[:, columns(i)] = mm(weights, value_ref[:, columns(i)], NN)
+
+
+def mixed_body(query_ref, inside_ref, prefix_ref, carry_ref, mixed_ref):
+    carry = carry_ref[...] > 0
+    for i in range(HEAD_STEP):
+        carried = mm(query_ref[:, columns(i)], prefix_ref[i], NN)
+        mixed_ref[:, columns(i)] = inside_ref[:, columns(i)] + zeroed(carry, carried)
+
+
+def local_body(query_ref, grad_ref, carry_ref, local_ref):
+    carry = carry_ref[...] > 0
+    for i in range(HEAD_STEP):
+        local_ref[i] = mm(zeroed(carry, query_ref[:, columns(i)]), grad_ref[:, columns(i)], TN)
+
+
+def grad_body(query_ref, key_ref, value_ref, grad_ref, weight_ref, prefix_ref, keep_ref, carry_ref,
+              query_out, key_out, value_out):
+    keep = keep_ref[...] > 0
+    carry = carry_ref[...] > 0
+    for i in range(HEAD_STEP):
+        grad = grad_ref[:, columns(i)]
+        grad_weights = zeroed(keep, mm(grad, value_ref[:, columns(i)], NT)).astype(jnp.bfloat16)
+        from_prefix = zeroed(carry, mm(grad, prefix_ref[i], NT))
+        query_out[:, columns(i)] = (mm(grad_weights, key_ref[:, columns(i)], NN) + from_prefix).astype(jnp.bfloat16)
+        key_out[:, columns(i)] = mm(grad_weights, query_ref[:, columns(i)], TN)
+        value_out[:, columns(i)] = mm(weight_ref[i], grad, TN)
+
+
+def tail_body(key_ref, value_ref, key_part, value_part, suffix_ref, tail_ref, key_out, value_out):
+    tail = tail_ref[...] > 0
+    for i in range(HEAD_STEP):
+        key_carry = zeroed(tail, mm(value_ref[:, columns(i)], suffix_ref[i], NT))
+        value_carry = zeroed(tail, mm(key_ref[:, columns(i)], suffix_ref[i], NN))
+        key_out[:, columns(i)] = (key_part[:, columns(i)] + key_carry).astype(jnp.bfloat16)
+        value_out[:, columns(i)] = (value_part[:, columns(i)] + value_carry).astype(jnp.bfloat16)
+
+
 def shards(queries, keys, values, lengths, out_grad):
     row_count, feat_width = queries.shape
     head_count = feat_width // HEAD
@@ -109,72 +200,42 @@
     has_start = jnp.any((starts >= first_row) & (starts < first_row + row_count))
     stops_back = jnp.logical_or(doc_ids[0] != doc_ids[row_count - 1], jnp.logical_not(continues))
     use_carry = lead_rows & continues
-    query_heads = queries.reshape(row_count, head_count, HEAD)
-    key_heads = keys.reshape(row_count, head_count, HEAD)
-    value_heads = values.reshape(row_count, head_count, HEAD)
-    scores = jnp.einsum("thd,shd->hts", query_heads, key_heads, preferred_element_type=jnp.float32)
-    weights = jnp.where(keep_mask[None], scores, 0.0).astype(jnp.bfloat16)
-    inside = jnp.einsum("hts,she->the", weights, value_heads, preferred_element_type=jnp.float32)
-    tail_keys = jnp.where(tail_rows[:, None, None], key_heads, jnp.zeros_like(key_heads))
-    state_local = jnp.einsum(
-        "shd,she->hde", tail_keys, value_heads, preferred_element_type=jnp.float32
-    )
-    start_flag = has_start.astype(jnp.float32).reshape(1, 1, 1)
+    keep = keep_mask.astype(jnp.float32)
+    tail = tail_rows.astype(jnp.float32)[:, None]
+    carry = use_carry.astype(jnp.float32)[:, None]
+    f32 = jnp.float32
+    state_shape = jax.ShapeDtypeStruct((head_count, HEAD, HEAD), f32)
+    wide = jax.ShapeDtypeStruct((row_count, feat_width), f32)
+    low = jax.ShapeDtypeStruct((row_count, feat_width), jnp.bfloat16)
+    (state_local,) = head_call(state_body, [keys, values, tail], [state_shape])
+    weights, inside = head_call(
+        inside_body, [queries, keys, values, keep],
+        [jax.ShapeDtypeStruct((head_count, row_count, row_count), jnp.bfloat16), wide],
+    )
+    start_flag = has_start.astype(f32).reshape(1, 1, 1)
     row_start, row_stop = row_flags(starts, row_count)
-    prefix = scan_states(state_local, 1.0 - row_start.astype(jnp.float32), start_flag, 1)
-    prefix = prefix * continues.astype(jnp.float32)
-    prefix_low = prefix.astype(jnp.bfloat16)
-    carried = jnp.einsum(
-        "thd,hde->the", query_heads, prefix_low, preferred_element_type=jnp.float32
-    )
-    mixed = (inside + jnp.where(use_carry[:, None, None], carried, 0.0)).reshape(
-        row_count, feat_width
-    )
+    prefix = scan_states(state_local, 1.0 - row_start.astype(f32), start_flag, 1)
+    prefix_low = (prefix * continues.astype(f32)).astype(jnp.bfloat16)
+    (mixed,) = head_call(mixed_body, [queries, inside, prefix_low, carry], [wide])
     rms_value = jnp.sqrt(jnp.mean(mixed * mixed, axis=1, keepdims=True) + 1e-05)
     normed = mixed / rms_value
     attn_out = normed.astype(jnp.bfloat16)
-    out_cot = out_grad.astype(jnp.float32)
+    out_cot = out_grad.astype(f32)
     grad_mix = (out_cot - normed * jnp.mean(out_cot * normed, axis=1, keepdims=True)) / rms_value
-    grad_low = grad_mix.astype(jnp.bfloat16).reshape(row_count, head_count, HEAD)
-    lead_queries = jnp.where(use_carry[:, None, None], query_heads, jnp.zeros_like(query_heads))
-    grad_local = jnp.einsum(
-        "thd,the->hde", lead_queries, grad_low, preferred_element_type=jnp.float32
-    )
-    back_flag = stops_back.astype(jnp.float32).reshape(1, 1, 1)
-    suffix = scan_states(grad_local, 1.0 - row_stop.astype(jnp.float32), back_flag, -1)
+    grad_low = grad_mix.astype(jnp.bfloat16)
+    (grad_local,) = head_call(local_body, [queries, grad_low, carry], [state_shape])
+    back_flag = stops_back.astype(f32).reshape(1, 1, 1)
+    suffix = scan_states(grad_local, 1.0 - row_stop.astype(f32), back_flag, -1)
     next_first = first_row + row_count
     next_open = (next_first < lax.axis_size("seq") * row_count) & jnp.logical_not(jnp.any(starts == next_first))
-    suffix = suffix * next_open.astype(jnp.float32)
-    grad_scores = jnp.einsum(
-        "the,she->hts", grad_low, value_heads, preferred_element_type=jnp.float32
-    )
-    grad_weights = jnp.where(keep_mask[None], grad_scores, 0.0).astype(jnp.bfloat16)
-    suffix_low = suffix.astype(jnp.bfloat16)
-    grad_queries = jnp.einsum(
-        "hts,shd->thd", grad_weights, key_heads, preferred_element_type=jnp.float32
-    )
-    query_carry = jnp.einsum(
-        "the,hde->thd", grad_low, prefix_low, preferred_element_type=jnp.float32
-    )
-    grad_queries = grad_queries + jnp.where(use_carry[:, None, None], query_carry, 0.0)
-    grad_keys = jnp.einsum(
-        "hts,thd->shd", grad_weights, query_heads, preferred_element_type=jnp.float32
-    )
-    key_carry = jnp.einsum(
-        "she,hde->shd", value_heads, suffix_low, preferred_element_type=jnp.float32
-    )
-    grad_keys = grad_keys + jnp.where(tail_rows[:, None, None], key_carry, 0.0)
-    grad_values = jnp.einsum("hts,the->she", weights, grad_low, preferred_element_type=jnp.float32)
-    value_carry = jnp.einsum(
-        "shd,hde->she", key_heads, suffix_low, preferred_element_type=jnp.float32
-    )
-    grad_values = grad_values + jnp.where(tail_rows[:, None, None], value_carry, 0.0)
-    return (
-        attn_out,
-        grad_queries.reshape(row_count, feat_width).astype(jnp.bfloat16),
-        grad_keys.reshape(row_count, feat_width).astype(jnp.bfloat16),
-        grad_values.reshape(row_count, feat_width).astype(jnp.bfloat16),
-    )
+    suffix_low = (suffix * next_open.astype(f32)).astype(jnp.bfloat16)
+    grad_queries, keys_part, values_part = head_call(
+        grad_body, [queries, keys, values, grad_low, weights, prefix_low, keep, carry], [low, wide, wide]
+    )
+    grad_keys, grad_values = head_call(
+        tail_body, [keys, values, keys_part, values_part, suffix_low, tail], [low, low]
+    )
+    return attn_out, grad_queries, grad_keys, grad_values
 
 
 def solution(mesh):

time: 177 us -> 171 us (0.966)
  Pallas kernels: 0 us -> 40.7 us
  matrix products: 32 us -> 0 us
  local copies, waits for them, and re-layouts: 37.3 us -> 7.32 us
  waiting for transfers between devices: 43.4 us -> 66.3 us
  other arithmetic: 24.6 us -> 19.2 us
  starting transfers between devices: 30.4 us -> 27.7 us
    pallas_call x0 -> x6, Pallas kernels: none -> 40.7 us  [head_call(): pl.pallas_call(body, grid=(heads // HEAD_STEP,), in_specs=[spec(x.shape)...]
    dot_general x12 -> x0, matrix products: 32 us -> none  [the longest x1 5.75 us: shards(): jnp.einsum('hts,thd->shd', grad_weights, query_heads, preferred_element_t...]
    unnamed x78 -> x4, local copies, waits for them, and re-layouts: 13.2 us -> 0.5 us
    ppermute x4, waiting for transfers between devices: 12.9 us -> 23.3 us  [row_scan(): window = total + total_keep * lax.ppermute(window, 'seq', pairs)]
    reshape x4 -> x0, local copies, waits for them, and re-layouts: 9.55 us -> none  [the longest x1 3.71 us: shards(): (inside + jnp.where(use_carry[:, None, None], carried, 0.0)).reshape(row_...]
    dynamic_update_slice x12, local copies, waits for them, and re-layouts: 7.46 us -> 0.26 us  [member_exchange(): lax.dynamic_update_index_in_dim(placed, piece, (member - offset) % GROUP, 0)]
    ppermute x12, waiting for transfers between devices: 24.5 us -> 31.1 us  [member_exchange(): got.append(lax.ppermute(piece, axis, pairs))]
    ppermute x2, waiting for transfers between devices: 5.97 us -> 11.9 us  [row_scan(): entering = lax.ppermute(window, 'seq', pairs)]
  transfers between devices with their start and end apart: 18 -> 18, of which waited for: 13 -> 14; matrix products, arithmetic and copies ran while one was open for 18% -> 2% of each run, Pallas kernels for 0% -> 11%
where the time goes in v4:
time: 171 us; the launch traced here: 170 us
  waiting for transfers between devices  66.3 us (39%)
  Pallas kernels  40.7 us (24%)
  starting transfers between devices  27.7 us (16%)
  other arithmetic  19.2 us (11%)
  between operations  8.68 us (5%)
  local copies, waits for them, and re-layouts  7.32 us (4%)
    pallas_call x6, Pallas kernels, head_call(): pl.pallas_call(body, grid=(heads // HEAD_STEP,), in_specs=[spec(x.shape)...  40.7 us
    ppermute x12, waiting for transfers between devices, member_exchange(): got.append(lax.ppermute(piece, axis, pairs))  31.1 us
    ppermute x4, waiting for transfers between devices, row_scan(): window = total + total_keep * lax.ppermute(window, 'seq', pairs)  23.3 us
    ppermute x2, waiting for transfers between devices, row_scan(): entering = lax.ppermute(window, 'seq', pairs)  11.9 us
    ppermute x12, starting transfers between devices, member_exchange(): got.append(lax.ppermute(piece, axis, pairs))  11.6 us
    ppermute x4, starting transfers between devices, row_scan(): window = total + total_keep * lax.ppermute(window, 'seq', pairs)  10.7 us
    ppermute x2, starting transfers between devices, row_scan(): entering = lax.ppermute(window, 'seq', pairs)  5.41 us
    add x2, other arithmetic, row_scan(): total = mine[index] + keep_row[index] * total  4.07 us
  transfers between devices with their start and end apart: 18, of which 14 were waited for; matrix products, arithmetic and copies ran while one was open for 2% of the time, Pallas kernels for 11%

profile of v4, /device:TPU:1, one launch (start us, length us, event | category | flops | bytes accessed | tf_op | source)
XLA Modules:
  0.0 170.0 jit_solution(10660051516681931706)
XLA Ops:
  0.7 0.8 reduce-window.9
  1.6 1.3 compare_reduce_fusion
  4.2 1.3 and_convert_fusion.1
  5.5 0.8 reshape.122.tail_ref
  6.3 4.6 %shard_map.85 = f32[16,128,128]{2,1,0:T(8,128)} custom-call(bf16[384,2048]{1,0:T(8,128)(2,1)} %key_ref.7, bf16[384,2048]{1,0:T(8,128)(2,1)} %value_ref.7, f32[384,1]{1,0:T(8,128)} %reshape.122.tail_ref), custom_call_target="tpu_custom_call" | custom-call | tf_op jit(solution)/shard_map/pallas_call | solution.py:121
  10.9 1.3 dynamic-slice_bitcast_fusion.9
  12.2 2.6 %collective-permute-start = (f32[4,128,128]{2,1,0:T(8,128)S(1)}, f32[4,128,128]{2,1,0:T(8,128)S(1)}, u32[]{:S(2)}, u32[]{:S(2)}) collective-permute-start(f32[4,128,128]{2,1,0:T(8,128)S(1)} %get-tuple-element.49), channel_id=1, source_target_pairs={{0,1},{1,2},{2,3},{3,0},{4,5},{5,6},{6,7},{7,4},{8,9},{9,10},{10,1... | collective-permute-start | bytes 786440 | tf_op jit(solution)/shard_map/ppermute | solution.py:48
  15.6 0.6 fusion.19
  16.8 3.5 %collective-permute-done = f32[4,128,128]{2,1,0:T(8,128)S(1)} collective-permute-done((f32[4,128,128]{2,1,0:T(8,128)S(1)}, f32[4,128,128]{2,1,0:T(8,128)S(1)}, u32[]{:S(2)}, u32[]{:S(2)}) %collective-permute-start) | collective-permute-done | bytes 262176 | tf_op jit(solution)/shard_map/ppermute | solution.py:48
  20.3 5.6 %collective-permute-done.1 = f32[4,128,128]{2,1,0:T(8,128)S(1)} collective-permute-done((f32[4,128,128]{2,1,0:T(8,128)S(1)}, f32[4,128,128]{2,1,0:T(8,128)S(1)}, u32[]{:S(2)}, u32[]{:S(2)}) %collective-permute-start.1) | collective-permute-done | bytes 262176 | tf_op jit(solution)/shard_map/ppermute | solution.py:48
  26.5 2.0 %fusion.10 = (f32[4,128,128]{2,1,0:T(8,128)S(1)}, f32[4,128,128]{2,1,0:T(8,128)S(1)}) fusion(f32[4,4,128,128]{3,2,1,0:T(8,128)S(1)} %bitcast_dynamic-update-slice_fusion.9, f32[]{:T(128)} %bitcast.11, f32[]{:T(128)} %bitcast.13, f32[]{:T(128)S(6)} %mul.172, f32[]{:T(128)} %bitcast.15), kind=kLoop, calls=%fused_computation.27 | loop fusion | flops 458752 | bytes 1572880 | tf_op jit(solution)/shard_map/add | solution.py:68
  28.5 4.0 %collective-permute-start.3 = (f32[4,128,128]{2,1,0:T(8,128)S(1)}, f32[4,128,128]{2,1,0:T(8,128)S(1)}, u32[]{:S(2)}, u32[]{:S(2)}) collective-permute-start(f32[4,128,128]{2,1,0:T(8,128)S(1)} %get-tuple-element.27), channel_id=1, source_target_pairs={{0,4},{1,5},{2,6},{3,7},{4,8},{5,9},{6,10},{7,11},{8,12},{9,13},{1... | collective-permute-start | bytes 786440 | tf_op jit(solution)/shard_map/ppermute | solution.py:74
  35.1 3.4 %collective-permute-done.3 = f32[4,128,128]{2,1,0:T(8,128)S(1)} collective-permute-done((f32[4,128,128]{2,1,0:T(8,128)S(1)}, f32[4,128,128]{2,1,0:T(8,128)S(1)}, u32[]{:S(2)}, u32[]{:S(2)}) %collective-permute-start.3) | collective-permute-done | bytes 262176 | tf_op jit(solution)/shard_map/ppermute | solution.py:74
  38.5 4.1 %collective-permute-start.4 = (f32[4,128,128]{2,1,0:T(8,128)S(1)}, f32[4,128,128]{2,1,0:T(8,128)S(1)}, u32[]{:S(2)}, u32[]{:S(2)}) collective-permute-start(f32[4,128,128]{2,1,0:T(8,128)S(1)} %multiply_add_fusion.3), channel_id=1, source_target_pairs={{0,4},{1,5},{2,6},{3,7},{4,8},{5,9},{6,10},{7,11},{8,12},{9,13},{1... | collective-permute-start | bytes 786440 | tf_op jit(solution)/shard_map/ppermute | solution.py:74
  42.7 5.1 %collective-permute-done.4 = f32[4,128,128]{2,1,0:T(8,128)S(1)} collective-permute-done((f32[4,128,128]{2,1,0:T(8,128)S(1)}, f32[4,128,128]{2,1,0:T(8,128)S(1)}, u32[]{:S(2)}, u32[]{:S(2)}) %collective-permute-start.4) | collective-permute-done | bytes 262176 | tf_op jit(solution)/shard_map/ppermute | solution.py:74
  47.8 4.1 %collective-permute-start.5 = (f32[4,128,128]{2,1,0:T(8,128)S(1)}, f32[4,128,128]{2,1,0:T(8,128)S(1)}, u32[]{:S(2)}, u32[]{:S(2)}) collective-permute-start(f32[4,128,128]{2,1,0:T(8,128)S(1)} %multiply_add_fusion.2), channel_id=1, source_target_pairs={{0,4},{1,5},{2,6},{3,7},{4,8},{5,9},{6,10},{7,11},{8,12},{9,13},{1... | collective-permute-start | bytes 786440 | tf_op jit(solution)/shard_map/ppermute | solution.py:75
  51.9 4.2 %collective-permute-done.5 = f32[4,128,128]{2,1,0:T(8,128)S(1)} collective-permute-done((f32[4,128,128]{2,1,0:T(8,128)S(1)}, f32[4,128,128]{2,1,0:T(8,128)S(1)}, u32[]{:S(2)}, u32[]{:S(2)}) %collective-permute-start.5) | collective-permute-done | bytes 262176 | tf_op jit(solution)/shard_map/ppermute | solution.py:75
  56.1 1.4 add_bitcast_fusion.5
  57.8 3.1 %collective-permute-start.6 = (f32[4,128,128]{2,1,0:T(8,128)S(1)}, f32[4,128,128]{2,1,0:T(8,128)S(1)}, u32[]{:S(2)}, u32[]{:S(2)}) collective-permute-start(f32[4,128,128]{2,1,0:T(8,128)S(1)} %get-tuple-element.45), channel_id=1, source_target_pairs={{0,1},{1,2},{2,3},{3,0},{4,5},{5,6},{6,7},{7,4},{8,9},{9,10},{10,1... | collective-permute-start | bytes 786440 | tf_op jit(solution)/shard_map/ppermute | solution.py:48
  60.9 1.0 and_convert_fusion.keep_ref
  62.7 0.8 reshape.123.carry_ref
  63.5 7.7 %shard_map.84 = (bf16[16,384,384]{2,1,0:T(8,128)(2,1)}, f32[384,2048]{1,0:T(8,128)}) custom-call(bf16[384,2048]{1,0:T(8,128)(2,1)} %query_ref.7, bf16[384,2048]{1,0:T(8,128)(2,1)} %key_ref.7, bf16[384,2048]{1,0:T(8,128)(2,1)} %value_ref.7, f32[384,384]{1,0:T(8,128)} %and_convert_fusion.keep_ref), custom_call_target="tpu_custom_call" | custom-call | tf_op jit(solution)/shard_map/pallas_call | solution.py:121
  71.3 5.7 %collective-permute-done.8 = f32[4,128,128]{2,1,0:T(8,128)S(1)} collective-permute-done((f32[4,128,128]{2,1,0:T(8,128)S(1)}, f32[4,128,128]{2,1,0:T(8,128)S(1)}, u32[]{:S(2)}, u32[]{:S(2)}) %collective-permute-start.8) | collective-permute-done | bytes 262176 | tf_op jit(solution)/shard_map/ppermute | solution.py:48
  77.0 0.9 multiply_convert_fusion.1
  78.0 5.4 %shard_map.86 = f32[384,2048]{1,0:T(8,128)} custom-call(bf16[384,2048]{1,0:T(8,128)(2,1)} %query_ref.7, f32[384,2048]{1,0:T(8,128)} %get-tuple-element.11.inside_ref, bf16[16,128,128]{2,1,0:T(8,128)(2,1)} %bitcast.128, f32[384,1]{1,0:T(8,128)} %reshape.123.carry_ref), custom_call_target="tpu_custom_call" | custom-call | tf_op jit(solution)/shard_map/pallas_call | solution.py:121
  83.4 2.3 %multiply_reduce_fusion = f32[384]{0:T(512)S(1)} fusion(f32[384,2048]{1,0:T(8,128)} %shard_map.86), kind=kLoop, calls=%fused_computation.5 | loop fusion | flops 1572480 | bytes 3147264 | tf_op jit(solution)/shard_map/reduce_sum | solution.py:220
  86.9 2.4 %fusion.2 = (bf16[384,2048]{1,0:T(8,128)(2,1)}, bf16[384,2048]{1,0:T(8,128)(2,1)}) fusion(bf16[384,2048]{1,0:T(8,128)(2,1)S(1)} %copy-done.1, f32[384]{0:T(512)S(1)} %broadcast_multiply_fusion, f32[384]{0:T(512)S(1)} %add_sqrt_fusion, f32[384,2048]{1,0:T(8,128)S(1)} %copy-done), kind=kLoop, calls=%fused_computation.4 | loop fusion | flops 5505024 | bytes 7867392 | tf_op jit(solution)/shard_map/convert_element_type | solution.py:225
  89.3 4.6 %shard_map.88 = f32[16,128,128]{2,1,0:T(8,128)} custom-call(bf16[384,2048]{1,0:T(8,128)(2,1)} %query_ref.7, bf16[384,2048]{1,0:T(8,128)(2,1)} %get-tuple-element.29.grad_ref, f32[384,1]{1,0:T(8,128)} %reshape.123.carry_ref), custom_call_target="tpu_custom_call" | custom-call | tf_op jit(solution)/shard_map/pallas_call | solution.py:121
  93.9 1.3 dynamic-slice_bitcast_fusion.3
  95.3 1.0 collective-permute-start.10
  96.3 0.7 fusion.18
  97.5 0.8 collective-permute-start.11
  98.2 1.3 collective-permute-done.9
  99.5 7.3 %collective-permute-done.10 = f32[4,128,128]{2,1,0:T(8,128)S(1)} collective-permute-done((f32[4,128,128]{2,1,0:T(8,128)S(1)}, f32[4,128,128]{2,1,0:T(8,128)S(1)}, u32[]{:S(2)}, u32[]{:S(2)}) %collective-permute-start.10) | collective-permute-done | bytes 262176 | tf_op jit(solution)/shard_map/ppermute | solution.py:48
  106.8 1.5 collective-permute-done.11
  108.4 2.1 %fusion.3 = (f32[4,128,128]{2,1,0:T(8,128)S(1)}, f32[4,128,128]{2,1,0:T(8,128)S(1)}) fusion(f32[4,4,128,128]{3,2,1,0:T(8,128)S(1)} %bitcast_dynamic-update-slice_fusion.3, f32[]{:T(128)} %bitcast.44, f32[]{:T(128)} %bitcast.38, f32[]{:T(128)S(6)} %mul.197, f32[]{:T(128)} %bitcast.40), kind=kLoop, calls=%fused_computation.13 | loop fusion | flops 458752 | bytes 1572880 | tf_op jit(solution)/shard_map/add | solution.py:68
  110.5 1.3 collective-permute-start.12
  114.3 6.0 %collective-permute-done.12 = f32[4,128,128]{2,1,0:T(8,128)S(1)} collective-permute-done((f32[4,128,128]{2,1,0:T(8,128)S(1)}, f32[4,128,128]{2,1,0:T(8,128)S(1)}, u32[]{:S(2)}, u32[]{:S(2)}) %collective-permute-start.12) | collective-permute-done | bytes 262176 | tf_op jit(solution)/shard_map/ppermute | solution.py:74
  120.4 1.3 collective-permute-start.13
  121.7 8.8 %collective-permute-done.13 = f32[4,128,128]{2,1,0:T(8,128)S(1)} collective-permute-done((f32[4,128,128]{2,1,0:T(8,128)S(1)}, f32[4,128,128]{2,1,0:T(8,128)S(1)}, u32[]{:S(2)}, u32[]{:S(2)}) %collective-permute-start.13) | collective-permute-done | bytes 262176 | tf_op jit(solution)/shard_map/ppermute | solution.py:74
  130.5 1.3 collective-permute-start.14
  131.8 7.7 %collective-permute-done.14 = f32[4,128,128]{2,1,0:T(8,128)S(1)} collective-permute-done((f32[4,128,128]{2,1,0:T(8,128)S(1)}, f32[4,128,128]{2,1,0:T(8,128)S(1)}, u32[]{:S(2)}, u32[]{:S(2)}) %collective-permute-start.14) | collective-permute-done | bytes 262176 | tf_op jit(solution)/shard_map/ppermute | solution.py:75
  139.6 1.3 add_bitcast_fusion.2
  141.2 2.4 %collective-permute-start.15 = (f32[4,128,128]{2,1,0:T(8,128)S(1)}, f32[4,128,128]{2,1,0:T(8,128)S(1)}, u32[]{:S(2)}, u32[]{:S(2)}) collective-permute-start(f32[4,128,128]{2,1,0:T(8,128)S(1)} %get-tuple-element.37), channel_id=1, source_target_pairs={{0,1},{1,2},{2,3},{3,0},{4,5},{5,6},{6,7},{7,4},{8,9},{9,10},{10,1... | collective-permute-start | bytes 786440 | tf_op jit(solution)/shard_map/ppermute | solution.py:48
  144.8 11.5 %shard_map.87 = (bf16[384,2048]{1,0:T(8,128)(2,1)}, f32[384,2048]{1,0:T(8,128)}, f32[384,2048]{1,0:T(8,128)}) custom-call(bf16[384,2048]{1,0:T(8,128)(2,1)} %query_ref.7, bf16[384,2048]{1,0:T(8,128)(2,1)} %key_ref.7, bf16[384,2048]{1,0:T(8,128)(2,1)} %value_ref.7, bf16[384,2048]{1,0:T(8,128)(2,1)} %get-tuple-element.29.grad_ref, ...), custom_call_target="tpu_custom_call" | custom-call | tf_op jit(solution)/shard_map/pallas_call | solution.py:121
  156.5 5.7 %collective-permute-done.17 = f32[4,128,128]{2,1,0:T(8,128)S(1)} collective-permute-done((f32[4,128,128]{2,1,0:T(8,128)S(1)}, f32[4,128,128]{2,1,0:T(8,128)S(1)}, u32[]{:S(2)}, u32[]{:S(2)}) %collective-permute-start.17) | collective-permute-done | bytes 262176 | tf_op jit(solution)/shard_map/ppermute | solution.py:48
  162.2 0.9 multiply_convert_fusion
  163.1 6.9 %shard_map.89 = (bf16[384,2048]{1,0:T(8,128)(2,1)}, bf16[384,2048]{1,0:T(8,128)(2,1)}) custom-call(bf16[384,2048]{1,0:T(8,128)(2,1)} %key_ref.7, bf16[384,2048]{1,0:T(8,128)(2,1)} %value_ref.7, f32[384,2048]{1,0:T(8,128)} %get-tuple-element.14.key_part, f32[384,2048]{1,0:T(8,128)} %get-tuple-element.15.value_part, bf16[16,128,128]{2,1,0:T(8,128)(2,1)} %bitcast.132, ...), custom_call_target="tpu_custom_call" | custom-call | tf_op jit(solution)/shard_map/pallas_call | solution.py:121
  (51 shorter events, 5.5 us)
Async XLA Ops:
  12.2 8.1 %collective-permute-start = (f32[4,128,128]{2,1,0:T(8,128)S(1)}, f32[4,128,128]{2,1,0:T(8,128)S(1)}, u32[]{:S(2)}, u32[]{:S(2)}) collective-permute-start(f32[4,128,128]{2,1,0:T(8,128)S(1)} %get-tuple-element.49), channel_id=1, source_target_pairs={{0,1},{1,2},{2,3},{3,0},{4,5},{5,6},{6,7},{7,4},{8,9},{9,10},{10,1... | collective-permute-start | bytes 786440 | tf_op jit(solution)/shard_map/ppermute | solution.py:48
  14.9 11.1 %collective-permute-start.1 = (f32[4,128,128]{2,1,0:T(8,128)S(1)}, f32[4,128,128]{2,1,0:T(8,128)S(1)}, u32[]{:S(2)}, u32[]{:S(2)}) collective-permute-start(f32[4,128,128]{2,1,0:T(8,128)S(1)} %get-tuple-element.48), channel_id=1, source_target_pairs={{0,2},{1,3},{2,0},{3,1},{4,6},{5,7},{6,4},{7,5},{8,10},{9,11},{10,... | collective-permute-start | bytes 786440 | tf_op jit(solution)/shard_map/ppermute | solution.py:48
  14.9 11.6 %collective-permute-start.2 = (f32[4,128,128]{2,1,0:T(8,128)S(1)}, f32[4,128,128]{2,1,0:T(8,128)S(1)}, u32[]{:S(2)}, u32[]{:S(2)}) collective-permute-start(f32[4,128,128]{2,1,0:T(8,128)S(1)} %get-tuple-element.47), channel_id=1, source_target_pairs={{0,3},{1,0},{2,1},{3,2},{4,7},{5,4},{6,5},{7,6},{8,11},{9,8},{10,9... | collective-permute-start | bytes 786440 | tf_op jit(solution)/shard_map/ppermute | solution.py:48
  28.5 10.0 %collective-permute-start.3 = (f32[4,128,128]{2,1,0:T(8,128)S(1)}, f32[4,128,128]{2,1,0:T(8,128)S(1)}, u32[]{:S(2)}, u32[]{:S(2)}) collective-permute-start(f32[4,128,128]{2,1,0:T(8,128)S(1)} %get-tuple-element.27), channel_id=1, source_target_pairs={{0,4},{1,5},{2,6},{3,7},{4,8},{5,9},{6,10},{7,11},{8,12},{9,13},{1... | collective-permute-start | bytes 786440 | tf_op jit(solution)/shard_map/ppermute | solution.py:74
  38.5 9.2 %collective-permute-start.4 = (f32[4,128,128]{2,1,0:T(8,128)S(1)}, f32[4,128,128]{2,1,0:T(8,128)S(1)}, u32[]{:S(2)}, u32[]{:S(2)}) collective-permute-start(f32[4,128,128]{2,1,0:T(8,128)S(1)} %multiply_add_fusion.3), channel_id=1, source_target_pairs={{0,4},{1,5},{2,6},{3,7},{4,8},{5,9},{6,10},{7,11},{8,12},{9,13},{1... | collective-permute-start | bytes 786440 | tf_op jit(solution)/shard_map/ppermute | solution.py:74
  47.8 8.4 %collective-permute-start.5 = (f32[4,128,128]{2,1,0:T(8,128)S(1)}, f32[4,128,128]{2,1,0:T(8,128)S(1)}, u32[]{:S(2)}, u32[]{:S(2)}) collective-permute-start(f32[4,128,128]{2,1,0:T(8,128)S(1)} %multiply_add_fusion.2), channel_id=1, source_target_pairs={{0,4},{1,5},{2,6},{3,7},{4,8},{5,9},{6,10},{7,11},{8,12},{9,13},{1... | collective-permute-start | bytes 786440 | tf_op jit(solution)/shard_map/ppermute | solution.py:75
  57.8 13.4 %collective-permute-start.6 = (f32[4,128,128]{2,1,0:T(8,128)S(1)}, f32[4,128,128]{2,1,0:T(8,128)S(1)}, u32[]{:S(2)}, u32[]{:S(2)}) collective-permute-start(f32[4,128,128]{2,1,0:T(8,128)S(1)} %get-tuple-element.45), channel_id=1, source_target_pairs={{0,1},{1,2},{2,3},{3,0},{4,5},{5,6},{6,7},{7,4},{8,9},{9,10},{10,1... | collective-permute-start | bytes 786440 | tf_op jit(solution)/shard_map/ppermute | solution.py:48
  61.9 9.3 %collective-permute-start.7 = (f32[4,128,128]{2,1,0:T(8,128)S(1)}, f32[4,128,128]{2,1,0:T(8,128)S(1)}, u32[]{:S(2)}, u32[]{:S(2)}) collective-permute-start(f32[4,128,128]{2,1,0:T(8,128)S(1)} %get-tuple-element.44), channel_id=1, source_target_pairs={{0,2},{1,3},{2,0},{3,1},{4,6},{5,7},{6,4},{7,5},{8,10},{9,11},{10,... | collective-permute-start | bytes 786440 | tf_op jit(solution)/shard_map/ppermute | solution.py:48
  71.2 5.8 %collective-permute-start.8 = (f32[4,128,128]{2,1,0:T(8,128)S(1)}, f32[4,128,128]{2,1,0:T(8,128)S(1)}, u32[]{:S(2)}, u32[]{:S(2)}) collective-permute-start(f32[4,128,128]{2,1,0:T(8,128)S(1)} %get-tuple-element.43), channel_id=1, source_target_pairs={{0,3},{1,0},{2,1},{3,2},{4,7},{5,4},{6,5},{7,6},{8,11},{9,8},{10,9... | collective-permute-start | bytes 786440 | tf_op jit(solution)/shard_map/ppermute | solution.py:48
  78.0 7.8 %copy-start.1 = (bf16[384,2048]{1,0:T(8,128)(2,1)S(1)}, bf16[384,2048]{1,0:T(8,128)(2,1)}, u32[]{:S(2)}) copy-start(bf16[384,2048]{1,0:T(8,128)(2,1)} %param.9) | copy-start | bytes 4718596
  83.4 2.8 %copy-start = (f32[384,2048]{1,0:T(8,128)S(1)}, f32[384,2048]{1,0:T(8,128)}, u32[]{:S(2)}) copy-start(f32[384,2048]{1,0:T(8,128)} %shard_map.86) | copy-start | bytes 9437188
  95.2 4.3 %collective-permute-start.9 = (f32[4,128,128]{2,1,0:T(8,128)S(1)}, f32[4,128,128]{2,1,0:T(8,128)S(1)}, u32[]{:S(2)}, u32[]{:S(2)}) collective-permute-start(f32[4,128,128]{2,1,0:T(8,128)S(1)} %get-tuple-element.41), channel_id=1, source_target_pairs={{0,1},{1,2},{2,3},{3,0},{4,5},{5,6},{6,7},{7,4},{8,9},{9,10},{10,1... | collective-permute-start | bytes 786440 | tf_op jit(solution)/shard_map/ppermute | solution.py:48
  95.3 11.5 %collective-permute-start.10 = (f32[4,128,128]{2,1,0:T(8,128)S(1)}, f32[4,128,128]{2,1,0:T(8,128)S(1)}, u32[]{:S(2)}, u32[]{:S(2)}) collective-permute-start(f32[4,128,128]{2,1,0:T(8,128)S(1)} %get-tuple-element.40), channel_id=1, source_target_pairs={{0,2},{1,3},{2,0},{3,1},{4,6},{5,7},{6,4},{7,5},{8,10},{9,11},{10,... | collective-permute-start | bytes 786440 | tf_op jit(solution)/shard_map/ppermute | solution.py:48
  97.5 10.9 %collective-permute-start.11 = (f32[4,128,128]{2,1,0:T(8,128)S(1)}, f32[4,128,128]{2,1,0:T(8,128)S(1)}, u32[]{:S(2)}, u32[]{:S(2)}) collective-permute-start(f32[4,128,128]{2,1,0:T(8,128)S(1)} %get-tuple-element.39), channel_id=1, source_target_pairs={{0,3},{1,0},{2,1},{3,2},{4,7},{5,4},{6,5},{7,6},{8,11},{9,8},{10,9... | collective-permute-start | bytes 786440 | tf_op jit(solution)/shard_map/ppermute | solution.py:48
  110.5 9.9 %collective-permute-start.12 = (f32[4,128,128]{2,1,0:T(8,128)S(1)}, f32[4,128,128]{2,1,0:T(8,128)S(1)}, u32[]{:S(2)}, u32[]{:S(2)}) collective-permute-start(f32[4,128,128]{2,1,0:T(8,128)S(1)} %get-tuple-element.24), channel_id=1, source_target_pairs={{4,0},{5,1},{6,2},{7,3},{8,4},{9,5},{10,6},{11,7},{12,8},{13,9},{1... | collective-permute-start | bytes 786440 | tf_op jit(solution)/shard_map/ppermute | solution.py:74
  120.4 10.1 %collective-permute-start.13 = (f32[4,128,128]{2,1,0:T(8,128)S(1)}, f32[4,128,128]{2,1,0:T(8,128)S(1)}, u32[]{:S(2)}, u32[]{:S(2)}) collective-permute-start(f32[4,128,128]{2,1,0:T(8,128)S(1)} %multiply_add_fusion.1), channel_id=1, source_target_pairs={{4,0},{5,1},{6,2},{7,3},{8,4},{9,5},{10,6},{11,7},{12,8},{13,9},{1... | collective-permute-start | bytes 786440 | tf_op jit(solution)/shard_map/ppermute | solution.py:74
  130.5 9.0 %collective-permute-start.14 = (f32[4,128,128]{2,1,0:T(8,128)S(1)}, f32[4,128,128]{2,1,0:T(8,128)S(1)}, u32[]{:S(2)}, u32[]{:S(2)}) collective-permute-start(f32[4,128,128]{2,1,0:T(8,128)S(1)} %multiply_add_fusion), channel_id=1, source_target_pairs={{4,0},{5,1},{6,2},{7,3},{8,4},{9,5},{10,6},{11,7},{12,8},{13,9},{1... | collective-permute-start | bytes 786440 | tf_op jit(solution)/shard_map/ppermute | solution.py:75
  141.2 15.2 %collective-permute-start.15 = (f32[4,128,128]{2,1,0:T(8,128)S(1)}, f32[4,128,128]{2,1,0:T(8,128)S(1)}, u32[]{:S(2)}, u32[]{:S(2)}) collective-permute-start(f32[4,128,128]{2,1,0:T(8,128)S(1)} %get-tuple-element.37), channel_id=1, source_target_pairs={{0,1},{1,2},{2,3},{3,0},{4,5},{5,6},{6,7},{7,4},{8,9},{9,10},{10,1... | collective-permute-start | bytes 786440 | tf_op jit(solution)/shard_map/ppermute | solution.py:48
  143.6 12.8 %collective-permute-start.16 = (f32[4,128,128]{2,1,0:T(8,128)S(1)}, f32[4,128,128]{2,1,0:T(8,128)S(1)}, u32[]{:S(2)}, u32[]{:S(2)}) collective-permute-start(f32[4,128,128]{2,1,0:T(8,128)S(1)} %get-tuple-element.36), channel_id=1, source_target_pairs={{0,2},{1,3},{2,0},{3,1},{4,6},{5,7},{6,4},{7,5},{8,10},{9,11},{10,... | collective-permute-start | bytes 786440 | tf_op jit(solution)/shard_map/ppermute | solution.py:48
  156.4 5.8 %collective-permute-start.17 = (f32[4,128,128]{2,1,0:T(8,128)S(1)}, f32[4,128,128]{2,1,0:T(8,128)S(1)}, u32[]{:S(2)}, u32[]{:S(2)}) collective-permute-start(f32[4,128,128]{2,1,0:T(8,128)S(1)} %get-tuple-element.35), channel_id=1, source_target_pairs={{0,3},{1,0},{2,1},{3,2},{4,7},{5,4},{6,5},{7,6},{8,11},{9,8},{10,9... | collective-permute-start | bytes 786440 | tf_op jit(solution)/shard_map/ppermute | solution.py:48

commit v5 on v4

--- a/solution.py
+++ b/solution.py
@@ -32,6 +32,7 @@
 
 
 GROUP = 4
+CHUNKS = 2
 
 
 def member_exchange(pieces, axis):
@@ -91,8 +92,12 @@
 
 
 def scan_states(state, keep_row, fallback_flag, direction):
-    if lax.axis_size("seq") % GROUP == 0 and state.shape[0] % GROUP == 0:
-        return row_scan(state, keep_row, direction)
+    heads = state.shape[0]
+    if lax.axis_size("seq") % GROUP == 0 and heads % (GROUP * CHUNKS) == 0:
+        size = heads // CHUNKS
+        return jnp.concatenate(
+            [row_scan(state[i * size:(i + 1) * size], keep_row, direction) for i in range(CHUNKS)]
+        )
     return windowed_prefix((state, fallback_flag), direction)[0]
 
 

time: 171 us -> 169 us (0.988)
  waiting for transfers between devices: 66.3 us -> 31.7 us
  starting transfers between devices: 27.7 us -> 52.8 us
  other arithmetic: 19.2 us -> 25.7 us
    ppermute x4 -> x8, waiting for transfers between devices: 23.3 us -> 8.73 us  [row_scan(): window = total + total_keep * lax.ppermute(window, 'seq', pairs)]
    ppermute x12 -> x24, starting transfers between devices: 11.6 us -> 25.9 us  [member_exchange(): got.append(lax.ppermute(piece, axis, pairs))]
    ppermute x2 -> x4, waiting for transfers between devices: 11.9 us -> 1 us  [row_scan(): entering = lax.ppermute(window, 'seq', pairs)]
    ppermute x12 -> x24, waiting for transfers between devices: 31.1 us -> 22 us  [member_exchange(): got.append(lax.ppermute(piece, axis, pairs))]
    ppermute x4 -> x8, starting transfers between devices: 10.7 us -> 17.6 us  [row_scan(): window = total + total_keep * lax.ppermute(window, 'seq', pairs)]
    ppermute x2 -> x4, starting transfers between devices: 5.41 us -> 9.31 us  [row_scan(): entering = lax.ppermute(window, 'seq', pairs)]
    add x2 -> x4, other arithmetic: 4.07 us -> 7.89 us  [row_scan(): total = mine[index] + keep_row[index] * total]
    another operation x4 -> x8, other arithmetic: 2.88 us -> 5.55 us  [row_scan(): jnp.stack([inner[index] + inner_keep[index] * entering for index in range...]
  transfers between devices with their start and end apart: 18 -> 36, of which waited for: 14 -> 19; matrix products, arithmetic and copies ran while one was open for 2% -> 10% of each run, Pallas kernels for 11% -> 12%
where the time goes in v5:
time: 169 us; the launch traced here: 168 us
  starting transfers between devices  52.8 us (31%)
  Pallas kernels  40.7 us (24%)
  waiting for transfers between devices  31.7 us (19%)
  other arithmetic  25.7 us (15%)
  between operations  9.26 us (5%)
  local copies, waits for them, and re-layouts  7.57 us (4%)
    pallas_call x6, Pallas kernels, head_call(): pl.pallas_call(body, grid=(heads // HEAD_STEP,), in_specs=[spec(x.shape)...  40.7 us
    ppermute x24, starting transfers between devices, member_exchange(): got.append(lax.ppermute(piece, axis, pairs))  25.9 us
    ppermute x24, waiting for transfers between devices, member_exchange(): got.append(lax.ppermute(piece, axis, pairs))  22 us
    ppermute x8, starting transfers between devices, row_scan(): window = total + total_keep * lax.ppermute(window, 'seq', pairs)  17.6 us
    ppermute x4, starting transfers between devices, row_scan(): entering = lax.ppermute(window, 'seq', pairs)  9.31 us
    ppermute x8, waiting for transfers between devices, row_scan(): window = total + total_keep * lax.ppermute(window, 'seq', pairs)  8.73 us
    add x4, other arithmetic, row_scan(): total = mine[index] + keep_row[index] * total  7.89 us
    another operation x8, other arithmetic, row_scan(): jnp.stack([inner[index] + inner_keep[index] * entering for index in range...  5.55 us
  transfers between devices with their start and end apart: 36, of which 19 were waited for; matrix products, arithmetic and copies ran while one was open for 10% of the time, Pallas kernels for 12%

profile of v5, /device:TPU:1, one launch (start us, length us, event | category | flops | bytes accessed | tf_op | source)
XLA Modules:
  0.0 167.8 jit_solution(4726716735262015699)
XLA Ops:
  1.6 1.3 compare_reduce_fusion
  4.2 1.3 and_convert_fusion.1
  6.3 4.5 %shard_map.85 = f32[16,128,128]{2,1,0:T(8,128)} custom-call(bf16[384,2048]{1,0:T(8,128)(2,1)} %key_ref.7, bf16[384,2048]{1,0:T(8,128)(2,1)} %value_ref.7, f32[384,1]{1,0:T(8,128)} %reshape.142.tail_ref), custom_call_target="tpu_custom_call" | custom-call | tf_op jit(solution)/shard_map/pallas_call | solution.py:126
  12.2 2.6 %collective-permute-start.9 = (f32[2,128,128]{2,1,0:T(8,128)S(1)}, f32[2,128,128]{2,1,0:T(8,128)S(1)}, u32[]{:S(2)}, u32[]{:S(2)}) collective-permute-start(f32[2,128,128]{2,1,0:T(8,128)S(1)} %get-tuple-element.77), channel_id=1, source_target_pairs={{0,1},{1,2},{2,3},{3,0},{4,5},{5,6},{6,7},{7,4},{8,9},{9,10},{10,1... | collective-permute-start | bytes 393224 | tf_op jit(solution)/shard_map/ppermute | solution.py:49
  15.5 1.3 collective-permute-start
  16.8 1.5 collective-permute-start.1
  23.1 7.8 %shard_map.84 = (bf16[16,384,384]{2,1,0:T(8,128)(2,1)}, f32[384,2048]{1,0:T(8,128)}) custom-call(bf16[384,2048]{1,0:T(8,128)(2,1)} %query_ref.7, bf16[384,2048]{1,0:T(8,128)(2,1)} %key_ref.7, bf16[384,2048]{1,0:T(8,128)(2,1)} %value_ref.7, f32[384,384]{1,0:T(8,128)} %and_convert_fusion.keep_ref), custom_call_target="tpu_custom_call" | custom-call | tf_op jit(solution)/shard_map/pallas_call | solution.py:126
  32.4 2.0 %fusion.16 = (f32[2,128,128]{2,1,0:T(8,128)S(1)}, f32[2,128,128]{2,1,0:T(8,128)S(1)}) fusion(f32[4,2,128,128]{3,2,1,0:T(8,128)S(1)} %bitcast_dynamic-update-slice_fusion.15, f32[]{:T(128)} %bitcast.11, f32[]{:T(128)} %bitcast.13, f32[]{:T(128)S(6)} %mul.244, f32[]{:T(128)} %bitcast.15), kind=kLoop, calls=%fused_computation.39 | loop fusion | flops 229376 | bytes 786448 | tf_op jit(solution)/shard_map/add | solution.py:69
  34.4 3.2 %collective-permute-start.12 = (f32[2,128,128]{2,1,0:T(8,128)S(1)}, f32[2,128,128]{2,1,0:T(8,128)S(1)}, u32[]{:S(2)}, u32[]{:S(2)}) collective-permute-start(f32[2,128,128]{2,1,0:T(8,128)S(1)} %get-tuple-element.31), channel_id=1, source_target_pairs={{0,4},{1,5},{2,6},{3,7},{4,8},{5,9},{6,10},{7,11},{8,12},{9,13},{1... | collective-permute-start | bytes 393224 | tf_op jit(solution)/shard_map/ppermute | solution.py:75
  37.7 2.0 %fusion.20 = (f32[2,128,128]{2,1,0:T(8,128)S(1)}, f32[2,128,128]{2,1,0:T(8,128)S(1)}) fusion(f32[4,2,128,128]{3,2,1,0:T(8,128)S(1)} %bitcast_dynamic-update-slice_fusion.21, f32[]{:T(128)} %bitcast.11, f32[]{:T(128)} %bitcast.13, f32[]{:T(128)S(6)} %mul.244, f32[]{:T(128)} %bitcast.15), kind=kLoop, calls=%fused_computation.47 | loop fusion | flops 229376 | bytes 786448 | tf_op jit(solution)/shard_map/add | solution.py:69
  39.8 3.2 %collective-permute-start.3 = (f32[2,128,128]{2,1,0:T(8,128)S(1)}, f32[2,128,128]{2,1,0:T(8,128)S(1)}, u32[]{:S(2)}, u32[]{:S(2)}) collective-permute-start(f32[2,128,128]{2,1,0:T(8,128)S(1)} %get-tuple-element.29), channel_id=1, source_target_pairs={{0,4},{1,5},{2,6},{3,7},{4,8},{5,9},{6,10},{7,11},{8,12},{9,13},{1... | collective-permute-start | bytes 393224 | tf_op jit(solution)/shard_map/ppermute | solution.py:75
  43.0 3.2 %collective-permute-start.13 = (f32[2,128,128]{2,1,0:T(8,128)S(1)}, f32[2,128,128]{2,1,0:T(8,128)S(1)}, u32[]{:S(2)}, u32[]{:S(2)}) collective-permute-start(f32[2,128,128]{2,1,0:T(8,128)S(1)} %multiply_add_fusion.5), channel_id=1, source_target_pairs={{0,4},{1,5},{2,6},{3,7},{4,8},{5,9},{6,10},{7,11},{8,12},{9,13},{1... | collective-permute-start | bytes 393224 | tf_op jit(solution)/shard_map/ppermute | solution.py:75
  46.3 2.8 %collective-permute-start.4 = (f32[2,128,128]{2,1,0:T(8,128)S(1)}, f32[2,128,128]{2,1,0:T(8,128)S(1)}, u32[]{:S(2)}, u32[]{:S(2)}) collective-permute-start(f32[2,128,128]{2,1,0:T(8,128)S(1)} %multiply_add_fusion.7), channel_id=1, source_target_pairs={{0,4},{1,5},{2,6},{3,7},{4,8},{5,9},{6,10},{7,11},{8,12},{9,13},{1... | collective-permute-start | bytes 393224 | tf_op jit(solution)/shard_map/ppermute | solution.py:75
  49.1 3.2 %collective-permute-start.14 = (f32[2,128,128]{2,1,0:T(8,128)S(1)}, f32[2,128,128]{2,1,0:T(8,128)S(1)}, u32[]{:S(2)}, u32[]{:S(2)}) collective-permute-start(f32[2,128,128]{2,1,0:T(8,128)S(1)} %multiply_add_fusion.4), channel_id=1, source_target_pairs={{0,4},{1,5},{2,6},{3,7},{4,8},{5,9},{6,10},{7,11},{8,12},{9,13},{1... | collective-permute-start | bytes 393224 | tf_op jit(solution)/shard_map/ppermute | solution.py:76
  52.4 3.5 %collective-permute-start.5 = (f32[2,128,128]{2,1,0:T(8,128)S(1)}, f32[2,128,128]{2,1,0:T(8,128)S(1)}, u32[]{:S(2)}, u32[]{:S(2)}) collective-permute-start(f32[2,128,128]{2,1,0:T(8,128)S(1)} %multiply_add_fusion.6), channel_id=1, source_target_pairs={{0,4},{1,5},{2,6},{3,7},{4,8},{5,9},{6,10},{7,11},{8,12},{9,13},{1... | collective-permute-start | bytes 393224 | tf_op jit(solution)/shard_map/ppermute | solution.py:76
  55.9 1.3 add_bitcast_fusion.8
  57.4 4.9 %collective-permute-start.15 = (f32[2,128,128]{2,1,0:T(8,128)S(1)}, f32[2,128,128]{2,1,0:T(8,128)S(1)}, u32[]{:S(2)}, u32[]{:S(2)}) collective-permute-start(f32[2,128,128]{2,1,0:T(8,128)S(1)} %get-tuple-element.73), channel_id=1, source_target_pairs={{0,1},{1,2},{2,3},{3,0},{4,5},{5,6},{6,7},{7,4},{8,9},{9,10},{10,1... | collective-permute-start | bytes 393224 | tf_op jit(solution)/shard_map/ppermute | solution.py:49
  62.7 1.3 add_bitcast_fusion.11
  64.2 1.3 collective-permute-start.6
  65.6 1.5 collective-permute-start.7
  68.5 2.0 %collective-permute-done.6 = f32[2,128,128]{2,1,0:T(8,128)S(1)} collective-permute-done((f32[2,128,128]{2,1,0:T(8,128)S(1)}, f32[2,128,128]{2,1,0:T(8,128)S(1)}, u32[]{:S(2)}, u32[]{:S(2)}) %collective-permute-start.6) | collective-permute-done | bytes 131104 | tf_op jit(solution)/shard_map/ppermute | solution.py:49
  70.6 2.8 %collective-permute-done.7 = f32[2,128,128]{2,1,0:T(8,128)S(1)} collective-permute-done((f32[2,128,128]{2,1,0:T(8,128)S(1)}, f32[2,128,128]{2,1,0:T(8,128)S(1)}, u32[]{:S(2)}, u32[]{:S(2)}) %collective-permute-start.7) | collective-permute-done | bytes 131104 | tf_op jit(solution)/shard_map/ppermute | solution.py:49
  74.7 5.5 %shard_map.86 = f32[384,2048]{1,0:T(8,128)} custom-call(bf16[384,2048]{1,0:T(8,128)(2,1)} %query_ref.7, f32[384,2048]{1,0:T(8,128)} %get-tuple-element.11.inside_ref, bf16[16,128,128]{2,1,0:T(8,128)(2,1)} %fusion.3.prefix_ref, f32[384,1]{1,0:T(8,128)} %reshape.143.carry_ref), custom_call_target="tpu_custom_call" | custom-call | tf_op jit(solution)/shard_map/pallas_call | solution.py:126
  80.1 2.3 %multiply_reduce_fusion = f32[384]{0:T(512)S(1)} fusion(f32[384,2048]{1,0:T(8,128)} %shard_map.86), kind=kLoop, calls=%fused_computation.5 | loop fusion | flops 1572480 | bytes 3147264 | tf_op jit(solution)/shard_map/reduce_sum | solution.py:225
  83.6 2.4 %fusion.2 = (bf16[384,2048]{1,0:T(8,128)(2,1)}, bf16[384,2048]{1,0:T(8,128)(2,1)}) fusion(bf16[384,2048]{1,0:T(8,128)(2,1)S(1)} %copy-done.1, f32[384]{0:T(512)S(1)} %broadcast_multiply_fusion, f32[384]{0:T(512)S(1)} %add_sqrt_fusion, f32[384,2048]{1,0:T(8,128)S(1)} %copy-done), kind=kLoop, calls=%fused_computation.4 | loop fusion | flops 5505024 | bytes 7867392 | tf_op jit(solution)/shard_map/convert_element_type | solution.py:230
  86.0 4.6 %shard_map.88 = f32[16,128,128]{2,1,0:T(8,128)} custom-call(bf16[384,2048]{1,0:T(8,128)(2,1)} %query_ref.7, bf16[384,2048]{1,0:T(8,128)(2,1)} %get-tuple-element.33.grad_ref, f32[384,1]{1,0:T(8,128)} %reshape.143.carry_ref), custom_call_target="tpu_custom_call" | custom-call | tf_op jit(solution)/shard_map/pallas_call | solution.py:126
  97.2 11.6 %shard_map.87 = (bf16[384,2048]{1,0:T(8,128)(2,1)}, f32[384,2048]{1,0:T(8,128)}, f32[384,2048]{1,0:T(8,128)}) custom-call(bf16[384,2048]{1,0:T(8,128)(2,1)} %query_ref.7, bf16[384,2048]{1,0:T(8,128)(2,1)} %key_ref.7, bf16[384,2048]{1,0:T(8,128)(2,1)} %value_ref.7, bf16[384,2048]{1,0:T(8,128)(2,1)} %get-tuple-element.33.grad_ref, ...), custom_call_target="tpu_custom_call" | custom-call | tf_op jit(solution)/shard_map/pallas_call | solution.py:126
  108.8 1.6 collective-permute-start.28
  113.7 1.8 %collective-permute-done.18 = f32[2,128,128]{2,1,0:T(8,128)S(1)} collective-permute-done((f32[2,128,128]{2,1,0:T(8,128)S(1)}, f32[2,128,128]{2,1,0:T(8,128)S(1)}, u32[]{:S(2)}, u32[]{:S(2)}) %collective-permute-start.18) | collective-permute-done | bytes 131104 | tf_op jit(solution)/shard_map/ppermute | solution.py:49
  115.6 3.9 %collective-permute-done.19 = f32[2,128,128]{2,1,0:T(8,128)S(1)} collective-permute-done((f32[2,128,128]{2,1,0:T(8,128)S(1)}, f32[2,128,128]{2,1,0:T(8,128)S(1)}, u32[]{:S(2)}, u32[]{:S(2)}) %collective-permute-start.19) | collective-permute-done | bytes 131104 | tf_op jit(solution)/shard_map/ppermute | solution.py:49
  119.5 1.6 collective-permute-done.20
  121.1 1.9 %fusion.5 = (f32[2,128,128]{2,1,0:T(8,128)S(1)}, f32[2,128,128]{2,1,0:T(8,128)S(1)}) fusion(f32[4,2,128,128]{3,2,1,0:T(8,128)S(1)} %get-tuple-element.95, f32[]{:T(128)} %bitcast.66, f32[]{:T(128)} %bitcast.60, f32[]{:T(128)S(6)} %mul.277, f32[]{:T(128)} %bitcast.62), kind=kLoop, calls=%fused_computation.17 | loop fusion | flops 229376 | bytes 786448 | tf_op jit(solution)/shard_map/add | solution.py:69
  123.1 1.3 collective-permute-start.30
  124.4 1.9 %fusion.9 = (f32[2,128,128]{2,1,0:T(8,128)S(1)}, f32[2,128,128]{2,1,0:T(8,128)S(1)}) fusion(f32[4,2,128,128]{3,2,1,0:T(8,128)S(1)} %get-tuple-element.96, f32[]{:T(128)} %bitcast.66, f32[]{:T(128)} %bitcast.60, f32[]{:T(128)S(6)} %mul.277, f32[]{:T(128)} %bitcast.62), kind=kLoop, calls=%fused_computation.25 | loop fusion | flops 229376 | bytes 786448 | tf_op jit(solution)/shard_map/add | solution.py:69
  126.3 1.3 collective-permute-start.21
  127.6 2.6 %collective-permute-done.30 = f32[2,128,128]{2,1,0:T(8,128)S(1)} collective-permute-done((f32[2,128,128]{2,1,0:T(8,128)S(1)}, f32[2,128,128]{2,1,0:T(8,128)S(1)}, u32[]{:S(2)}, u32[]{:S(2)}) %collective-permute-start.30) | collective-permute-done | bytes 131104 | tf_op jit(solution)/shard_map/ppermute | solution.py:75
  130.2 1.3 collective-permute-start.31
  131.5 2.5 %collective-permute-done.21 = f32[2,128,128]{2,1,0:T(8,128)S(1)} collective-permute-done((f32[2,128,128]{2,1,0:T(8,128)S(1)}, f32[2,128,128]{2,1,0:T(8,128)S(1)}, u32[]{:S(2)}, u32[]{:S(2)}) %collective-permute-start.21) | collective-permute-done | bytes 131104 | tf_op jit(solution)/shard_map/ppermute | solution.py:75
  134.1 1.3 collective-permute-start.22
  136.4 1.3 collective-permute-start.32
  137.7 2.5 %collective-permute-done.22 = f32[2,128,128]{2,1,0:T(8,128)S(1)} collective-permute-done((f32[2,128,128]{2,1,0:T(8,128)S(1)}, f32[2,128,128]{2,1,0:T(8,128)S(1)}, u32[]{:S(2)}, u32[]{:S(2)}) %collective-permute-start.22) | collective-permute-done | bytes 131104 | tf_op jit(solution)/shard_map/ppermute | solution.py:75
  142.6 1.4 add_bitcast_fusion.2
  144.1 3.8 %collective-permute-start.33 = (f32[2,128,128]{2,1,0:T(8,128)S(1)}, f32[2,128,128]{2,1,0:T(8,128)S(1)}, u32[]{:S(2)}, u32[]{:S(2)}) collective-permute-start(f32[2,128,128]{2,1,0:T(8,128)S(1)} %get-tuple-element.57), channel_id=1, source_target_pairs={{0,1},{1,2},{2,3},{3,0},{4,5},{5,6},{6,7},{7,4},{8,9},{9,10},{10,1... | collective-permute-start | bytes 393224 | tf_op jit(solution)/shard_map/ppermute | solution.py:49
  148.4 1.4 add_bitcast_fusion.5
  149.9 2.5 %collective-permute-start.24 = (f32[2,128,128]{2,1,0:T(8,128)S(1)}, f32[2,128,128]{2,1,0:T(8,128)S(1)}, u32[]{:S(2)}, u32[]{:S(2)}) collective-permute-start(f32[2,128,128]{2,1,0:T(8,128)S(1)} %get-tuple-element.49), channel_id=1, source_target_pairs={{0,1},{1,2},{2,3},{3,0},{4,5},{5,6},{6,7},{7,4},{8,9},{9,10},{10,1... | collective-permute-start | bytes 393224 | tf_op jit(solution)/shard_map/ppermute | solution.py:49
  153.7 1.6 collective-permute-done.35
  156.2 3.1 %collective-permute-done.25 = f32[2,128,128]{2,1,0:T(8,128)S(1)} collective-permute-done((f32[2,128,128]{2,1,0:T(8,128)S(1)}, f32[2,128,128]{2,1,0:T(8,128)S(1)}, u32[]{:S(2)}, u32[]{:S(2)}) %collective-permute-start.25) | collective-permute-done | bytes 131104 | tf_op jit(solution)/shard_map/ppermute | solution.py:49
  160.9 6.8 %shard_map.89 = (bf16[384,2048]{1,0:T(8,128)(2,1)}, bf16[384,2048]{1,0:T(8,128)(2,1)}) custom-call(bf16[384,2048]{1,0:T(8,128)(2,1)} %key_ref.7, bf16[384,2048]{1,0:T(8,128)(2,1)} %value_ref.7, f32[384,2048]{1,0:T(8,128)} %get-tuple-element.14.key_part, f32[384,2048]{1,0:T(8,128)} %get-tuple-element.15.value_part, bf16[16,128,128]{2,1,0:T(8,128)(2,1)} %fusion.4.suffix_ref, ...), custom_call_target="tpu_custom_call" | custom-call | tf_op jit(solution)/shard_map/pallas_call | solution.py:126
  (119 shorter events, 26.1 us)
Async XLA Ops:
  12.2 20.0 %collective-permute-start.9 = (f32[2,128,128]{2,1,0:T(8,128)S(1)}, f32[2,128,128]{2,1,0:T(8,128)S(1)}, u32[]{:S(2)}, u32[]{:S(2)}) collective-permute-start(f32[2,128,128]{2,1,0:T(8,128)S(1)} %get-tuple-element.77), channel_id=1, source_target_pairs={{0,1},{1,2},{2,3},{3,0},{4,5},{5,6},{6,7},{7,4},{8,9},{9,10},{10,1... | collective-permute-start | bytes 393224 | tf_op jit(solution)/shard_map/ppermute | solution.py:49
  14.9 17.4 %collective-permute-start.10 = (f32[2,128,128]{2,1,0:T(8,128)S(1)}, f32[2,128,128]{2,1,0:T(8,128)S(1)}, u32[]{:S(2)}, u32[]{:S(2)}) collective-permute-start(f32[2,128,128]{2,1,0:T(8,128)S(1)} %get-tuple-element.76), channel_id=1, source_target_pairs={{0,2},{1,3},{2,0},{3,1},{4,6},{5,7},{6,4},{7,5},{8,10},{9,11},{10,... | collective-permute-start | bytes 393224 | tf_op jit(solution)/shard_map/ppermute | solution.py:49
  14.9 17.5 %collective-permute-start.11 = (f32[2,128,128]{2,1,0:T(8,128)S(1)}, f32[2,128,128]{2,1,0:T(8,128)S(1)}, u32[]{:S(2)}, u32[]{:S(2)}) collective-permute-start(f32[2,128,128]{2,1,0:T(8,128)S(1)} %get-tuple-element.75), channel_id=1, source_target_pairs={{0,3},{1,0},{2,1},{3,2},{4,7},{5,4},{6,5},{7,6},{8,11},{9,8},{10,9... | collective-permute-start | bytes 393224 | tf_op jit(solution)/shard_map/ppermute | solution.py:49
  15.5 22.2 %collective-permute-start = (f32[2,128,128]{2,1,0:T(8,128)S(1)}, f32[2,128,128]{2,1,0:T(8,128)S(1)}, u32[]{:S(2)}, u32[]{:S(2)}) collective-permute-start(f32[2,128,128]{2,1,0:T(8,128)S(1)} %get-tuple-element.69), channel_id=1, source_target_pairs={{0,1},{1,2},{2,3},{3,0},{4,5},{5,6},{6,7},{7,4},{8,9},{9,10},{10,1... | collective-permute-start | bytes 393224 | tf_op jit(solution)/shard_map/ppermute | solution.py:49
  16.8 20.9 %collective-permute-start.1 = (f32[2,128,128]{2,1,0:T(8,128)S(1)}, f32[2,128,128]{2,1,0:T(8,128)S(1)}, u32[]{:S(2)}, u32[]{:S(2)}) collective-permute-start(f32[2,128,128]{2,1,0:T(8,128)S(1)} %get-tuple-element.68), channel_id=1, source_target_pairs={{0,2},{1,3},{2,0},{3,1},{4,6},{5,7},{6,4},{7,5},{8,10},{9,11},{10,... | collective-permute-start | bytes 393224 | tf_op jit(solution)/shard_map/ppermute | solution.py:49
  32.2 5.5 %collective-permute-start.2 = (f32[2,128,128]{2,1,0:T(8,128)S(1)}, f32[2,128,128]{2,1,0:T(8,128)S(1)}, u32[]{:S(2)}, u32[]{:S(2)}) collective-permute-start(f32[2,128,128]{2,1,0:T(8,128)S(1)} %get-tuple-element.67), channel_id=1, source_target_pairs={{0,3},{1,0},{2,1},{3,2},{4,7},{5,4},{6,5},{7,6},{8,11},{9,8},{10,9... | collective-permute-start | bytes 393224 | tf_op jit(solution)/shard_map/ppermute | solution.py:49
  34.4 8.6 %collective-permute-start.12 = (f32[2,128,128]{2,1,0:T(8,128)S(1)}, f32[2,128,128]{2,1,0:T(8,128)S(1)}, u32[]{:S(2)}, u32[]{:S(2)}) collective-permute-start(f32[2,128,128]{2,1,0:T(8,128)S(1)} %get-tuple-element.31), channel_id=1, source_target_pairs={{0,4},{1,5},{2,6},{3,7},{4,8},{5,9},{6,10},{7,11},{8,12},{9,13},{1... | collective-permute-start | bytes 393224 | tf_op jit(solution)/shard_map/ppermute | solution.py:75
  39.8 6.5 %collective-permute-start.3 = (f32[2,128,128]{2,1,0:T(8,128)S(1)}, f32[2,128,128]{2,1,0:T(8,128)S(1)}, u32[]{:S(2)}, u32[]{:S(2)}) collective-permute-start(f32[2,128,128]{2,1,0:T(8,128)S(1)} %get-tuple-element.29), channel_id=1, source_target_pairs={{0,4},{1,5},{2,6},{3,7},{4,8},{5,9},{6,10},{7,11},{8,12},{9,13},{1... | collective-permute-start | bytes 393224 | tf_op jit(solution)/shard_map/ppermute | solution.py:75
  43.0 6.0 %collective-permute-start.13 = (f32[2,128,128]{2,1,0:T(8,128)S(1)}, f32[2,128,128]{2,1,0:T(8,128)S(1)}, u32[]{:S(2)}, u32[]{:S(2)}) collective-permute-start(f32[2,128,128]{2,1,0:T(8,128)S(1)} %multiply_add_fusion.5), channel_id=1, source_target_pairs={{0,4},{1,5},{2,6},{3,7},{4,8},{5,9},{6,10},{7,11},{8,12},{9,13},{1... | collective-permute-start | bytes 393224 | tf_op jit(solution)/shard_map/ppermute | solution.py:75
  46.3 6.0 %collective-permute-start.4 = (f32[2,128,128]{2,1,0:T(8,128)S(1)}, f32[2,128,128]{2,1,0:T(8,128)S(1)}, u32[]{:S(2)}, u32[]{:S(2)}) collective-permute-start(f32[2,128,128]{2,1,0:T(8,128)S(1)} %multiply_add_fusion.7), channel_id=1, source_target_pairs={{0,4},{1,5},{2,6},{3,7},{4,8},{5,9},{6,10},{7,11},{8,12},{9,13},{1... | collective-permute-start | bytes 393224 | tf_op jit(solution)/shard_map/ppermute | solution.py:75
  49.1 6.8 %collective-permute-start.14 = (f32[2,128,128]{2,1,0:T(8,128)S(1)}, f32[2,128,128]{2,1,0:T(8,128)S(1)}, u32[]{:S(2)}, u32[]{:S(2)}) collective-permute-start(f32[2,128,128]{2,1,0:T(8,128)S(1)} %multiply_add_fusion.4), channel_id=1, source_target_pairs={{0,4},{1,5},{2,6},{3,7},{4,8},{5,9},{6,10},{7,11},{8,12},{9,13},{1... | collective-permute-start | bytes 393224 | tf_op jit(solution)/shard_map/ppermute | solution.py:76
  52.4 10.4 %collective-permute-start.5 = (f32[2,128,128]{2,1,0:T(8,128)S(1)}, f32[2,128,128]{2,1,0:T(8,128)S(1)}, u32[]{:S(2)}, u32[]{:S(2)}) collective-permute-start(f32[2,128,128]{2,1,0:T(8,128)S(1)} %multiply_add_fusion.6), channel_id=1, source_target_pairs={{0,4},{1,5},{2,6},{3,7},{4,8},{5,9},{6,10},{7,11},{8,12},{9,13},{1... | collective-permute-start | bytes 393224 | tf_op jit(solution)/shard_map/ppermute | solution.py:76
  57.4 9.6 %collective-permute-start.15 = (f32[2,128,128]{2,1,0:T(8,128)S(1)}, f32[2,128,128]{2,1,0:T(8,128)S(1)}, u32[]{:S(2)}, u32[]{:S(2)}) collective-permute-start(f32[2,128,128]{2,1,0:T(8,128)S(1)} %get-tuple-element.73), channel_id=1, source_target_pairs={{0,1},{1,2},{2,3},{3,0},{4,5},{5,6},{6,7},{7,4},{8,9},{9,10},{10,1... | collective-permute-start | bytes 393224 | tf_op jit(solution)/shard_map/ppermute | solution.py:49
  62.3 5.5 %collective-permute-start.16 = (f32[2,128,128]{2,1,0:T(8,128)S(1)}, f32[2,128,128]{2,1,0:T(8,128)S(1)}, u32[]{:S(2)}, u32[]{:S(2)}) collective-permute-start(f32[2,128,128]{2,1,0:T(8,128)S(1)} %get-tuple-element.72), channel_id=1, source_target_pairs={{0,2},{1,3},{2,0},{3,1},{4,6},{5,7},{6,4},{7,5},{8,10},{9,11},{10,... | collective-permute-start | bytes 393224 | tf_op jit(solution)/shard_map/ppermute | solution.py:49
  62.3 6.2 %collective-permute-start.17 = (f32[2,128,128]{2,1,0:T(8,128)S(1)}, f32[2,128,128]{2,1,0:T(8,128)S(1)}, u32[]{:S(2)}, u32[]{:S(2)}) collective-permute-start(f32[2,128,128]{2,1,0:T(8,128)S(1)} %get-tuple-element.71), channel_id=1, source_target_pairs={{0,3},{1,0},{2,1},{3,2},{4,7},{5,4},{6,5},{7,6},{8,11},{9,8},{10,9... | collective-permute-start | bytes 393224 | tf_op jit(solution)/shard_map/ppermute | solution.py:49
  64.2 6.3 %collective-permute-start.6 = (f32[2,128,128]{2,1,0:T(8,128)S(1)}, f32[2,128,128]{2,1,0:T(8,128)S(1)}, u32[]{:S(2)}, u32[]{:S(2)}) collective-permute-start(f32[2,128,128]{2,1,0:T(8,128)S(1)} %get-tuple-element.65), channel_id=1, source_target_pairs={{0,1},{1,2},{2,3},{3,0},{4,5},{5,6},{6,7},{7,4},{8,9},{9,10},{10,1... | collective-permute-start | bytes 393224 | tf_op jit(solution)/shard_map/ppermute | solution.py:49
  65.6 7.8 %collective-permute-start.7 = (f32[2,128,128]{2,1,0:T(8,128)S(1)}, f32[2,128,128]{2,1,0:T(8,128)S(1)}, u32[]{:S(2)}, u32[]{:S(2)}) collective-permute-start(f32[2,128,128]{2,1,0:T(8,128)S(1)} %get-tuple-element.64), channel_id=1, source_target_pairs={{0,2},{1,3},{2,0},{3,1},{4,6},{5,7},{6,4},{7,5},{8,10},{9,11},{10,... | collective-permute-start | bytes 393224 | tf_op jit(solution)/shard_map/ppermute | solution.py:49
  67.0 6.7 %collective-permute-start.8 = (f32[2,128,128]{2,1,0:T(8,128)S(1)}, f32[2,128,128]{2,1,0:T(8,128)S(1)}, u32[]{:S(2)}, u32[]{:S(2)}) collective-permute-start(f32[2,128,128]{2,1,0:T(8,128)S(1)} %get-tuple-element.63), channel_id=1, source_target_pairs={{0,3},{1,0},{2,1},{3,2},{4,7},{5,4},{6,5},{7,6},{8,11},{9,8},{10,9... | collective-permute-start | bytes 393224 | tf_op jit(solution)/shard_map/ppermute | solution.py:49
  74.7 7.8 %copy-start.1 = (bf16[384,2048]{1,0:T(8,128)(2,1)S(1)}, bf16[384,2048]{1,0:T(8,128)(2,1)}, u32[]{:S(2)}) copy-start(bf16[384,2048]{1,0:T(8,128)(2,1)} %param.9) | copy-start | bytes 4718596
  80.1 2.8 %copy-start = (f32[384,2048]{1,0:T(8,128)S(1)}, f32[384,2048]{1,0:T(8,128)}, u32[]{:S(2)}) copy-start(f32[384,2048]{1,0:T(8,128)} %shard_map.86) | copy-start | bytes 9437188
  91.9 20.7 %collective-permute-start.27 = (f32[2,128,128]{2,1,0:T(8,128)S(1)}, f32[2,128,128]{2,1,0:T(8,128)S(1)}, u32[]{:S(2)}, u32[]{:S(2)}) collective-permute-start(f32[2,128,128]{2,1,0:T(8,128)S(1)} %get-tuple-element.61), channel_id=1, source_target_pairs={{0,1},{1,2},{2,3},{3,0},{4,5},{5,6},{6,7},{7,4},{8,9},{9,10},{10,1... | collective-permute-start | bytes 393224 | tf_op jit(solution)/shard_map/ppermute | solution.py:49
  108.8 5.0 %collective-permute-start.28 = (f32[2,128,128]{2,1,0:T(8,128)S(1)}, f32[2,128,128]{2,1,0:T(8,128)S(1)}, u32[]{:S(2)}, u32[]{:S(2)}) collective-permute-start(f32[2,128,128]{2,1,0:T(8,128)S(1)} %get-tuple-element.60), channel_id=1, source_target_pairs={{0,2},{1,3},{2,0},{3,1},{4,6},{5,7},{6,4},{7,5},{8,10},{9,11},{10,... | collective-permute-start | bytes 393224 | tf_op jit(solution)/shard_map/ppermute | solution.py:49
  110.3 9.1 %collective-permute-start.29 = (f32[2,128,128]{2,1,0:T(8,128)S(1)}, f32[2,128,128]{2,1,0:T(8,128)S(1)}, u32[]{:S(2)}, u32[]{:S(2)}) collective-permute-start(f32[2,128,128]{2,1,0:T(8,128)S(1)} %get-tuple-element.59), channel_id=1, source_target_pairs={{0,3},{1,0},{2,1},{3,2},{4,7},{5,4},{6,5},{7,6},{8,11},{9,8},{10,9... | collective-permute-start | bytes 393224 | tf_op jit(solution)/shard_map/ppermute | solution.py:49
  111.2 4.3 %collective-permute-start.18 = (f32[2,128,128]{2,1,0:T(8,128)S(1)}, f32[2,128,128]{2,1,0:T(8,128)S(1)}, u32[]{:S(2)}, u32[]{:S(2)}) collective-permute-start(f32[2,128,128]{2,1,0:T(8,128)S(1)} %get-tuple-element.53), channel_id=1, source_target_pairs={{0,1},{1,2},{2,3},{3,0},{4,5},{5,6},{6,7},{7,4},{8,9},{9,10},{10,1... | collective-permute-start | bytes 393224 | tf_op jit(solution)/shard_map/ppermute | solution.py:49
  112.2 7.2 %collective-permute-start.19 = (f32[2,128,128]{2,1,0:T(8,128)S(1)}, f32[2,128,128]{2,1,0:T(8,128)S(1)}, u32[]{:S(2)}, u32[]{:S(2)}) collective-permute-start(f32[2,128,128]{2,1,0:T(8,128)S(1)} %get-tuple-element.52), channel_id=1, source_target_pairs={{0,2},{1,3},{2,0},{3,1},{4,6},{5,7},{6,4},{7,5},{8,10},{9,11},{10,... | collective-permute-start | bytes 393224 | tf_op jit(solution)/shard_map/ppermute | solution.py:49
  112.6 8.5 %collective-permute-start.20 = (f32[2,128,128]{2,1,0:T(8,128)S(1)}, f32[2,128,128]{2,1,0:T(8,128)S(1)}, u32[]{:S(2)}, u32[]{:S(2)}) collective-permute-start(f32[2,128,128]{2,1,0:T(8,128)S(1)} %get-tuple-element.51), channel_id=1, source_target_pairs={{0,3},{1,0},{2,1},{3,2},{4,7},{5,4},{6,5},{7,6},{8,11},{9,8},{10,9... | collective-permute-start | bytes 393224 | tf_op jit(solution)/shard_map/ppermute | solution.py:49
  123.1 7.1 %collective-permute-start.30 = (f32[2,128,128]{2,1,0:T(8,128)S(1)}, f32[2,128,128]{2,1,0:T(8,128)S(1)}, u32[]{:S(2)}, u32[]{:S(2)}) collective-permute-start(f32[2,128,128]{2,1,0:T(8,128)S(1)} %get-tuple-element.26), channel_id=1, source_target_pairs={{4,0},{5,1},{6,2},{7,3},{8,4},{9,5},{10,6},{11,7},{12,8},{13,9},{1... | collective-permute-start | bytes 393224 | tf_op jit(solution)/shard_map/ppermute | solution.py:75
  126.3 7.8 %collective-permute-start.21 = (f32[2,128,128]{2,1,0:T(8,128)S(1)}, f32[2,128,128]{2,1,0:T(8,128)S(1)}, u32[]{:S(2)}, u32[]{:S(2)}) collective-permute-start(f32[2,128,128]{2,1,0:T(8,128)S(1)} %get-tuple-element.24), channel_id=1, source_target_pairs={{4,0},{5,1},{6,2},{7,3},{8,4},{9,5},{10,6},{11,7},{12,8},{13,9},{1... | collective-permute-start | bytes 393224 | tf_op jit(solution)/shard_map/ppermute | solution.py:75
  130.2 6.2 %collective-permute-start.31 = (f32[2,128,128]{2,1,0:T(8,128)S(1)}, f32[2,128,128]{2,1,0:T(8,128)S(1)}, u32[]{:S(2)}, u32[]{:S(2)}) collective-permute-start(f32[2,128,128]{2,1,0:T(8,128)S(1)} %multiply_add_fusion.1), channel_id=1, source_target_pairs={{4,0},{5,1},{6,2},{7,3},{8,4},{9,5},{10,6},{11,7},{12,8},{13,9},{1... | collective-permute-start | bytes 393224 | tf_op jit(solution)/shard_map/ppermute | solution.py:75
  134.1 6.2 %collective-permute-start.22 = (f32[2,128,128]{2,1,0:T(8,128)S(1)}, f32[2,128,128]{2,1,0:T(8,128)S(1)}, u32[]{:S(2)}, u32[]{:S(2)}) collective-permute-start(f32[2,128,128]{2,1,0:T(8,128)S(1)} %multiply_add_fusion.3), channel_id=1, source_target_pairs={{4,0},{5,1},{6,2},{7,3},{8,4},{9,5},{10,6},{11,7},{12,8},{13,9},{1... | collective-permute-start | bytes 393224 | tf_op jit(solution)/shard_map/ppermute | solution.py:75
  136.4 6.2 %collective-permute-start.32 = (f32[2,128,128]{2,1,0:T(8,128)S(1)}, f32[2,128,128]{2,1,0:T(8,128)S(1)}, u32[]{:S(2)}, u32[]{:S(2)}) collective-permute-start(f32[2,128,128]{2,1,0:T(8,128)S(1)} %multiply_add_fusion), channel_id=1, source_target_pairs={{4,0},{5,1},{6,2},{7,3},{8,4},{9,5},{10,6},{11,7},{12,8},{13,9},{1... | collective-permute-start | bytes 393224 | tf_op jit(solution)/shard_map/ppermute | solution.py:76
  140.3 8.1 %collective-permute-start.23 = (f32[2,128,128]{2,1,0:T(8,128)S(1)}, f32[2,128,128]{2,1,0:T(8,128)S(1)}, u32[]{:S(2)}, u32[]{:S(2)}) collective-permute-start(f32[2,128,128]{2,1,0:T(8,128)S(1)} %multiply_add_fusion.2), channel_id=1, source_target_pairs={{4,0},{5,1},{6,2},{7,3},{8,4},{9,5},{10,6},{11,7},{12,8},{13,9},{1... | collective-permute-start | bytes 393224 | tf_op jit(solution)/shard_map/ppermute | solution.py:76
  144.1 8.6 %collective-permute-start.33 = (f32[2,128,128]{2,1,0:T(8,128)S(1)}, f32[2,128,128]{2,1,0:T(8,128)S(1)}, u32[]{:S(2)}, u32[]{:S(2)}) collective-permute-start(f32[2,128,128]{2,1,0:T(8,128)S(1)} %get-tuple-element.57), channel_id=1, source_target_pairs={{0,1},{1,2},{2,3},{3,0},{4,5},{5,6},{6,7},{7,4},{8,9},{9,10},{10,1... | collective-permute-start | bytes 393224 | tf_op jit(solution)/shard_map/ppermute | solution.py:49
  147.9 5.8 %collective-permute-start.34 = (f32[2,128,128]{2,1,0:T(8,128)S(1)}, f32[2,128,128]{2,1,0:T(8,128)S(1)}, u32[]{:S(2)}, u32[]{:S(2)}) collective-permute-start(f32[2,128,128]{2,1,0:T(8,128)S(1)} %get-tuple-element.56), channel_id=1, source_target_pairs={{0,2},{1,3},{2,0},{3,1},{4,6},{5,7},{6,4},{7,5},{8,10},{9,11},{10,... | collective-permute-start | bytes 393224 | tf_op jit(solution)/shard_map/ppermute | solution.py:49
  147.9 7.4 %collective-permute-start.35 = (f32[2,128,128]{2,1,0:T(8,128)S(1)}, f32[2,128,128]{2,1,0:T(8,128)S(1)}, u32[]{:S(2)}, u32[]{:S(2)}) collective-permute-start(f32[2,128,128]{2,1,0:T(8,128)S(1)} %get-tuple-element.55), channel_id=1, source_target_pairs={{0,3},{1,0},{2,1},{3,2},{4,7},{5,4},{6,5},{7,6},{8,11},{9,8},{10,9... | collective-permute-start | bytes 393224 | tf_op jit(solution)/shard_map/ppermute | solution.py:49
  149.9 6.3 %collective-permute-start.24 = (f32[2,128,128]{2,1,0:T(8,128)S(1)}, f32[2,128,128]{2,1,0:T(8,128)S(1)}, u32[]{:S(2)}, u32[]{:S(2)}) collective-permute-start(f32[2,128,128]{2,1,0:T(8,128)S(1)} %get-tuple-element.49), channel_id=1, source_target_pairs={{0,1},{1,2},{2,3},{3,0},{4,5},{5,6},{6,7},{7,4},{8,9},{9,10},{10,1... | collective-permute-start | bytes 393224 | tf_op jit(solution)/shard_map/ppermute | solution.py:49
  152.4 6.9 %collective-permute-start.25 = (f32[2,128,128]{2,1,0:T(8,128)S(1)}, f32[2,128,128]{2,1,0:T(8,128)S(1)}, u32[]{:S(2)}, u32[]{:S(2)}) collective-permute-start(f32[2,128,128]{2,1,0:T(8,128)S(1)} %get-tuple-element.48), channel_id=1, source_target_pairs={{0,2},{1,3},{2,0},{3,1},{4,6},{5,7},{6,4},{7,5},{8,10},{9,11},{10,... | collective-permute-start | bytes 393224 | tf_op jit(solution)/shard_map/ppermute | solution.py:49
  152.7 7.3 %collective-permute-start.26 = (f32[2,128,128]{2,1,0:T(8,128)S(1)}, f32[2,128,128]{2,1,0:T(8,128)S(1)}, u32[]{:S(2)}, u32[]{:S(2)}) collective-permute-start(f32[2,128,128]{2,1,0:T(8,128)S(1)} %get-tuple-element.47), channel_id=1, source_target_pairs={{0,3},{1,0},{2,1},{3,2},{4,7},{5,4},{6,5},{7,6},{8,11},{9,8},{10,9... | collective-permute-start | bytes 393224 | tf_op jit(solution)/shard_map/ppermute | solution.py:49

commit v6 on v5

--- a/solution.py
+++ b/solution.py
@@ -32,7 +32,7 @@
 
 
 GROUP = 4
-CHUNKS = 2
+CHUNKS = 1
 
 
 def member_exchange(pieces, axis):
@@ -53,7 +53,8 @@
     return placed
 
 
-def row_scan(state, keep_row, direction):
+def row_scan(state, keep_of, direction):
+    keep_row = keep_of((lax.axis_index("seq") // GROUP) * GROUP + lax.iota(jnp.int32, GROUP))
     count = lax.axis_size("seq")
     heads = state.shape[0]
     pieces = state.reshape((GROUP, heads // GROUP) + state.shape[1:])
@@ -68,18 +69,20 @@
         inner_keep[index] = total_keep
         total = mine[index] + keep_row[index] * total
         total_keep = total_keep * keep_row[index]
-    shift = GROUP * direction
-    pairs = [(source, source + shift) for source in range(count) if 0 <= source + shift < count]
-    window = total
-    for _ in range(-(-SPAN // GROUP) - 1):
-        window = total + total_keep * lax.ppermute(window, "seq", pairs)
-    entering = lax.ppermute(window, "seq", pairs)
+    row = lax.axis_index("seq") // GROUP
+    entering = jnp.zeros_like(total)
+    weight = jnp.ones((), jnp.float32)
+    for reach in range(1, -(-SPAN // GROUP) + 1):
+        shift = GROUP * direction * reach
+        pairs = [(source, source + shift) for source in range(count) if 0 <= source + shift < count]
+        entering = entering + weight * lax.ppermute(total, "seq", pairs)
+        other = (row - direction * reach) * GROUP + lax.iota(jnp.int32, GROUP)
+        weight = weight * jnp.prod(keep_of(other))
     scanned = jnp.stack([inner[index] + inner_keep[index] * entering for index in range(GROUP)])
     return member_exchange(scanned, "seq").reshape(state.shape)
 
 
-def row_flags(starts, row_count):
-    blocks = (lax.axis_index("seq") // GROUP) * GROUP + lax.iota(jnp.int32, GROUP)
+def block_flags(starts, blocks, row_count):
     first = blocks * row_count
     last = first + row_count - 1
     doc_first = jnp.sum((starts[None, :] <= first[:, None]).astype(jnp.int32), axis=1)
@@ -91,12 +94,12 @@
     return has_start, stops_back
 
 
-def scan_states(state, keep_row, fallback_flag, direction):
+def scan_states(state, keep_of, fallback_flag, direction):
     heads = state.shape[0]
     if lax.axis_size("seq") % GROUP == 0 and heads % (GROUP * CHUNKS) == 0:
         size = heads // CHUNKS
         return jnp.concatenate(
-            [row_scan(state[i * size:(i + 1) * size], keep_row, direction) for i in range(CHUNKS)]
+            [row_scan(state[i * size:(i + 1) * size], keep_of, direction) for i in range(CHUNKS)]
         )
     return windowed_prefix((state, fallback_flag), direction)[0]
 
@@ -218,8 +221,14 @@
         [jax.ShapeDtypeStruct((head_count, row_count, row_count), jnp.bfloat16), wide],
     )
     start_flag = has_start.astype(f32).reshape(1, 1, 1)
-    row_start, row_stop = row_flags(starts, row_count)
-    prefix = scan_states(state_local, 1.0 - row_start.astype(f32), start_flag, 1)
+
+    def start_keep(blocks):
+        return 1.0 - block_flags(starts, blocks, row_count)[0].astype(f32)
+
+    def stop_keep(blocks):
+        return 1.0 - block_flags(starts, blocks, row_count)[1].astype(f32)
+
+    prefix = scan_states(state_local, start_keep, start_flag, 1)
     prefix_low = (prefix * continues.astype(f32)).astype(jnp.bfloat16)
     (mixed,) = head_call(mixed_body, [queries, inside, prefix_low, carry], [wide])
     rms_value = jnp.sqrt(jnp.mean(mixed * mixed, axis=1, keepdims=True) + 1e-05)
@@ -230,7 +239,7 @@
     grad_low = grad_mix.astype(jnp.bfloat16)
     (grad_local,) = head_call(local_body, [queries, grad_low, carry], [state_shape])
     back_flag = stops_back.astype(f32).reshape(1, 1, 1)
-    suffix = scan_states(grad_local, 1.0 - row_stop.astype(f32), back_flag, -1)
+    suffix = scan_states(grad_local, stop_keep, back_flag, -1)
     next_first = first_row + row_count
     next_open = (next_first < lax.axis_size("seq") * row_count) & jnp.logical_not(jnp.any(starts == next_first))
     suffix_low = (suffix * next_open.astype(f32)).astype(jnp.bfloat16)

time: 169 us -> 168 us (level)
  waiting for transfers between devices: 31.7 us -> 64.2 us
  starting transfers between devices: 52.8 us -> 21.6 us
  other arithmetic: 25.7 us -> 23.2 us
    ppermute x12 -> x6, waiting for transfers between devices: 9.73 us -> 33.3 us  [row_scan(): entering = entering + weight * lax.ppermute(total, 'seq', pairs)]
    ppermute x24 -> x12, starting transfers between devices: 25.9 us -> 8.15 us  [member_exchange(): got.append(lax.ppermute(piece, axis, pairs))]
    ppermute x12 -> x6, starting transfers between devices: 26.9 us -> 13.4 us  [row_scan(): entering = entering + weight * lax.ppermute(total, 'seq', pairs)]
    ppermute x24 -> x12, waiting for transfers between devices: 22 us -> 31 us  [member_exchange(): got.append(lax.ppermute(piece, axis, pairs))]
    add x4 -> x2, other arithmetic: 7.89 us -> 4.07 us  [row_scan(): total = mine[index] + keep_row[index] * total]
    reduce_prod x0 -> x4, other arithmetic: none -> 2.68 us  [row_scan(): weight = weight * jnp.prod(keep_of(other))]
    slice x2 -> x0, local copies, waits for them, and re-layouts: 2.55 us -> none  [scan_states(): state[i * size:(i + 1) * size]]
    squeeze x8 -> x4, local copies, waits for them, and re-layouts: 0.39 us -> 2.7 us  [member_exchange(): lax.dynamic_index_in_dim(pieces, (member + offset) % GROUP, keepdims=False)]
  transfers between devices with their start and end apart: 36 -> 18, of which waited for: 19 -> 13; matrix products, arithmetic and copies ran while one was open for 10% -> 4% of each run, Pallas kernels for 12% -> 12%
where the time goes in v6:
time: 168 us; the launch traced here: 167 us
  waiting for transfers between devices  64.2 us (38%)
  Pallas kernels  40.7 us (24%)
  other arithmetic  23.2 us (14%)
  starting transfers between devices  21.6 us (13%)
  between operations  10.1 us (6%)
  local copies, waits for them, and re-layouts  7.32 us (4%)
    pallas_call x6, Pallas kernels, head_call(): pl.pallas_call(body, grid=(heads // HEAD_STEP,), in_specs=[spec(x.shape)...  40.7 us
    ppermute x6, waiting for transfers between devices, row_scan(): entering = entering + weight * lax.ppermute(total, 'seq', pairs)  33.3 us
    ppermute x12, waiting for transfers between devices, member_exchange(): got.append(lax.ppermute(piece, axis, pairs))  31 us
    ppermute x6, starting transfers between devices, row_scan(): entering = entering + weight * lax.ppermute(total, 'seq', pairs)  13.4 us
    ppermute x12, starting transfers between devices, member_exchange(): got.append(lax.ppermute(piece, axis, pairs))  8.15 us
    another operation x6, other arithmetic, row_scan(): jnp.stack([inner[index] + inner_keep[index] * entering for index in range...  4.2 us
    add x2, other arithmetic, row_scan(): total = mine[index] + keep_row[index] * total  4.07 us
  transfers between devices with their start and end apart: 18, of which 13 were waited for; matrix products, arithmetic and copies ran while one was open for 4% of the time, Pallas kernels for 12%

profile of v6, /device:TPU:1, one launch (start us, length us, event | category | flops | bytes accessed | tf_op | source)
XLA Modules:
  0.0 167.1 jit_solution(5274574449278200455)
XLA Ops:
  0.7 0.8 reduce-window.9
  1.6 1.3 compare_reduce_fusion
  4.2 1.3 and_convert_fusion.1
  5.5 0.8 reshape.154.tail_ref
  6.3 4.6 %shard_map.85 = f32[16,128,128]{2,1,0:T(8,128)} custom-call(bf16[384,2048]{1,0:T(8,128)(2,1)} %key_ref.7, bf16[384,2048]{1,0:T(8,128)(2,1)} %value_ref.7, f32[384,1]{1,0:T(8,128)} %reshape.154.tail_ref), custom_call_target="tpu_custom_call" | custom-call | tf_op jit(solution)/shard_map/pallas_call | solution.py:129
  10.9 1.3 dynamic-slice_bitcast_fusion.9
  12.2 2.6 %collective-permute-start = (f32[4,128,128]{2,1,0:T(8,128)S(1)}, f32[4,128,128]{2,1,0:T(8,128)S(1)}, u32[]{:S(2)}, u32[]{:S(2)}) collective-permute-start(f32[4,128,128]{2,1,0:T(8,128)S(1)} %get-tuple-element.59), channel_id=1, source_target_pairs={{0,1},{1,2},{2,3},{3,0},{4,5},{5,6},{6,7},{7,4},{8,9},{9,10},{10,1... | collective-permute-start | bytes 786440 | tf_op jit(solution)/shard_map/ppermute | solution.py:49
  17.0 3.3 %collective-permute-done = f32[4,128,128]{2,1,0:T(8,128)S(1)} collective-permute-done((f32[4,128,128]{2,1,0:T(8,128)S(1)}, f32[4,128,128]{2,1,0:T(8,128)S(1)}, u32[]{:S(2)}, u32[]{:S(2)}) %collective-permute-start) | collective-permute-done | bytes 262176 | tf_op jit(solution)/shard_map/ppermute | solution.py:49
  20.3 5.6 %collective-permute-done.1 = f32[4,128,128]{2,1,0:T(8,128)S(1)} collective-permute-done((f32[4,128,128]{2,1,0:T(8,128)S(1)}, f32[4,128,128]{2,1,0:T(8,128)S(1)}, u32[]{:S(2)}, u32[]{:S(2)}) %collective-permute-start.1) | collective-permute-done | bytes 262176 | tf_op jit(solution)/shard_map/ppermute | solution.py:49
  26.5 2.1 %fusion.10 = (f32[4,128,128]{2,1,0:T(8,128)S(1)}, f32[4,128,128]{2,1,0:T(8,128)S(1)}) fusion(f32[4,4,128,128]{3,2,1,0:T(8,128)S(1)} %bitcast_dynamic-update-slice_fusion.9, f32[]{:T(128)} %bitcast.11, f32[]{:T(128)} %bitcast.13, f32[]{:T(128)S(6)} %mul.230, f32[]{:T(128)} %bitcast.15), kind=kLoop, calls=%fused_computation.27 | loop fusion | flops 458752 | bytes 1572880 | tf_op jit(solution)/shard_map/add | solution.py:70
  28.6 6.1 %collective-permute-start.5 = (f32[4,128,128]{2,1,0:T(8,128)S(1)}, f32[4,128,128]{2,1,0:T(8,128)S(1)}, u32[]{:S(2)}, u32[]{:S(2)}) collective-permute-start(f32[4,128,128]{2,1,0:T(8,128)S(1)} %get-tuple-element.41), channel_id=1, source_target_pairs={{0,12},{1,13},{2,14},{3,15},{16,28},{17,29},{18,30},{19,31}} | collective-permute-start | bytes 786440 | tf_op jit(solution)/shard_map/ppermute | solution.py:78
  34.6 1.3 collective-permute-start.3
  35.9 2.2 %collective-permute-start.4 = (f32[4,128,128]{2,1,0:T(8,128)S(1)}, f32[4,128,128]{2,1,0:T(8,128)S(1)}, u32[]{:S(2)}, u32[]{:S(2)}) collective-permute-start(f32[4,128,128]{2,1,0:T(8,128)S(1)} %get-tuple-element.41), channel_id=1, source_target_pairs={{0,8},{1,9},{2,10},{3,11},{4,12},{5,13},{6,14},{7,15},{16,24},{17,... | collective-permute-start | bytes 786440 | tf_op jit(solution)/shard_map/ppermute | solution.py:78
  40.7 0.7 subtract_reduce_fusion
  42.8 3.4 %collective-permute-done.3 = f32[4,128,128]{2,1,0:T(8,128)S(1)} collective-permute-done((f32[4,128,128]{2,1,0:T(8,128)S(1)}, f32[4,128,128]{2,1,0:T(8,128)S(1)}, u32[]{:S(2)}, u32[]{:S(2)}) %collective-permute-start.3) | collective-permute-done | bytes 262176 | tf_op jit(solution)/shard_map/ppermute | solution.py:78
  46.2 5.6 %collective-permute-done.4 = f32[4,128,128]{2,1,0:T(8,128)S(1)} collective-permute-done((f32[4,128,128]{2,1,0:T(8,128)S(1)}, f32[4,128,128]{2,1,0:T(8,128)S(1)}, u32[]{:S(2)}, u32[]{:S(2)}) %collective-permute-start.4) | collective-permute-done | bytes 262176 | tf_op jit(solution)/shard_map/ppermute | solution.py:78
  51.8 1.4 add_bitcast_fusion.5
  53.2 0.7 add_bitcast_fusion.4
  54.4 1.0 and_convert_fusion.keep_ref
  55.3 1.8 %collective-permute-start.7 = (f32[4,128,128]{2,1,0:T(8,128)S(1)}, f32[4,128,128]{2,1,0:T(8,128)S(1)}, u32[]{:S(2)}, u32[]{:S(2)}) collective-permute-start(f32[4,128,128]{2,1,0:T(8,128)S(1)} %get-tuple-element.54), channel_id=1, source_target_pairs={{0,2},{1,3},{2,0},{3,1},{4,6},{5,7},{6,4},{7,5},{8,10},{9,11},{10,... | collective-permute-start | bytes 786440 | tf_op jit(solution)/shard_map/ppermute | solution.py:49
  57.4 0.8 reshape.155.carry_ref
  58.2 7.7 %shard_map.84 = (bf16[16,384,384]{2,1,0:T(8,128)(2,1)}, f32[384,2048]{1,0:T(8,128)}) custom-call(bf16[384,2048]{1,0:T(8,128)(2,1)} %query_ref.7, bf16[384,2048]{1,0:T(8,128)(2,1)} %key_ref.7, bf16[384,2048]{1,0:T(8,128)(2,1)} %value_ref.7, f32[384,384]{1,0:T(8,128)} %and_convert_fusion.keep_ref), custom_call_target="tpu_custom_call" | custom-call | tf_op jit(solution)/shard_map/pallas_call | solution.py:129
  66.0 5.7 %collective-permute-done.8 = f32[4,128,128]{2,1,0:T(8,128)S(1)} collective-permute-done((f32[4,128,128]{2,1,0:T(8,128)S(1)}, f32[4,128,128]{2,1,0:T(8,128)S(1)}, u32[]{:S(2)}, u32[]{:S(2)}) %collective-permute-start.8) | collective-permute-done | bytes 262176 | tf_op jit(solution)/shard_map/ppermute | solution.py:49
  71.7 0.9 multiply_convert_fusion.1
  72.6 5.5 %shard_map.86 = f32[384,2048]{1,0:T(8,128)} custom-call(bf16[384,2048]{1,0:T(8,128)(2,1)} %query_ref.7, f32[384,2048]{1,0:T(8,128)} %get-tuple-element.11.inside_ref, bf16[16,128,128]{2,1,0:T(8,128)(2,1)} %bitcast.128, f32[384,1]{1,0:T(8,128)} %reshape.155.carry_ref), custom_call_target="tpu_custom_call" | custom-call | tf_op jit(solution)/shard_map/pallas_call | solution.py:129
  78.1 2.3 %multiply_reduce_fusion = f32[384]{0:T(512)S(1)} fusion(f32[384,2048]{1,0:T(8,128)} %shard_map.86), kind=kLoop, calls=%fused_computation.5 | loop fusion | flops 1572480 | bytes 3147264 | tf_op jit(solution)/shard_map/reduce_sum | solution.py:234
  81.6 2.4 %fusion.2 = (bf16[384,2048]{1,0:T(8,128)(2,1)}, bf16[384,2048]{1,0:T(8,128)(2,1)}) fusion(bf16[384,2048]{1,0:T(8,128)(2,1)S(1)} %copy-done.1, f32[384]{0:T(512)S(1)} %broadcast_multiply_fusion, f32[384]{0:T(512)S(1)} %add_sqrt_fusion, f32[384,2048]{1,0:T(8,128)S(1)} %copy-done), kind=kLoop, calls=%fused_computation.4 | loop fusion | flops 5505024 | bytes 7867392 | tf_op jit(solution)/shard_map/convert_element_type | solution.py:239
  84.0 4.6 %shard_map.88 = f32[16,128,128]{2,1,0:T(8,128)} custom-call(bf16[384,2048]{1,0:T(8,128)(2,1)} %query_ref.7, bf16[384,2048]{1,0:T(8,128)(2,1)} %get-tuple-element.43.grad_ref, f32[384,1]{1,0:T(8,128)} %reshape.155.carry_ref), custom_call_target="tpu_custom_call" | custom-call | tf_op jit(solution)/shard_map/pallas_call | solution.py:129
  88.6 1.3 dynamic-slice_bitcast_fusion.3
  91.3 0.7 collective-permute-start.11
  92.0 3.1 %collective-permute-done.9 = f32[4,128,128]{2,1,0:T(8,128)S(1)} collective-permute-done((f32[4,128,128]{2,1,0:T(8,128)S(1)}, f32[4,128,128]{2,1,0:T(8,128)S(1)}, u32[]{:S(2)}, u32[]{:S(2)}) %collective-permute-start.9) | collective-permute-done | bytes 262176 | tf_op jit(solution)/shard_map/ppermute | solution.py:49
  95.1 5.6 %collective-permute-done.10 = f32[4,128,128]{2,1,0:T(8,128)S(1)} collective-permute-done((f32[4,128,128]{2,1,0:T(8,128)S(1)}, f32[4,128,128]{2,1,0:T(8,128)S(1)}, u32[]{:S(2)}, u32[]{:S(2)}) %collective-permute-start.10) | collective-permute-done | bytes 262176 | tf_op jit(solution)/shard_map/ppermute | solution.py:49
  100.7 1.4 collective-permute-done.11
  102.2 2.0 %fusion.3 = (f32[4,128,128]{2,1,0:T(8,128)S(1)}, f32[4,128,128]{2,1,0:T(8,128)S(1)}) fusion(f32[4,4,128,128]{3,2,1,0:T(8,128)S(1)} %bitcast_dynamic-update-slice_fusion.3, f32[]{:T(128)} %bitcast.44, f32[]{:T(128)} %bitcast.38, f32[]{:T(128)S(6)} %mul.260, f32[]{:T(128)} %bitcast.40), kind=kLoop, calls=%fused_computation.13 | loop fusion | flops 458752 | bytes 1572880 | tf_op jit(solution)/shard_map/add | solution.py:70
  104.2 1.3 collective-permute-start.14
  105.5 1.3 collective-permute-start.12
  106.8 1.3 collective-permute-start.13
  110.6 0.7 fusion.16
  112.6 8.0 %collective-permute-done.14 = f32[4,128,128]{2,1,0:T(8,128)S(1)} collective-permute-done((f32[4,128,128]{2,1,0:T(8,128)S(1)}, f32[4,128,128]{2,1,0:T(8,128)S(1)}, u32[]{:S(2)}, u32[]{:S(2)}) %collective-permute-start.14) | collective-permute-done | bytes 262176 | tf_op jit(solution)/shard_map/ppermute | solution.py:78
  120.6 4.1 %collective-permute-done.12 = f32[4,128,128]{2,1,0:T(8,128)S(1)} collective-permute-done((f32[4,128,128]{2,1,0:T(8,128)S(1)}, f32[4,128,128]{2,1,0:T(8,128)S(1)}, u32[]{:S(2)}, u32[]{:S(2)}) %collective-permute-start.12) | collective-permute-done | bytes 262176 | tf_op jit(solution)/shard_map/ppermute | solution.py:78
  124.6 12.1 %collective-permute-done.13 = f32[4,128,128]{2,1,0:T(8,128)S(1)} collective-permute-done((f32[4,128,128]{2,1,0:T(8,128)S(1)}, f32[4,128,128]{2,1,0:T(8,128)S(1)}, u32[]{:S(2)}, u32[]{:S(2)}) %collective-permute-start.13) | collective-permute-done | bytes 262176 | tf_op jit(solution)/shard_map/ppermute | solution.py:78
  136.8 1.4 add_bitcast_fusion.2
  139.0 1.0 collective-permute-start.15
  140.0 1.2 collective-permute-start.16
  141.9 11.6 %shard_map.87 = (bf16[384,2048]{1,0:T(8,128)(2,1)}, f32[384,2048]{1,0:T(8,128)}, f32[384,2048]{1,0:T(8,128)}) custom-call(bf16[384,2048]{1,0:T(8,128)(2,1)} %query_ref.7, bf16[384,2048]{1,0:T(8,128)(2,1)} %key_ref.7, bf16[384,2048]{1,0:T(8,128)(2,1)} %value_ref.7, bf16[384,2048]{1,0:T(8,128)(2,1)} %get-tuple-element.43.grad_ref, ...), custom_call_target="tpu_custom_call" | custom-call | tf_op jit(solution)/shard_map/pallas_call | solution.py:129
  153.6 5.7 %collective-permute-done.17 = f32[4,128,128]{2,1,0:T(8,128)S(1)} collective-permute-done((f32[4,128,128]{2,1,0:T(8,128)S(1)}, f32[4,128,128]{2,1,0:T(8,128)S(1)}, u32[]{:S(2)}, u32[]{:S(2)}) %collective-permute-start.17) | collective-permute-done | bytes 262176 | tf_op jit(solution)/shard_map/ppermute | solution.py:49
  159.3 0.9 multiply_convert_fusion
  160.2 6.9 %shard_map.89 = (bf16[384,2048]{1,0:T(8,128)(2,1)}, bf16[384,2048]{1,0:T(8,128)(2,1)}) custom-call(bf16[384,2048]{1,0:T(8,128)(2,1)} %key_ref.7, bf16[384,2048]{1,0:T(8,128)(2,1)} %value_ref.7, f32[384,2048]{1,0:T(8,128)} %get-tuple-element.14.key_part, f32[384,2048]{1,0:T(8,128)} %get-tuple-element.15.value_part, bf16[16,128,128]{2,1,0:T(8,128)(2,1)} %bitcast.134, ...), custom_call_target="tpu_custom_call" | custom-call | tf_op jit(solution)/shard_map/pallas_call | solution.py:129
  (57 shorter events, 7.8 us)
Async XLA Ops:
  12.2 8.1 %collective-permute-start = (f32[4,128,128]{2,1,0:T(8,128)S(1)}, f32[4,128,128]{2,1,0:T(8,128)S(1)}, u32[]{:S(2)}, u32[]{:S(2)}) collective-permute-start(f32[4,128,128]{2,1,0:T(8,128)S(1)} %get-tuple-element.59), channel_id=1, source_target_pairs={{0,1},{1,2},{2,3},{3,0},{4,5},{5,6},{6,7},{7,4},{8,9},{9,10},{10,1... | collective-permute-start | bytes 786440 | tf_op jit(solution)/shard_map/ppermute | solution.py:49
  14.9 11.1 %collective-permute-start.1 = (f32[4,128,128]{2,1,0:T(8,128)S(1)}, f32[4,128,128]{2,1,0:T(8,128)S(1)}, u32[]{:S(2)}, u32[]{:S(2)}) collective-permute-start(f32[4,128,128]{2,1,0:T(8,128)S(1)} %get-tuple-element.58), channel_id=1, source_target_pairs={{0,2},{1,3},{2,0},{3,1},{4,6},{5,7},{6,4},{7,5},{8,10},{9,11},{10,... | collective-permute-start | bytes 786440 | tf_op jit(solution)/shard_map/ppermute | solution.py:49
  14.9 11.6 %collective-permute-start.2 = (f32[4,128,128]{2,1,0:T(8,128)S(1)}, f32[4,128,128]{2,1,0:T(8,128)S(1)}, u32[]{:S(2)}, u32[]{:S(2)}) collective-permute-start(f32[4,128,128]{2,1,0:T(8,128)S(1)} %get-tuple-element.57), channel_id=1, source_target_pairs={{0,3},{1,0},{2,1},{3,2},{4,7},{5,4},{6,5},{7,6},{8,11},{9,8},{10,9... | collective-permute-start | bytes 786440 | tf_op jit(solution)/shard_map/ppermute | solution.py:49
  28.6 14.2 %collective-permute-start.5 = (f32[4,128,128]{2,1,0:T(8,128)S(1)}, f32[4,128,128]{2,1,0:T(8,128)S(1)}, u32[]{:S(2)}, u32[]{:S(2)}) collective-permute-start(f32[4,128,128]{2,1,0:T(8,128)S(1)} %get-tuple-element.41), channel_id=1, source_target_pairs={{0,12},{1,13},{2,14},{3,15},{16,28},{17,29},{18,30},{19,31}} | collective-permute-start | bytes 786440 | tf_op jit(solution)/shard_map/ppermute | solution.py:78
  34.6 11.6 %collective-permute-start.3 = (f32[4,128,128]{2,1,0:T(8,128)S(1)}, f32[4,128,128]{2,1,0:T(8,128)S(1)}, u32[]{:S(2)}, u32[]{:S(2)}) collective-permute-start(f32[4,128,128]{2,1,0:T(8,128)S(1)} %get-tuple-element.41), channel_id=1, source_target_pairs={{0,4},{1,5},{2,6},{3,7},{4,8},{5,9},{6,10},{7,11},{8,12},{9,13},{1... | collective-permute-start | bytes 786440 | tf_op jit(solution)/shard_map/ppermute | solution.py:78
  35.9 15.9 %collective-permute-start.4 = (f32[4,128,128]{2,1,0:T(8,128)S(1)}, f32[4,128,128]{2,1,0:T(8,128)S(1)}, u32[]{:S(2)}, u32[]{:S(2)}) collective-permute-start(f32[4,128,128]{2,1,0:T(8,128)S(1)} %get-tuple-element.41), channel_id=1, source_target_pairs={{0,8},{1,9},{2,10},{3,11},{4,12},{5,13},{6,14},{7,15},{16,24},{17,... | collective-permute-start | bytes 786440 | tf_op jit(solution)/shard_map/ppermute | solution.py:78
  54.2 11.7 %collective-permute-start.6 = (f32[4,128,128]{2,1,0:T(8,128)S(1)}, f32[4,128,128]{2,1,0:T(8,128)S(1)}, u32[]{:S(2)}, u32[]{:S(2)}) collective-permute-start(f32[4,128,128]{2,1,0:T(8,128)S(1)} %get-tuple-element.55), channel_id=1, source_target_pairs={{0,1},{1,2},{2,3},{3,0},{4,5},{5,6},{6,7},{7,4},{8,9},{9,10},{10,1... | collective-permute-start | bytes 786440 | tf_op jit(solution)/shard_map/ppermute | solution.py:49
  55.3 10.6 %collective-permute-start.7 = (f32[4,128,128]{2,1,0:T(8,128)S(1)}, f32[4,128,128]{2,1,0:T(8,128)S(1)}, u32[]{:S(2)}, u32[]{:S(2)}) collective-permute-start(f32[4,128,128]{2,1,0:T(8,128)S(1)} %get-tuple-element.54), channel_id=1, source_target_pairs={{0,2},{1,3},{2,0},{3,1},{4,6},{5,7},{6,4},{7,5},{8,10},{9,11},{10,... | collective-permute-start | bytes 786440 | tf_op jit(solution)/shard_map/ppermute | solution.py:49
  65.9 5.8 %collective-permute-start.8 = (f32[4,128,128]{2,1,0:T(8,128)S(1)}, f32[4,128,128]{2,1,0:T(8,128)S(1)}, u32[]{:S(2)}, u32[]{:S(2)}) collective-permute-start(f32[4,128,128]{2,1,0:T(8,128)S(1)} %get-tuple-element.53), channel_id=1, source_target_pairs={{0,3},{1,0},{2,1},{3,2},{4,7},{5,4},{6,5},{7,6},{8,11},{9,8},{10,9... | collective-permute-start | bytes 786440 | tf_op jit(solution)/shard_map/ppermute | solution.py:49
  72.6 7.8 %copy-start.1 = (bf16[384,2048]{1,0:T(8,128)(2,1)S(1)}, bf16[384,2048]{1,0:T(8,128)(2,1)}, u32[]{:S(2)}) copy-start(bf16[384,2048]{1,0:T(8,128)(2,1)} %param.9) | copy-start | bytes 4718596
  78.1 2.8 %copy-start = (f32[384,2048]{1,0:T(8,128)S(1)}, f32[384,2048]{1,0:T(8,128)}, u32[]{:S(2)}) copy-start(f32[384,2048]{1,0:T(8,128)} %shard_map.86) | copy-start | bytes 9437188
  89.9 5.2 %collective-permute-start.9 = (f32[4,128,128]{2,1,0:T(8,128)S(1)}, f32[4,128,128]{2,1,0:T(8,128)S(1)}, u32[]{:S(2)}, u32[]{:S(2)}) collective-permute-start(f32[4,128,128]{2,1,0:T(8,128)S(1)} %get-tuple-element.51), channel_id=1, source_target_pairs={{0,1},{1,2},{2,3},{3,0},{4,5},{5,6},{6,7},{7,4},{8,9},{9,10},{10,1... | collective-permute-start | bytes 786440 | tf_op jit(solution)/shard_map/ppermute | solution.py:49
  90.0 10.8 %collective-permute-start.10 = (f32[4,128,128]{2,1,0:T(8,128)S(1)}, f32[4,128,128]{2,1,0:T(8,128)S(1)}, u32[]{:S(2)}, u32[]{:S(2)}) collective-permute-start(f32[4,128,128]{2,1,0:T(8,128)S(1)} %get-tuple-element.50), channel_id=1, source_target_pairs={{0,2},{1,3},{2,0},{3,1},{4,6},{5,7},{6,4},{7,5},{8,10},{9,11},{10,... | collective-permute-start | bytes 786440 | tf_op jit(solution)/shard_map/ppermute | solution.py:49
  91.3 10.9 %collective-permute-start.11 = (f32[4,128,128]{2,1,0:T(8,128)S(1)}, f32[4,128,128]{2,1,0:T(8,128)S(1)}, u32[]{:S(2)}, u32[]{:S(2)}) collective-permute-start(f32[4,128,128]{2,1,0:T(8,128)S(1)} %get-tuple-element.49), channel_id=1, source_target_pairs={{0,3},{1,0},{2,1},{3,2},{4,7},{5,4},{6,5},{7,6},{8,11},{9,8},{10,9... | collective-permute-start | bytes 786440 | tf_op jit(solution)/shard_map/ppermute | solution.py:49
  104.2 16.4 %collective-permute-start.14 = (f32[4,128,128]{2,1,0:T(8,128)S(1)}, f32[4,128,128]{2,1,0:T(8,128)S(1)}, u32[]{:S(2)}, u32[]{:S(2)}) collective-permute-start(f32[4,128,128]{2,1,0:T(8,128)S(1)} %get-tuple-element.36), channel_id=1, source_target_pairs={{12,0},{13,1},{14,2},{15,3},{28,16},{29,17},{30,18},{31,19}} | collective-permute-start | bytes 786440 | tf_op jit(solution)/shard_map/ppermute | solution.py:78
  105.5 19.2 %collective-permute-start.12 = (f32[4,128,128]{2,1,0:T(8,128)S(1)}, f32[4,128,128]{2,1,0:T(8,128)S(1)}, u32[]{:S(2)}, u32[]{:S(2)}) collective-permute-start(f32[4,128,128]{2,1,0:T(8,128)S(1)} %get-tuple-element.36), channel_id=1, source_target_pairs={{4,0},{5,1},{6,2},{7,3},{8,4},{9,5},{10,6},{11,7},{12,8},{13,9},{1... | collective-permute-start | bytes 786440 | tf_op jit(solution)/shard_map/ppermute | solution.py:78
  106.8 30.0 %collective-permute-start.13 = (f32[4,128,128]{2,1,0:T(8,128)S(1)}, f32[4,128,128]{2,1,0:T(8,128)S(1)}, u32[]{:S(2)}, u32[]{:S(2)}) collective-permute-start(f32[4,128,128]{2,1,0:T(8,128)S(1)} %get-tuple-element.36), channel_id=1, source_target_pairs={{8,0},{9,1},{10,2},{11,3},{12,4},{13,5},{14,6},{15,7},{24,16},{25,... | collective-permute-start | bytes 786440 | tf_op jit(solution)/shard_map/ppermute | solution.py:78
  139.0 14.5 %collective-permute-start.15 = (f32[4,128,128]{2,1,0:T(8,128)S(1)}, f32[4,128,128]{2,1,0:T(8,128)S(1)}, u32[]{:S(2)}, u32[]{:S(2)}) collective-permute-start(f32[4,128,128]{2,1,0:T(8,128)S(1)} %get-tuple-element.47), channel_id=1, source_target_pairs={{0,1},{1,2},{2,3},{3,0},{4,5},{5,6},{6,7},{7,4},{8,9},{9,10},{10,1... | collective-permute-start | bytes 786440 | tf_op jit(solution)/shard_map/ppermute | solution.py:49
  140.0 13.5 %collective-permute-start.16 = (f32[4,128,128]{2,1,0:T(8,128)S(1)}, f32[4,128,128]{2,1,0:T(8,128)S(1)}, u32[]{:S(2)}, u32[]{:S(2)}) collective-permute-start(f32[4,128,128]{2,1,0:T(8,128)S(1)} %get-tuple-element.46), channel_id=1, source_target_pairs={{0,2},{1,3},{2,0},{3,1},{4,6},{5,7},{6,4},{7,5},{8,10},{9,11},{10,... | collective-permute-start | bytes 786440 | tf_op jit(solution)/shard_map/ppermute | solution.py:49
  153.5 5.8 %collective-permute-start.17 = (f32[4,128,128]{2,1,0:T(8,128)S(1)}, f32[4,128,128]{2,1,0:T(8,128)S(1)}, u32[]{:S(2)}, u32[]{:S(2)}) collective-permute-start(f32[4,128,128]{2,1,0:T(8,128)S(1)} %get-tuple-element.45), channel_id=1, source_target_pairs={{0,3},{1,0},{2,1},{3,2},{4,7},{5,4},{6,5},{7,6},{8,11},{9,8},{10,9... | collective-permute-start | bytes 786440 | tf_op jit(solution)/shard_map/ppermute | solution.py:49

commit v7 on v6

--- a/solution.py
+++ b/solution.py
@@ -53,7 +53,7 @@
     return placed
 
 
-def row_scan(state, keep_of, direction):
+def row_scan(state, keep_of, direction, filler, filler_inputs):
     keep_row = keep_of((lax.axis_index("seq") // GROUP) * GROUP + lax.iota(jnp.int32, GROUP))
     count = lax.axis_size("seq")
     heads = state.shape[0]
@@ -72,14 +72,20 @@
     row = lax.axis_index("seq") // GROUP
     entering = jnp.zeros_like(total)
     weight = jnp.ones((), jnp.float32)
+    total, filler_inputs = lax.optimization_barrier((total, filler_inputs))
+    received = []
     for reach in range(1, -(-SPAN // GROUP) + 1):
         shift = GROUP * direction * reach
         pairs = [(source, source + shift) for source in range(count) if 0 <= source + shift < count]
-        entering = entering + weight * lax.ppermute(total, "seq", pairs)
+        received.append(lax.ppermute(total, "seq", pairs))
+    filled = filler(*filler_inputs)
+    received, filled = lax.optimization_barrier((received, filled))
+    for reach in range(1, -(-SPAN // GROUP) + 1):
+        entering = entering + weight * received[reach - 1]
         other = (row - direction * reach) * GROUP + lax.iota(jnp.int32, GROUP)
         weight = weight * jnp.prod(keep_of(other))
     scanned = jnp.stack([inner[index] + inner_keep[index] * entering for index in range(GROUP)])
-    return member_exchange(scanned, "seq").reshape(state.shape)
+    return member_exchange(scanned, "seq").reshape(state.shape), filled
 
 
 def block_flags(starts, blocks, row_count):
@@ -94,14 +100,10 @@
     return has_start, stops_back
 
 
-def scan_states(state, keep_of, fallback_flag, direction):
-    heads = state.shape[0]
-    if lax.axis_size("seq") % GROUP == 0 and heads % (GROUP * CHUNKS) == 0:
-        size = heads // CHUNKS
-        return jnp.concatenate(
-            [row_scan(state[i * size:(i + 1) * size], keep_of, direction) for i in range(CHUNKS)]
-        )
-    return windowed_prefix((state, fallback_flag), direction)[0]
+def scan_states(state, keep_of, fallback_flag, direction, filler, filler_inputs):
+    if lax.axis_size("seq") % GROUP == 0 and state.shape[0] % GROUP == 0:
+        return row_scan(state, keep_of, direction, filler, filler_inputs)
+    return windowed_prefix((state, fallback_flag), direction)[0], filler(*filler_inputs)
 
 
 HEAD_STEP = 4
@@ -216,10 +218,6 @@
     wide = jax.ShapeDtypeStruct((row_count, feat_width), f32)
     low = jax.ShapeDtypeStruct((row_count, feat_width), jnp.bfloat16)
     (state_local,) = head_call(state_body, [keys, values, tail], [state_shape])
-    weights, inside = head_call(
-        inside_body, [queries, keys, values, keep],
-        [jax.ShapeDtypeStruct((head_count, row_count, row_count), jnp.bfloat16), wide],
-    )
     start_flag = has_start.astype(f32).reshape(1, 1, 1)
 
     def start_keep(blocks):
@@ -228,7 +226,12 @@
     def stop_keep(blocks):
         return 1.0 - block_flags(starts, blocks, row_count)[1].astype(f32)
 
-    prefix = scan_states(state_local, start_keep, start_flag, 1)
+    weight_shape = jax.ShapeDtypeStruct((head_count, row_count, row_count), jnp.bfloat16)
+    prefix, (weights, inside) = scan_states(
+        state_local, start_keep, start_flag, 1,
+        lambda *xs: head_call(inside_body, list(xs), [weight_shape, wide]),
+        (queries, keys, values, keep),
+    )
     prefix_low = (prefix * continues.astype(f32)).astype(jnp.bfloat16)
     (mixed,) = head_call(mixed_body, [queries, inside, prefix_low, carry], [wide])
     rms_value = jnp.sqrt(jnp.mean(mixed * mixed, axis=1, keepdims=True) + 1e-05)
@@ -239,13 +242,14 @@
     grad_low = grad_mix.astype(jnp.bfloat16)
     (grad_local,) = head_call(local_body, [queries, grad_low, carry], [state_shape])
     back_flag = stops_back.astype(f32).reshape(1, 1, 1)
-    suffix = scan_states(grad_local, stop_keep, back_flag, -1)
+    suffix, (grad_queries, keys_part, values_part) = scan_states(
+        grad_local, stop_keep, back_flag, -1,
+        lambda *xs: head_call(grad_body, list(xs), [low, wide, wide]),
+        (queries, keys, values, grad_low, weights, prefix_low, keep, carry),
+    )
     next_first = first_row + row_count
     next_open = (next_first < lax.axis_size("seq") * row_count) & jnp.logical_not(jnp.any(starts == next_first))
     suffix_low = (suffix * next_open.astype(f32)).astype(jnp.bfloat16)
-    grad_queries, keys_part, values_part = head_call(
-        grad_body, [queries, keys, values, grad_low, weights, prefix_low, keep, carry], [low, wide, wide]
-    )
     grad_keys, grad_values = head_call(
         tail_body, [keys, values, keys_part, values_part, suffix_low, tail], [low, low]
     )

time: 168 us -> 157 us (0.935)
  waiting for transfers between devices: 64.2 us -> 51.8 us
    ppermute x6, waiting for transfers between devices: 33.3 us -> 11.2 us  [row_scan(): received.append(lax.ppermute(total, 'seq', pairs))]
    ppermute x12, waiting for transfers between devices: 31 us -> 40.6 us  [member_exchange(): got.append(lax.ppermute(piece, axis, pairs))]
  transfers between devices with their start and end apart: 18 -> 18, of which waited for: 13 -> 13; matrix products, arithmetic and copies ran while one was open for 4% -> 5% of each run, Pallas kernels for 12% -> 12%
where the time goes in v7:
time: 157 us; the launch traced here: 156 us
  waiting for transfers between devices  51.8 us (33%)
  Pallas kernels  40.7 us (26%)
  other arithmetic  23 us (15%)
  starting transfers between devices  22.4 us (14%)
  between operations  10.1 us (6%)
  local copies, waits for them, and re-layouts  8.09 us (5%)
    pallas_call x6, Pallas kernels, head_call(): pl.pallas_call(body, grid=(heads // HEAD_STEP,), in_specs=[spec(x.shape)...  40.7 us
    ppermute x12, waiting for transfers between devices, member_exchange(): got.append(lax.ppermute(piece, axis, pairs))  40.6 us
    ppermute x6, starting transfers between devices, row_scan(): received.append(lax.ppermute(total, 'seq', pairs))  13.4 us
    ppermute x6, waiting for transfers between devices, row_scan(): received.append(lax.ppermute(total, 'seq', pairs))  11.2 us
    ppermute x12, starting transfers between devices, member_exchange(): got.append(lax.ppermute(piece, axis, pairs))  8.97 us
    another operation x6, other arithmetic, row_scan(): jnp.stack([inner[index] + inner_keep[index] * entering for index in range...  4.23 us
    add x2, other arithmetic, row_scan(): total = mine[index] + keep_row[index] * total  3.93 us
  transfers between devices with their start and end apart: 18, of which 13 were waited for; matrix products, arithmetic and copies ran while one was open for 5% of the time, Pallas kernels for 12%

profile of v7, /device:TPU:1, one launch (start us, length us, event | category | flops | bytes accessed | tf_op | source)
XLA Modules:
  0.0 156.1 jit_solution(17552766711774554522)
XLA Ops:
  0.7 0.8 reduce-window.9
  1.6 1.4 compare_reduce_fusion
  4.2 1.3 and_convert_fusion.1
  5.6 0.8 reshape.154.tail_ref
  6.3 4.5 %shard_map.84 = f32[16,128,128]{2,1,0:T(8,128)} custom-call(bf16[384,2048]{1,0:T(8,128)(2,1)} %key_ref.5, bf16[384,2048]{1,0:T(8,128)(2,1)} %value_ref.5, f32[384,1]{1,0:T(8,128)} %reshape.154.tail_ref), custom_call_target="tpu_custom_call" | custom-call | tf_op jit(solution)/shard_map/pallas_call | solution.py:131
  11.0 1.3 dynamic-slice_bitcast_fusion.9
  12.3 2.6 %collective-permute-start = (f32[4,128,128]{2,1,0:T(8,128)S(1)}, f32[4,128,128]{2,1,0:T(8,128)S(1)}, u32[]{:S(2)}, u32[]{:S(2)}) collective-permute-start(f32[4,128,128]{2,1,0:T(8,128)S(1)} %get-tuple-element.109), channel_id=1, source_target_pairs={{0,1},{1,2},{2,3},{3,0},{4,5},{5,6},{6,7},{7,4},{8,9},{9,10},{10,1... | collective-permute-start | bytes 786440 | tf_op jit(solution)/shard_map/ppermute | solution.py:49
  15.4 1.0 and_convert_fusion.keep_ref
  18.0 2.4 %collective-permute-done = f32[4,128,128]{2,1,0:T(8,128)S(1)} collective-permute-done((f32[4,128,128]{2,1,0:T(8,128)S(1)}, f32[4,128,128]{2,1,0:T(8,128)S(1)}, u32[]{:S(2)}, u32[]{:S(2)}) %collective-permute-start) | collective-permute-done | bytes 262176 | tf_op jit(solution)/shard_map/ppermute | solution.py:49
  20.4 5.6 %collective-permute-done.1 = f32[4,128,128]{2,1,0:T(8,128)S(1)} collective-permute-done((f32[4,128,128]{2,1,0:T(8,128)S(1)}, f32[4,128,128]{2,1,0:T(8,128)S(1)}, u32[]{:S(2)}, u32[]{:S(2)}) %collective-permute-start.1) | collective-permute-done | bytes 262176 | tf_op jit(solution)/shard_map/ppermute | solution.py:49
  26.6 2.0 %fusion.10 = (f32[4,128,128]{2,1,0:T(8,128)S(1)}, f32[4,128,128]{2,1,0:T(8,128)S(1)}) fusion(f32[4,4,128,128]{3,2,1,0:T(8,128)S(1)} %bitcast_dynamic-update-slice_fusion.9, f32[]{:T(128)} %bitcast.11, f32[]{:T(128)} %bitcast.13, f32[]{:T(128)S(6)} %mul.230, f32[]{:T(128)} %bitcast.15), kind=kLoop, calls=%fused_computation.27 | loop fusion | flops 458752 | bytes 1572880 | tf_op jit(solution)/shard_map/add | solution.py:70
  28.6 4.0 %collective-permute-start.3 = (f32[4,128,128]{2,1,0:T(8,128)S(1)}, f32[4,128,128]{2,1,0:T(8,128)S(1)}, u32[]{:S(2)}, u32[]{:S(2)}) collective-permute-start(f32[4,128,128]{2,1,0:T(8,128)S(1)} %get-tuple-element.36), channel_id=1, source_target_pairs={{0,4},{1,5},{2,6},{3,7},{4,8},{5,9},{6,10},{7,11},{8,12},{9,13},{1... | collective-permute-start | bytes 786440 | tf_op jit(solution)/shard_map/ppermute | solution.py:80
  32.6 4.2 %collective-permute-start.4 = (f32[4,128,128]{2,1,0:T(8,128)S(1)}, f32[4,128,128]{2,1,0:T(8,128)S(1)}, u32[]{:S(2)}, u32[]{:S(2)}) collective-permute-start(f32[4,128,128]{2,1,0:T(8,128)S(1)} %get-tuple-element.36), channel_id=1, source_target_pairs={{0,8},{1,9},{2,10},{3,11},{4,12},{5,13},{6,14},{7,15},{16,24},{17,... | collective-permute-start | bytes 786440 | tf_op jit(solution)/shard_map/ppermute | solution.py:80
  36.8 1.3 collective-permute-start.5
  42.7 7.7 %shard_map.85 = (bf16[16,384,384]{2,1,0:T(8,128)(2,1)}, f32[384,2048]{1,0:T(8,128)}) custom-call(bf16[384,2048]{1,0:T(8,128)(2,1)} %query_ref.5, bf16[384,2048]{1,0:T(8,128)(2,1)} %key_ref.5, bf16[384,2048]{1,0:T(8,128)(2,1)} %value_ref.5, f32[384,384]{1,0:T(8,128)} %and_convert_fusion.keep_ref), custom_call_target="tpu_custom_call" | custom-call | tf_op jit(solution)/shard_map/pallas_call | solution.py:131
  50.4 1.4 add_bitcast_fusion.5
  51.8 0.7 add_bitcast_fusion.4
  53.2 1.2 collective-permute-start.7
  54.7 0.8 copy.15.carry_ref
  55.9 1.7 %collective-permute-done.6 = f32[4,128,128]{2,1,0:T(8,128)S(1)} collective-permute-done((f32[4,128,128]{2,1,0:T(8,128)S(1)}, f32[4,128,128]{2,1,0:T(8,128)S(1)}, u32[]{:S(2)}, u32[]{:S(2)}) %collective-permute-start.6) | collective-permute-done | bytes 262176 | tf_op jit(solution)/shard_map/ppermute | solution.py:49
  57.6 8.2 %collective-permute-done.7 = f32[4,128,128]{2,1,0:T(8,128)S(1)} collective-permute-done((f32[4,128,128]{2,1,0:T(8,128)S(1)}, f32[4,128,128]{2,1,0:T(8,128)S(1)}, u32[]{:S(2)}, u32[]{:S(2)}) %collective-permute-start.7) | collective-permute-done | bytes 262176 | tf_op jit(solution)/shard_map/ppermute | solution.py:49
  65.8 0.8 collective-permute-done.8
  66.6 0.9 multiply_convert_fusion.1
  67.6 5.5 %shard_map.86 = f32[384,2048]{1,0:T(8,128)} custom-call(bf16[384,2048]{1,0:T(8,128)(2,1)} %query_ref.5, f32[384,2048]{1,0:T(8,128)} %get-tuple-element.43.inside_ref, bf16[16,128,128]{2,1,0:T(8,128)(2,1)} %bitcast.128, f32[384,1]{1,0:T(8,128)} %copy.15.carry_ref), custom_call_target="tpu_custom_call" | custom-call | tf_op jit(solution)/shard_map/pallas_call | solution.py:131
  73.0 2.3 %multiply_reduce_fusion = f32[384]{0:T(512)S(1)} fusion(f32[384,2048]{1,0:T(8,128)} %shard_map.86), kind=kLoop, calls=%fused_computation.5 | loop fusion | flops 1572480 | bytes 3147264 | tf_op jit(solution)/shard_map/reduce_sum | solution.py:237
  76.5 2.4 %fusion.2 = (bf16[384,2048]{1,0:T(8,128)(2,1)}, bf16[384,2048]{1,0:T(8,128)(2,1)}) fusion(bf16[384,2048]{1,0:T(8,128)(2,1)S(1)} %copy-done.1, f32[384]{0:T(512)S(1)} %broadcast_multiply_fusion, f32[384]{0:T(512)S(1)} %add_sqrt_fusion, f32[384,2048]{1,0:T(8,128)S(1)} %copy-done), kind=kLoop, calls=%fused_computation.4 | loop fusion | flops 5505024 | bytes 7867392 | tf_op jit(solution)/shard_map/convert_element_type | solution.py:242
  78.9 4.6 %shard_map.87 = f32[16,128,128]{2,1,0:T(8,128)} custom-call(bf16[384,2048]{1,0:T(8,128)(2,1)} %query_ref.5, bf16[384,2048]{1,0:T(8,128)(2,1)} %get-tuple-element.52.grad_ref, f32[384,1]{1,0:T(8,128)} %copy.15.carry_ref), custom_call_target="tpu_custom_call" | custom-call | tf_op jit(solution)/shard_map/pallas_call | solution.py:131
  83.5 1.3 dynamic-slice_bitcast_fusion.3
  85.2 0.6 fusion.22
  86.6 0.8 collective-permute-start.11
  87.3 2.5 %collective-permute-done.9 = f32[4,128,128]{2,1,0:T(8,128)S(1)} collective-permute-done((f32[4,128,128]{2,1,0:T(8,128)S(1)}, f32[4,128,128]{2,1,0:T(8,128)S(1)}, u32[]{:S(2)}, u32[]{:S(2)}) %collective-permute-start.9) | collective-permute-done | bytes 262176 | tf_op jit(solution)/shard_map/ppermute | solution.py:49
  89.8 5.6 %collective-permute-done.10 = f32[4,128,128]{2,1,0:T(8,128)S(1)} collective-permute-done((f32[4,128,128]{2,1,0:T(8,128)S(1)}, f32[4,128,128]{2,1,0:T(8,128)S(1)}, u32[]{:S(2)}, u32[]{:S(2)}) %collective-permute-start.10) | collective-permute-done | bytes 262176 | tf_op jit(solution)/shard_map/ppermute | solution.py:49
  95.4 1.9 %collective-permute-done.11 = f32[4,128,128]{2,1,0:T(8,128)S(1)} collective-permute-done((f32[4,128,128]{2,1,0:T(8,128)S(1)}, f32[4,128,128]{2,1,0:T(8,128)S(1)}, u32[]{:S(2)}, u32[]{:S(2)}) %collective-permute-start.11) | collective-permute-done | bytes 262176 | tf_op jit(solution)/shard_map/ppermute | solution.py:49
  97.4 1.9 %fusion.6 = (f32[4,128,128]{2,1,0:T(8,128)S(1)}, f32[4,128,128]{2,1,0:T(8,128)S(1)}) fusion(f32[4,4,128,128]{3,2,1,0:T(8,128)S(1)} %bitcast_dynamic-update-slice_fusion.3, f32[]{:T(128)} %bitcast.38, f32[]{:T(128)} %bitcast.40, f32[]{:T(128)S(6)} %mul.261, f32[]{:T(128)} %bitcast.42), kind=kLoop, calls=%fused_computation.19 | loop fusion | flops 458752 | bytes 1572880 | tf_op jit(solution)/shard_map/add | solution.py:70
  99.3 1.3 collective-permute-start.12
  100.6 1.3 collective-permute-start.13
  101.9 1.3 collective-permute-start.14
  105.7 0.6 fusion.17
  107.6 0.8 copy.17.carry_ref
  108.4 11.6 %shard_map.88 = (bf16[384,2048]{1,0:T(8,128)(2,1)}, f32[384,2048]{1,0:T(8,128)}, f32[384,2048]{1,0:T(8,128)}) custom-call(bf16[384,2048]{1,0:T(8,128)(2,1)} %query_ref.5, bf16[384,2048]{1,0:T(8,128)(2,1)} %key_ref.5, bf16[384,2048]{1,0:T(8,128)(2,1)} %value_ref.5, bf16[384,2048]{1,0:T(8,128)(2,1)} %get-tuple-element.52.grad_ref, ...), custom_call_target="tpu_custom_call" | custom-call | tf_op jit(solution)/shard_map/pallas_call | solution.py:131
  120.0 11.2 %collective-permute-done.13 = f32[4,128,128]{2,1,0:T(8,128)S(1)} collective-permute-done((f32[4,128,128]{2,1,0:T(8,128)S(1)}, f32[4,128,128]{2,1,0:T(8,128)S(1)}, u32[]{:S(2)}, u32[]{:S(2)}) %collective-permute-start.13) | collective-permute-done | bytes 262176 | tf_op jit(solution)/shard_map/ppermute | solution.py:80
  131.2 1.3 add_bitcast_fusion.2
  132.5 0.7 add_bitcast_fusion.1
  133.6 2.5 %collective-permute-start.16 = (f32[4,128,128]{2,1,0:T(8,128)S(1)}, f32[4,128,128]{2,1,0:T(8,128)S(1)}, u32[]{:S(2)}, u32[]{:S(2)}) collective-permute-start(f32[4,128,128]{2,1,0:T(8,128)S(1)} %get-tuple-element.96), channel_id=1, source_target_pairs={{0,2},{1,3},{2,0},{3,1},{4,6},{5,7},{6,4},{7,5},{8,10},{9,11},{10,... | collective-permute-start | bytes 786440 | tf_op jit(solution)/shard_map/ppermute | solution.py:49
  136.8 1.1 collective-permute-done.15
  137.9 9.7 %collective-permute-done.16 = f32[4,128,128]{2,1,0:T(8,128)S(1)} collective-permute-done((f32[4,128,128]{2,1,0:T(8,128)S(1)}, f32[4,128,128]{2,1,0:T(8,128)S(1)}, u32[]{:S(2)}, u32[]{:S(2)}) %collective-permute-start.16) | collective-permute-done | bytes 262176 | tf_op jit(solution)/shard_map/ppermute | solution.py:49
  148.3 0.9 multiply_convert_fusion
  149.2 6.9 %shard_map.89 = (bf16[384,2048]{1,0:T(8,128)(2,1)}, bf16[384,2048]{1,0:T(8,128)(2,1)}) custom-call(bf16[384,2048]{1,0:T(8,128)(2,1)} %key_ref.5, bf16[384,2048]{1,0:T(8,128)(2,1)} %value_ref.5, f32[384,2048]{1,0:T(8,128)} %get-tuple-element.61.key_part, f32[384,2048]{1,0:T(8,128)} %get-tuple-element.62.value_part, bf16[16,128,128]{2,1,0:T(8,128)(2,1)} %bitcast.134, ...), custom_call_target="tpu_custom_call" | custom-call | tf_op jit(solution)/shard_map/pallas_call | solution.py:131
  (59 shorter events, 8.9 us)
Async XLA Ops:
  12.3 8.1 %collective-permute-start = (f32[4,128,128]{2,1,0:T(8,128)S(1)}, f32[4,128,128]{2,1,0:T(8,128)S(1)}, u32[]{:S(2)}, u32[]{:S(2)}) collective-permute-start(f32[4,128,128]{2,1,0:T(8,128)S(1)} %get-tuple-element.109), channel_id=1, source_target_pairs={{0,1},{1,2},{2,3},{3,0},{4,5},{5,6},{6,7},{7,4},{8,9},{9,10},{10,1... | collective-permute-start | bytes 786440 | tf_op jit(solution)/shard_map/ppermute | solution.py:49
  14.9 11.1 %collective-permute-start.1 = (f32[4,128,128]{2,1,0:T(8,128)S(1)}, f32[4,128,128]{2,1,0:T(8,128)S(1)}, u32[]{:S(2)}, u32[]{:S(2)}) collective-permute-start(f32[4,128,128]{2,1,0:T(8,128)S(1)} %get-tuple-element.108), channel_id=1, source_target_pairs={{0,2},{1,3},{2,0},{3,1},{4,6},{5,7},{6,4},{7,5},{8,10},{9,11},{10,... | collective-permute-start | bytes 786440 | tf_op jit(solution)/shard_map/ppermute | solution.py:49
  14.9 11.6 %collective-permute-start.2 = (f32[4,128,128]{2,1,0:T(8,128)S(1)}, f32[4,128,128]{2,1,0:T(8,128)S(1)}, u32[]{:S(2)}, u32[]{:S(2)}) collective-permute-start(f32[4,128,128]{2,1,0:T(8,128)S(1)} %get-tuple-element.107), channel_id=1, source_target_pairs={{0,3},{1,0},{2,1},{3,2},{4,7},{5,4},{6,5},{7,6},{8,11},{9,8},{10,9... | collective-permute-start | bytes 786440 | tf_op jit(solution)/shard_map/ppermute | solution.py:49
  28.6 21.8 %collective-permute-start.3 = (f32[4,128,128]{2,1,0:T(8,128)S(1)}, f32[4,128,128]{2,1,0:T(8,128)S(1)}, u32[]{:S(2)}, u32[]{:S(2)}) collective-permute-start(f32[4,128,128]{2,1,0:T(8,128)S(1)} %get-tuple-element.36), channel_id=1, source_target_pairs={{0,4},{1,5},{2,6},{3,7},{4,8},{5,9},{6,10},{7,11},{8,12},{9,13},{1... | collective-permute-start | bytes 786440 | tf_op jit(solution)/shard_map/ppermute | solution.py:80
  32.6 17.8 %collective-permute-start.4 = (f32[4,128,128]{2,1,0:T(8,128)S(1)}, f32[4,128,128]{2,1,0:T(8,128)S(1)}, u32[]{:S(2)}, u32[]{:S(2)}) collective-permute-start(f32[4,128,128]{2,1,0:T(8,128)S(1)} %get-tuple-element.36), channel_id=1, source_target_pairs={{0,8},{1,9},{2,10},{3,11},{4,12},{5,13},{6,14},{7,15},{16,24},{17,... | collective-permute-start | bytes 786440 | tf_op jit(solution)/shard_map/ppermute | solution.py:80
  36.8 13.5 %collective-permute-start.5 = (f32[4,128,128]{2,1,0:T(8,128)S(1)}, f32[4,128,128]{2,1,0:T(8,128)S(1)}, u32[]{:S(2)}, u32[]{:S(2)}) collective-permute-start(f32[4,128,128]{2,1,0:T(8,128)S(1)} %get-tuple-element.36), channel_id=1, source_target_pairs={{0,12},{1,13},{2,14},{3,15},{16,28},{17,29},{18,30},{19,31}} | collective-permute-start | bytes 786440 | tf_op jit(solution)/shard_map/ppermute | solution.py:80
  52.8 4.8 %collective-permute-start.6 = (f32[4,128,128]{2,1,0:T(8,128)S(1)}, f32[4,128,128]{2,1,0:T(8,128)S(1)}, u32[]{:S(2)}, u32[]{:S(2)}) collective-permute-start(f32[4,128,128]{2,1,0:T(8,128)S(1)} %get-tuple-element.105), channel_id=1, source_target_pairs={{0,1},{1,2},{2,3},{3,0},{4,5},{5,6},{6,7},{7,4},{8,9},{9,10},{10,1... | collective-permute-start | bytes 786440 | tf_op jit(solution)/shard_map/ppermute | solution.py:49
  53.2 12.6 %collective-permute-start.7 = (f32[4,128,128]{2,1,0:T(8,128)S(1)}, f32[4,128,128]{2,1,0:T(8,128)S(1)}, u32[]{:S(2)}, u32[]{:S(2)}) collective-permute-start(f32[4,128,128]{2,1,0:T(8,128)S(1)} %get-tuple-element.104), channel_id=1, source_target_pairs={{0,2},{1,3},{2,0},{3,1},{4,6},{5,7},{6,4},{7,5},{8,10},{9,11},{10,... | collective-permute-start | bytes 786440 | tf_op jit(solution)/shard_map/ppermute | solution.py:49
  55.5 11.1 %collective-permute-start.8 = (f32[4,128,128]{2,1,0:T(8,128)S(1)}, f32[4,128,128]{2,1,0:T(8,128)S(1)}, u32[]{:S(2)}, u32[]{:S(2)}) collective-permute-start(f32[4,128,128]{2,1,0:T(8,128)S(1)} %get-tuple-element.103), channel_id=1, source_target_pairs={{0,3},{1,0},{2,1},{3,2},{4,7},{5,4},{6,5},{7,6},{8,11},{9,8},{10,9... | collective-permute-start | bytes 786440 | tf_op jit(solution)/shard_map/ppermute | solution.py:49
  67.5 7.8 %copy-start.1 = (bf16[384,2048]{1,0:T(8,128)(2,1)S(1)}, bf16[384,2048]{1,0:T(8,128)(2,1)}, u32[]{:S(2)}) copy-start(bf16[384,2048]{1,0:T(8,128)(2,1)} %param.9) | copy-start | bytes 4718596
  73.0 2.8 %copy-start = (f32[384,2048]{1,0:T(8,128)S(1)}, f32[384,2048]{1,0:T(8,128)}, u32[]{:S(2)}) copy-start(f32[384,2048]{1,0:T(8,128)} %shard_map.86) | copy-start | bytes 9437188
  84.8 4.9 %collective-permute-start.9 = (f32[4,128,128]{2,1,0:T(8,128)S(1)}, f32[4,128,128]{2,1,0:T(8,128)S(1)}, u32[]{:S(2)}, u32[]{:S(2)}) collective-permute-start(f32[4,128,128]{2,1,0:T(8,128)S(1)} %get-tuple-element.101), channel_id=1, source_target_pairs={{0,1},{1,2},{2,3},{3,0},{4,5},{5,6},{6,7},{7,4},{8,9},{9,10},{10,1... | collective-permute-start | bytes 786440 | tf_op jit(solution)/shard_map/ppermute | solution.py:49
  84.9 10.5 %collective-permute-start.10 = (f32[4,128,128]{2,1,0:T(8,128)S(1)}, f32[4,128,128]{2,1,0:T(8,128)S(1)}, u32[]{:S(2)}, u32[]{:S(2)}) collective-permute-start(f32[4,128,128]{2,1,0:T(8,128)S(1)} %get-tuple-element.100), channel_id=1, source_target_pairs={{0,2},{1,3},{2,0},{3,1},{4,6},{5,7},{6,4},{7,5},{8,10},{9,11},{10,... | collective-permute-start | bytes 786440 | tf_op jit(solution)/shard_map/ppermute | solution.py:49
  86.6 10.8 %collective-permute-start.11 = (f32[4,128,128]{2,1,0:T(8,128)S(1)}, f32[4,128,128]{2,1,0:T(8,128)S(1)}, u32[]{:S(2)}, u32[]{:S(2)}) collective-permute-start(f32[4,128,128]{2,1,0:T(8,128)S(1)} %get-tuple-element.99), channel_id=1, source_target_pairs={{0,3},{1,0},{2,1},{3,2},{4,7},{5,4},{6,5},{7,6},{8,11},{9,8},{10,9... | collective-permute-start | bytes 786440 | tf_op jit(solution)/shard_map/ppermute | solution.py:49
  99.3 20.7 %collective-permute-start.12 = (f32[4,128,128]{2,1,0:T(8,128)S(1)}, f32[4,128,128]{2,1,0:T(8,128)S(1)}, u32[]{:S(2)}, u32[]{:S(2)}) collective-permute-start(f32[4,128,128]{2,1,0:T(8,128)S(1)} %get-tuple-element.48), channel_id=1, source_target_pairs={{4,0},{5,1},{6,2},{7,3},{8,4},{9,5},{10,6},{11,7},{12,8},{13,9},{1... | collective-permute-start | bytes 786440 | tf_op jit(solution)/shard_map/ppermute | solution.py:80
  100.6 30.6 %collective-permute-start.13 = (f32[4,128,128]{2,1,0:T(8,128)S(1)}, f32[4,128,128]{2,1,0:T(8,128)S(1)}, u32[]{:S(2)}, u32[]{:S(2)}) collective-permute-start(f32[4,128,128]{2,1,0:T(8,128)S(1)} %get-tuple-element.48), channel_id=1, source_target_pairs={{8,0},{9,1},{10,2},{11,3},{12,4},{13,5},{14,6},{15,7},{24,16},{25,... | collective-permute-start | bytes 786440 | tf_op jit(solution)/shard_map/ppermute | solution.py:80
  101.9 29.3 %collective-permute-start.14 = (f32[4,128,128]{2,1,0:T(8,128)S(1)}, f32[4,128,128]{2,1,0:T(8,128)S(1)}, u32[]{:S(2)}, u32[]{:S(2)}) collective-permute-start(f32[4,128,128]{2,1,0:T(8,128)S(1)} %get-tuple-element.48), channel_id=1, source_target_pairs={{12,0},{13,1},{14,2},{15,3},{28,16},{29,17},{30,18},{31,19}} | collective-permute-start | bytes 786440 | tf_op jit(solution)/shard_map/ppermute | solution.py:80
  133.5 4.4 %collective-permute-start.15 = (f32[4,128,128]{2,1,0:T(8,128)S(1)}, f32[4,128,128]{2,1,0:T(8,128)S(1)}, u32[]{:S(2)}, u32[]{:S(2)}) collective-permute-start(f32[4,128,128]{2,1,0:T(8,128)S(1)} %get-tuple-element.97), channel_id=1, source_target_pairs={{0,1},{1,2},{2,3},{3,0},{4,5},{5,6},{6,7},{7,4},{8,9},{9,10},{10,1... | collective-permute-start | bytes 786440 | tf_op jit(solution)/shard_map/ppermute | solution.py:49
  133.6 14.0 %collective-permute-start.16 = (f32[4,128,128]{2,1,0:T(8,128)S(1)}, f32[4,128,128]{2,1,0:T(8,128)S(1)}, u32[]{:S(2)}, u32[]{:S(2)}) collective-permute-start(f32[4,128,128]{2,1,0:T(8,128)S(1)} %get-tuple-element.96), channel_id=1, source_target_pairs={{0,2},{1,3},{2,0},{3,1},{4,6},{5,7},{6,4},{7,5},{8,10},{9,11},{10,... | collective-permute-start | bytes 786440 | tf_op jit(solution)/shard_map/ppermute | solution.py:49
  136.7 11.5 %collective-permute-start.17 = (f32[4,128,128]{2,1,0:T(8,128)S(1)}, f32[4,128,128]{2,1,0:T(8,128)S(1)}, u32[]{:S(2)}, u32[]{:S(2)}) collective-permute-start(f32[4,128,128]{2,1,0:T(8,128)S(1)} %get-tuple-element.95), channel_id=1, source_target_pairs={{0,3},{1,0},{2,1},{3,2},{4,7},{5,4},{6,5},{7,6},{8,11},{9,8},{10,9... | collective-permute-start | bytes 786440 | tf_op jit(solution)/shard_map/ppermute | solution.py:49

commit v8 on v7

--- a/solution.py
+++ b/solution.py
@@ -3,6 +3,7 @@
 from jax import lax
 from jax.sharding import PartitionSpec as P
 from jax.experimental import pallas as pl
+from jax.experimental.pallas import tpu as pltpu
 
 HEAD = 128
 SPAN = 12
@@ -196,6 +197,52 @@
         value_out[:, columns(i)] = (value_part[:, columns(i)] + value_carry).astype(jnp.bfloat16)
 
 
+MIDDLE_ROWS = 128
+
+
+def middle_body(query_ref, inside_ref, prefix_ref, cot_ref, carry_ref, attn_ref, grad_ref, local_ref, mixed_ref):
+    carry = carry_ref[...] > 0
+    heads = prefix_ref.shape[0]
+    for i in range(heads):
+        carried = mm(query_ref[:, columns(i)], prefix_ref[i], NN)
+        mixed_ref[:, columns(i)] = inside_ref[:, columns(i)] + zeroed(carry, carried)
+    mixed = mixed_ref[...]
+    rms_value = jnp.sqrt(jnp.mean(mixed * mixed, axis=1, keepdims=True) + 1e-05)
+    normed = mixed / rms_value
+    attn_ref[...] = normed.astype(jnp.bfloat16)
+    out_cot = cot_ref[...].astype(jnp.float32)
+    grad_mix = (out_cot - normed * jnp.mean(out_cot * normed, axis=1, keepdims=True)) / rms_value
+    grad_ref[...] = grad_mix.astype(jnp.bfloat16)
+
+    @pl.when(pl.program_id(0) == 0)
+    def _():
+        local_ref[...] = jnp.zeros_like(local_ref)
+
+    for i in range(heads):
+        local_ref[i] += mm(zeroed(carry, query_ref[:, columns(i)]), grad_ref[:, columns(i)], TN)
+
+
+def middle_call(queries, inside, prefix_low, out_grad, carry):
+    rows, width = queries.shape
+    step = MIDDLE_ROWS if rows % MIDDLE_ROWS == 0 else rows
+    row_block = pl.BlockSpec((step, width), lambda i: (i, 0))
+    whole = pl.BlockSpec(prefix_low.shape, lambda i: (0, 0, 0))
+    return pl.pallas_call(
+        middle_body,
+        grid=(rows // step,),
+        in_specs=[row_block, row_block, whole, row_block, pl.BlockSpec((step, 1), lambda i: (i, 0))],
+        out_specs=[row_block, row_block, whole],
+        out_shape=[
+            jax.ShapeDtypeStruct((rows, width), jnp.bfloat16),
+            jax.ShapeDtypeStruct((rows, width), jnp.bfloat16),
+            jax.ShapeDtypeStruct(prefix_low.shape, jnp.float32),
+        ],
+        scratch_shapes=[pltpu.VMEM((step, width), jnp.float32)],
+        compiler_params=pltpu.CompilerParams(dimension_semantics=("arbitrary",)),
+        interpret=INTERPRET,
+    )(queries, inside, prefix_low, out_grad, carry)
+
+
 def shards(queries, keys, values, lengths, out_grad):
     row_count, feat_width = queries.shape
     head_count = feat_width // HEAD
@@ -233,14 +280,7 @@
         (queries, keys, values, keep),
     )
     prefix_low = (prefix * continues.astype(f32)).astype(jnp.bfloat16)
-    (mixed,) = head_call(mixed_body, [queries, inside, prefix_low, carry], [wide])
-    rms_value = jnp.sqrt(jnp.mean(mixed * mixed, axis=1, keepdims=True) + 1e-05)
-    normed = mixed / rms_value
-    attn_out = normed.astype(jnp.bfloat16)
-    out_cot = out_grad.astype(f32)
-    grad_mix = (out_cot - normed * jnp.mean(out_cot * normed, axis=1, keepdims=True)) / rms_value
-    grad_low = grad_mix.astype(jnp.bfloat16)
-    (grad_local,) = head_call(local_body, [queries, grad_low, carry], [state_shape])
+    attn_out, grad_low, grad_local = middle_call(queries, inside, prefix_low, out_grad, carry)
     back_flag = stops_back.astype(f32).reshape(1, 1, 1)
     suffix, (grad_queries, keys_part, values_part) = scan_states(
         grad_local, stop_keep, back_flag, -1,

time: 157 us -> 148 us (0.943)
  other arithmetic: 23 us -> 17.7 us
  Pallas kernels: 40.7 us -> 37.7 us
    pallas_call x6 -> x4, Pallas kernels: 40.7 us -> 30.7 us  [head_call(): pl.pallas_call(body, grid=(heads // HEAD_STEP,), in_specs=[spec(x.shape)...]
    pallas_call x0 -> x1, Pallas kernels: none -> 7.07 us  [middle_call(): pl.pallas_call(middle_body, grid=(rows // step,), in_specs=[row_block, ro...]
    reduce_sum x2 -> x0, other arithmetic: 2.94 us -> none  [the longest x1 2.32 us: shards(): rms_value = jnp.sqrt(jnp.mean(mixed * mixed, axis=1, keepdims=True) + 1e-05)]
    squeeze x4, local copies, waits for them, and re-layouts: 2.7 us -> 0.3 us  [member_exchange(): lax.dynamic_index_in_dim(pieces, (member + offset) % GROUP, keepdims=False)]
    convert_element_type x1 -> x0, other arithmetic: 2.4 us -> none  [shards(): grad_low = grad_mix.astype(jnp.bfloat16)]
    unnamed x4, local copies, waits for them, and re-layouts: 0.5 us -> 2.24 us
  transfers between devices with their start and end apart: 18 -> 18, of which waited for: 13 -> 13; matrix products, arithmetic and copies ran while one was open for 5% -> 5% of each run, Pallas kernels for 12% -> 13%
where the time goes in v8:
time: 148 us; the launch traced here: 147 us
  waiting for transfers between devices  51.8 us (35%)
  Pallas kernels  37.7 us (25%)
  starting transfers between devices  22.4 us (15%)
  other arithmetic  17.7 us (12%)
  between operations  10.1 us (7%)
  local copies, waits for them, and re-layouts  7.44 us (5%)
    ppermute x12, waiting for transfers between devices, member_exchange(): got.append(lax.ppermute(piece, axis, pairs))  40.6 us
    pallas_call x4, Pallas kernels, head_call(): pl.pallas_call(body, grid=(heads // HEAD_STEP,), in_specs=[spec(x.shape)...  30.7 us
    ppermute x6, starting transfers between devices, row_scan(): received.append(lax.ppermute(total, 'seq', pairs))  13.4 us
    ppermute x6, waiting for transfers between devices, row_scan(): received.append(lax.ppermute(total, 'seq', pairs))  11.2 us
    ppermute x12, starting transfers between devices, member_exchange(): got.append(lax.ppermute(piece, axis, pairs))  8.96 us
    pallas_call x1, Pallas kernels, middle_call(): pl.pallas_call(middle_body, grid=(rows // step,), in_specs=[row_block, ro...  7.07 us
    another operation x6, other arithmetic, row_scan(): jnp.stack([inner[index] + inner_keep[index] * entering for index in range...  4.23 us
    add x2, other arithmetic, row_scan(): total = mine[index] + keep_row[index] * total  3.93 us
  transfers between devices with their start and end apart: 18, of which 13 were waited for; matrix products, arithmetic and copies ran while one was open for 5% of the time, Pallas kernels for 13%

profile of v8, /device:TPU:1, one launch (start us, length us, event | category | flops | bytes accessed | tf_op | source)
XLA Modules:
  0.0 147.1 jit_solution(11624966143595949453)
XLA Ops:
  0.7 0.8 reduce-window.9
  1.6 1.4 compare_reduce_fusion
  4.2 1.3 and_convert_fusion.1
  5.6 0.8 reshape.142.tail_ref
  6.3 4.5 %shard_map.84 = f32[16,128,128]{2,1,0:T(8,128)} custom-call(bf16[384,2048]{1,0:T(8,128)(2,1)} %key_ref.5, bf16[384,2048]{1,0:T(8,128)(2,1)} %value_ref.5, f32[384,1]{1,0:T(8,128)} %reshape.142.tail_ref), custom_call_target="tpu_custom_call" | custom-call | tf_op jit(solution)/shard_map/pallas_call | solution.py:132
  11.0 1.1 copy-done
  12.2 2.6 %collective-permute-start = (f32[4,128,128]{2,1,0:T(8,128)S(1)}, f32[4,128,128]{2,1,0:T(8,128)S(1)}, u32[]{:S(2)}, u32[]{:S(2)}) collective-permute-start(f32[4,128,128]{2,1,0:T(8,128)S(1)} %get-tuple-element.113), channel_id=1, source_target_pairs={{0,1},{1,2},{2,3},{3,0},{4,5},{5,6},{6,7},{7,4},{8,9},{9,10},{10,1... | collective-permute-start | bytes 786440 | tf_op jit(solution)/shard_map/ppermute | solution.py:50
  15.3 1.0 and_convert_fusion.keep_ref
  17.9 2.4 %collective-permute-done = f32[4,128,128]{2,1,0:T(8,128)S(1)} collective-permute-done((f32[4,128,128]{2,1,0:T(8,128)S(1)}, f32[4,128,128]{2,1,0:T(8,128)S(1)}, u32[]{:S(2)}, u32[]{:S(2)}) %collective-permute-start) | collective-permute-done | bytes 262176 | tf_op jit(solution)/shard_map/ppermute | solution.py:50
  20.3 5.6 %collective-permute-done.1 = f32[4,128,128]{2,1,0:T(8,128)S(1)} collective-permute-done((f32[4,128,128]{2,1,0:T(8,128)S(1)}, f32[4,128,128]{2,1,0:T(8,128)S(1)}, u32[]{:S(2)}, u32[]{:S(2)}) %collective-permute-start.1) | collective-permute-done | bytes 262176 | tf_op jit(solution)/shard_map/ppermute | solution.py:50
  26.5 2.0 %fusion.7 = (f32[4,128,128]{2,1,0:T(8,128)S(1)}, f32[4,128,128]{2,1,0:T(8,128)S(1)}) fusion(f32[4,4,128,128]{3,2,1,0:T(8,128)S(1)} %bitcast_dynamic-update-slice_fusion.9, f32[]{:T(128)} %bitcast.11, f32[]{:T(128)} %bitcast.13, f32[]{:T(128)S(6)} %mul.216, f32[]{:T(128)} %bitcast.15), kind=kLoop, calls=%fused_computation.20 | loop fusion | flops 458752 | bytes 1572880 | tf_op jit(solution)/shard_map/add | solution.py:71
  28.5 4.0 %collective-permute-start.3 = (f32[4,128,128]{2,1,0:T(8,128)S(1)}, f32[4,128,128]{2,1,0:T(8,128)S(1)}, u32[]{:S(2)}, u32[]{:S(2)}) collective-permute-start(f32[4,128,128]{2,1,0:T(8,128)S(1)} %get-tuple-element.39), channel_id=1, source_target_pairs={{0,4},{1,5},{2,6},{3,7},{4,8},{5,9},{6,10},{7,11},{8,12},{9,13},{1... | collective-permute-start | bytes 786440 | tf_op jit(solution)/shard_map/ppermute | solution.py:81
  32.5 4.2 %collective-permute-start.4 = (f32[4,128,128]{2,1,0:T(8,128)S(1)}, f32[4,128,128]{2,1,0:T(8,128)S(1)}, u32[]{:S(2)}, u32[]{:S(2)}) collective-permute-start(f32[4,128,128]{2,1,0:T(8,128)S(1)} %get-tuple-element.39), channel_id=1, source_target_pairs={{0,8},{1,9},{2,10},{3,11},{4,12},{5,13},{6,14},{7,15},{16,24},{17,... | collective-permute-start | bytes 786440 | tf_op jit(solution)/shard_map/ppermute | solution.py:81
  36.8 1.3 collective-permute-start.5
  40.0 0.6 subtract_reduce_fusion
  42.6 7.7 %shard_map.85 = (bf16[16,384,384]{2,1,0:T(8,128)(2,1)}, f32[384,2048]{1,0:T(8,128)}) custom-call(bf16[384,2048]{1,0:T(8,128)(2,1)} %query_ref.3, bf16[384,2048]{1,0:T(8,128)(2,1)} %key_ref.5, bf16[384,2048]{1,0:T(8,128)(2,1)} %value_ref.5, f32[384,384]{1,0:T(8,128)} %and_convert_fusion.keep_ref), custom_call_target="tpu_custom_call" | custom-call | tf_op jit(solution)/shard_map/pallas_call | solution.py:132
  50.3 1.4 add_bitcast_fusion.5
  51.7 0.7 add_bitcast_fusion.4
  53.1 1.2 collective-permute-start.7
  54.6 0.8 copy.14.carry_ref
  55.8 1.7 %collective-permute-done.6 = f32[4,128,128]{2,1,0:T(8,128)S(1)} collective-permute-done((f32[4,128,128]{2,1,0:T(8,128)S(1)}, f32[4,128,128]{2,1,0:T(8,128)S(1)}, u32[]{:S(2)}, u32[]{:S(2)}) %collective-permute-start.6) | collective-permute-done | bytes 262176 | tf_op jit(solution)/shard_map/ppermute | solution.py:50
  57.5 8.2 %collective-permute-done.7 = f32[4,128,128]{2,1,0:T(8,128)S(1)} collective-permute-done((f32[4,128,128]{2,1,0:T(8,128)S(1)}, f32[4,128,128]{2,1,0:T(8,128)S(1)}, u32[]{:S(2)}, u32[]{:S(2)}) %collective-permute-start.7) | collective-permute-done | bytes 262176 | tf_op jit(solution)/shard_map/ppermute | solution.py:50
  65.7 0.8 collective-permute-done.8
  66.6 0.9 multiply_convert_fusion.1
  67.5 7.1 %shard_map.86 = (bf16[384,2048]{1,0:T(8,128)(2,1)}, bf16[384,2048]{1,0:T(8,128)(2,1)}, f32[16,128,128]{2,1,0:T(8,128)}) custom-call(bf16[384,2048]{1,0:T(8,128)(2,1)} %query_ref.3, f32[384,2048]{1,0:T(8,128)} %get-tuple-element.46.inside_ref, bf16[16,128,128]{2,1,0:T(8,128)(2,1)} %bitcast.128, bf16[384,2048]{1,0:T(8,128)(2,1)} %cot_ref.1, ...), custom_call_target="tpu_custom_call" | custom-call | tf_op jit(solution)/shard_map/pallas_call | solution.py:230
  74.7 1.1 copy-done.1
  76.2 0.6 fusion.18
  77.6 0.8 collective-permute-start.11
  78.3 2.5 %collective-permute-done.9 = f32[4,128,128]{2,1,0:T(8,128)S(1)} collective-permute-done((f32[4,128,128]{2,1,0:T(8,128)S(1)}, f32[4,128,128]{2,1,0:T(8,128)S(1)}, u32[]{:S(2)}, u32[]{:S(2)}) %collective-permute-start.9) | collective-permute-done | bytes 262176 | tf_op jit(solution)/shard_map/ppermute | solution.py:50
  80.8 5.6 %collective-permute-done.10 = f32[4,128,128]{2,1,0:T(8,128)S(1)} collective-permute-done((f32[4,128,128]{2,1,0:T(8,128)S(1)}, f32[4,128,128]{2,1,0:T(8,128)S(1)}, u32[]{:S(2)}, u32[]{:S(2)}) %collective-permute-start.10) | collective-permute-done | bytes 262176 | tf_op jit(solution)/shard_map/ppermute | solution.py:50
  86.5 1.9 %collective-permute-done.11 = f32[4,128,128]{2,1,0:T(8,128)S(1)} collective-permute-done((f32[4,128,128]{2,1,0:T(8,128)S(1)}, f32[4,128,128]{2,1,0:T(8,128)S(1)}, u32[]{:S(2)}, u32[]{:S(2)}) %collective-permute-start.11) | collective-permute-done | bytes 262176 | tf_op jit(solution)/shard_map/ppermute | solution.py:50
  88.4 1.9 %fusion.3 = (f32[4,128,128]{2,1,0:T(8,128)S(1)}, f32[4,128,128]{2,1,0:T(8,128)S(1)}) fusion(f32[4,4,128,128]{3,2,1,0:T(8,128)S(1)} %bitcast_dynamic-update-slice_fusion.3, f32[]{:T(128)} %bitcast.38, f32[]{:T(128)} %bitcast.40, f32[]{:T(128)S(6)} %mul.243, f32[]{:T(128)} %bitcast.42), kind=kLoop, calls=%fused_computation.12 | loop fusion | flops 458752 | bytes 1572880 | tf_op jit(solution)/shard_map/add | solution.py:71
  90.3 1.3 collective-permute-start.12
  91.6 1.3 collective-permute-start.13
  92.9 1.3 collective-permute-start.14
  96.1 0.6 fusion.13
  96.7 0.6 fusion.14
  98.6 0.8 copy.15.carry_ref
  99.4 11.6 %shard_map.87 = (bf16[384,2048]{1,0:T(8,128)(2,1)}, f32[384,2048]{1,0:T(8,128)}, f32[384,2048]{1,0:T(8,128)}) custom-call(bf16[384,2048]{1,0:T(8,128)(2,1)} %query_ref.3, bf16[384,2048]{1,0:T(8,128)(2,1)} %key_ref.5, bf16[384,2048]{1,0:T(8,128)(2,1)} %value_ref.5, bf16[384,2048]{1,0:T(8,128)(2,1)} %get-tuple-element.58.grad_ref, ...), custom_call_target="tpu_custom_call" | custom-call | tf_op jit(solution)/shard_map/pallas_call | solution.py:132
  111.0 11.2 %collective-permute-done.13 = f32[4,128,128]{2,1,0:T(8,128)S(1)} collective-permute-done((f32[4,128,128]{2,1,0:T(8,128)S(1)}, f32[4,128,128]{2,1,0:T(8,128)S(1)}, u32[]{:S(2)}, u32[]{:S(2)}) %collective-permute-start.13) | collective-permute-done | bytes 262176 | tf_op jit(solution)/shard_map/ppermute | solution.py:81
  122.2 1.3 add_bitcast_fusion.2
  123.5 0.7 add_bitcast_fusion.1
  124.6 2.5 %collective-permute-start.16 = (f32[4,128,128]{2,1,0:T(8,128)S(1)}, f32[4,128,128]{2,1,0:T(8,128)S(1)}, u32[]{:S(2)}, u32[]{:S(2)}) collective-permute-start(f32[4,128,128]{2,1,0:T(8,128)S(1)} %get-tuple-element.100), channel_id=1, source_target_pairs={{0,2},{1,3},{2,0},{3,1},{4,6},{5,7},{6,4},{7,5},{8,10},{9,11},{10,... | collective-permute-start | bytes 786440 | tf_op jit(solution)/shard_map/ppermute | solution.py:50
  127.8 1.1 collective-permute-done.15
  128.9 9.7 %collective-permute-done.16 = f32[4,128,128]{2,1,0:T(8,128)S(1)} collective-permute-done((f32[4,128,128]{2,1,0:T(8,128)S(1)}, f32[4,128,128]{2,1,0:T(8,128)S(1)}, u32[]{:S(2)}, u32[]{:S(2)}) %collective-permute-start.16) | collective-permute-done | bytes 262176 | tf_op jit(solution)/shard_map/ppermute | solution.py:50
  138.7 0.6 collective-permute-done.17
  139.3 0.9 multiply_convert_fusion
  140.2 6.9 %shard_map.88 = (bf16[384,2048]{1,0:T(8,128)(2,1)}, bf16[384,2048]{1,0:T(8,128)(2,1)}) custom-call(bf16[384,2048]{1,0:T(8,128)(2,1)} %key_ref.5, bf16[384,2048]{1,0:T(8,128)(2,1)} %value_ref.5, f32[384,2048]{1,0:T(8,128)} %get-tuple-element.67.key_part, f32[384,2048]{1,0:T(8,128)} %get-tuple-element.68.value_part, bf16[16,128,128]{2,1,0:T(8,128)(2,1)} %bitcast.133, ...), custom_call_target="tpu_custom_call" | custom-call | tf_op jit(solution)/shard_map/pallas_call | solution.py:132
  (53 shorter events, 5.9 us)
Async XLA Ops:
  10.9 1.2 copy-start
  12.2 8.1 %collective-permute-start = (f32[4,128,128]{2,1,0:T(8,128)S(1)}, f32[4,128,128]{2,1,0:T(8,128)S(1)}, u32[]{:S(2)}, u32[]{:S(2)}) collective-permute-start(f32[4,128,128]{2,1,0:T(8,128)S(1)} %get-tuple-element.113), channel_id=1, source_target_pairs={{0,1},{1,2},{2,3},{3,0},{4,5},{5,6},{6,7},{7,4},{8,9},{9,10},{10,1... | collective-permute-start | bytes 786440 | tf_op jit(solution)/shard_map/ppermute | solution.py:50
  14.8 11.1 %collective-permute-start.1 = (f32[4,128,128]{2,1,0:T(8,128)S(1)}, f32[4,128,128]{2,1,0:T(8,128)S(1)}, u32[]{:S(2)}, u32[]{:S(2)}) collective-permute-start(f32[4,128,128]{2,1,0:T(8,128)S(1)} %get-tuple-element.112), channel_id=1, source_target_pairs={{0,2},{1,3},{2,0},{3,1},{4,6},{5,7},{6,4},{7,5},{8,10},{9,11},{10,... | collective-permute-start | bytes 786440 | tf_op jit(solution)/shard_map/ppermute | solution.py:50
  14.8 11.6 %collective-permute-start.2 = (f32[4,128,128]{2,1,0:T(8,128)S(1)}, f32[4,128,128]{2,1,0:T(8,128)S(1)}, u32[]{:S(2)}, u32[]{:S(2)}) collective-permute-start(f32[4,128,128]{2,1,0:T(8,128)S(1)} %get-tuple-element.111), channel_id=1, source_target_pairs={{0,3},{1,0},{2,1},{3,2},{4,7},{5,4},{6,5},{7,6},{8,11},{9,8},{10,9... | collective-permute-start | bytes 786440 | tf_op jit(solution)/shard_map/ppermute | solution.py:50
  28.5 21.8 %collective-permute-start.3 = (f32[4,128,128]{2,1,0:T(8,128)S(1)}, f32[4,128,128]{2,1,0:T(8,128)S(1)}, u32[]{:S(2)}, u32[]{:S(2)}) collective-permute-start(f32[4,128,128]{2,1,0:T(8,128)S(1)} %get-tuple-element.39), channel_id=1, source_target_pairs={{0,4},{1,5},{2,6},{3,7},{4,8},{5,9},{6,10},{7,11},{8,12},{9,13},{1... | collective-permute-start | bytes 786440 | tf_op jit(solution)/shard_map/ppermute | solution.py:81
  32.5 17.8 %collective-permute-start.4 = (f32[4,128,128]{2,1,0:T(8,128)S(1)}, f32[4,128,128]{2,1,0:T(8,128)S(1)}, u32[]{:S(2)}, u32[]{:S(2)}) collective-permute-start(f32[4,128,128]{2,1,0:T(8,128)S(1)} %get-tuple-element.39), channel_id=1, source_target_pairs={{0,8},{1,9},{2,10},{3,11},{4,12},{5,13},{6,14},{7,15},{16,24},{17,... | collective-permute-start | bytes 786440 | tf_op jit(solution)/shard_map/ppermute | solution.py:81
  36.8 13.5 %collective-permute-start.5 = (f32[4,128,128]{2,1,0:T(8,128)S(1)}, f32[4,128,128]{2,1,0:T(8,128)S(1)}, u32[]{:S(2)}, u32[]{:S(2)}) collective-permute-start(f32[4,128,128]{2,1,0:T(8,128)S(1)} %get-tuple-element.39), channel_id=1, source_target_pairs={{0,12},{1,13},{2,14},{3,15},{16,28},{17,29},{18,30},{19,31}} | collective-permute-start | bytes 786440 | tf_op jit(solution)/shard_map/ppermute | solution.py:81
  52.7 4.8 %collective-permute-start.6 = (f32[4,128,128]{2,1,0:T(8,128)S(1)}, f32[4,128,128]{2,1,0:T(8,128)S(1)}, u32[]{:S(2)}, u32[]{:S(2)}) collective-permute-start(f32[4,128,128]{2,1,0:T(8,128)S(1)} %get-tuple-element.109), channel_id=1, source_target_pairs={{0,1},{1,2},{2,3},{3,0},{4,5},{5,6},{6,7},{7,4},{8,9},{9,10},{10,1... | collective-permute-start | bytes 786440 | tf_op jit(solution)/shard_map/ppermute | solution.py:50
  53.1 12.6 %collective-permute-start.7 = (f32[4,128,128]{2,1,0:T(8,128)S(1)}, f32[4,128,128]{2,1,0:T(8,128)S(1)}, u32[]{:S(2)}, u32[]{:S(2)}) collective-permute-start(f32[4,128,128]{2,1,0:T(8,128)S(1)} %get-tuple-element.108), channel_id=1, source_target_pairs={{0,2},{1,3},{2,0},{3,1},{4,6},{5,7},{6,4},{7,5},{8,10},{9,11},{10,... | collective-permute-start | bytes 786440 | tf_op jit(solution)/shard_map/ppermute | solution.py:50
  55.4 11.1 %collective-permute-start.8 = (f32[4,128,128]{2,1,0:T(8,128)S(1)}, f32[4,128,128]{2,1,0:T(8,128)S(1)}, u32[]{:S(2)}, u32[]{:S(2)}) collective-permute-start(f32[4,128,128]{2,1,0:T(8,128)S(1)} %get-tuple-element.107), channel_id=1, source_target_pairs={{0,3},{1,0},{2,1},{3,2},{4,7},{5,4},{6,5},{7,6},{8,11},{9,8},{10,9... | collective-permute-start | bytes 786440 | tf_op jit(solution)/shard_map/ppermute | solution.py:50
  74.6 1.2 copy-start.1
  75.9 5.0 %collective-permute-start.9 = (f32[4,128,128]{2,1,0:T(8,128)S(1)}, f32[4,128,128]{2,1,0:T(8,128)S(1)}, u32[]{:S(2)}, u32[]{:S(2)}) collective-permute-start(f32[4,128,128]{2,1,0:T(8,128)S(1)} %get-tuple-element.105), channel_id=1, source_target_pairs={{0,1},{1,2},{2,3},{3,0},{4,5},{5,6},{6,7},{7,4},{8,9},{9,10},{10,1... | collective-permute-start | bytes 786440 | tf_op jit(solution)/shard_map/ppermute | solution.py:50
  75.9 10.5 %collective-permute-start.10 = (f32[4,128,128]{2,1,0:T(8,128)S(1)}, f32[4,128,128]{2,1,0:T(8,128)S(1)}, u32[]{:S(2)}, u32[]{:S(2)}) collective-permute-start(f32[4,128,128]{2,1,0:T(8,128)S(1)} %get-tuple-element.104), channel_id=1, source_target_pairs={{0,2},{1,3},{2,0},{3,1},{4,6},{5,7},{6,4},{7,5},{8,10},{9,11},{10,... | collective-permute-start | bytes 786440 | tf_op jit(solution)/shard_map/ppermute | solution.py:50
  77.6 10.8 %collective-permute-start.11 = (f32[4,128,128]{2,1,0:T(8,128)S(1)}, f32[4,128,128]{2,1,0:T(8,128)S(1)}, u32[]{:S(2)}, u32[]{:S(2)}) collective-permute-start(f32[4,128,128]{2,1,0:T(8,128)S(1)} %get-tuple-element.103), channel_id=1, source_target_pairs={{0,3},{1,0},{2,1},{3,2},{4,7},{5,4},{6,5},{7,6},{8,11},{9,8},{10,9... | collective-permute-start | bytes 786440 | tf_op jit(solution)/shard_map/ppermute | solution.py:50
  90.3 20.7 %collective-permute-start.12 = (f32[4,128,128]{2,1,0:T(8,128)S(1)}, f32[4,128,128]{2,1,0:T(8,128)S(1)}, u32[]{:S(2)}, u32[]{:S(2)}) collective-permute-start(f32[4,128,128]{2,1,0:T(8,128)S(1)} %get-tuple-element.54), channel_id=1, source_target_pairs={{4,0},{5,1},{6,2},{7,3},{8,4},{9,5},{10,6},{11,7},{12,8},{13,9},{1... | collective-permute-start | bytes 786440 | tf_op jit(solution)/shard_map/ppermute | solution.py:81
  91.6 30.6 %collective-permute-start.13 = (f32[4,128,128]{2,1,0:T(8,128)S(1)}, f32[4,128,128]{2,1,0:T(8,128)S(1)}, u32[]{:S(2)}, u32[]{:S(2)}) collective-permute-start(f32[4,128,128]{2,1,0:T(8,128)S(1)} %get-tuple-element.54), channel_id=1, source_target_pairs={{8,0},{9,1},{10,2},{11,3},{12,4},{13,5},{14,6},{15,7},{24,16},{25,... | collective-permute-start | bytes 786440 | tf_op jit(solution)/shard_map/ppermute | solution.py:81
  92.9 29.3 %collective-permute-start.14 = (f32[4,128,128]{2,1,0:T(8,128)S(1)}, f32[4,128,128]{2,1,0:T(8,128)S(1)}, u32[]{:S(2)}, u32[]{:S(2)}) collective-permute-start(f32[4,128,128]{2,1,0:T(8,128)S(1)} %get-tuple-element.54), channel_id=1, source_target_pairs={{12,0},{13,1},{14,2},{15,3},{28,16},{29,17},{30,18},{31,19}} | collective-permute-start | bytes 786440 | tf_op jit(solution)/shard_map/ppermute | solution.py:81
  124.5 4.4 %collective-permute-start.15 = (f32[4,128,128]{2,1,0:T(8,128)S(1)}, f32[4,128,128]{2,1,0:T(8,128)S(1)}, u32[]{:S(2)}, u32[]{:S(2)}) collective-permute-start(f32[4,128,128]{2,1,0:T(8,128)S(1)} %get-tuple-element.101), channel_id=1, source_target_pairs={{0,1},{1,2},{2,3},{3,0},{4,5},{5,6},{6,7},{7,4},{8,9},{9,10},{10,1... | collective-permute-start | bytes 786440 | tf_op jit(solution)/shard_map/ppermute | solution.py:50
  124.6 14.0 %collective-permute-start.16 = (f32[4,128,128]{2,1,0:T(8,128)S(1)}, f32[4,128,128]{2,1,0:T(8,128)S(1)}, u32[]{:S(2)}, u32[]{:S(2)}) collective-permute-start(f32[4,128,128]{2,1,0:T(8,128)S(1)} %get-tuple-element.100), channel_id=1, source_target_pairs={{0,2},{1,3},{2,0},{3,1},{4,6},{5,7},{6,4},{7,5},{8,10},{9,11},{10,... | collective-permute-start | bytes 786440 | tf_op jit(solution)/shard_map/ppermute | solution.py:50
  127.8 11.5 %collective-permute-start.17 = (f32[4,128,128]{2,1,0:T(8,128)S(1)}, f32[4,128,128]{2,1,0:T(8,128)S(1)}, u32[]{:S(2)}, u32[]{:S(2)}) collective-permute-start(f32[4,128,128]{2,1,0:T(8,128)S(1)} %get-tuple-element.99), channel_id=1, source_target_pairs={{0,3},{1,0},{2,1},{3,2},{4,7},{5,4},{6,5},{7,6},{8,11},{9,8},{10,9... | collective-permute-start | bytes 786440 | tf_op jit(solution)/shard_map/ppermute | solution.py:50

commit v9 on v8

--- a/solution.py
+++ b/solution.py
@@ -147,14 +147,33 @@
     return jnp.where(mask, value, jnp.zeros_like(value))
 
 
-def state_body(key_ref, value_ref, tail_ref, state_ref):
-    tail = tail_ref[...] > 0
+def row_masks(rel_ref, rows):
+    rel = rel_ref[rows]
+    tail = rel == rel_ref[-1:, :]
+    lead = rel_ref[0:1, :]
+    carry = (rel == lead) & (lead < 0)
+    return rel, tail, carry
+
+
+def keep_mask(rel):
+    size = rel.shape[0]
+    row = lax.broadcasted_iota(jnp.int32, (size, size), 0)
+    col = lax.broadcasted_iota(jnp.int32, (size, size), 1)
+    return (col <= row) & (col >= rel)
+
+
+def gated(prefix, rel_ref):
+    return zeroed(rel_ref[0:1, :] < 0, prefix).astype(jnp.bfloat16)
+
+
+def state_body(key_ref, value_ref, rel_ref, state_ref):
+    _, tail, _ = row_masks(rel_ref, slice(None))
     for i in range(HEAD_STEP):
         state_ref[i] = mm(zeroed(tail, key_ref[:, columns(i)]), value_ref[:, columns(i)], TN)
 
 
-def inside_body(query_ref, key_ref, value_ref, keep_ref, weight_ref, inside_ref):
-    keep = keep_ref[...] > 0
+def inside_body(query_ref, key_ref, value_ref, rel_ref, weight_ref, inside_ref):
+    keep = keep_mask(rel_ref[...])
     for i in range(HEAD_STEP):
         scores = mm(query_ref[:, columns(i)], key_ref[:, columns(i)], NT)
         weights = zeroed(keep, scores).astype(jnp.bfloat16)
@@ -162,34 +181,21 @@
         inside_ref[:, columns(i)] = mm(weights, value_ref[:, columns(i)], NN)
 
 
-def mixed_body(query_ref, inside_ref, prefix_ref, carry_ref, mixed_ref):
-    carry = carry_ref[...] > 0
-    for i in range(HEAD_STEP):
-        carried = mm(query_ref[:, columns(i)], prefix_ref[i], NN)
-        mixed_ref[:, columns(i)] = inside_ref[:, columns(i)] + zeroed(carry, carried)
-
-
-def local_body(query_ref, grad_ref, carry_ref, local_ref):
-    carry = carry_ref[...] > 0
-    for i in range(HEAD_STEP):
-        local_ref[i] = mm(zeroed(carry, query_ref[:, columns(i)]), grad_ref[:, columns(i)], TN)
-
-
-def grad_body(query_ref, key_ref, value_ref, grad_ref, weight_ref, prefix_ref, keep_ref, carry_ref,
+def grad_body(query_ref, key_ref, value_ref, grad_ref, weight_ref, prefix_ref, rel_ref,
               query_out, key_out, value_out):
-    keep = keep_ref[...] > 0
-    carry = carry_ref[...] > 0
+    rel, _, carry = row_masks(rel_ref, slice(None))
+    keep = keep_mask(rel)
     for i in range(HEAD_STEP):
         grad = grad_ref[:, columns(i)]
         grad_weights = zeroed(keep, mm(grad, value_ref[:, columns(i)], NT)).astype(jnp.bfloat16)
-        from_prefix = zeroed(carry, mm(grad, prefix_ref[i], NT))
+        from_prefix = zeroed(carry, mm(grad, gated(prefix_ref[i], rel_ref), NT))
         query_out[:, columns(i)] = (mm(grad_weights, key_ref[:, columns(i)], NN) + from_prefix).astype(jnp.bfloat16)
         key_out[:, columns(i)] = mm(grad_weights, query_ref[:, columns(i)], TN)
         value_out[:, columns(i)] = mm(weight_ref[i], grad, TN)
 
 
-def tail_body(key_ref, value_ref, key_part, value_part, suffix_ref, tail_ref, key_out, value_out):
-    tail = tail_ref[...] > 0
+def tail_body(key_ref, value_ref, key_part, value_part, suffix_ref, rel_ref, key_out, value_out):
+    _, tail, _ = row_masks(rel_ref, slice(None))
     for i in range(HEAD_STEP):
         key_carry = zeroed(tail, mm(value_ref[:, columns(i)], suffix_ref[i], NT))
         value_carry = zeroed(tail, mm(key_ref[:, columns(i)], suffix_ref[i], NN))
@@ -200,11 +206,13 @@
 MIDDLE_ROWS = 128
 
 
-def middle_body(query_ref, inside_ref, prefix_ref, cot_ref, carry_ref, attn_ref, grad_ref, local_ref, mixed_ref):
-    carry = carry_ref[...] > 0
+def middle_body(query_ref, inside_ref, prefix_ref, cot_ref, rel_ref, attn_ref, grad_ref, local_ref, mixed_ref):
+    step = query_ref.shape[0]
+    rows = pl.ds(pl.multiple_of(pl.program_id(0) * step, 8), step)
+    _, _, carry = row_masks(rel_ref, rows)
     heads = prefix_ref.shape[0]
     for i in range(heads):
-        carried = mm(query_ref[:, columns(i)], prefix_ref[i], NN)
+        carried = mm(query_ref[:, columns(i)], gated(prefix_ref[i], rel_ref), NN)
         mixed_ref[:, columns(i)] = inside_ref[:, columns(i)] + zeroed(carry, carried)
     mixed = mixed_ref[...]
     rms_value = jnp.sqrt(jnp.mean(mixed * mixed, axis=1, keepdims=True) + 1e-05)
@@ -222,25 +230,25 @@
         local_ref[i] += mm(zeroed(carry, query_ref[:, columns(i)]), grad_ref[:, columns(i)], TN)
 
 
-def middle_call(queries, inside, prefix_low, out_grad, carry):
+def middle_call(queries, inside, prefix, out_grad, rel):
     rows, width = queries.shape
     step = MIDDLE_ROWS if rows % MIDDLE_ROWS == 0 else rows
     row_block = pl.BlockSpec((step, width), lambda i: (i, 0))
-    whole = pl.BlockSpec(prefix_low.shape, lambda i: (0, 0, 0))
+    whole = pl.BlockSpec(prefix.shape, lambda i: (0, 0, 0))
     return pl.pallas_call(
         middle_body,
         grid=(rows // step,),
-        in_specs=[row_block, row_block, whole, row_block, pl.BlockSpec((step, 1), lambda i: (i, 0))],
+        in_specs=[row_block, row_block, whole, row_block, pl.BlockSpec(rel.shape, lambda i: (0, 0))],
         out_specs=[row_block, row_block, whole],
         out_shape=[
             jax.ShapeDtypeStruct((rows, width), jnp.bfloat16),
             jax.ShapeDtypeStruct((rows, width), jnp.bfloat16),
-            jax.ShapeDtypeStruct(prefix_low.shape, jnp.float32),
+            jax.ShapeDtypeStruct(prefix.shape, jnp.float32),
         ],
         scratch_shapes=[pltpu.VMEM((step, width), jnp.float32)],
         compiler_params=pltpu.CompilerParams(dimension_semantics=("arbitrary",)),
         interpret=INTERPRET,
-    )(queries, inside, prefix_low, out_grad, carry)
+    )(queries, inside, prefix, out_grad, rel)
 
 
 def shards(queries, keys, values, lengths, out_grad):
@@ -248,23 +256,18 @@
     head_count = feat_width // HEAD
     first_row = lax.axis_index("seq") * row_count
     position = first_row + lax.iota(jnp.int32, row_count)
-    starts = jnp.cumsum(lengths) - lengths
-    doc_ids = jnp.sum((starts[None, :] <= position[:, None]).astype(jnp.int32), axis=1)
-    keep_mask = (position[None, :] <= position[:, None]) & (doc_ids[None, :] == doc_ids[:, None])
-    lead_rows = doc_ids == doc_ids[0]
-    tail_rows = doc_ids == doc_ids[row_count - 1]
-    continues = jnp.logical_not(jnp.any(starts == first_row))
-    has_start = jnp.any((starts >= first_row) & (starts < first_row + row_count))
-    stops_back = jnp.logical_or(doc_ids[0] != doc_ids[row_count - 1], jnp.logical_not(continues))
-    use_carry = lead_rows & continues
-    keep = keep_mask.astype(jnp.float32)
-    tail = tail_rows.astype(jnp.float32)[:, None]
-    carry = use_carry.astype(jnp.float32)[:, None]
+    order = lax.iota(jnp.int32, lengths.shape[0])
+    starts = jnp.sum(jnp.where(order[None, :] < order[:, None], lengths[None, :], 0), axis=1)
+    doc_start = jnp.max(jnp.where(starts[None, :] <= position[:, None], starts[None, :], 0), axis=1)
+    rel = (doc_start - first_row)[:, None]
     f32 = jnp.float32
     state_shape = jax.ShapeDtypeStruct((head_count, HEAD, HEAD), f32)
     wide = jax.ShapeDtypeStruct((row_count, feat_width), f32)
     low = jax.ShapeDtypeStruct((row_count, feat_width), jnp.bfloat16)
-    (state_local,) = head_call(state_body, [keys, values, tail], [state_shape])
+    (state_local,) = head_call(state_body, [keys, values, rel], [state_shape])
+    has_start = jnp.any((starts >= first_row) & (starts < first_row + row_count))
+    continues = jnp.logical_not(jnp.any(starts == first_row))
+    stops_back = jnp.logical_or(rel[0, 0] != rel[row_count - 1, 0], jnp.logical_not(continues))
     start_flag = has_start.astype(f32).reshape(1, 1, 1)
 
     def start_keep(blocks):
@@ -277,21 +280,20 @@
     prefix, (weights, inside) = scan_states(
         state_local, start_keep, start_flag, 1,
         lambda *xs: head_call(inside_body, list(xs), [weight_shape, wide]),
-        (queries, keys, values, keep),
-    )
-    prefix_low = (prefix * continues.astype(f32)).astype(jnp.bfloat16)
-    attn_out, grad_low, grad_local = middle_call(queries, inside, prefix_low, out_grad, carry)
+        (queries, keys, values, rel),
+    )
+    attn_out, grad_low, grad_local = middle_call(queries, inside, prefix, out_grad, rel)
     back_flag = stops_back.astype(f32).reshape(1, 1, 1)
     suffix, (grad_queries, keys_part, values_part) = scan_states(
         grad_local, stop_keep, back_flag, -1,
         lambda *xs: head_call(grad_body, list(xs), [low, wide, wide]),
-        (queries, keys, values, grad_low, weights, prefix_low, keep, carry),
+        (queries, keys, values, grad_low, weights, prefix, rel),
     )
     next_first = first_row + row_count
     next_open = (next_first < lax.axis_size("seq") * row_count) & jnp.logical_not(jnp.any(starts == next_first))
     suffix_low = (suffix * next_open.astype(f32)).astype(jnp.bfloat16)
     grad_keys, grad_values = head_call(
-        tail_body, [keys, values, keys_part, values_part, suffix_low, tail], [low, low]
+        tail_body, [keys, values, keys_part, values_part, suffix_low, rel], [low, low]
     )
     return attn_out, grad_queries, grad_keys, grad_values
 

time: 148 us -> 144 us (0.973)
  other arithmetic: 17.7 us -> 13.8 us
    convert_element_type x3 -> x0, other arithmetic: 3.21 us -> none  [the longest x1 1.3 us: shards(): carry = use_carry.astype(jnp.float32)[:, None]]
    convert_element_type x3 -> x0, local copies, waits for them, and re-layouts: 1.62 us -> none  [the longest x2 0.83 us: shards(): carry = use_carry.astype(jnp.float32)[:, None]]
    unnamed x4 -> x6, local copies, waits for them, and re-layouts: 2.24 us -> 3.21 us
where the time goes in v9:
time: 144 us
  waiting for transfers between devices  51.8 us (36%)
  Pallas kernels  38 us (26%)
  starting transfers between devices  22.4 us (16%)
  other arithmetic  13.8 us (10%)
  between operations  9.58 us (7%)
  local copies, waits for them, and re-layouts  7.89 us (5%)
    ppermute x12, waiting for transfers between devices, member_exchange(): got.append(lax.ppermute(piece, axis, pairs))  41.7 us
    pallas_call x4, Pallas kernels, head_call(): pl.pallas_call(body, grid=(heads // HEAD_STEP,), in_specs=[spec(x.shape)...  30.7 us
    ppermute x6, starting transfers between devices, row_scan(): received.append(lax.ppermute(total, 'seq', pairs))  13.4 us
    ppermute x6, waiting for transfers between devices, row_scan(): received.append(lax.ppermute(total, 'seq', pairs))  10.2 us
    ppermute x12, starting transfers between devices, member_exchange(): got.append(lax.ppermute(piece, axis, pairs))  9.02 us
    pallas_call x1, Pallas kernels, middle_call(): pl.pallas_call(middle_body, grid=(rows // step,), in_specs=[row_block, ro...  7.29 us
    another operation x6, other arithmetic, row_scan(): jnp.stack([inner[index] + inner_keep[index] * entering for index in range...  4.35 us
    add x2, other arithmetic, row_scan(): total = mine[index] + keep_row[index] * total  3.89 us
  transfers between devices with their start and end apart: 18, of which 13 were waited for; matrix products, arithmetic and copies ran while one was open for 5% of the time, Pallas kernels for 13%

profile of v9, /device:TPU:1, one launch (start us, length us, event | category | flops | bytes accessed | tf_op | source)
XLA Modules:
  0.0 143.6 jit_solution(4272294148756902156)
XLA Ops:
  0.7 0.8 select_reduce_fusion.1
  1.6 0.8 copy.14.rel_ref
  2.5 4.6 %shard_map.84 = f32[16,128,128]{2,1,0:T(8,128)} custom-call(bf16[384,2048]{1,0:T(8,128)(2,1)} %key_ref.5, bf16[384,2048]{1,0:T(8,128)(2,1)} %value_ref.5, s32[384,1]{1,0:T(8,128)} %copy.14.rel_ref), custom_call_target="tpu_custom_call" | custom-call | tf_op jit(solution)/shard_map/pallas_call | solution.py:132
  7.1 1.1 copy-done.1
  8.3 2.6 %collective-permute-start = (f32[4,128,128]{2,1,0:T(8,128)S(1)}, f32[4,128,128]{2,1,0:T(8,128)S(1)}, u32[]{:S(2)}, u32[]{:S(2)}) collective-permute-start(f32[4,128,128]{2,1,0:T(8,128)S(1)} %get-tuple-element.108), channel_id=1, source_target_pairs={{0,1},{1,2},{2,3},{3,0},{4,5},{5,6},{6,7},{7,4},{8,9},{9,10},{10,1... | collective-permute-start | bytes 786440 | tf_op jit(solution)/shard_map/ppermute | solution.py:50
  11.8 0.6 fusion.18
  13.0 3.4 %collective-permute-done = f32[4,128,128]{2,1,0:T(8,128)S(1)} collective-permute-done((f32[4,128,128]{2,1,0:T(8,128)S(1)}, f32[4,128,128]{2,1,0:T(8,128)S(1)}, u32[]{:S(2)}, u32[]{:S(2)}) %collective-permute-start) | collective-permute-done | bytes 262176 | tf_op jit(solution)/shard_map/ppermute | solution.py:50
  16.5 5.6 %collective-permute-done.1 = f32[4,128,128]{2,1,0:T(8,128)S(1)} collective-permute-done((f32[4,128,128]{2,1,0:T(8,128)S(1)}, f32[4,128,128]{2,1,0:T(8,128)S(1)}, u32[]{:S(2)}, u32[]{:S(2)}) %collective-permute-start.1) | collective-permute-done | bytes 262176 | tf_op jit(solution)/shard_map/ppermute | solution.py:50
  22.1 0.5 collective-permute-done.2
  22.6 2.0 %fusion.7 = (f32[4,128,128]{2,1,0:T(8,128)S(1)}, f32[4,128,128]{2,1,0:T(8,128)S(1)}) fusion(f32[4,4,128,128]{3,2,1,0:T(8,128)S(1)} %bitcast_dynamic-update-slice_fusion.9, f32[]{:T(128)} %bitcast.8, f32[]{:T(128)} %bitcast.10, f32[]{:T(128)S(6)} %mul.209, f32[]{:T(128)} %bitcast.12), kind=kLoop, calls=%fused_computation.18 | loop fusion | flops 458752 | bytes 1572880 | tf_op jit(solution)/shard_map/add | solution.py:71
  24.6 4.0 %collective-permute-start.3 = (f32[4,128,128]{2,1,0:T(8,128)S(1)}, f32[4,128,128]{2,1,0:T(8,128)S(1)}, u32[]{:S(2)}, u32[]{:S(2)}) collective-permute-start(f32[4,128,128]{2,1,0:T(8,128)S(1)} %get-tuple-element.38), channel_id=1, source_target_pairs={{0,4},{1,5},{2,6},{3,7},{4,8},{5,9},{6,10},{7,11},{8,12},{9,13},{1... | collective-permute-start | bytes 786440 | tf_op jit(solution)/shard_map/ppermute | solution.py:81
  28.7 4.2 %collective-permute-start.4 = (f32[4,128,128]{2,1,0:T(8,128)S(1)}, f32[4,128,128]{2,1,0:T(8,128)S(1)}, u32[]{:S(2)}, u32[]{:S(2)}) collective-permute-start(f32[4,128,128]{2,1,0:T(8,128)S(1)} %get-tuple-element.38), channel_id=1, source_target_pairs={{0,8},{1,9},{2,10},{3,11},{4,12},{5,13},{6,14},{7,15},{16,24},{17,... | collective-permute-start | bytes 786440 | tf_op jit(solution)/shard_map/ppermute | solution.py:81
  32.9 1.3 collective-permute-start.5
  36.1 0.6 subtract_reduce_fusion
  36.8 0.6 subtract_reduce_fusion.1
  38.7 0.8 copy.15.rel_ref
  39.5 7.7 %shard_map.85 = (bf16[16,384,384]{2,1,0:T(8,128)(2,1)}, f32[384,2048]{1,0:T(8,128)}) custom-call(bf16[384,2048]{1,0:T(8,128)(2,1)} %query_ref.3, bf16[384,2048]{1,0:T(8,128)(2,1)} %key_ref.5, bf16[384,2048]{1,0:T(8,128)(2,1)} %value_ref.5, s32[384,1]{1,0:T(8,128)} %copy.15.rel_ref), custom_call_target="tpu_custom_call" | custom-call | tf_op jit(solution)/shard_map/pallas_call | solution.py:132
  47.2 1.4 add_bitcast_fusion.5
  48.6 0.7 add_bitcast_fusion.4
  50.1 1.2 collective-permute-start.7
  52.0 2.4 %collective-permute-done.6 = f32[4,128,128]{2,1,0:T(8,128)S(1)} collective-permute-done((f32[4,128,128]{2,1,0:T(8,128)S(1)}, f32[4,128,128]{2,1,0:T(8,128)S(1)}, u32[]{:S(2)}, u32[]{:S(2)}) %collective-permute-start.6) | collective-permute-done | bytes 262176 | tf_op jit(solution)/shard_map/ppermute | solution.py:50
  54.4 8.2 %collective-permute-done.7 = f32[4,128,128]{2,1,0:T(8,128)S(1)} collective-permute-done((f32[4,128,128]{2,1,0:T(8,128)S(1)}, f32[4,128,128]{2,1,0:T(8,128)S(1)}, u32[]{:S(2)}, u32[]{:S(2)}) %collective-permute-start.7) | collective-permute-done | bytes 262176 | tf_op jit(solution)/shard_map/ppermute | solution.py:50
  62.6 0.8 collective-permute-done.8
  63.5 1.0 copy-done
  64.5 7.3 %shard_map.86 = (bf16[384,2048]{1,0:T(8,128)(2,1)}, bf16[384,2048]{1,0:T(8,128)(2,1)}, f32[16,128,128]{2,1,0:T(8,128)}) custom-call(bf16[384,2048]{1,0:T(8,128)(2,1)} %query_ref.3, f32[384,2048]{1,0:T(8,128)} %get-tuple-element.45.inside_ref, f32[16,128,128]{2,1,0:T(8,128)} %bitcast.122, bf16[384,2048]{1,0:T(8,128)(2,1)} %cot_ref.1, s32[384,1]{1,0:T(8,128)} %copy.14.rel_ref), custom_call_target="tpu_custom_call" | custom-call | tf_op jit(solution)/shard_map/pallas_call | solution.py:238
  71.9 1.1 copy-done.2
  73.4 0.7 fusion.17
  74.8 0.8 collective-permute-start.11
  75.6 2.4 %collective-permute-done.9 = f32[4,128,128]{2,1,0:T(8,128)S(1)} collective-permute-done((f32[4,128,128]{2,1,0:T(8,128)S(1)}, f32[4,128,128]{2,1,0:T(8,128)S(1)}, u32[]{:S(2)}, u32[]{:S(2)}) %collective-permute-start.9) | collective-permute-done | bytes 262176 | tf_op jit(solution)/shard_map/ppermute | solution.py:50
  78.0 5.6 %collective-permute-done.10 = f32[4,128,128]{2,1,0:T(8,128)S(1)} collective-permute-done((f32[4,128,128]{2,1,0:T(8,128)S(1)}, f32[4,128,128]{2,1,0:T(8,128)S(1)}, u32[]{:S(2)}, u32[]{:S(2)}) %collective-permute-start.10) | collective-permute-done | bytes 262176 | tf_op jit(solution)/shard_map/ppermute | solution.py:50
  83.6 1.9 %collective-permute-done.11 = f32[4,128,128]{2,1,0:T(8,128)S(1)} collective-permute-done((f32[4,128,128]{2,1,0:T(8,128)S(1)}, f32[4,128,128]{2,1,0:T(8,128)S(1)}, u32[]{:S(2)}, u32[]{:S(2)}) %collective-permute-start.11) | collective-permute-done | bytes 262176 | tf_op jit(solution)/shard_map/ppermute | solution.py:50
  85.6 1.9 %fusion.3 = (f32[4,128,128]{2,1,0:T(8,128)S(1)}, f32[4,128,128]{2,1,0:T(8,128)S(1)}) fusion(f32[4,4,128,128]{3,2,1,0:T(8,128)S(1)} %bitcast_dynamic-update-slice_fusion.3, f32[]{:T(128)} %bitcast.34, f32[]{:T(128)} %bitcast.36, f32[]{:T(128)S(6)} %mul.234, f32[]{:T(128)} %bitcast.38), kind=kLoop, calls=%fused_computation.10 | loop fusion | flops 458752 | bytes 1572880 | tf_op jit(solution)/shard_map/add | solution.py:71
  87.5 1.3 collective-permute-start.12
  88.8 1.3 collective-permute-start.13
  90.1 1.3 collective-permute-start.14
  93.3 0.6 fusion.13
  93.9 0.7 fusion.14
  96.0 0.8 copy.17.rel_ref
  96.8 11.7 %shard_map.87 = (bf16[384,2048]{1,0:T(8,128)(2,1)}, f32[384,2048]{1,0:T(8,128)}, f32[384,2048]{1,0:T(8,128)}) custom-call(bf16[384,2048]{1,0:T(8,128)(2,1)} %query_ref.3, bf16[384,2048]{1,0:T(8,128)(2,1)} %key_ref.5, bf16[384,2048]{1,0:T(8,128)(2,1)} %value_ref.5, bf16[384,2048]{1,0:T(8,128)(2,1)} %get-tuple-element.57.grad_ref, ...), custom_call_target="tpu_custom_call" | custom-call | tf_op jit(solution)/shard_map/pallas_call | solution.py:132
  108.5 10.1 %collective-permute-done.13 = f32[4,128,128]{2,1,0:T(8,128)S(1)} collective-permute-done((f32[4,128,128]{2,1,0:T(8,128)S(1)}, f32[4,128,128]{2,1,0:T(8,128)S(1)}, u32[]{:S(2)}, u32[]{:S(2)}) %collective-permute-start.13) | collective-permute-done | bytes 262176 | tf_op jit(solution)/shard_map/ppermute | solution.py:81
  118.6 1.4 add_bitcast_fusion.2
  120.0 0.7 add_bitcast_fusion.1
  121.1 2.5 %collective-permute-start.16 = (f32[4,128,128]{2,1,0:T(8,128)S(1)}, f32[4,128,128]{2,1,0:T(8,128)S(1)}, u32[]{:S(2)}, u32[]{:S(2)}) collective-permute-start(f32[4,128,128]{2,1,0:T(8,128)S(1)} %get-tuple-element.95), channel_id=1, source_target_pairs={{0,2},{1,3},{2,0},{3,1},{4,6},{5,7},{6,4},{7,5},{8,10},{9,11},{10,... | collective-permute-start | bytes 786440 | tf_op jit(solution)/shard_map/ppermute | solution.py:50
  123.6 0.6 compare_reduce_fusion
  125.4 9.7 %collective-permute-done.16 = f32[4,128,128]{2,1,0:T(8,128)S(1)} collective-permute-done((f32[4,128,128]{2,1,0:T(8,128)S(1)}, f32[4,128,128]{2,1,0:T(8,128)S(1)}, u32[]{:S(2)}, u32[]{:S(2)}) %collective-permute-start.16) | collective-permute-done | bytes 262176 | tf_op jit(solution)/shard_map/ppermute | solution.py:50
  135.2 0.6 collective-permute-done.17
  135.8 0.9 multiply_convert_fusion
  136.7 6.8 %shard_map.88 = (bf16[384,2048]{1,0:T(8,128)(2,1)}, bf16[384,2048]{1,0:T(8,128)(2,1)}) custom-call(bf16[384,2048]{1,0:T(8,128)(2,1)} %key_ref.5, bf16[384,2048]{1,0:T(8,128)(2,1)} %value_ref.5, f32[384,2048]{1,0:T(8,128)} %get-tuple-element.65.key_part, f32[384,2048]{1,0:T(8,128)} %get-tuple-element.66.value_part, bf16[16,128,128]{2,1,0:T(8,128)(2,1)} %bitcast.127, ...), custom_call_target="tpu_custom_call" | custom-call | tf_op jit(solution)/shard_map/pallas_call | solution.py:132
  (52 shorter events, 4.1 us)
Async XLA Ops:
  7.0 1.2 copy-start.1
  8.3 8.1 %collective-permute-start = (f32[4,128,128]{2,1,0:T(8,128)S(1)}, f32[4,128,128]{2,1,0:T(8,128)S(1)}, u32[]{:S(2)}, u32[]{:S(2)}) collective-permute-start(f32[4,128,128]{2,1,0:T(8,128)S(1)} %get-tuple-element.108), channel_id=1, source_target_pairs={{0,1},{1,2},{2,3},{3,0},{4,5},{5,6},{6,7},{7,4},{8,9},{9,10},{10,1... | collective-permute-start | bytes 786440 | tf_op jit(solution)/shard_map/ppermute | solution.py:50
  11.0 11.1 %collective-permute-start.1 = (f32[4,128,128]{2,1,0:T(8,128)S(1)}, f32[4,128,128]{2,1,0:T(8,128)S(1)}, u32[]{:S(2)}, u32[]{:S(2)}) collective-permute-start(f32[4,128,128]{2,1,0:T(8,128)S(1)} %get-tuple-element.107), channel_id=1, source_target_pairs={{0,2},{1,3},{2,0},{3,1},{4,6},{5,7},{6,4},{7,5},{8,10},{9,11},{10,... | collective-permute-start | bytes 786440 | tf_op jit(solution)/shard_map/ppermute | solution.py:50
  11.0 11.6 %collective-permute-start.2 = (f32[4,128,128]{2,1,0:T(8,128)S(1)}, f32[4,128,128]{2,1,0:T(8,128)S(1)}, u32[]{:S(2)}, u32[]{:S(2)}) collective-permute-start(f32[4,128,128]{2,1,0:T(8,128)S(1)} %get-tuple-element.106), channel_id=1, source_target_pairs={{0,3},{1,0},{2,1},{3,2},{4,7},{5,4},{6,5},{7,6},{8,11},{9,8},{10,9... | collective-permute-start | bytes 786440 | tf_op jit(solution)/shard_map/ppermute | solution.py:50
  24.6 22.6 %collective-permute-start.3 = (f32[4,128,128]{2,1,0:T(8,128)S(1)}, f32[4,128,128]{2,1,0:T(8,128)S(1)}, u32[]{:S(2)}, u32[]{:S(2)}) collective-permute-start(f32[4,128,128]{2,1,0:T(8,128)S(1)} %get-tuple-element.38), channel_id=1, source_target_pairs={{0,4},{1,5},{2,6},{3,7},{4,8},{5,9},{6,10},{7,11},{8,12},{9,13},{1... | collective-permute-start | bytes 786440 | tf_op jit(solution)/shard_map/ppermute | solution.py:81
  28.7 18.6 %collective-permute-start.4 = (f32[4,128,128]{2,1,0:T(8,128)S(1)}, f32[4,128,128]{2,1,0:T(8,128)S(1)}, u32[]{:S(2)}, u32[]{:S(2)}) collective-permute-start(f32[4,128,128]{2,1,0:T(8,128)S(1)} %get-tuple-element.38), channel_id=1, source_target_pairs={{0,8},{1,9},{2,10},{3,11},{4,12},{5,13},{6,14},{7,15},{16,24},{17,... | collective-permute-start | bytes 786440 | tf_op jit(solution)/shard_map/ppermute | solution.py:81
  32.9 14.3 %collective-permute-start.5 = (f32[4,128,128]{2,1,0:T(8,128)S(1)}, f32[4,128,128]{2,1,0:T(8,128)S(1)}, u32[]{:S(2)}, u32[]{:S(2)}) collective-permute-start(f32[4,128,128]{2,1,0:T(8,128)S(1)} %get-tuple-element.38), channel_id=1, source_target_pairs={{0,12},{1,13},{2,14},{3,15},{16,28},{17,29},{18,30},{19,31}} | collective-permute-start | bytes 786440 | tf_op jit(solution)/shard_map/ppermute | solution.py:81
  49.6 4.8 %collective-permute-start.6 = (f32[4,128,128]{2,1,0:T(8,128)S(1)}, f32[4,128,128]{2,1,0:T(8,128)S(1)}, u32[]{:S(2)}, u32[]{:S(2)}) collective-permute-start(f32[4,128,128]{2,1,0:T(8,128)S(1)} %get-tuple-element.104), channel_id=1, source_target_pairs={{0,1},{1,2},{2,3},{3,0},{4,5},{5,6},{6,7},{7,4},{8,9},{9,10},{10,1... | collective-permute-start | bytes 786440 | tf_op jit(solution)/shard_map/ppermute | solution.py:50
  50.1 12.6 %collective-permute-start.7 = (f32[4,128,128]{2,1,0:T(8,128)S(1)}, f32[4,128,128]{2,1,0:T(8,128)S(1)}, u32[]{:S(2)}, u32[]{:S(2)}) collective-permute-start(f32[4,128,128]{2,1,0:T(8,128)S(1)} %get-tuple-element.103), channel_id=1, source_target_pairs={{0,2},{1,3},{2,0},{3,1},{4,6},{5,7},{6,4},{7,5},{8,10},{9,11},{10,... | collective-permute-start | bytes 786440 | tf_op jit(solution)/shard_map/ppermute | solution.py:50
  51.5 11.9 %collective-permute-start.8 = (f32[4,128,128]{2,1,0:T(8,128)S(1)}, f32[4,128,128]{2,1,0:T(8,128)S(1)}, u32[]{:S(2)}, u32[]{:S(2)}) collective-permute-start(f32[4,128,128]{2,1,0:T(8,128)S(1)} %get-tuple-element.102), channel_id=1, source_target_pairs={{0,3},{1,0},{2,1},{3,2},{4,7},{5,4},{6,5},{7,6},{8,11},{9,8},{10,9... | collective-permute-start | bytes 786440 | tf_op jit(solution)/shard_map/ppermute | solution.py:50
  63.5 1.0 copy-start
  71.7 1.2 copy-start.2
  73.0 5.0 %collective-permute-start.9 = (f32[4,128,128]{2,1,0:T(8,128)S(1)}, f32[4,128,128]{2,1,0:T(8,128)S(1)}, u32[]{:S(2)}, u32[]{:S(2)}) collective-permute-start(f32[4,128,128]{2,1,0:T(8,128)S(1)} %get-tuple-element.100), channel_id=1, source_target_pairs={{0,1},{1,2},{2,3},{3,0},{4,5},{5,6},{6,7},{7,4},{8,9},{9,10},{10,1... | collective-permute-start | bytes 786440 | tf_op jit(solution)/shard_map/ppermute | solution.py:50
  73.1 10.5 %collective-permute-start.10 = (f32[4,128,128]{2,1,0:T(8,128)S(1)}, f32[4,128,128]{2,1,0:T(8,128)S(1)}, u32[]{:S(2)}, u32[]{:S(2)}) collective-permute-start(f32[4,128,128]{2,1,0:T(8,128)S(1)} %get-tuple-element.99), channel_id=1, source_target_pairs={{0,2},{1,3},{2,0},{3,1},{4,6},{5,7},{6,4},{7,5},{8,10},{9,11},{10,... | collective-permute-start | bytes 786440 | tf_op jit(solution)/shard_map/ppermute | solution.py:50
  74.8 10.7 %collective-permute-start.11 = (f32[4,128,128]{2,1,0:T(8,128)S(1)}, f32[4,128,128]{2,1,0:T(8,128)S(1)}, u32[]{:S(2)}, u32[]{:S(2)}) collective-permute-start(f32[4,128,128]{2,1,0:T(8,128)S(1)} %get-tuple-element.98), channel_id=1, source_target_pairs={{0,3},{1,0},{2,1},{3,2},{4,7},{5,4},{6,5},{7,6},{8,11},{9,8},{10,9... | collective-permute-start | bytes 786440 | tf_op jit(solution)/shard_map/ppermute | solution.py:50
  87.5 21.0 %collective-permute-start.12 = (f32[4,128,128]{2,1,0:T(8,128)S(1)}, f32[4,128,128]{2,1,0:T(8,128)S(1)}, u32[]{:S(2)}, u32[]{:S(2)}) collective-permute-start(f32[4,128,128]{2,1,0:T(8,128)S(1)} %get-tuple-element.53), channel_id=1, source_target_pairs={{4,0},{5,1},{6,2},{7,3},{8,4},{9,5},{10,6},{11,7},{12,8},{13,9},{1... | collective-permute-start | bytes 786440 | tf_op jit(solution)/shard_map/ppermute | solution.py:81
  88.8 29.8 %collective-permute-start.13 = (f32[4,128,128]{2,1,0:T(8,128)S(1)}, f32[4,128,128]{2,1,0:T(8,128)S(1)}, u32[]{:S(2)}, u32[]{:S(2)}) collective-permute-start(f32[4,128,128]{2,1,0:T(8,128)S(1)} %get-tuple-element.53), channel_id=1, source_target_pairs={{8,0},{9,1},{10,2},{11,3},{12,4},{13,5},{14,6},{15,7},{24,16},{25,... | collective-permute-start | bytes 786440 | tf_op jit(solution)/shard_map/ppermute | solution.py:81
  90.1 28.6 %collective-permute-start.14 = (f32[4,128,128]{2,1,0:T(8,128)S(1)}, f32[4,128,128]{2,1,0:T(8,128)S(1)}, u32[]{:S(2)}, u32[]{:S(2)}) collective-permute-start(f32[4,128,128]{2,1,0:T(8,128)S(1)} %get-tuple-element.53), channel_id=1, source_target_pairs={{12,0},{13,1},{14,2},{15,3},{28,16},{29,17},{30,18},{31,19}} | collective-permute-start | bytes 786440 | tf_op jit(solution)/shard_map/ppermute | solution.py:81
  121.0 4.4 %collective-permute-start.15 = (f32[4,128,128]{2,1,0:T(8,128)S(1)}, f32[4,128,128]{2,1,0:T(8,128)S(1)}, u32[]{:S(2)}, u32[]{:S(2)}) collective-permute-start(f32[4,128,128]{2,1,0:T(8,128)S(1)} %get-tuple-element.96), channel_id=1, source_target_pairs={{0,1},{1,2},{2,3},{3,0},{4,5},{5,6},{6,7},{7,4},{8,9},{9,10},{10,1... | collective-permute-start | bytes 786440 | tf_op jit(solution)/shard_map/ppermute | solution.py:50
  121.1 14.0 %collective-permute-start.16 = (f32[4,128,128]{2,1,0:T(8,128)S(1)}, f32[4,128,128]{2,1,0:T(8,128)S(1)}, u32[]{:S(2)}, u32[]{:S(2)}) collective-permute-start(f32[4,128,128]{2,1,0:T(8,128)S(1)} %get-tuple-element.95), channel_id=1, source_target_pairs={{0,2},{1,3},{2,0},{3,1},{4,6},{5,7},{6,4},{7,5},{8,10},{9,11},{10,... | collective-permute-start | bytes 786440 | tf_op jit(solution)/shard_map/ppermute | solution.py:50
  124.9 10.9 %collective-permute-start.17 = (f32[4,128,128]{2,1,0:T(8,128)S(1)}, f32[4,128,128]{2,1,0:T(8,128)S(1)}, u32[]{:S(2)}, u32[]{:S(2)}) collective-permute-start(f32[4,128,128]{2,1,0:T(8,128)S(1)} %get-tuple-element.94), channel_id=1, source_target_pairs={{0,3},{1,0},{2,1},{3,2},{4,7},{5,4},{6,5},{7,6},{8,11},{9,8},{10,9... | collective-permute-start | bytes 786440 | tf_op jit(solution)/shard_map/ppermute | solution.py:50

commit v10 on v9

--- a/solution.py
+++ b/solution.py
@@ -124,7 +124,7 @@
     def spec(shape):
         if len(shape) == 3:
             return pl.BlockSpec((HEAD_STEP,) + shape[1:], lambda g: (g, 0, 0))
-        if shape[1] == rows or shape[1] == 1:
+        if shape[1] == rows or shape[1] <= HEAD:
             return pl.BlockSpec(shape, lambda g: (0, 0))
         return pl.BlockSpec((shape[0], HEAD_STEP * HEAD), lambda g: (0, g))
 
@@ -148,9 +148,9 @@
 
 
 def row_masks(rel_ref, rows):
-    rel = rel_ref[rows]
-    tail = rel == rel_ref[-1:, :]
-    lead = rel_ref[0:1, :]
+    rel = rel_ref[rows, 0:1]
+    tail = rel == rel_ref[-1:, 0:1]
+    lead = rel_ref[0:1, 0:1]
     carry = (rel == lead) & (lead < 0)
     return rel, tail, carry
 
@@ -163,7 +163,7 @@
 
 
 def gated(prefix, rel_ref):
-    return zeroed(rel_ref[0:1, :] < 0, prefix).astype(jnp.bfloat16)
+    return zeroed(rel_ref[0:1, 0:1] < 0, prefix).astype(jnp.bfloat16)
 
 
 def state_body(key_ref, value_ref, rel_ref, state_ref):
@@ -173,7 +173,7 @@
 
 
 def inside_body(query_ref, key_ref, value_ref, rel_ref, weight_ref, inside_ref):
-    keep = keep_mask(rel_ref[...])
+    keep = keep_mask(rel_ref[:, 0:1])
     for i in range(HEAD_STEP):
         scores = mm(query_ref[:, columns(i)], key_ref[:, columns(i)], NT)
         weights = zeroed(keep, scores).astype(jnp.bfloat16)
@@ -196,9 +196,11 @@
 
 def tail_body(key_ref, value_ref, key_part, value_part, suffix_ref, rel_ref, key_out, value_out):
     _, tail, _ = row_masks(rel_ref, slice(None))
+    opened = rel_ref[0:1, 1:2] > 0
     for i in range(HEAD_STEP):
-        key_carry = zeroed(tail, mm(value_ref[:, columns(i)], suffix_ref[i], NT))
-        value_carry = zeroed(tail, mm(key_ref[:, columns(i)], suffix_ref[i], NN))
+        suffix = zeroed(opened, suffix_ref[i]).astype(jnp.bfloat16)
+        key_carry = zeroed(tail, mm(value_ref[:, columns(i)], suffix, NT))
+        value_carry = zeroed(tail, mm(key_ref[:, columns(i)], suffix, NN))
         key_out[:, columns(i)] = (key_part[:, columns(i)] + key_carry).astype(jnp.bfloat16)
         value_out[:, columns(i)] = (value_part[:, columns(i)] + value_carry).astype(jnp.bfloat16)
 
@@ -259,7 +261,10 @@
     order = lax.iota(jnp.int32, lengths.shape[0])
     starts = jnp.sum(jnp.where(order[None, :] < order[:, None], lengths[None, :], 0), axis=1)
     doc_start = jnp.max(jnp.where(starts[None, :] <= position[:, None], starts[None, :], 0), axis=1)
-    rel = (doc_start - first_row)[:, None]
+    next_first = first_row + row_count
+    next_open = (next_first < lax.axis_size("seq") * row_count) & jnp.logical_not(jnp.any(starts == next_first))
+    lane = lax.broadcasted_iota(jnp.int32, (row_count, 128), 1)
+    rel = jnp.where(lane == 0, (doc_start - first_row)[:, None], jnp.where(lane == 1, next_open.astype(jnp.int32), 0))
     f32 = jnp.float32
     state_shape = jax.ShapeDtypeStruct((head_count, HEAD, HEAD), f32)
     wide = jax.ShapeDtypeStruct((row_count, feat_width), f32)
@@ -267,7 +272,7 @@
     (state_local,) = head_call(state_body, [keys, values, rel], [state_shape])
     has_start = jnp.any((starts >= first_row) & (starts < first_row + row_count))
     continues = jnp.logical_not(jnp.any(starts == first_row))
-    stops_back = jnp.logical_or(rel[0, 0] != rel[row_count - 1, 0], jnp.logical_not(continues))
+    stops_back = jnp.logical_or(doc_start[0] != doc_start[row_count - 1], jnp.logical_not(continues))
     start_flag = has_start.astype(f32).reshape(1, 1, 1)
 
     def start_keep(blocks):
@@ -289,11 +294,8 @@
         lambda *xs: head_call(grad_body, list(xs), [low, wide, wide]),
         (queries, keys, values, grad_low, weights, prefix, rel),
     )
-    next_first = first_row + row_count
-    next_open = (next_first < lax.axis_size("seq") * row_count) & jnp.logical_not(jnp.any(starts == next_first))
-    suffix_low = (suffix * next_open.astype(f32)).astype(jnp.bfloat16)
     grad_keys, grad_values = head_call(
-        tail_body, [keys, values, keys_part, values_part, suffix_low, rel], [low, low]
+        tail_body, [keys, values, keys_part, values_part, suffix, rel], [low, low]
     )
     return attn_out, grad_queries, grad_keys, grad_values
 

time: 144 us -> 146 us (1.014)
  waiting for transfers between devices: 51.8 us -> 55.2 us
  local copies, waits for them, and re-layouts: 7.89 us -> 6.33 us
    ppermute x6, waiting for transfers between devices: 10.2 us -> 12 us  [row_scan(): received.append(lax.ppermute(total, 'seq', pairs))]
    optimization_barrier x2 -> x0, local copies, waits for them, and re-layouts: 1.64 us -> none  [row_scan(): total, filler_inputs = lax.optimization_barrier((total, filler_inputs))]
    ppermute x12, waiting for transfers between devices: 41.7 us -> 43.2 us  [member_exchange(): got.append(lax.ppermute(piece, axis, pairs))]
    unnamed x6 -> x8, local copies, waits for them, and re-layouts: 3.21 us -> 4.19 us
  transfers between devices with their start and end apart: 18 -> 18, of which waited for: 13 -> 13; matrix products, arithmetic and copies ran while one was open for 5% -> 3% of each run, Pallas kernels for 13% -> 13%
where the time goes in v10:
time: 146 us; the launch traced here: 145 us
  waiting for transfers between devices  55.2 us (38%)
  Pallas kernels  38.4 us (26%)
  starting transfers between devices  22.4 us (15%)
  other arithmetic  13.5 us (9%)
  between operations  9.31 us (6%)
  local copies, waits for them, and re-layouts  6.33 us (4%)
    ppermute x12, waiting for transfers between devices, member_exchange(): got.append(lax.ppermute(piece, axis, pairs))  43.2 us
    pallas_call x4, Pallas kernels, head_call(): pl.pallas_call(body, grid=(heads // HEAD_STEP,), in_specs=[spec(x.shape)...  31.1 us
    ppermute x6, starting transfers between devices, row_scan(): received.append(lax.ppermute(total, 'seq', pairs))  13.4 us
    ppermute x6, waiting for transfers between devices, row_scan(): received.append(lax.ppermute(total, 'seq', pairs))  12 us
    ppermute x12, starting transfers between devices, member_exchange(): got.append(lax.ppermute(piece, axis, pairs))  8.96 us
    pallas_call x1, Pallas kernels, middle_call(): pl.pallas_call(middle_body, grid=(rows // step,), in_specs=[row_block, ro...  7.29 us
    unnamed x8, local copies, waits for them, and re-layouts  4.19 us
    another operation x6, other arithmetic, row_scan(): jnp.stack([inner[index] + inner_keep[index] * entering for index in range...  4.17 us
  transfers between devices with their start and end apart: 18, of which 13 were waited for; matrix products, arithmetic and copies ran while one was open for 3% of the time, Pallas kernels for 13%

profile of v10, /device:TPU:1, one launch (start us, length us, event | category | flops | bytes accessed | tf_op | source)
XLA Modules:
  0.0 145.1 jit_solution(18147407726907768563)
XLA Ops:
  0.7 0.8 select_reduce_fusion.1
  1.5 0.6 compare_reduce_fusion.3
  2.9 0.8 broadcast_select_fusion.rel_ref
  3.8 4.6 %shard_map.84 = f32[16,128,128]{2,1,0:T(8,128)} custom-call(bf16[384,2048]{1,0:T(8,128)(2,1)} %key_ref.5, bf16[384,2048]{1,0:T(8,128)(2,1)} %value_ref.5, s32[384,128]{1,0:T(8,128)} %broadcast_select_fusion.rel_ref), custom_call_target="tpu_custom_call" | custom-call | tf_op jit(solution)/shard_map/pallas_call | solution.py:132
  8.4 1.1 copy-done.1
  9.6 2.6 %collective-permute-start = (f32[4,128,128]{2,1,0:T(8,128)S(1)}, f32[4,128,128]{2,1,0:T(8,128)S(1)}, u32[]{:S(2)}, u32[]{:S(2)}) collective-permute-start(f32[4,128,128]{2,1,0:T(8,128)S(1)} %get-tuple-element.108), channel_id=1, source_target_pairs={{0,1},{1,2},{2,3},{3,0},{4,5},{5,6},{6,7},{7,4},{8,9},{9,10},{10,1... | collective-permute-start | bytes 786440 | tf_op jit(solution)/shard_map/ppermute | solution.py:50
  12.3 0.5 collective-permute-start.2
  13.1 0.6 fusion.18
  14.3 3.4 %collective-permute-done = f32[4,128,128]{2,1,0:T(8,128)S(1)} collective-permute-done((f32[4,128,128]{2,1,0:T(8,128)S(1)}, f32[4,128,128]{2,1,0:T(8,128)S(1)}, u32[]{:S(2)}, u32[]{:S(2)}) %collective-permute-start) | collective-permute-done | bytes 262176 | tf_op jit(solution)/shard_map/ppermute | solution.py:50
  17.8 5.6 %collective-permute-done.1 = f32[4,128,128]{2,1,0:T(8,128)S(1)} collective-permute-done((f32[4,128,128]{2,1,0:T(8,128)S(1)}, f32[4,128,128]{2,1,0:T(8,128)S(1)}, u32[]{:S(2)}, u32[]{:S(2)}) %collective-permute-start.1) | collective-permute-done | bytes 262176 | tf_op jit(solution)/shard_map/ppermute | solution.py:50
  23.4 0.5 collective-permute-done.2
  23.9 2.0 %fusion.7 = (f32[4,128,128]{2,1,0:T(8,128)S(1)}, f32[4,128,128]{2,1,0:T(8,128)S(1)}) fusion(f32[4,4,128,128]{3,2,1,0:T(8,128)S(1)} %bitcast_dynamic-update-slice_fusion.9, f32[]{:T(128)} %bitcast.8, f32[]{:T(128)} %bitcast.10, f32[]{:T(128)S(6)} %mul.202, f32[]{:T(128)} %bitcast.12), kind=kLoop, calls=%fused_computation.17 | loop fusion | flops 458752 | bytes 1572880 | tf_op jit(solution)/shard_map/add | solution.py:71
  25.9 4.0 %collective-permute-start.3 = (f32[4,128,128]{2,1,0:T(8,128)S(1)}, f32[4,128,128]{2,1,0:T(8,128)S(1)}, u32[]{:S(2)}, u32[]{:S(2)}) collective-permute-start(f32[4,128,128]{2,1,0:T(8,128)S(1)} %get-tuple-element.38), channel_id=1, source_target_pairs={{0,4},{1,5},{2,6},{3,7},{4,8},{5,9},{6,10},{7,11},{8,12},{9,13},{1... | collective-permute-start | bytes 786440 | tf_op jit(solution)/shard_map/ppermute | solution.py:81
  30.0 4.2 %collective-permute-start.4 = (f32[4,128,128]{2,1,0:T(8,128)S(1)}, f32[4,128,128]{2,1,0:T(8,128)S(1)}, u32[]{:S(2)}, u32[]{:S(2)}) collective-permute-start(f32[4,128,128]{2,1,0:T(8,128)S(1)} %get-tuple-element.38), channel_id=1, source_target_pairs={{0,8},{1,9},{2,10},{3,11},{4,12},{5,13},{6,14},{7,15},{16,24},{17,... | collective-permute-start | bytes 786440 | tf_op jit(solution)/shard_map/ppermute | solution.py:81
  34.2 1.3 collective-permute-start.5
  37.4 0.6 subtract_reduce_fusion
  38.1 0.6 subtract_reduce_fusion.1
  40.0 7.7 %shard_map.85 = (bf16[16,384,384]{2,1,0:T(8,128)(2,1)}, f32[384,2048]{1,0:T(8,128)}) custom-call(bf16[384,2048]{1,0:T(8,128)(2,1)} %query_ref.3, bf16[384,2048]{1,0:T(8,128)(2,1)} %key_ref.5, bf16[384,2048]{1,0:T(8,128)(2,1)} %value_ref.5, s32[384,128]{1,0:T(8,128)} %broadcast_select_fusion.rel_ref), custom_call_target="tpu_custom_call" | custom-call | tf_op jit(solution)/shard_map/pallas_call | solution.py:132
  47.7 1.4 add_bitcast_fusion.5
  49.1 0.7 add_bitcast_fusion.4
  50.6 1.2 collective-permute-start.7
  52.5 2.4 %collective-permute-done.6 = f32[4,128,128]{2,1,0:T(8,128)S(1)} collective-permute-done((f32[4,128,128]{2,1,0:T(8,128)S(1)}, f32[4,128,128]{2,1,0:T(8,128)S(1)}, u32[]{:S(2)}, u32[]{:S(2)}) %collective-permute-start.6) | collective-permute-done | bytes 262176 | tf_op jit(solution)/shard_map/ppermute | solution.py:50
  54.9 8.2 %collective-permute-done.7 = f32[4,128,128]{2,1,0:T(8,128)S(1)} collective-permute-done((f32[4,128,128]{2,1,0:T(8,128)S(1)}, f32[4,128,128]{2,1,0:T(8,128)S(1)}, u32[]{:S(2)}, u32[]{:S(2)}) %collective-permute-start.7) | collective-permute-done | bytes 262176 | tf_op jit(solution)/shard_map/ppermute | solution.py:50
  63.2 0.8 collective-permute-done.8
  64.0 1.0 copy-done
  65.0 7.3 %shard_map.86 = (bf16[384,2048]{1,0:T(8,128)(2,1)}, bf16[384,2048]{1,0:T(8,128)(2,1)}, f32[16,128,128]{2,1,0:T(8,128)}) custom-call(bf16[384,2048]{1,0:T(8,128)(2,1)} %query_ref.3, f32[384,2048]{1,0:T(8,128)} %get-tuple-element.45.inside_ref, f32[16,128,128]{2,1,0:T(8,128)} %bitcast.122, bf16[384,2048]{1,0:T(8,128)(2,1)} %cot_ref.1, ...), custom_call_target="tpu_custom_call" | custom-call | tf_op jit(solution)/shard_map/pallas_call | solution.py:240
  72.4 1.1 copy-done.3
  73.9 0.6 fusion.17
  75.1 0.8 collective-permute-start.11
  75.9 2.6 %collective-permute-done.9 = f32[4,128,128]{2,1,0:T(8,128)S(1)} collective-permute-done((f32[4,128,128]{2,1,0:T(8,128)S(1)}, f32[4,128,128]{2,1,0:T(8,128)S(1)}, u32[]{:S(2)}, u32[]{:S(2)}) %collective-permute-start.9) | collective-permute-done | bytes 262176 | tf_op jit(solution)/shard_map/ppermute | solution.py:50
  78.5 5.6 %collective-permute-done.10 = f32[4,128,128]{2,1,0:T(8,128)S(1)} collective-permute-done((f32[4,128,128]{2,1,0:T(8,128)S(1)}, f32[4,128,128]{2,1,0:T(8,128)S(1)}, u32[]{:S(2)}, u32[]{:S(2)}) %collective-permute-start.10) | collective-permute-done | bytes 262176 | tf_op jit(solution)/shard_map/ppermute | solution.py:50
  84.2 1.9 %collective-permute-done.11 = f32[4,128,128]{2,1,0:T(8,128)S(1)} collective-permute-done((f32[4,128,128]{2,1,0:T(8,128)S(1)}, f32[4,128,128]{2,1,0:T(8,128)S(1)}, u32[]{:S(2)}, u32[]{:S(2)}) %collective-permute-start.11) | collective-permute-done | bytes 262176 | tf_op jit(solution)/shard_map/ppermute | solution.py:50
  86.1 1.9 %fusion.3 = (f32[4,128,128]{2,1,0:T(8,128)S(1)}, f32[4,128,128]{2,1,0:T(8,128)S(1)}) fusion(f32[4,4,128,128]{3,2,1,0:T(8,128)S(1)} %bitcast_dynamic-update-slice_fusion.3, f32[]{:T(128)} %bitcast.34, f32[]{:T(128)} %bitcast.36, f32[]{:T(128)S(6)} %mul.227, f32[]{:T(128)} %bitcast.38), kind=kLoop, calls=%fused_computation.9 | loop fusion | flops 458752 | bytes 1572880 | tf_op jit(solution)/shard_map/add | solution.py:71
  88.0 1.3 collective-permute-start.12
  89.3 1.3 collective-permute-start.13
  90.6 1.3 collective-permute-start.14
  93.7 0.6 fusion.13
  94.3 0.7 fusion.14
  96.3 11.7 %shard_map.87 = (bf16[384,2048]{1,0:T(8,128)(2,1)}, f32[384,2048]{1,0:T(8,128)}, f32[384,2048]{1,0:T(8,128)}) custom-call(bf16[384,2048]{1,0:T(8,128)(2,1)} %query_ref.3, bf16[384,2048]{1,0:T(8,128)(2,1)} %key_ref.5, bf16[384,2048]{1,0:T(8,128)(2,1)} %value_ref.5, bf16[384,2048]{1,0:T(8,128)(2,1)} %get-tuple-element.57.grad_ref, ...), custom_call_target="tpu_custom_call" | custom-call | tf_op jit(solution)/shard_map/pallas_call | solution.py:132
  107.9 12.0 %collective-permute-done.13 = f32[4,128,128]{2,1,0:T(8,128)S(1)} collective-permute-done((f32[4,128,128]{2,1,0:T(8,128)S(1)}, f32[4,128,128]{2,1,0:T(8,128)S(1)}, u32[]{:S(2)}, u32[]{:S(2)}) %collective-permute-start.13) | collective-permute-done | bytes 262176 | tf_op jit(solution)/shard_map/ppermute | solution.py:81
  119.9 1.3 add_bitcast_fusion.2
  121.2 0.6 add_bitcast_fusion.1
  122.3 2.5 %collective-permute-start.16 = (f32[4,128,128]{2,1,0:T(8,128)S(1)}, f32[4,128,128]{2,1,0:T(8,128)S(1)}, u32[]{:S(2)}, u32[]{:S(2)}) collective-permute-start(f32[4,128,128]{2,1,0:T(8,128)S(1)} %get-tuple-element.95), channel_id=1, source_target_pairs={{0,2},{1,3},{2,0},{3,1},{4,6},{5,7},{6,4},{7,5},{8,10},{9,11},{10,... | collective-permute-start | bytes 786440 | tf_op jit(solution)/shard_map/ppermute | solution.py:50
  124.8 1.8 %collective-permute-done.15 = f32[4,128,128]{2,1,0:T(8,128)S(1)} collective-permute-done((f32[4,128,128]{2,1,0:T(8,128)S(1)}, f32[4,128,128]{2,1,0:T(8,128)S(1)}, u32[]{:S(2)}, u32[]{:S(2)}) %collective-permute-start.15) | collective-permute-done | bytes 262176 | tf_op jit(solution)/shard_map/ppermute | solution.py:50
  126.6 9.7 %collective-permute-done.16 = f32[4,128,128]{2,1,0:T(8,128)S(1)} collective-permute-done((f32[4,128,128]{2,1,0:T(8,128)S(1)}, f32[4,128,128]{2,1,0:T(8,128)S(1)}, u32[]{:S(2)}, u32[]{:S(2)}) %collective-permute-start.16) | collective-permute-done | bytes 262176 | tf_op jit(solution)/shard_map/ppermute | solution.py:50
  136.3 0.6 collective-permute-done.17
  137.0 1.0 copy-done.2
  138.0 7.2 %shard_map.88 = (bf16[384,2048]{1,0:T(8,128)(2,1)}, bf16[384,2048]{1,0:T(8,128)(2,1)}) custom-call(bf16[384,2048]{1,0:T(8,128)(2,1)} %key_ref.5, bf16[384,2048]{1,0:T(8,128)(2,1)} %value_ref.5, f32[384,2048]{1,0:T(8,128)} %get-tuple-element.65.key_part, f32[384,2048]{1,0:T(8,128)} %get-tuple-element.66.value_part, f32[16,128,128]{2,1,0:T(8,128)} %bitcast.125, ...), custom_call_target="tpu_custom_call" | custom-call | tf_op jit(solution)/shard_map/pallas_call | solution.py:132
  (52 shorter events, 3.2 us)
Async XLA Ops:
  8.3 1.2 copy-start.1
  9.6 8.1 %collective-permute-start = (f32[4,128,128]{2,1,0:T(8,128)S(1)}, f32[4,128,128]{2,1,0:T(8,128)S(1)}, u32[]{:S(2)}, u32[]{:S(2)}) collective-permute-start(f32[4,128,128]{2,1,0:T(8,128)S(1)} %get-tuple-element.108), channel_id=1, source_target_pairs={{0,1},{1,2},{2,3},{3,0},{4,5},{5,6},{6,7},{7,4},{8,9},{9,10},{10,1... | collective-permute-start | bytes 786440 | tf_op jit(solution)/shard_map/ppermute | solution.py:50
  12.3 11.1 %collective-permute-start.1 = (f32[4,128,128]{2,1,0:T(8,128)S(1)}, f32[4,128,128]{2,1,0:T(8,128)S(1)}, u32[]{:S(2)}, u32[]{:S(2)}) collective-permute-start(f32[4,128,128]{2,1,0:T(8,128)S(1)} %get-tuple-element.107), channel_id=1, source_target_pairs={{0,2},{1,3},{2,0},{3,1},{4,6},{5,7},{6,4},{7,5},{8,10},{9,11},{10,... | collective-permute-start | bytes 786440 | tf_op jit(solution)/shard_map/ppermute | solution.py:50
  12.3 11.6 %collective-permute-start.2 = (f32[4,128,128]{2,1,0:T(8,128)S(1)}, f32[4,128,128]{2,1,0:T(8,128)S(1)}, u32[]{:S(2)}, u32[]{:S(2)}) collective-permute-start(f32[4,128,128]{2,1,0:T(8,128)S(1)} %get-tuple-element.106), channel_id=1, source_target_pairs={{0,3},{1,0},{2,1},{3,2},{4,7},{5,4},{6,5},{7,6},{8,11},{9,8},{10,9... | collective-permute-start | bytes 786440 | tf_op jit(solution)/shard_map/ppermute | solution.py:50
  25.9 21.8 %collective-permute-start.3 = (f32[4,128,128]{2,1,0:T(8,128)S(1)}, f32[4,128,128]{2,1,0:T(8,128)S(1)}, u32[]{:S(2)}, u32[]{:S(2)}) collective-permute-start(f32[4,128,128]{2,1,0:T(8,128)S(1)} %get-tuple-element.38), channel_id=1, source_target_pairs={{0,4},{1,5},{2,6},{3,7},{4,8},{5,9},{6,10},{7,11},{8,12},{9,13},{1... | collective-permute-start | bytes 786440 | tf_op jit(solution)/shard_map/ppermute | solution.py:81
  30.0 17.7 %collective-permute-start.4 = (f32[4,128,128]{2,1,0:T(8,128)S(1)}, f32[4,128,128]{2,1,0:T(8,128)S(1)}, u32[]{:S(2)}, u32[]{:S(2)}) collective-permute-start(f32[4,128,128]{2,1,0:T(8,128)S(1)} %get-tuple-element.38), channel_id=1, source_target_pairs={{0,8},{1,9},{2,10},{3,11},{4,12},{5,13},{6,14},{7,15},{16,24},{17,... | collective-permute-start | bytes 786440 | tf_op jit(solution)/shard_map/ppermute | solution.py:81
  34.2 13.5 %collective-permute-start.5 = (f32[4,128,128]{2,1,0:T(8,128)S(1)}, f32[4,128,128]{2,1,0:T(8,128)S(1)}, u32[]{:S(2)}, u32[]{:S(2)}) collective-permute-start(f32[4,128,128]{2,1,0:T(8,128)S(1)} %get-tuple-element.38), channel_id=1, source_target_pairs={{0,12},{1,13},{2,14},{3,15},{16,28},{17,29},{18,30},{19,31}} | collective-permute-start | bytes 786440 | tf_op jit(solution)/shard_map/ppermute | solution.py:81
  50.1 4.8 %collective-permute-start.6 = (f32[4,128,128]{2,1,0:T(8,128)S(1)}, f32[4,128,128]{2,1,0:T(8,128)S(1)}, u32[]{:S(2)}, u32[]{:S(2)}) collective-permute-start(f32[4,128,128]{2,1,0:T(8,128)S(1)} %get-tuple-element.104), channel_id=1, source_target_pairs={{0,1},{1,2},{2,3},{3,0},{4,5},{5,6},{6,7},{7,4},{8,9},{9,10},{10,1... | collective-permute-start | bytes 786440 | tf_op jit(solution)/shard_map/ppermute | solution.py:50
  50.6 12.6 %collective-permute-start.7 = (f32[4,128,128]{2,1,0:T(8,128)S(1)}, f32[4,128,128]{2,1,0:T(8,128)S(1)}, u32[]{:S(2)}, u32[]{:S(2)}) collective-permute-start(f32[4,128,128]{2,1,0:T(8,128)S(1)} %get-tuple-element.103), channel_id=1, source_target_pairs={{0,2},{1,3},{2,0},{3,1},{4,6},{5,7},{6,4},{7,5},{8,10},{9,11},{10,... | collective-permute-start | bytes 786440 | tf_op jit(solution)/shard_map/ppermute | solution.py:50
  52.0 11.9 %collective-permute-start.8 = (f32[4,128,128]{2,1,0:T(8,128)S(1)}, f32[4,128,128]{2,1,0:T(8,128)S(1)}, u32[]{:S(2)}, u32[]{:S(2)}) collective-permute-start(f32[4,128,128]{2,1,0:T(8,128)S(1)} %get-tuple-element.102), channel_id=1, source_target_pairs={{0,3},{1,0},{2,1},{3,2},{4,7},{5,4},{6,5},{7,6},{8,11},{9,8},{10,9... | collective-permute-start | bytes 786440 | tf_op jit(solution)/shard_map/ppermute | solution.py:50
  64.0 1.0 copy-start
  72.3 1.2 copy-start.3
  73.6 5.0 %collective-permute-start.9 = (f32[4,128,128]{2,1,0:T(8,128)S(1)}, f32[4,128,128]{2,1,0:T(8,128)S(1)}, u32[]{:S(2)}, u32[]{:S(2)}) collective-permute-start(f32[4,128,128]{2,1,0:T(8,128)S(1)} %get-tuple-element.100), channel_id=1, source_target_pairs={{0,1},{1,2},{2,3},{3,0},{4,5},{5,6},{6,7},{7,4},{8,9},{9,10},{10,1... | collective-permute-start | bytes 786440 | tf_op jit(solution)/shard_map/ppermute | solution.py:50
  73.6 10.5 %collective-permute-start.10 = (f32[4,128,128]{2,1,0:T(8,128)S(1)}, f32[4,128,128]{2,1,0:T(8,128)S(1)}, u32[]{:S(2)}, u32[]{:S(2)}) collective-permute-start(f32[4,128,128]{2,1,0:T(8,128)S(1)} %get-tuple-element.99), channel_id=1, source_target_pairs={{0,2},{1,3},{2,0},{3,1},{4,6},{5,7},{6,4},{7,5},{8,10},{9,11},{10,... | collective-permute-start | bytes 786440 | tf_op jit(solution)/shard_map/ppermute | solution.py:50
  75.1 10.9 %collective-permute-start.11 = (f32[4,128,128]{2,1,0:T(8,128)S(1)}, f32[4,128,128]{2,1,0:T(8,128)S(1)}, u32[]{:S(2)}, u32[]{:S(2)}) collective-permute-start(f32[4,128,128]{2,1,0:T(8,128)S(1)} %get-tuple-element.98), channel_id=1, source_target_pairs={{0,3},{1,0},{2,1},{3,2},{4,7},{5,4},{6,5},{7,6},{8,11},{9,8},{10,9... | collective-permute-start | bytes 786440 | tf_op jit(solution)/shard_map/ppermute | solution.py:50
  88.0 20.0 %collective-permute-start.12 = (f32[4,128,128]{2,1,0:T(8,128)S(1)}, f32[4,128,128]{2,1,0:T(8,128)S(1)}, u32[]{:S(2)}, u32[]{:S(2)}) collective-permute-start(f32[4,128,128]{2,1,0:T(8,128)S(1)} %get-tuple-element.53), channel_id=1, source_target_pairs={{4,0},{5,1},{6,2},{7,3},{8,4},{9,5},{10,6},{11,7},{12,8},{13,9},{1... | collective-permute-start | bytes 786440 | tf_op jit(solution)/shard_map/ppermute | solution.py:81
  89.3 30.6 %collective-permute-start.13 = (f32[4,128,128]{2,1,0:T(8,128)S(1)}, f32[4,128,128]{2,1,0:T(8,128)S(1)}, u32[]{:S(2)}, u32[]{:S(2)}) collective-permute-start(f32[4,128,128]{2,1,0:T(8,128)S(1)} %get-tuple-element.53), channel_id=1, source_target_pairs={{8,0},{9,1},{10,2},{11,3},{12,4},{13,5},{14,6},{15,7},{24,16},{25,... | collective-permute-start | bytes 786440 | tf_op jit(solution)/shard_map/ppermute | solution.py:81
  90.6 29.4 %collective-permute-start.14 = (f32[4,128,128]{2,1,0:T(8,128)S(1)}, f32[4,128,128]{2,1,0:T(8,128)S(1)}, u32[]{:S(2)}, u32[]{:S(2)}) collective-permute-start(f32[4,128,128]{2,1,0:T(8,128)S(1)} %get-tuple-element.53), channel_id=1, source_target_pairs={{12,0},{13,1},{14,2},{15,3},{28,16},{29,17},{30,18},{31,19}} | collective-permute-start | bytes 786440 | tf_op jit(solution)/shard_map/ppermute | solution.py:81
  122.2 4.4 %collective-permute-start.15 = (f32[4,128,128]{2,1,0:T(8,128)S(1)}, f32[4,128,128]{2,1,0:T(8,128)S(1)}, u32[]{:S(2)}, u32[]{:S(2)}) collective-permute-start(f32[4,128,128]{2,1,0:T(8,128)S(1)} %get-tuple-element.96), channel_id=1, source_target_pairs={{0,1},{1,2},{2,3},{3,0},{4,5},{5,6},{6,7},{7,4},{8,9},{9,10},{10,1... | collective-permute-start | bytes 786440 | tf_op jit(solution)/shard_map/ppermute | solution.py:50
  122.3 14.0 %collective-permute-start.16 = (f32[4,128,128]{2,1,0:T(8,128)S(1)}, f32[4,128,128]{2,1,0:T(8,128)S(1)}, u32[]{:S(2)}, u32[]{:S(2)}) collective-permute-start(f32[4,128,128]{2,1,0:T(8,128)S(1)} %get-tuple-element.95), channel_id=1, source_target_pairs={{0,2},{1,3},{2,0},{3,1},{4,6},{5,7},{6,4},{7,5},{8,10},{9,11},{10,... | collective-permute-start | bytes 786440 | tf_op jit(solution)/shard_map/ppermute | solution.py:50
  124.8 12.2 %collective-permute-start.17 = (f32[4,128,128]{2,1,0:T(8,128)S(1)}, f32[4,128,128]{2,1,0:T(8,128)S(1)}, u32[]{:S(2)}, u32[]{:S(2)}) collective-permute-start(f32[4,128,128]{2,1,0:T(8,128)S(1)} %get-tuple-element.94), channel_id=1, source_target_pairs={{0,3},{1,0},{2,1},{3,2},{4,7},{5,4},{6,5},{7,6},{8,11},{9,8},{10,9... | collective-permute-start | bytes 786440 | tf_op jit(solution)/shard_map/ppermute | solution.py:50
  137.0 1.0 copy-start.2

commit v11 on v10

--- a/solution.py
+++ b/solution.py
@@ -194,9 +194,9 @@
         value_out[:, columns(i)] = mm(weight_ref[i], grad, TN)
 
 
-def tail_body(key_ref, value_ref, key_part, value_part, suffix_ref, rel_ref, key_out, value_out):
+def tail_body(key_ref, value_ref, key_part, value_part, suffix_ref, rel_ref, gate_ref, key_out, value_out):
     _, tail, _ = row_masks(rel_ref, slice(None))
-    opened = rel_ref[0:1, 1:2] > 0
+    opened = gate_ref[0:1, 0:1] > 0
     for i in range(HEAD_STEP):
         suffix = zeroed(opened, suffix_ref[i]).astype(jnp.bfloat16)
         key_carry = zeroed(tail, mm(value_ref[:, columns(i)], suffix, NT))
@@ -263,8 +263,7 @@
     doc_start = jnp.max(jnp.where(starts[None, :] <= position[:, None], starts[None, :], 0), axis=1)
     next_first = first_row + row_count
     next_open = (next_first < lax.axis_size("seq") * row_count) & jnp.logical_not(jnp.any(starts == next_first))
-    lane = lax.broadcasted_iota(jnp.int32, (row_count, 128), 1)
-    rel = jnp.where(lane == 0, (doc_start - first_row)[:, None], jnp.where(lane == 1, next_open.astype(jnp.int32), 0))
+    rel = jnp.broadcast_to((doc_start - first_row)[:, None], (row_count, HEAD))
     f32 = jnp.float32
     state_shape = jax.ShapeDtypeStruct((head_count, HEAD, HEAD), f32)
     wide = jax.ShapeDtypeStruct((row_count, feat_width), f32)
@@ -295,7 +294,8 @@
         (queries, keys, values, grad_low, weights, prefix, rel),
     )
     grad_keys, grad_values = head_call(
-        tail_body, [keys, values, keys_part, values_part, suffix, rel], [low, low]
+        tail_body, [keys, values, keys_part, values_part, suffix, rel, jnp.broadcast_to(next_open.astype(f32), (8, HEAD))],
+        [low, low],
     )
     return attn_out, grad_queries, grad_keys, grad_values
 

time: 146 us -> 145 us (level)
  transfers between devices with their start and end apart: 18 -> 18, of which waited for: 13 -> 13; matrix products, arithmetic and copies ran while one was open for 3% -> 4% of each run, Pallas kernels for 13% -> 13%
where the time goes in v11:
time: 145 us; the launch traced here: 144 us
  waiting for transfers between devices  53.9 us (37%)
  Pallas kernels  38.2 us (26%)
  starting transfers between devices  22.4 us (15%)
  other arithmetic  12.7 us (9%)
  between operations  9.3 us (6%)
  local copies, waits for them, and re-layouts  7.13 us (5%)
    ppermute x12, waiting for transfers between devices, member_exchange(): got.append(lax.ppermute(piece, axis, pairs))  41.9 us
    pallas_call x4, Pallas kernels, head_call(): pl.pallas_call(body, grid=(heads // HEAD_STEP,), in_specs=[spec(x.shape)...  30.9 us
    ppermute x6, starting transfers between devices, row_scan(): received.append(lax.ppermute(total, 'seq', pairs))  13.4 us
    ppermute x6, waiting for transfers between devices, row_scan(): received.append(lax.ppermute(total, 'seq', pairs))  12 us
    ppermute x12, starting transfers between devices, member_exchange(): got.append(lax.ppermute(piece, axis, pairs))  9.01 us
    pallas_call x1, Pallas kernels, middle_call(): pl.pallas_call(middle_body, grid=(rows // step,), in_specs=[row_block, ro...  7.29 us
    another operation x6, other arithmetic, row_scan(): jnp.stack([inner[index] + inner_keep[index] * entering for index in range...  4.17 us
    add x2, other arithmetic, row_scan(): total = mine[index] + keep_row[index] * total  3.89 us
  transfers between devices with their start and end apart: 18, of which 13 were waited for; matrix products, arithmetic and copies ran while one was open for 4% of the time, Pallas kernels for 13%

profile of v11, /device:TPU:1, one launch (start us, length us, event | category | flops | bytes accessed | tf_op | source)
XLA Modules:
  0.0 143.7 jit_solution(17028768211675335801)
XLA Ops:
  0.7 0.8 select_reduce_fusion.1
  1.6 0.8 broadcast_in_dim.111.rel_ref
  2.4 4.6 %shard_map.84 = f32[16,128,128]{2,1,0:T(8,128)} custom-call(bf16[384,2048]{1,0:T(8,128)(2,1)} %key_ref.5, bf16[384,2048]{1,0:T(8,128)(2,1)} %value_ref.5, s32[384,128]{1,0:T(8,128)} %broadcast_in_dim.111.rel_ref), custom_call_target="tpu_custom_call" | custom-call | tf_op jit(solution)/shard_map/pallas_call | solution.py:132
  7.1 1.1 copy-done.2
  8.3 2.6 %collective-permute-start = (f32[4,128,128]{2,1,0:T(8,128)S(1)}, f32[4,128,128]{2,1,0:T(8,128)S(1)}, u32[]{:S(2)}, u32[]{:S(2)}) collective-permute-start(f32[4,128,128]{2,1,0:T(8,128)S(1)} %get-tuple-element.108), channel_id=1, source_target_pairs={{0,1},{1,2},{2,3},{3,0},{4,5},{5,6},{6,7},{7,4},{8,9},{9,10},{10,1... | collective-permute-start | bytes 786440 | tf_op jit(solution)/shard_map/ppermute | solution.py:50
  10.9 0.5 collective-permute-start.2
  11.8 0.6 fusion.18
  13.0 3.4 %collective-permute-done = f32[4,128,128]{2,1,0:T(8,128)S(1)} collective-permute-done((f32[4,128,128]{2,1,0:T(8,128)S(1)}, f32[4,128,128]{2,1,0:T(8,128)S(1)}, u32[]{:S(2)}, u32[]{:S(2)}) %collective-permute-start) | collective-permute-done | bytes 262176 | tf_op jit(solution)/shard_map/ppermute | solution.py:50
  16.4 5.6 %collective-permute-done.1 = f32[4,128,128]{2,1,0:T(8,128)S(1)} collective-permute-done((f32[4,128,128]{2,1,0:T(8,128)S(1)}, f32[4,128,128]{2,1,0:T(8,128)S(1)}, u32[]{:S(2)}, u32[]{:S(2)}) %collective-permute-start.1) | collective-permute-done | bytes 262176 | tf_op jit(solution)/shard_map/ppermute | solution.py:50
  22.1 0.5 collective-permute-done.2
  22.6 2.0 %fusion.7 = (f32[4,128,128]{2,1,0:T(8,128)S(1)}, f32[4,128,128]{2,1,0:T(8,128)S(1)}) fusion(f32[4,4,128,128]{3,2,1,0:T(8,128)S(1)} %bitcast_dynamic-update-slice_fusion.9, f32[]{:T(128)} %bitcast.8, f32[]{:T(128)} %bitcast.10, f32[]{:T(128)S(6)} %mul.202, f32[]{:T(128)} %bitcast.12), kind=kLoop, calls=%fused_computation.17 | loop fusion | flops 458752 | bytes 1572880 | tf_op jit(solution)/shard_map/add | solution.py:71
  24.6 4.0 %collective-permute-start.3 = (f32[4,128,128]{2,1,0:T(8,128)S(1)}, f32[4,128,128]{2,1,0:T(8,128)S(1)}, u32[]{:S(2)}, u32[]{:S(2)}) collective-permute-start(f32[4,128,128]{2,1,0:T(8,128)S(1)} %get-tuple-element.38), channel_id=1, source_target_pairs={{0,4},{1,5},{2,6},{3,7},{4,8},{5,9},{6,10},{7,11},{8,12},{9,13},{1... | collective-permute-start | bytes 786440 | tf_op jit(solution)/shard_map/ppermute | solution.py:81
  28.6 4.2 %collective-permute-start.4 = (f32[4,128,128]{2,1,0:T(8,128)S(1)}, f32[4,128,128]{2,1,0:T(8,128)S(1)}, u32[]{:S(2)}, u32[]{:S(2)}) collective-permute-start(f32[4,128,128]{2,1,0:T(8,128)S(1)} %get-tuple-element.38), channel_id=1, source_target_pairs={{0,8},{1,9},{2,10},{3,11},{4,12},{5,13},{6,14},{7,15},{16,24},{17,... | collective-permute-start | bytes 786440 | tf_op jit(solution)/shard_map/ppermute | solution.py:81
  32.9 1.3 collective-permute-start.5
  36.1 0.6 subtract_reduce_fusion
  36.8 0.6 subtract_reduce_fusion.1
  38.7 7.7 %shard_map.85 = (bf16[16,384,384]{2,1,0:T(8,128)(2,1)}, f32[384,2048]{1,0:T(8,128)}) custom-call(bf16[384,2048]{1,0:T(8,128)(2,1)} %query_ref.3, bf16[384,2048]{1,0:T(8,128)(2,1)} %key_ref.5, bf16[384,2048]{1,0:T(8,128)(2,1)} %value_ref.5, s32[384,128]{1,0:T(8,128)} %broadcast_in_dim.111.rel_ref), custom_call_target="tpu_custom_call" | custom-call | tf_op jit(solution)/shard_map/pallas_call | solution.py:132
  46.4 1.4 add_bitcast_fusion.5
  47.8 0.7 add_bitcast_fusion.4
  48.8 0.5 collective-permute-start.6
  49.2 1.2 collective-permute-start.7
  51.1 2.4 %collective-permute-done.6 = f32[4,128,128]{2,1,0:T(8,128)S(1)} collective-permute-done((f32[4,128,128]{2,1,0:T(8,128)S(1)}, f32[4,128,128]{2,1,0:T(8,128)S(1)}, u32[]{:S(2)}, u32[]{:S(2)}) %collective-permute-start.6) | collective-permute-done | bytes 262176 | tf_op jit(solution)/shard_map/ppermute | solution.py:50
  53.6 8.2 %collective-permute-done.7 = f32[4,128,128]{2,1,0:T(8,128)S(1)} collective-permute-done((f32[4,128,128]{2,1,0:T(8,128)S(1)}, f32[4,128,128]{2,1,0:T(8,128)S(1)}, u32[]{:S(2)}, u32[]{:S(2)}) %collective-permute-start.7) | collective-permute-done | bytes 262176 | tf_op jit(solution)/shard_map/ppermute | solution.py:50
  61.8 0.8 collective-permute-done.8
  62.7 1.0 copy-done
  63.6 7.3 %shard_map.86 = (bf16[384,2048]{1,0:T(8,128)(2,1)}, bf16[384,2048]{1,0:T(8,128)(2,1)}, f32[16,128,128]{2,1,0:T(8,128)}) custom-call(bf16[384,2048]{1,0:T(8,128)(2,1)} %query_ref.3, f32[384,2048]{1,0:T(8,128)} %get-tuple-element.45.inside_ref, f32[16,128,128]{2,1,0:T(8,128)} %bitcast.122, bf16[384,2048]{1,0:T(8,128)(2,1)} %cot_ref.1, ...), custom_call_target="tpu_custom_call" | custom-call | tf_op jit(solution)/shard_map/pallas_call | solution.py:240
  71.0 1.1 copy-done.3
  72.6 0.6 fusion.17
  73.8 0.8 collective-permute-start.11
  74.5 2.6 %collective-permute-done.9 = f32[4,128,128]{2,1,0:T(8,128)S(1)} collective-permute-done((f32[4,128,128]{2,1,0:T(8,128)S(1)}, f32[4,128,128]{2,1,0:T(8,128)S(1)}, u32[]{:S(2)}, u32[]{:S(2)}) %collective-permute-start.9) | collective-permute-done | bytes 262176 | tf_op jit(solution)/shard_map/ppermute | solution.py:50
  77.2 5.6 %collective-permute-done.10 = f32[4,128,128]{2,1,0:T(8,128)S(1)} collective-permute-done((f32[4,128,128]{2,1,0:T(8,128)S(1)}, f32[4,128,128]{2,1,0:T(8,128)S(1)}, u32[]{:S(2)}, u32[]{:S(2)}) %collective-permute-start.10) | collective-permute-done | bytes 262176 | tf_op jit(solution)/shard_map/ppermute | solution.py:50
  82.8 1.9 %collective-permute-done.11 = f32[4,128,128]{2,1,0:T(8,128)S(1)} collective-permute-done((f32[4,128,128]{2,1,0:T(8,128)S(1)}, f32[4,128,128]{2,1,0:T(8,128)S(1)}, u32[]{:S(2)}, u32[]{:S(2)}) %collective-permute-start.11) | collective-permute-done | bytes 262176 | tf_op jit(solution)/shard_map/ppermute | solution.py:50
  84.7 1.9 %fusion.3 = (f32[4,128,128]{2,1,0:T(8,128)S(1)}, f32[4,128,128]{2,1,0:T(8,128)S(1)}) fusion(f32[4,4,128,128]{3,2,1,0:T(8,128)S(1)} %bitcast_dynamic-update-slice_fusion.3, f32[]{:T(128)} %bitcast.34, f32[]{:T(128)} %bitcast.36, f32[]{:T(128)S(6)} %mul.227, f32[]{:T(128)} %bitcast.38), kind=kLoop, calls=%fused_computation.9 | loop fusion | flops 458752 | bytes 1572880 | tf_op jit(solution)/shard_map/add | solution.py:71
  86.6 1.3 collective-permute-start.12
  87.9 1.3 collective-permute-start.13
  89.2 1.3 collective-permute-start.14
  92.4 0.6 fusion.13
  93.0 0.7 fusion.14
  94.9 11.7 %shard_map.87 = (bf16[384,2048]{1,0:T(8,128)(2,1)}, f32[384,2048]{1,0:T(8,128)}, f32[384,2048]{1,0:T(8,128)}) custom-call(bf16[384,2048]{1,0:T(8,128)(2,1)} %query_ref.3, bf16[384,2048]{1,0:T(8,128)(2,1)} %key_ref.5, bf16[384,2048]{1,0:T(8,128)(2,1)} %value_ref.5, bf16[384,2048]{1,0:T(8,128)(2,1)} %get-tuple-element.57.grad_ref, ...), custom_call_target="tpu_custom_call" | custom-call | tf_op jit(solution)/shard_map/pallas_call | solution.py:132
  106.6 12.0 %collective-permute-done.13 = f32[4,128,128]{2,1,0:T(8,128)S(1)} collective-permute-done((f32[4,128,128]{2,1,0:T(8,128)S(1)}, f32[4,128,128]{2,1,0:T(8,128)S(1)}, u32[]{:S(2)}, u32[]{:S(2)}) %collective-permute-start.13) | collective-permute-done | bytes 262176 | tf_op jit(solution)/shard_map/ppermute | solution.py:81
  118.6 1.3 add_bitcast_fusion.2
  119.9 0.6 add_bitcast_fusion.1
  120.9 2.5 %collective-permute-start.16 = (f32[4,128,128]{2,1,0:T(8,128)S(1)}, f32[4,128,128]{2,1,0:T(8,128)S(1)}, u32[]{:S(2)}, u32[]{:S(2)}) collective-permute-start(f32[4,128,128]{2,1,0:T(8,128)S(1)} %get-tuple-element.95), channel_id=1, source_target_pairs={{0,2},{1,3},{2,0},{3,1},{4,6},{5,7},{6,4},{7,5},{8,10},{9,11},{10,... | collective-permute-start | bytes 786440 | tf_op jit(solution)/shard_map/ppermute | solution.py:50
  123.4 0.6 compare_reduce_fusion
  125.2 9.7 %collective-permute-done.16 = f32[4,128,128]{2,1,0:T(8,128)S(1)} collective-permute-done((f32[4,128,128]{2,1,0:T(8,128)S(1)}, f32[4,128,128]{2,1,0:T(8,128)S(1)}, u32[]{:S(2)}, u32[]{:S(2)}) %collective-permute-start.16) | collective-permute-done | bytes 262176 | tf_op jit(solution)/shard_map/ppermute | solution.py:50
  135.0 0.6 collective-permute-done.17
  135.7 0.6 broadcast_in_dim.124.gate_ref
  136.6 7.0 %shard_map.88 = (bf16[384,2048]{1,0:T(8,128)(2,1)}, bf16[384,2048]{1,0:T(8,128)(2,1)}) custom-call(bf16[384,2048]{1,0:T(8,128)(2,1)} %key_ref.5, bf16[384,2048]{1,0:T(8,128)(2,1)} %value_ref.5, f32[384,2048]{1,0:T(8,128)} %get-tuple-element.65.key_part, f32[384,2048]{1,0:T(8,128)} %get-tuple-element.66.value_part, f32[16,128,128]{2,1,0:T(8,128)} %bitcast.124, ...), custom_call_target="tpu_custom_call" | custom-call | tf_op jit(solution)/shard_map/pallas_call | solution.py:132
  (51 shorter events, 3.6 us)
Async XLA Ops:
  7.0 1.2 copy-start.2
  8.3 8.1 %collective-permute-start = (f32[4,128,128]{2,1,0:T(8,128)S(1)}, f32[4,128,128]{2,1,0:T(8,128)S(1)}, u32[]{:S(2)}, u32[]{:S(2)}) collective-permute-start(f32[4,128,128]{2,1,0:T(8,128)S(1)} %get-tuple-element.108), channel_id=1, source_target_pairs={{0,1},{1,2},{2,3},{3,0},{4,5},{5,6},{6,7},{7,4},{8,9},{9,10},{10,1... | collective-permute-start | bytes 786440 | tf_op jit(solution)/shard_map/ppermute | solution.py:50
  10.9 11.1 %collective-permute-start.1 = (f32[4,128,128]{2,1,0:T(8,128)S(1)}, f32[4,128,128]{2,1,0:T(8,128)S(1)}, u32[]{:S(2)}, u32[]{:S(2)}) collective-permute-start(f32[4,128,128]{2,1,0:T(8,128)S(1)} %get-tuple-element.107), channel_id=1, source_target_pairs={{0,2},{1,3},{2,0},{3,1},{4,6},{5,7},{6,4},{7,5},{8,10},{9,11},{10,... | collective-permute-start | bytes 786440 | tf_op jit(solution)/shard_map/ppermute | solution.py:50
  10.9 11.6 %collective-permute-start.2 = (f32[4,128,128]{2,1,0:T(8,128)S(1)}, f32[4,128,128]{2,1,0:T(8,128)S(1)}, u32[]{:S(2)}, u32[]{:S(2)}) collective-permute-start(f32[4,128,128]{2,1,0:T(8,128)S(1)} %get-tuple-element.106), channel_id=1, source_target_pairs={{0,3},{1,0},{2,1},{3,2},{4,7},{5,4},{6,5},{7,6},{8,11},{9,8},{10,9... | collective-permute-start | bytes 786440 | tf_op jit(solution)/shard_map/ppermute | solution.py:50
  24.6 21.8 %collective-permute-start.3 = (f32[4,128,128]{2,1,0:T(8,128)S(1)}, f32[4,128,128]{2,1,0:T(8,128)S(1)}, u32[]{:S(2)}, u32[]{:S(2)}) collective-permute-start(f32[4,128,128]{2,1,0:T(8,128)S(1)} %get-tuple-element.38), channel_id=1, source_target_pairs={{0,4},{1,5},{2,6},{3,7},{4,8},{5,9},{6,10},{7,11},{8,12},{9,13},{1... | collective-permute-start | bytes 786440 | tf_op jit(solution)/shard_map/ppermute | solution.py:81
  28.6 17.7 %collective-permute-start.4 = (f32[4,128,128]{2,1,0:T(8,128)S(1)}, f32[4,128,128]{2,1,0:T(8,128)S(1)}, u32[]{:S(2)}, u32[]{:S(2)}) collective-permute-start(f32[4,128,128]{2,1,0:T(8,128)S(1)} %get-tuple-element.38), channel_id=1, source_target_pairs={{0,8},{1,9},{2,10},{3,11},{4,12},{5,13},{6,14},{7,15},{16,24},{17,... | collective-permute-start | bytes 786440 | tf_op jit(solution)/shard_map/ppermute | solution.py:81
  32.9 13.5 %collective-permute-start.5 = (f32[4,128,128]{2,1,0:T(8,128)S(1)}, f32[4,128,128]{2,1,0:T(8,128)S(1)}, u32[]{:S(2)}, u32[]{:S(2)}) collective-permute-start(f32[4,128,128]{2,1,0:T(8,128)S(1)} %get-tuple-element.38), channel_id=1, source_target_pairs={{0,12},{1,13},{2,14},{3,15},{16,28},{17,29},{18,30},{19,31}} | collective-permute-start | bytes 786440 | tf_op jit(solution)/shard_map/ppermute | solution.py:81
  48.8 4.8 %collective-permute-start.6 = (f32[4,128,128]{2,1,0:T(8,128)S(1)}, f32[4,128,128]{2,1,0:T(8,128)S(1)}, u32[]{:S(2)}, u32[]{:S(2)}) collective-permute-start(f32[4,128,128]{2,1,0:T(8,128)S(1)} %get-tuple-element.104), channel_id=1, source_target_pairs={{0,1},{1,2},{2,3},{3,0},{4,5},{5,6},{6,7},{7,4},{8,9},{9,10},{10,1... | collective-permute-start | bytes 786440 | tf_op jit(solution)/shard_map/ppermute | solution.py:50
  49.2 12.6 %collective-permute-start.7 = (f32[4,128,128]{2,1,0:T(8,128)S(1)}, f32[4,128,128]{2,1,0:T(8,128)S(1)}, u32[]{:S(2)}, u32[]{:S(2)}) collective-permute-start(f32[4,128,128]{2,1,0:T(8,128)S(1)} %get-tuple-element.103), channel_id=1, source_target_pairs={{0,2},{1,3},{2,0},{3,1},{4,6},{5,7},{6,4},{7,5},{8,10},{9,11},{10,... | collective-permute-start | bytes 786440 | tf_op jit(solution)/shard_map/ppermute | solution.py:50
  50.7 11.9 %collective-permute-start.8 = (f32[4,128,128]{2,1,0:T(8,128)S(1)}, f32[4,128,128]{2,1,0:T(8,128)S(1)}, u32[]{:S(2)}, u32[]{:S(2)}) collective-permute-start(f32[4,128,128]{2,1,0:T(8,128)S(1)} %get-tuple-element.102), channel_id=1, source_target_pairs={{0,3},{1,0},{2,1},{3,2},{4,7},{5,4},{6,5},{7,6},{8,11},{9,8},{10,9... | collective-permute-start | bytes 786440 | tf_op jit(solution)/shard_map/ppermute | solution.py:50
  62.7 1.0 copy-start
  70.9 1.2 copy-start.3
  72.2 5.0 %collective-permute-start.9 = (f32[4,128,128]{2,1,0:T(8,128)S(1)}, f32[4,128,128]{2,1,0:T(8,128)S(1)}, u32[]{:S(2)}, u32[]{:S(2)}) collective-permute-start(f32[4,128,128]{2,1,0:T(8,128)S(1)} %get-tuple-element.100), channel_id=1, source_target_pairs={{0,1},{1,2},{2,3},{3,0},{4,5},{5,6},{6,7},{7,4},{8,9},{9,10},{10,1... | collective-permute-start | bytes 786440 | tf_op jit(solution)/shard_map/ppermute | solution.py:50
  72.3 10.5 %collective-permute-start.10 = (f32[4,128,128]{2,1,0:T(8,128)S(1)}, f32[4,128,128]{2,1,0:T(8,128)S(1)}, u32[]{:S(2)}, u32[]{:S(2)}) collective-permute-start(f32[4,128,128]{2,1,0:T(8,128)S(1)} %get-tuple-element.99), channel_id=1, source_target_pairs={{0,2},{1,3},{2,0},{3,1},{4,6},{5,7},{6,4},{7,5},{8,10},{9,11},{10,... | collective-permute-start | bytes 786440 | tf_op jit(solution)/shard_map/ppermute | solution.py:50
  73.8 10.9 %collective-permute-start.11 = (f32[4,128,128]{2,1,0:T(8,128)S(1)}, f32[4,128,128]{2,1,0:T(8,128)S(1)}, u32[]{:S(2)}, u32[]{:S(2)}) collective-permute-start(f32[4,128,128]{2,1,0:T(8,128)S(1)} %get-tuple-element.98), channel_id=1, source_target_pairs={{0,3},{1,0},{2,1},{3,2},{4,7},{5,4},{6,5},{7,6},{8,11},{9,8},{10,9... | collective-permute-start | bytes 786440 | tf_op jit(solution)/shard_map/ppermute | solution.py:50
  86.6 20.0 %collective-permute-start.12 = (f32[4,128,128]{2,1,0:T(8,128)S(1)}, f32[4,128,128]{2,1,0:T(8,128)S(1)}, u32[]{:S(2)}, u32[]{:S(2)}) collective-permute-start(f32[4,128,128]{2,1,0:T(8,128)S(1)} %get-tuple-element.53), channel_id=1, source_target_pairs={{4,0},{5,1},{6,2},{7,3},{8,4},{9,5},{10,6},{11,7},{12,8},{13,9},{1... | collective-permute-start | bytes 786440 | tf_op jit(solution)/shard_map/ppermute | solution.py:81
  87.9 30.7 %collective-permute-start.13 = (f32[4,128,128]{2,1,0:T(8,128)S(1)}, f32[4,128,128]{2,1,0:T(8,128)S(1)}, u32[]{:S(2)}, u32[]{:S(2)}) collective-permute-start(f32[4,128,128]{2,1,0:T(8,128)S(1)} %get-tuple-element.53), channel_id=1, source_target_pairs={{8,0},{9,1},{10,2},{11,3},{12,4},{13,5},{14,6},{15,7},{24,16},{25,... | collective-permute-start | bytes 786440 | tf_op jit(solution)/shard_map/ppermute | solution.py:81
  89.2 29.4 %collective-permute-start.14 = (f32[4,128,128]{2,1,0:T(8,128)S(1)}, f32[4,128,128]{2,1,0:T(8,128)S(1)}, u32[]{:S(2)}, u32[]{:S(2)}) collective-permute-start(f32[4,128,128]{2,1,0:T(8,128)S(1)} %get-tuple-element.53), channel_id=1, source_target_pairs={{12,0},{13,1},{14,2},{15,3},{28,16},{29,17},{30,18},{31,19}} | collective-permute-start | bytes 786440 | tf_op jit(solution)/shard_map/ppermute | solution.py:81
  120.8 4.4 %collective-permute-start.15 = (f32[4,128,128]{2,1,0:T(8,128)S(1)}, f32[4,128,128]{2,1,0:T(8,128)S(1)}, u32[]{:S(2)}, u32[]{:S(2)}) collective-permute-start(f32[4,128,128]{2,1,0:T(8,128)S(1)} %get-tuple-element.96), channel_id=1, source_target_pairs={{0,1},{1,2},{2,3},{3,0},{4,5},{5,6},{6,7},{7,4},{8,9},{9,10},{10,1... | collective-permute-start | bytes 786440 | tf_op jit(solution)/shard_map/ppermute | solution.py:50
  120.9 14.0 %collective-permute-start.16 = (f32[4,128,128]{2,1,0:T(8,128)S(1)}, f32[4,128,128]{2,1,0:T(8,128)S(1)}, u32[]{:S(2)}, u32[]{:S(2)}) collective-permute-start(f32[4,128,128]{2,1,0:T(8,128)S(1)} %get-tuple-element.95), channel_id=1, source_target_pairs={{0,2},{1,3},{2,0},{3,1},{4,6},{5,7},{6,4},{7,5},{8,10},{9,11},{10,... | collective-permute-start | bytes 786440 | tf_op jit(solution)/shard_map/ppermute | solution.py:50
  124.7 10.9 %collective-permute-start.17 = (f32[4,128,128]{2,1,0:T(8,128)S(1)}, f32[4,128,128]{2,1,0:T(8,128)S(1)}, u32[]{:S(2)}, u32[]{:S(2)}) collective-permute-start(f32[4,128,128]{2,1,0:T(8,128)S(1)} %get-tuple-element.94), channel_id=1, source_target_pairs={{0,3},{1,0},{2,1},{3,2},{4,7},{5,4},{6,5},{7,6},{8,11},{9,8},{10,9... | collective-permute-start | bytes 786440 | tf_op jit(solution)/shard_map/ppermute | solution.py:50
  135.6 1.0 copy-start.1

commit v12 on v11

--- a/solution.py
+++ b/solution.py
@@ -74,17 +74,29 @@
     entering = jnp.zeros_like(total)
     weight = jnp.ones((), jnp.float32)
     total, filler_inputs = lax.optimization_barrier((total, filler_inputs))
-    received = []
-    for reach in range(1, -(-SPAN // GROUP) + 1):
+    reaches = -(-SPAN // GROUP)
+
+    def shifted(value, reach):
         shift = GROUP * direction * reach
         pairs = [(source, source + shift) for source in range(count) if 0 <= source + shift < count]
-        received.append(lax.ppermute(total, "seq", pairs))
-    filled = filler(*filler_inputs)
-    received, filled = lax.optimization_barrier((received, filled))
-    for reach in range(1, -(-SPAN // GROUP) + 1):
-        entering = entering + weight * received[reach - 1]
-        other = (row - direction * reach) * GROUP + lax.iota(jnp.int32, GROUP)
-        weight = weight * jnp.prod(keep_of(other))
+        return lax.ppermute(value, "seq", pairs)
+
+    def row_keep(reach):
+        return jnp.prod(keep_of((row - direction * reach) * GROUP + lax.iota(jnp.int32, GROUP)))
+
+    if reaches == 3:
+        previous = shifted(total, 1)
+        paired = total + total_keep * previous
+        filled = filler(*filler_inputs)
+        farther, filled = lax.optimization_barrier((shifted(paired, 2), filled))
+        entering = previous + row_keep(1) * farther
+    else:
+        received = [shifted(total, reach) for reach in range(1, reaches + 1)]
+        filled = filler(*filler_inputs)
+        received, filled = lax.optimization_barrier((received, filled))
+        for reach in range(1, reaches + 1):
+            entering = entering + weight * received[reach - 1]
+            weight = weight * row_keep(reach)
     scanned = jnp.stack([inner[index] + inner_keep[index] * entering for index in range(GROUP)])
     return member_exchange(scanned, "seq").reshape(state.shape), filled
 

time: 145 us -> 143 us (0.986)
  waiting for transfers between devices: 53.9 us -> 57.2 us
  starting transfers between devices: 22.4 us -> 20.4 us
    ppermute x6 -> x4, waiting for transfers between devices: 12 us -> 15.1 us  [shifted(): return lax.ppermute(value, 'seq', pairs)]
    ppermute x6 -> x4, starting transfers between devices: 13.4 us -> 11.7 us  [shifted(): return lax.ppermute(value, 'seq', pairs)]
  transfers between devices with their start and end apart: 18 -> 16, of which waited for: 13 -> 15; matrix products, arithmetic and copies ran while one was open for 4% -> 3% of each run, Pallas kernels for 13% -> 14%
where the time goes in v12:
time: 143 us
  waiting for transfers between devices  57.2 us (40%)
  Pallas kernels  38.1 us (27%)
  starting transfers between devices  20.4 us (14%)
  other arithmetic  11.6 us (8%)
  between operations  8.14 us (6%)
  local copies, waits for them, and re-layouts  7.17 us (5%)
    ppermute x12, waiting for transfers between devices, member_exchange(): got.append(lax.ppermute(piece, axis, pairs))  42.1 us
    pallas_call x4, Pallas kernels, head_call(): pl.pallas_call(body, grid=(heads // HEAD_STEP,), in_specs=[spec(x.shape)...  30.8 us
    ppermute x4, waiting for transfers between devices, shifted(): return lax.ppermute(value, 'seq', pairs)  15.1 us
    ppermute x4, starting transfers between devices, shifted(): return lax.ppermute(value, 'seq', pairs)  11.7 us
    ppermute x12, starting transfers between devices, member_exchange(): got.append(lax.ppermute(piece, axis, pairs))  8.7 us
    pallas_call x1, Pallas kernels, middle_call(): pl.pallas_call(middle_body, grid=(rows // step,), in_specs=[row_block, ro...  7.29 us
    another operation x6, other arithmetic, row_scan(): jnp.stack([inner[index] + inner_keep[index] * entering for index in range...  4.3 us
    add x2, other arithmetic, row_scan(): total = mine[index] + keep_row[index] * total  3.89 us
  transfers between devices with their start and end apart: 16, of which 15 were waited for; matrix products, arithmetic and copies ran while one was open for 3% of the time, Pallas kernels for 14%

profile of v12, /device:TPU:1, one launch (start us, length us, event | category | flops | bytes accessed | tf_op | source)
XLA Modules:
  0.0 142.6 jit_solution(9449161734484778505)
XLA Ops:
  0.7 0.8 select_reduce_fusion.1
  1.6 0.8 broadcast_in_dim.101.rel_ref
  2.4 4.6 %shard_map.84 = f32[16,128,128]{2,1,0:T(8,128)} custom-call(bf16[384,2048]{1,0:T(8,128)(2,1)} %key_ref.5, bf16[384,2048]{1,0:T(8,128)(2,1)} %value_ref.5, s32[384,128]{1,0:T(8,128)} %broadcast_in_dim.101.rel_ref), custom_call_target="tpu_custom_call" | custom-call | tf_op jit(solution)/shard_map/pallas_call | solution.py:144
  7.1 1.1 copy-done.2
  8.3 2.6 %collective-permute-start = (f32[4,128,128]{2,1,0:T(8,128)S(1)}, f32[4,128,128]{2,1,0:T(8,128)S(1)}, u32[]{:S(2)}, u32[]{:S(2)}) collective-permute-start(f32[4,128,128]{2,1,0:T(8,128)S(1)} %get-tuple-element.96), channel_id=1, source_target_pairs={{0,1},{1,2},{2,3},{3,0},{4,5},{5,6},{6,7},{7,4},{8,9},{9,10},{10,1... | collective-permute-start | bytes 786440 | tf_op jit(solution)/shard_map/ppermute | solution.py:50
  10.9 0.5 collective-permute-start.2
  11.7 0.6 fusion.16
  12.9 3.5 %collective-permute-done = f32[4,128,128]{2,1,0:T(8,128)S(1)} collective-permute-done((f32[4,128,128]{2,1,0:T(8,128)S(1)}, f32[4,128,128]{2,1,0:T(8,128)S(1)}, u32[]{:S(2)}, u32[]{:S(2)}) %collective-permute-start) | collective-permute-done | bytes 262176 | tf_op jit(solution)/shard_map/ppermute | solution.py:50
  16.4 5.6 %collective-permute-done.1 = f32[4,128,128]{2,1,0:T(8,128)S(1)} collective-permute-done((f32[4,128,128]{2,1,0:T(8,128)S(1)}, f32[4,128,128]{2,1,0:T(8,128)S(1)}, u32[]{:S(2)}, u32[]{:S(2)}) %collective-permute-start.1) | collective-permute-done | bytes 262176 | tf_op jit(solution)/shard_map/ppermute | solution.py:50
  22.0 0.5 collective-permute-done.2
  22.6 2.0 %fusion.7 = (f32[4,128,128]{2,1,0:T(8,128)S(1)}, f32[4,128,128]{2,1,0:T(8,128)S(1)}) fusion(f32[4,4,128,128]{3,2,1,0:T(8,128)S(1)} %bitcast_dynamic-update-slice_fusion.9, f32[]{:T(128)} %bitcast.8, f32[]{:T(128)} %bitcast.10, f32[]{:T(128)S(6)} %mul.176, f32[]{:T(128)} %bitcast.12), kind=kLoop, calls=%fused_computation.17 | loop fusion | flops 458752 | bytes 1572880 | tf_op jit(solution)/shard_map/add | solution.py:71
  24.6 4.0 %collective-permute-start.3 = (f32[4,128,128]{2,1,0:T(8,128)S(1)}, f32[4,128,128]{2,1,0:T(8,128)S(1)}, u32[]{:S(2)}, u32[]{:S(2)}) collective-permute-start(f32[4,128,128]{2,1,0:T(8,128)S(1)} %get-tuple-element.34), channel_id=1, source_target_pairs={{0,4},{1,5},{2,6},{3,7},{4,8},{5,9},{6,10},{7,11},{8,12},{9,13},{1... | collective-permute-start | bytes 786440 | tf_op jit(solution)/shard_map/ppermute | solution.py:82
  31.2 3.3 %collective-permute-done.3 = f32[4,128,128]{2,1,0:T(8,128)S(1)} collective-permute-done((f32[4,128,128]{2,1,0:T(8,128)S(1)}, f32[4,128,128]{2,1,0:T(8,128)S(1)}, u32[]{:S(2)}, u32[]{:S(2)}) %collective-permute-start.3) | collective-permute-done | bytes 262176 | tf_op jit(solution)/shard_map/ppermute | solution.py:82
  34.6 5.1 %collective-permute-start.4 = (f32[4,128,128]{2,1,0:T(8,128)S(1)}, f32[4,128,128]{2,1,0:T(8,128)S(1)}, u32[]{:S(2)}, u32[]{:S(2)}) collective-permute-start(f32[4,128,128]{2,1,0:T(8,128)S(1)} %multiply_add_fusion.3), channel_id=1, source_target_pairs={{0,8},{1,9},{2,10},{3,11},{4,12},{5,13},{6,14},{7,15},{16,24},{17,... | collective-permute-start | bytes 786440 | tf_op jit(solution)/shard_map/ppermute | solution.py:82
  39.8 0.6 subtract_reduce_fusion
  40.4 7.7 %shard_map.85 = (bf16[16,384,384]{2,1,0:T(8,128)(2,1)}, f32[384,2048]{1,0:T(8,128)}) custom-call(bf16[384,2048]{1,0:T(8,128)(2,1)} %query_ref.3, bf16[384,2048]{1,0:T(8,128)(2,1)} %key_ref.5, bf16[384,2048]{1,0:T(8,128)(2,1)} %value_ref.5, s32[384,128]{1,0:T(8,128)} %broadcast_in_dim.101.rel_ref), custom_call_target="tpu_custom_call" | custom-call | tf_op jit(solution)/shard_map/pallas_call | solution.py:144
  48.1 1.3 add_bitcast_fusion.5
  49.4 0.7 add_bitcast_fusion.4
  50.4 0.4 collective-permute-start.5
  50.8 1.8 %collective-permute-start.6 = (f32[4,128,128]{2,1,0:T(8,128)S(1)}, f32[4,128,128]{2,1,0:T(8,128)S(1)}, u32[]{:S(2)}, u32[]{:S(2)}) collective-permute-start(f32[4,128,128]{2,1,0:T(8,128)S(1)} %get-tuple-element.91), channel_id=1, source_target_pairs={{0,2},{1,3},{2,0},{3,1},{4,6},{5,7},{6,4},{7,5},{8,10},{9,11},{10,... | collective-permute-start | bytes 786440 | tf_op jit(solution)/shard_map/ppermute | solution.py:50
  53.0 3.1 %collective-permute-done.5 = f32[4,128,128]{2,1,0:T(8,128)S(1)} collective-permute-done((f32[4,128,128]{2,1,0:T(8,128)S(1)}, f32[4,128,128]{2,1,0:T(8,128)S(1)}, u32[]{:S(2)}, u32[]{:S(2)}) %collective-permute-start.5) | collective-permute-done | bytes 262176 | tf_op jit(solution)/shard_map/ppermute | solution.py:50
  56.1 8.1 %collective-permute-done.6 = f32[4,128,128]{2,1,0:T(8,128)S(1)} collective-permute-done((f32[4,128,128]{2,1,0:T(8,128)S(1)}, f32[4,128,128]{2,1,0:T(8,128)S(1)}, u32[]{:S(2)}, u32[]{:S(2)}) %collective-permute-start.6) | collective-permute-done | bytes 262176 | tf_op jit(solution)/shard_map/ppermute | solution.py:50
  64.2 0.6 collective-permute-done.7
  64.9 1.0 copy-done
  65.9 7.3 %shard_map.86 = (bf16[384,2048]{1,0:T(8,128)(2,1)}, bf16[384,2048]{1,0:T(8,128)(2,1)}, f32[16,128,128]{2,1,0:T(8,128)}) custom-call(bf16[384,2048]{1,0:T(8,128)(2,1)} %query_ref.3, f32[384,2048]{1,0:T(8,128)} %get-tuple-element.41.inside_ref, f32[16,128,128]{2,1,0:T(8,128)} %bitcast.122, bf16[384,2048]{1,0:T(8,128)(2,1)} %cot_ref.1, ...), custom_call_target="tpu_custom_call" | custom-call | tf_op jit(solution)/shard_map/pallas_call | solution.py:252
  73.3 1.1 copy-done.3
  74.6 0.7 fusion.15
  75.9 0.5 collective-permute-start.10
  76.4 3.5 %collective-permute-done.8 = f32[4,128,128]{2,1,0:T(8,128)S(1)} collective-permute-done((f32[4,128,128]{2,1,0:T(8,128)S(1)}, f32[4,128,128]{2,1,0:T(8,128)S(1)}, u32[]{:S(2)}, u32[]{:S(2)}) %collective-permute-start.8) | collective-permute-done | bytes 262176 | tf_op jit(solution)/shard_map/ppermute | solution.py:50
  80.0 5.6 %collective-permute-done.9 = f32[4,128,128]{2,1,0:T(8,128)S(1)} collective-permute-done((f32[4,128,128]{2,1,0:T(8,128)S(1)}, f32[4,128,128]{2,1,0:T(8,128)S(1)}, u32[]{:S(2)}, u32[]{:S(2)}) %collective-permute-start.9) | collective-permute-done | bytes 262176 | tf_op jit(solution)/shard_map/ppermute | solution.py:50
  85.6 0.7 collective-permute-done.10
  86.3 1.9 %fusion.3 = (f32[4,128,128]{2,1,0:T(8,128)S(1)}, f32[4,128,128]{2,1,0:T(8,128)S(1)}) fusion(f32[4,4,128,128]{3,2,1,0:T(8,128)S(1)} %bitcast_dynamic-update-slice_fusion.3, f32[]{:T(128)} %bitcast.34, f32[]{:T(128)} %bitcast.36, f32[]{:T(128)S(6)} %mul.199, f32[]{:T(128)} %bitcast.38), kind=kLoop, calls=%fused_computation.9 | loop fusion | flops 458752 | bytes 1572880 | tf_op jit(solution)/shard_map/add | solution.py:71
  88.2 1.3 collective-permute-start.11
  92.0 9.5 %collective-permute-done.11 = f32[4,128,128]{2,1,0:T(8,128)S(1)} collective-permute-done((f32[4,128,128]{2,1,0:T(8,128)S(1)}, f32[4,128,128]{2,1,0:T(8,128)S(1)}, u32[]{:S(2)}, u32[]{:S(2)}) %collective-permute-start.11) | collective-permute-done | bytes 262176 | tf_op jit(solution)/shard_map/ppermute | solution.py:82
  101.5 1.3 collective-permute-start.12
  102.8 0.7 fusion.12
  103.5 11.6 %shard_map.87 = (bf16[384,2048]{1,0:T(8,128)(2,1)}, f32[384,2048]{1,0:T(8,128)}, f32[384,2048]{1,0:T(8,128)}) custom-call(bf16[384,2048]{1,0:T(8,128)(2,1)} %query_ref.3, bf16[384,2048]{1,0:T(8,128)(2,1)} %key_ref.5, bf16[384,2048]{1,0:T(8,128)(2,1)} %value_ref.5, bf16[384,2048]{1,0:T(8,128)(2,1)} %get-tuple-element.51.grad_ref, ...), custom_call_target="tpu_custom_call" | custom-call | tf_op jit(solution)/shard_map/pallas_call | solution.py:144
  115.1 2.3 %collective-permute-done.12 = f32[4,128,128]{2,1,0:T(8,128)S(1)} collective-permute-done((f32[4,128,128]{2,1,0:T(8,128)S(1)}, f32[4,128,128]{2,1,0:T(8,128)S(1)}, u32[]{:S(2)}, u32[]{:S(2)}) %collective-permute-start.12) | collective-permute-done | bytes 262176 | tf_op jit(solution)/shard_map/ppermute | solution.py:82
  117.4 1.3 add_bitcast_fusion.2
  118.7 0.7 add_bitcast_fusion.1
  119.8 1.4 collective-permute-start.13
  121.1 1.3 collective-permute-start.14
  122.4 0.6 compare_reduce_fusion
  123.8 2.8 %collective-permute-done.13 = f32[4,128,128]{2,1,0:T(8,128)S(1)} collective-permute-done((f32[4,128,128]{2,1,0:T(8,128)S(1)}, f32[4,128,128]{2,1,0:T(8,128)S(1)}, u32[]{:S(2)}, u32[]{:S(2)}) %collective-permute-start.13) | collective-permute-done | bytes 262176 | tf_op jit(solution)/shard_map/ppermute | solution.py:50
  126.6 7.3 %collective-permute-done.14 = f32[4,128,128]{2,1,0:T(8,128)S(1)} collective-permute-done((f32[4,128,128]{2,1,0:T(8,128)S(1)}, f32[4,128,128]{2,1,0:T(8,128)S(1)}, u32[]{:S(2)}, u32[]{:S(2)}) %collective-permute-start.14) | collective-permute-done | bytes 262176 | tf_op jit(solution)/shard_map/ppermute | solution.py:50
  134.0 0.6 collective-permute-done.15
  134.6 0.6 broadcast_in_dim.114.gate_ref
  135.6 7.0 %shard_map.88 = (bf16[384,2048]{1,0:T(8,128)(2,1)}, bf16[384,2048]{1,0:T(8,128)(2,1)}) custom-call(bf16[384,2048]{1,0:T(8,128)(2,1)} %key_ref.5, bf16[384,2048]{1,0:T(8,128)(2,1)} %value_ref.5, f32[384,2048]{1,0:T(8,128)} %get-tuple-element.59.key_part, f32[384,2048]{1,0:T(8,128)} %get-tuple-element.60.value_part, f32[16,128,128]{2,1,0:T(8,128)} %bitcast.124, ...), custom_call_target="tpu_custom_call" | custom-call | tf_op jit(solution)/shard_map/pallas_call | solution.py:144
  (45 shorter events, 2.3 us)
Async XLA Ops:
  7.0 1.2 copy-start.2
  8.3 8.1 %collective-permute-start = (f32[4,128,128]{2,1,0:T(8,128)S(1)}, f32[4,128,128]{2,1,0:T(8,128)S(1)}, u32[]{:S(2)}, u32[]{:S(2)}) collective-permute-start(f32[4,128,128]{2,1,0:T(8,128)S(1)} %get-tuple-element.96), channel_id=1, source_target_pairs={{0,1},{1,2},{2,3},{3,0},{4,5},{5,6},{6,7},{7,4},{8,9},{9,10},{10,1... | collective-permute-start | bytes 786440 | tf_op jit(solution)/shard_map/ppermute | solution.py:50
  10.9 11.1 %collective-permute-start.1 = (f32[4,128,128]{2,1,0:T(8,128)S(1)}, f32[4,128,128]{2,1,0:T(8,128)S(1)}, u32[]{:S(2)}, u32[]{:S(2)}) collective-permute-start(f32[4,128,128]{2,1,0:T(8,128)S(1)} %get-tuple-element.95), channel_id=1, source_target_pairs={{0,2},{1,3},{2,0},{3,1},{4,6},{5,7},{6,4},{7,5},{8,10},{9,11},{10,... | collective-permute-start | bytes 786440 | tf_op jit(solution)/shard_map/ppermute | solution.py:50
  10.9 11.6 %collective-permute-start.2 = (f32[4,128,128]{2,1,0:T(8,128)S(1)}, f32[4,128,128]{2,1,0:T(8,128)S(1)}, u32[]{:S(2)}, u32[]{:S(2)}) collective-permute-start(f32[4,128,128]{2,1,0:T(8,128)S(1)} %get-tuple-element.94), channel_id=1, source_target_pairs={{0,3},{1,0},{2,1},{3,2},{4,7},{5,4},{6,5},{7,6},{8,11},{9,8},{10,9... | collective-permute-start | bytes 786440 | tf_op jit(solution)/shard_map/ppermute | solution.py:50
  24.6 10.0 %collective-permute-start.3 = (f32[4,128,128]{2,1,0:T(8,128)S(1)}, f32[4,128,128]{2,1,0:T(8,128)S(1)}, u32[]{:S(2)}, u32[]{:S(2)}) collective-permute-start(f32[4,128,128]{2,1,0:T(8,128)S(1)} %get-tuple-element.34), channel_id=1, source_target_pairs={{0,4},{1,5},{2,6},{3,7},{4,8},{5,9},{6,10},{7,11},{8,12},{9,13},{1... | collective-permute-start | bytes 786440 | tf_op jit(solution)/shard_map/ppermute | solution.py:82
  34.6 13.5 %collective-permute-start.4 = (f32[4,128,128]{2,1,0:T(8,128)S(1)}, f32[4,128,128]{2,1,0:T(8,128)S(1)}, u32[]{:S(2)}, u32[]{:S(2)}) collective-permute-start(f32[4,128,128]{2,1,0:T(8,128)S(1)} %multiply_add_fusion.3), channel_id=1, source_target_pairs={{0,8},{1,9},{2,10},{3,11},{4,12},{5,13},{6,14},{7,15},{16,24},{17,... | collective-permute-start | bytes 786440 | tf_op jit(solution)/shard_map/ppermute | solution.py:82
  50.4 5.6 %collective-permute-start.5 = (f32[4,128,128]{2,1,0:T(8,128)S(1)}, f32[4,128,128]{2,1,0:T(8,128)S(1)}, u32[]{:S(2)}, u32[]{:S(2)}) collective-permute-start(f32[4,128,128]{2,1,0:T(8,128)S(1)} %get-tuple-element.92), channel_id=1, source_target_pairs={{0,1},{1,2},{2,3},{3,0},{4,5},{5,6},{6,7},{7,4},{8,9},{9,10},{10,1... | collective-permute-start | bytes 786440 | tf_op jit(solution)/shard_map/ppermute | solution.py:50
  50.8 13.4 %collective-permute-start.6 = (f32[4,128,128]{2,1,0:T(8,128)S(1)}, f32[4,128,128]{2,1,0:T(8,128)S(1)}, u32[]{:S(2)}, u32[]{:S(2)}) collective-permute-start(f32[4,128,128]{2,1,0:T(8,128)S(1)} %get-tuple-element.91), channel_id=1, source_target_pairs={{0,2},{1,3},{2,0},{3,1},{4,6},{5,7},{6,4},{7,5},{8,10},{9,11},{10,... | collective-permute-start | bytes 786440 | tf_op jit(solution)/shard_map/ppermute | solution.py:50
  52.9 12.0 %collective-permute-start.7 = (f32[4,128,128]{2,1,0:T(8,128)S(1)}, f32[4,128,128]{2,1,0:T(8,128)S(1)}, u32[]{:S(2)}, u32[]{:S(2)}) collective-permute-start(f32[4,128,128]{2,1,0:T(8,128)S(1)} %get-tuple-element.90), channel_id=1, source_target_pairs={{0,3},{1,0},{2,1},{3,2},{4,7},{5,4},{6,5},{7,6},{8,11},{9,8},{10,9... | collective-permute-start | bytes 786440 | tf_op jit(solution)/shard_map/ppermute | solution.py:50
  64.9 1.0 copy-start
  73.1 1.2 copy-start.3
  74.4 5.5 %collective-permute-start.8 = (f32[4,128,128]{2,1,0:T(8,128)S(1)}, f32[4,128,128]{2,1,0:T(8,128)S(1)}, u32[]{:S(2)}, u32[]{:S(2)}) collective-permute-start(f32[4,128,128]{2,1,0:T(8,128)S(1)} %get-tuple-element.88), channel_id=1, source_target_pairs={{0,1},{1,2},{2,3},{3,0},{4,5},{5,6},{6,7},{7,4},{8,9},{9,10},{10,1... | collective-permute-start | bytes 786440 | tf_op jit(solution)/shard_map/ppermute | solution.py:50
  74.5 11.0 %collective-permute-start.9 = (f32[4,128,128]{2,1,0:T(8,128)S(1)}, f32[4,128,128]{2,1,0:T(8,128)S(1)}, u32[]{:S(2)}, u32[]{:S(2)}) collective-permute-start(f32[4,128,128]{2,1,0:T(8,128)S(1)} %get-tuple-element.87), channel_id=1, source_target_pairs={{0,2},{1,3},{2,0},{3,1},{4,6},{5,7},{6,4},{7,5},{8,10},{9,11},{10,... | collective-permute-start | bytes 786440 | tf_op jit(solution)/shard_map/ppermute | solution.py:50
  75.9 10.4 %collective-permute-start.10 = (f32[4,128,128]{2,1,0:T(8,128)S(1)}, f32[4,128,128]{2,1,0:T(8,128)S(1)}, u32[]{:S(2)}, u32[]{:S(2)}) collective-permute-start(f32[4,128,128]{2,1,0:T(8,128)S(1)} %get-tuple-element.86), channel_id=1, source_target_pairs={{0,3},{1,0},{2,1},{3,2},{4,7},{5,4},{6,5},{7,6},{8,11},{9,8},{10,9... | collective-permute-start | bytes 786440 | tf_op jit(solution)/shard_map/ppermute | solution.py:50
  88.2 13.2 %collective-permute-start.11 = (f32[4,128,128]{2,1,0:T(8,128)S(1)}, f32[4,128,128]{2,1,0:T(8,128)S(1)}, u32[]{:S(2)}, u32[]{:S(2)}) collective-permute-start(f32[4,128,128]{2,1,0:T(8,128)S(1)} %get-tuple-element.47), channel_id=1, source_target_pairs={{4,0},{5,1},{6,2},{7,3},{8,4},{9,5},{10,6},{11,7},{12,8},{13,9},{1... | collective-permute-start | bytes 786440 | tf_op jit(solution)/shard_map/ppermute | solution.py:82
  101.5 15.9 %collective-permute-start.12 = (f32[4,128,128]{2,1,0:T(8,128)S(1)}, f32[4,128,128]{2,1,0:T(8,128)S(1)}, u32[]{:S(2)}, u32[]{:S(2)}) collective-permute-start(f32[4,128,128]{2,1,0:T(8,128)S(1)} %multiply_add_fusion.1), channel_id=1, source_target_pairs={{8,0},{9,1},{10,2},{11,3},{12,4},{13,5},{14,6},{15,7},{24,16},{25,... | collective-permute-start | bytes 786440 | tf_op jit(solution)/shard_map/ppermute | solution.py:82
  119.8 6.8 %collective-permute-start.13 = (f32[4,128,128]{2,1,0:T(8,128)S(1)}, f32[4,128,128]{2,1,0:T(8,128)S(1)}, u32[]{:S(2)}, u32[]{:S(2)}) collective-permute-start(f32[4,128,128]{2,1,0:T(8,128)S(1)} %get-tuple-element.84), channel_id=1, source_target_pairs={{0,1},{1,2},{2,3},{3,0},{4,5},{5,6},{6,7},{7,4},{8,9},{9,10},{10,1... | collective-permute-start | bytes 786440 | tf_op jit(solution)/shard_map/ppermute | solution.py:50
  121.1 12.8 %collective-permute-start.14 = (f32[4,128,128]{2,1,0:T(8,128)S(1)}, f32[4,128,128]{2,1,0:T(8,128)S(1)}, u32[]{:S(2)}, u32[]{:S(2)}) collective-permute-start(f32[4,128,128]{2,1,0:T(8,128)S(1)} %get-tuple-element.83), channel_id=1, source_target_pairs={{0,2},{1,3},{2,0},{3,1},{4,6},{5,7},{6,4},{7,5},{8,10},{9,11},{10,... | collective-permute-start | bytes 786440 | tf_op jit(solution)/shard_map/ppermute | solution.py:50
  123.7 10.9 %collective-permute-start.15 = (f32[4,128,128]{2,1,0:T(8,128)S(1)}, f32[4,128,128]{2,1,0:T(8,128)S(1)}, u32[]{:S(2)}, u32[]{:S(2)}) collective-permute-start(f32[4,128,128]{2,1,0:T(8,128)S(1)} %get-tuple-element.82), channel_id=1, source_target_pairs={{0,3},{1,0},{2,1},{3,2},{4,7},{5,4},{6,5},{7,6},{8,11},{9,8},{10,9... | collective-permute-start | bytes 786440 | tf_op jit(solution)/shard_map/ppermute | solution.py:50
  134.6 1.0 copy-start.1

commit v13 on v12

--- a/solution.py
+++ b/solution.py
@@ -86,8 +86,10 @@
 
     if reaches == 3:
         previous = shifted(total, 1)
+        filled = filler(*filler_inputs)
+        if direction < 0:
+            previous, filled = lax.optimization_barrier((previous, filled))
         paired = total + total_keep * previous
-        filled = filler(*filler_inputs)
         farther, filled = lax.optimization_barrier((shifted(paired, 2), filled))
         entering = previous + row_keep(1) * farther
     else:

time: 143 us -> 149 us (1.042)
  waiting for transfers between devices: 57.2 us -> 63.8 us
    ppermute x4, waiting for transfers between devices: 15.1 us -> 21.7 us  [shifted(): return lax.ppermute(value, 'seq', pairs)]
  transfers between devices with their start and end apart: 16 -> 16, of which waited for: 15 -> 14; matrix products, arithmetic and copies ran while one was open for 3% -> 3% of each run, Pallas kernels for 14% -> 13%
where the time goes in v13:
time: 149 us; the launch traced here: 148 us
  waiting for transfers between devices  63.8 us (43%)
  Pallas kernels  38.2 us (26%)
  starting transfers between devices  19.7 us (13%)
  other arithmetic  11.5 us (8%)
  between operations  8.14 us (5%)
  local copies, waits for them, and re-layouts  7.17 us (5%)
    ppermute x12, waiting for transfers between devices, member_exchange(): got.append(lax.ppermute(piece, axis, pairs))  42.1 us
    pallas_call x4, Pallas kernels, head_call(): pl.pallas_call(body, grid=(heads // HEAD_STEP,), in_specs=[spec(x.shape)...  30.9 us
    ppermute x4, waiting for transfers between devices, shifted(): return lax.ppermute(value, 'seq', pairs)  21.7 us
    ppermute x4, starting transfers between devices, shifted(): return lax.ppermute(value, 'seq', pairs)  11.7 us
    ppermute x12, starting transfers between devices, member_exchange(): got.append(lax.ppermute(piece, axis, pairs))  7.95 us
    pallas_call x1, Pallas kernels, middle_call(): pl.pallas_call(middle_body, grid=(rows // step,), in_specs=[row_block, ro...  7.29 us
    another operation x6, other arithmetic, row_scan(): jnp.stack([inner[index] + inner_keep[index] * entering for index in range...  4.28 us
    add x2, other arithmetic, row_scan(): total = mine[index] + keep_row[index] * total  3.89 us
  transfers between devices with their start and end apart: 16, of which 14 were waited for; matrix products, arithmetic and copies ran while one was open for 3% of the time, Pallas kernels for 13%

profile of v13, /device:TPU:1, one launch (start us, length us, event | category | flops | bytes accessed | tf_op | source)
XLA Modules:
  0.0 148.4 jit_solution(17701924357605856487)
XLA Ops:
  0.7 0.8 select_reduce_fusion.1
  1.6 0.8 broadcast_in_dim.101.rel_ref
  2.4 4.6 %shard_map.84 = f32[16,128,128]{2,1,0:T(8,128)} custom-call(bf16[384,2048]{1,0:T(8,128)(2,1)} %key_ref.5, bf16[384,2048]{1,0:T(8,128)(2,1)} %value_ref.5, s32[384,128]{1,0:T(8,128)} %broadcast_in_dim.101.rel_ref), custom_call_target="tpu_custom_call" | custom-call | tf_op jit(solution)/shard_map/pallas_call | solution.py:146
  7.1 1.1 copy-done.2
  8.3 2.6 %collective-permute-start = (f32[4,128,128]{2,1,0:T(8,128)S(1)}, f32[4,128,128]{2,1,0:T(8,128)S(1)}, u32[]{:S(2)}, u32[]{:S(2)}) collective-permute-start(f32[4,128,128]{2,1,0:T(8,128)S(1)} %get-tuple-element.104), channel_id=1, source_target_pairs={{0,1},{1,2},{2,3},{3,0},{4,5},{5,6},{6,7},{7,4},{8,9},{9,10},{10,1... | collective-permute-start | bytes 786440 | tf_op jit(solution)/shard_map/ppermute | solution.py:50
  10.9 0.5 collective-permute-start.2
  11.4 0.2 compare_reduce_fusion.1
  11.7 0.6 fusion.16
  12.9 3.5 %collective-permute-done = f32[4,128,128]{2,1,0:T(8,128)S(1)} collective-permute-done((f32[4,128,128]{2,1,0:T(8,128)S(1)}, f32[4,128,128]{2,1,0:T(8,128)S(1)}, u32[]{:S(2)}, u32[]{:S(2)}) %collective-permute-start) | collective-permute-done | bytes 262176 | tf_op jit(solution)/shard_map/ppermute | solution.py:50
  16.4 5.6 %collective-permute-done.1 = f32[4,128,128]{2,1,0:T(8,128)S(1)} collective-permute-done((f32[4,128,128]{2,1,0:T(8,128)S(1)}, f32[4,128,128]{2,1,0:T(8,128)S(1)}, u32[]{:S(2)}, u32[]{:S(2)}) %collective-permute-start.1) | collective-permute-done | bytes 262176 | tf_op jit(solution)/shard_map/ppermute | solution.py:50
  22.0 0.5 collective-permute-done.2
  22.6 2.0 %fusion.7 = (f32[4,128,128]{2,1,0:T(8,128)S(1)}, f32[4,128,128]{2,1,0:T(8,128)S(1)}) fusion(f32[4,4,128,128]{3,2,1,0:T(8,128)S(1)} %bitcast_dynamic-update-slice_fusion.9, f32[]{:T(128)} %bitcast.8, f32[]{:T(128)} %bitcast.10, f32[]{:T(128)S(6)} %mul.176, f32[]{:T(128)} %bitcast.12), kind=kLoop, calls=%fused_computation.17 | loop fusion | flops 458752 | bytes 1572880 | tf_op jit(solution)/shard_map/add | solution.py:71
  24.6 4.0 %collective-permute-start.3 = (f32[4,128,128]{2,1,0:T(8,128)S(1)}, f32[4,128,128]{2,1,0:T(8,128)S(1)}, u32[]{:S(2)}, u32[]{:S(2)}) collective-permute-start(f32[4,128,128]{2,1,0:T(8,128)S(1)} %get-tuple-element.38), channel_id=1, source_target_pairs={{0,4},{1,5},{2,6},{3,7},{4,8},{5,9},{6,10},{7,11},{8,12},{9,13},{1... | collective-permute-start | bytes 786440 | tf_op jit(solution)/shard_map/ppermute | solution.py:82
  31.2 3.3 %collective-permute-done.3 = f32[4,128,128]{2,1,0:T(8,128)S(1)} collective-permute-done((f32[4,128,128]{2,1,0:T(8,128)S(1)}, f32[4,128,128]{2,1,0:T(8,128)S(1)}, u32[]{:S(2)}, u32[]{:S(2)}) %collective-permute-start.3) | collective-permute-done | bytes 262176 | tf_op jit(solution)/shard_map/ppermute | solution.py:82
  34.6 5.1 %collective-permute-start.4 = (f32[4,128,128]{2,1,0:T(8,128)S(1)}, f32[4,128,128]{2,1,0:T(8,128)S(1)}, u32[]{:S(2)}, u32[]{:S(2)}) collective-permute-start(f32[4,128,128]{2,1,0:T(8,128)S(1)} %multiply_add_fusion.3), channel_id=1, source_target_pairs={{0,8},{1,9},{2,10},{3,11},{4,12},{5,13},{6,14},{7,15},{16,24},{17,... | collective-permute-start | bytes 786440 | tf_op jit(solution)/shard_map/ppermute | solution.py:82
  39.8 0.6 subtract_reduce_fusion
  40.4 7.7 %shard_map.85 = (bf16[16,384,384]{2,1,0:T(8,128)(2,1)}, f32[384,2048]{1,0:T(8,128)}) custom-call(bf16[384,2048]{1,0:T(8,128)(2,1)} %query_ref.3, bf16[384,2048]{1,0:T(8,128)(2,1)} %key_ref.5, bf16[384,2048]{1,0:T(8,128)(2,1)} %value_ref.5, s32[384,128]{1,0:T(8,128)} %broadcast_in_dim.101.rel_ref), custom_call_target="tpu_custom_call" | custom-call | tf_op jit(solution)/shard_map/pallas_call | solution.py:146
  48.1 1.3 add_bitcast_fusion.5
  49.4 0.7 add_bitcast_fusion.4
  50.4 0.4 collective-permute-start.5
  50.8 1.8 %collective-permute-start.6 = (f32[4,128,128]{2,1,0:T(8,128)S(1)}, f32[4,128,128]{2,1,0:T(8,128)S(1)}, u32[]{:S(2)}, u32[]{:S(2)}) collective-permute-start(f32[4,128,128]{2,1,0:T(8,128)S(1)} %get-tuple-element.99), channel_id=1, source_target_pairs={{0,2},{1,3},{2,0},{3,1},{4,6},{5,7},{6,4},{7,5},{8,10},{9,11},{10,... | collective-permute-start | bytes 786440 | tf_op jit(solution)/shard_map/ppermute | solution.py:50
  53.0 3.1 %collective-permute-done.5 = f32[4,128,128]{2,1,0:T(8,128)S(1)} collective-permute-done((f32[4,128,128]{2,1,0:T(8,128)S(1)}, f32[4,128,128]{2,1,0:T(8,128)S(1)}, u32[]{:S(2)}, u32[]{:S(2)}) %collective-permute-start.5) | collective-permute-done | bytes 262176 | tf_op jit(solution)/shard_map/ppermute | solution.py:50
  56.1 8.1 %collective-permute-done.6 = f32[4,128,128]{2,1,0:T(8,128)S(1)} collective-permute-done((f32[4,128,128]{2,1,0:T(8,128)S(1)}, f32[4,128,128]{2,1,0:T(8,128)S(1)}, u32[]{:S(2)}, u32[]{:S(2)}) %collective-permute-start.6) | collective-permute-done | bytes 262176 | tf_op jit(solution)/shard_map/ppermute | solution.py:50
  64.2 0.6 collective-permute-done.7
  64.9 1.0 copy-done
  65.9 7.3 %shard_map.86 = (bf16[384,2048]{1,0:T(8,128)(2,1)}, bf16[384,2048]{1,0:T(8,128)(2,1)}, f32[16,128,128]{2,1,0:T(8,128)}) custom-call(bf16[384,2048]{1,0:T(8,128)(2,1)} %query_ref.3, f32[384,2048]{1,0:T(8,128)} %get-tuple-element.45.inside_ref, f32[16,128,128]{2,1,0:T(8,128)} %bitcast.122, bf16[384,2048]{1,0:T(8,128)(2,1)} %cot_ref.1, ...), custom_call_target="tpu_custom_call" | custom-call | tf_op jit(solution)/shard_map/pallas_call | solution.py:254
  73.3 1.1 copy-done.3
  74.6 0.7 fusion.15
  75.9 0.5 collective-permute-start.10
  76.4 3.5 %collective-permute-done.8 = f32[4,128,128]{2,1,0:T(8,128)S(1)} collective-permute-done((f32[4,128,128]{2,1,0:T(8,128)S(1)}, f32[4,128,128]{2,1,0:T(8,128)S(1)}, u32[]{:S(2)}, u32[]{:S(2)}) %collective-permute-start.8) | collective-permute-done | bytes 262176 | tf_op jit(solution)/shard_map/ppermute | solution.py:50
  80.0 5.6 %collective-permute-done.9 = f32[4,128,128]{2,1,0:T(8,128)S(1)} collective-permute-done((f32[4,128,128]{2,1,0:T(8,128)S(1)}, f32[4,128,128]{2,1,0:T(8,128)S(1)}, u32[]{:S(2)}, u32[]{:S(2)}) %collective-permute-start.9) | collective-permute-done | bytes 262176 | tf_op jit(solution)/shard_map/ppermute | solution.py:50
  85.6 0.7 collective-permute-done.10
  86.3 1.9 %fusion.3 = (f32[4,128,128]{2,1,0:T(8,128)S(1)}, f32[4,128,128]{2,1,0:T(8,128)S(1)}) fusion(f32[4,4,128,128]{3,2,1,0:T(8,128)S(1)} %bitcast_dynamic-update-slice_fusion.3, f32[]{:T(128)} %bitcast.34, f32[]{:T(128)} %bitcast.36, f32[]{:T(128)S(6)} %mul.199, f32[]{:T(128)} %bitcast.38), kind=kLoop, calls=%fused_computation.9 | loop fusion | flops 458752 | bytes 1572880 | tf_op jit(solution)/shard_map/add | solution.py:71
  88.2 1.3 collective-permute-start.11
  92.0 11.6 %shard_map.87 = (bf16[384,2048]{1,0:T(8,128)(2,1)}, f32[384,2048]{1,0:T(8,128)}, f32[384,2048]{1,0:T(8,128)}) custom-call(bf16[384,2048]{1,0:T(8,128)(2,1)} %query_ref.3, bf16[384,2048]{1,0:T(8,128)(2,1)} %key_ref.5, bf16[384,2048]{1,0:T(8,128)(2,1)} %value_ref.5, bf16[384,2048]{1,0:T(8,128)(2,1)} %get-tuple-element.55.grad_ref, ...), custom_call_target="tpu_custom_call" | custom-call | tf_op jit(solution)/shard_map/pallas_call | solution.py:146
  103.7 1.3 collective-permute-start.12
  105.0 0.6 fusion.12
  105.6 18.3 %collective-permute-done.12 = f32[4,128,128]{2,1,0:T(8,128)S(1)} collective-permute-done((f32[4,128,128]{2,1,0:T(8,128)S(1)}, f32[4,128,128]{2,1,0:T(8,128)S(1)}, u32[]{:S(2)}, u32[]{:S(2)}) %collective-permute-start.12) | collective-permute-done | bytes 262176 | tf_op jit(solution)/shard_map/ppermute | solution.py:82
  123.9 1.3 add_bitcast_fusion.2
  125.3 0.7 add_bitcast_fusion.1
  126.4 1.8 %collective-permute-start.14 = (f32[4,128,128]{2,1,0:T(8,128)S(1)}, f32[4,128,128]{2,1,0:T(8,128)S(1)}, u32[]{:S(2)}, u32[]{:S(2)}) collective-permute-start(f32[4,128,128]{2,1,0:T(8,128)S(1)} %get-tuple-element.91), channel_id=1, source_target_pairs={{0,2},{1,3},{2,0},{3,1},{4,6},{5,7},{6,4},{7,5},{8,10},{9,11},{10,... | collective-permute-start | bytes 786440 | tf_op jit(solution)/shard_map/ppermute | solution.py:50
  128.2 0.6 compare_reduce_fusion
  129.6 1.8 %collective-permute-done.13 = f32[4,128,128]{2,1,0:T(8,128)S(1)} collective-permute-done((f32[4,128,128]{2,1,0:T(8,128)S(1)}, f32[4,128,128]{2,1,0:T(8,128)S(1)}, u32[]{:S(2)}, u32[]{:S(2)}) %collective-permute-start.13) | collective-permute-done | bytes 262176 | tf_op jit(solution)/shard_map/ppermute | solution.py:50
  131.4 8.3 %collective-permute-done.14 = f32[4,128,128]{2,1,0:T(8,128)S(1)} collective-permute-done((f32[4,128,128]{2,1,0:T(8,128)S(1)}, f32[4,128,128]{2,1,0:T(8,128)S(1)}, u32[]{:S(2)}, u32[]{:S(2)}) %collective-permute-start.14) | collective-permute-done | bytes 262176 | tf_op jit(solution)/shard_map/ppermute | solution.py:50
  139.7 0.6 collective-permute-done.15
  140.4 0.6 broadcast_in_dim.114.gate_ref
  141.0 0.3 copy-done.1
  141.4 7.0 %shard_map.88 = (bf16[384,2048]{1,0:T(8,128)(2,1)}, bf16[384,2048]{1,0:T(8,128)(2,1)}) custom-call(bf16[384,2048]{1,0:T(8,128)(2,1)} %key_ref.5, bf16[384,2048]{1,0:T(8,128)(2,1)} %value_ref.5, f32[384,2048]{1,0:T(8,128)} %get-tuple-element.67.key_part, f32[384,2048]{1,0:T(8,128)} %get-tuple-element.68.value_part, f32[16,128,128]{2,1,0:T(8,128)} %bitcast.124, ...), custom_call_target="tpu_custom_call" | custom-call | tf_op jit(solution)/shard_map/pallas_call | solution.py:146
  (45 shorter events, 1.9 us)
Async XLA Ops:
  7.0 1.2 copy-start.2
  8.3 8.1 %collective-permute-start = (f32[4,128,128]{2,1,0:T(8,128)S(1)}, f32[4,128,128]{2,1,0:T(8,128)S(1)}, u32[]{:S(2)}, u32[]{:S(2)}) collective-permute-start(f32[4,128,128]{2,1,0:T(8,128)S(1)} %get-tuple-element.104), channel_id=1, source_target_pairs={{0,1},{1,2},{2,3},{3,0},{4,5},{5,6},{6,7},{7,4},{8,9},{9,10},{10,1... | collective-permute-start | bytes 786440 | tf_op jit(solution)/shard_map/ppermute | solution.py:50
  10.9 11.1 %collective-permute-start.1 = (f32[4,128,128]{2,1,0:T(8,128)S(1)}, f32[4,128,128]{2,1,0:T(8,128)S(1)}, u32[]{:S(2)}, u32[]{:S(2)}) collective-permute-start(f32[4,128,128]{2,1,0:T(8,128)S(1)} %get-tuple-element.103), channel_id=1, source_target_pairs={{0,2},{1,3},{2,0},{3,1},{4,6},{5,7},{6,4},{7,5},{8,10},{9,11},{10,... | collective-permute-start | bytes 786440 | tf_op jit(solution)/shard_map/ppermute | solution.py:50
  10.9 11.6 %collective-permute-start.2 = (f32[4,128,128]{2,1,0:T(8,128)S(1)}, f32[4,128,128]{2,1,0:T(8,128)S(1)}, u32[]{:S(2)}, u32[]{:S(2)}) collective-permute-start(f32[4,128,128]{2,1,0:T(8,128)S(1)} %get-tuple-element.102), channel_id=1, source_target_pairs={{0,3},{1,0},{2,1},{3,2},{4,7},{5,4},{6,5},{7,6},{8,11},{9,8},{10,9... | collective-permute-start | bytes 786440 | tf_op jit(solution)/shard_map/ppermute | solution.py:50
  24.6 10.0 %collective-permute-start.3 = (f32[4,128,128]{2,1,0:T(8,128)S(1)}, f32[4,128,128]{2,1,0:T(8,128)S(1)}, u32[]{:S(2)}, u32[]{:S(2)}) collective-permute-start(f32[4,128,128]{2,1,0:T(8,128)S(1)} %get-tuple-element.38), channel_id=1, source_target_pairs={{0,4},{1,5},{2,6},{3,7},{4,8},{5,9},{6,10},{7,11},{8,12},{9,13},{1... | collective-permute-start | bytes 786440 | tf_op jit(solution)/shard_map/ppermute | solution.py:82
  34.6 13.5 %collective-permute-start.4 = (f32[4,128,128]{2,1,0:T(8,128)S(1)}, f32[4,128,128]{2,1,0:T(8,128)S(1)}, u32[]{:S(2)}, u32[]{:S(2)}) collective-permute-start(f32[4,128,128]{2,1,0:T(8,128)S(1)} %multiply_add_fusion.3), channel_id=1, source_target_pairs={{0,8},{1,9},{2,10},{3,11},{4,12},{5,13},{6,14},{7,15},{16,24},{17,... | collective-permute-start | bytes 786440 | tf_op jit(solution)/shard_map/ppermute | solution.py:82
  50.4 5.6 %collective-permute-start.5 = (f32[4,128,128]{2,1,0:T(8,128)S(1)}, f32[4,128,128]{2,1,0:T(8,128)S(1)}, u32[]{:S(2)}, u32[]{:S(2)}) collective-permute-start(f32[4,128,128]{2,1,0:T(8,128)S(1)} %get-tuple-element.100), channel_id=1, source_target_pairs={{0,1},{1,2},{2,3},{3,0},{4,5},{5,6},{6,7},{7,4},{8,9},{9,10},{10,1... | collective-permute-start | bytes 786440 | tf_op jit(solution)/shard_map/ppermute | solution.py:50
  50.8 13.4 %collective-permute-start.6 = (f32[4,128,128]{2,1,0:T(8,128)S(1)}, f32[4,128,128]{2,1,0:T(8,128)S(1)}, u32[]{:S(2)}, u32[]{:S(2)}) collective-permute-start(f32[4,128,128]{2,1,0:T(8,128)S(1)} %get-tuple-element.99), channel_id=1, source_target_pairs={{0,2},{1,3},{2,0},{3,1},{4,6},{5,7},{6,4},{7,5},{8,10},{9,11},{10,... | collective-permute-start | bytes 786440 | tf_op jit(solution)/shard_map/ppermute | solution.py:50
  52.9 12.0 %collective-permute-start.7 = (f32[4,128,128]{2,1,0:T(8,128)S(1)}, f32[4,128,128]{2,1,0:T(8,128)S(1)}, u32[]{:S(2)}, u32[]{:S(2)}) collective-permute-start(f32[4,128,128]{2,1,0:T(8,128)S(1)} %get-tuple-element.98), channel_id=1, source_target_pairs={{0,3},{1,0},{2,1},{3,2},{4,7},{5,4},{6,5},{7,6},{8,11},{9,8},{10,9... | collective-permute-start | bytes 786440 | tf_op jit(solution)/shard_map/ppermute | solution.py:50
  64.9 1.0 copy-start
  73.1 1.2 copy-start.3
  74.4 5.5 %collective-permute-start.8 = (f32[4,128,128]{2,1,0:T(8,128)S(1)}, f32[4,128,128]{2,1,0:T(8,128)S(1)}, u32[]{:S(2)}, u32[]{:S(2)}) collective-permute-start(f32[4,128,128]{2,1,0:T(8,128)S(1)} %get-tuple-element.96), channel_id=1, source_target_pairs={{0,1},{1,2},{2,3},{3,0},{4,5},{5,6},{6,7},{7,4},{8,9},{9,10},{10,1... | collective-permute-start | bytes 786440 | tf_op jit(solution)/shard_map/ppermute | solution.py:50
  74.5 11.0 %collective-permute-start.9 = (f32[4,128,128]{2,1,0:T(8,128)S(1)}, f32[4,128,128]{2,1,0:T(8,128)S(1)}, u32[]{:S(2)}, u32[]{:S(2)}) collective-permute-start(f32[4,128,128]{2,1,0:T(8,128)S(1)} %get-tuple-element.95), channel_id=1, source_target_pairs={{0,2},{1,3},{2,0},{3,1},{4,6},{5,7},{6,4},{7,5},{8,10},{9,11},{10,... | collective-permute-start | bytes 786440 | tf_op jit(solution)/shard_map/ppermute | solution.py:50
  75.9 10.4 %collective-permute-start.10 = (f32[4,128,128]{2,1,0:T(8,128)S(1)}, f32[4,128,128]{2,1,0:T(8,128)S(1)}, u32[]{:S(2)}, u32[]{:S(2)}) collective-permute-start(f32[4,128,128]{2,1,0:T(8,128)S(1)} %get-tuple-element.94), channel_id=1, source_target_pairs={{0,3},{1,0},{2,1},{3,2},{4,7},{5,4},{6,5},{7,6},{8,11},{9,8},{10,9... | collective-permute-start | bytes 786440 | tf_op jit(solution)/shard_map/ppermute | solution.py:50
  88.2 15.4 %collective-permute-start.11 = (f32[4,128,128]{2,1,0:T(8,128)S(1)}, f32[4,128,128]{2,1,0:T(8,128)S(1)}, u32[]{:S(2)}, u32[]{:S(2)}) collective-permute-start(f32[4,128,128]{2,1,0:T(8,128)S(1)} %get-tuple-element.51), channel_id=1, source_target_pairs={{4,0},{5,1},{6,2},{7,3},{8,4},{9,5},{10,6},{11,7},{12,8},{13,9},{1... | collective-permute-start | bytes 786440 | tf_op jit(solution)/shard_map/ppermute | solution.py:82
  103.7 20.3 %collective-permute-start.12 = (f32[4,128,128]{2,1,0:T(8,128)S(1)}, f32[4,128,128]{2,1,0:T(8,128)S(1)}, u32[]{:S(2)}, u32[]{:S(2)}) collective-permute-start(f32[4,128,128]{2,1,0:T(8,128)S(1)} %multiply_add_fusion.1), channel_id=1, source_target_pairs={{8,0},{9,1},{10,2},{11,3},{12,4},{13,5},{14,6},{15,7},{24,16},{25,... | collective-permute-start | bytes 786440 | tf_op jit(solution)/shard_map/ppermute | solution.py:82
  126.3 5.1 %collective-permute-start.13 = (f32[4,128,128]{2,1,0:T(8,128)S(1)}, f32[4,128,128]{2,1,0:T(8,128)S(1)}, u32[]{:S(2)}, u32[]{:S(2)}) collective-permute-start(f32[4,128,128]{2,1,0:T(8,128)S(1)} %get-tuple-element.92), channel_id=1, source_target_pairs={{0,1},{1,2},{2,3},{3,0},{4,5},{5,6},{6,7},{7,4},{8,9},{9,10},{10,1... | collective-permute-start | bytes 786440 | tf_op jit(solution)/shard_map/ppermute | solution.py:50
  126.4 13.3 %collective-permute-start.14 = (f32[4,128,128]{2,1,0:T(8,128)S(1)}, f32[4,128,128]{2,1,0:T(8,128)S(1)}, u32[]{:S(2)}, u32[]{:S(2)}) collective-permute-start(f32[4,128,128]{2,1,0:T(8,128)S(1)} %get-tuple-element.91), channel_id=1, source_target_pairs={{0,2},{1,3},{2,0},{3,1},{4,6},{5,7},{6,4},{7,5},{8,10},{9,11},{10,... | collective-permute-start | bytes 786440 | tf_op jit(solution)/shard_map/ppermute | solution.py:50
  129.5 10.9 %collective-permute-start.15 = (f32[4,128,128]{2,1,0:T(8,128)S(1)}, f32[4,128,128]{2,1,0:T(8,128)S(1)}, u32[]{:S(2)}, u32[]{:S(2)}) collective-permute-start(f32[4,128,128]{2,1,0:T(8,128)S(1)} %get-tuple-element.90), channel_id=1, source_target_pairs={{0,3},{1,0},{2,1},{3,2},{4,7},{5,4},{6,5},{7,6},{8,11},{9,8},{10,9... | collective-permute-start | bytes 786440 | tf_op jit(solution)/shard_map/ppermute | solution.py:50
  140.4 1.0 copy-start.1

commit v14 on v12

--- a/solution.py
+++ b/solution.py
@@ -58,8 +58,14 @@
     keep_row = keep_of((lax.axis_index("seq") // GROUP) * GROUP + lax.iota(jnp.int32, GROUP))
     count = lax.axis_size("seq")
     heads = state.shape[0]
+    early = direction < 0
+    if early:
+        state, filler_inputs = lax.optimization_barrier((state, filler_inputs))
     pieces = state.reshape((GROUP, heads // GROUP) + state.shape[1:])
     mine = member_exchange(pieces, "seq")
+    if early:
+        filled = filler(*filler_inputs)
+        mine, filled = lax.optimization_barrier((mine, filled))
     order = range(GROUP) if direction > 0 else range(GROUP - 1, -1, -1)
     inner = [None] * GROUP
     inner_keep = [None] * GROUP
@@ -73,7 +79,8 @@
     row = lax.axis_index("seq") // GROUP
     entering = jnp.zeros_like(total)
     weight = jnp.ones((), jnp.float32)
-    total, filler_inputs = lax.optimization_barrier((total, filler_inputs))
+    if not early:
+        total, filler_inputs = lax.optimization_barrier((total, filler_inputs))
     reaches = -(-SPAN // GROUP)
 
     def shifted(value, reach):
@@ -87,13 +94,16 @@
     if reaches == 3:
         previous = shifted(total, 1)
         paired = total + total_keep * previous
-        filled = filler(*filler_inputs)
-        farther, filled = lax.optimization_barrier((shifted(paired, 2), filled))
+        farther = shifted(paired, 2)
+        if not early:
+            filled = filler(*filler_inputs)
+            farther, filled = lax.optimization_barrier((farther, filled))
         entering = previous + row_keep(1) * farther
     else:
         received = [shifted(total, reach) for reach in range(1, reaches + 1)]
-        filled = filler(*filler_inputs)
-        received, filled = lax.optimization_barrier((received, filled))
+        if not early:
+            filled = filler(*filler_inputs)
+            received, filled = lax.optimization_barrier((received, filled))
         for reach in range(1, reaches + 1):
             entering = entering + weight * received[reach - 1]
             weight = weight * row_keep(reach)

time: 143 us -> 145 us (1.014)
    ppermute x12, waiting for transfers between devices: 42.1 us -> 31.3 us  [member_exchange(): got.append(lax.ppermute(piece, axis, pairs))]
    ppermute x4, waiting for transfers between devices: 15.1 us -> 25.7 us  [shifted(): return lax.ppermute(value, 'seq', pairs)]
  transfers between devices with their start and end apart: 16 -> 16, of which waited for: 15 -> 12; matrix products, arithmetic and copies ran while one was open for 3% -> 3% of each run, Pallas kernels for 14% -> 13%
where the time goes in v14:
time: 145 us; the launch traced here: 144 us
  waiting for transfers between devices  57 us (39%)
  Pallas kernels  38.1 us (26%)
  starting transfers between devices  21.6 us (15%)
  other arithmetic  11.6 us (8%)
  between operations  8.17 us (6%)
  local copies, waits for them, and re-layouts  7.19 us (5%)
    ppermute x12, waiting for transfers between devices, member_exchange(): got.append(lax.ppermute(piece, axis, pairs))  31.3 us
    pallas_call x4, Pallas kernels, head_call(): pl.pallas_call(body, grid=(heads // HEAD_STEP,), in_specs=[spec(x.shape)...  30.9 us
    ppermute x4, waiting for transfers between devices, shifted(): return lax.ppermute(value, 'seq', pairs)  25.7 us
    ppermute x4, starting transfers between devices, shifted(): return lax.ppermute(value, 'seq', pairs)  11.7 us
    ppermute x12, starting transfers between devices, member_exchange(): got.append(lax.ppermute(piece, axis, pairs))  9.82 us
    pallas_call x1, Pallas kernels, middle_call(): pl.pallas_call(middle_body, grid=(rows // step,), in_specs=[row_block, ro...  7.29 us
    another operation x6, other arithmetic, row_scan(): jnp.stack([inner[index] + inner_keep[index] * entering for index in range...  4.23 us
    add x2, other arithmetic, row_scan(): total = mine[index] + keep_row[index] * total  4.06 us
  transfers between devices with their start and end apart: 16, of which 12 were waited for; matrix products, arithmetic and copies ran while one was open for 3% of the time, Pallas kernels for 13%

profile of v14, /device:TPU:1, one launch (start us, length us, event | category | flops | bytes accessed | tf_op | source)
XLA Modules:
  0.0 143.7 jit_solution(17123929427227551780)
XLA Ops:
  0.7 0.8 select_reduce_fusion.1
  1.6 0.8 broadcast_in_dim.101.rel_ref
  2.4 4.6 %shard_map.84 = f32[16,128,128]{2,1,0:T(8,128)} custom-call(bf16[384,2048]{1,0:T(8,128)(2,1)} %key_ref.5, bf16[384,2048]{1,0:T(8,128)(2,1)} %value_ref.5, s32[384,128]{1,0:T(8,128)} %broadcast_in_dim.101.rel_ref), custom_call_target="tpu_custom_call" | custom-call | tf_op jit(solution)/shard_map/pallas_call | solution.py:154
  7.1 1.1 copy-done.2
  8.3 2.6 %collective-permute-start = (f32[4,128,128]{2,1,0:T(8,128)S(1)}, f32[4,128,128]{2,1,0:T(8,128)S(1)}, u32[]{:S(2)}, u32[]{:S(2)}) collective-permute-start(f32[4,128,128]{2,1,0:T(8,128)S(1)} %get-tuple-element.96), channel_id=1, source_target_pairs={{0,1},{1,2},{2,3},{3,0},{4,5},{5,6},{6,7},{7,4},{8,9},{9,10},{10,1... | collective-permute-start | bytes 786440 | tf_op jit(solution)/shard_map/ppermute | solution.py:50
  11.0 0.5 collective-permute-start.2
  11.5 0.2 compare_reduce_fusion.1
  11.7 0.6 fusion.14
  12.9 3.5 %collective-permute-done = f32[4,128,128]{2,1,0:T(8,128)S(1)} collective-permute-done((f32[4,128,128]{2,1,0:T(8,128)S(1)}, f32[4,128,128]{2,1,0:T(8,128)S(1)}, u32[]{:S(2)}, u32[]{:S(2)}) %collective-permute-start) | collective-permute-done | bytes 262176 | tf_op jit(solution)/shard_map/ppermute | solution.py:50
  16.4 5.6 %collective-permute-done.1 = f32[4,128,128]{2,1,0:T(8,128)S(1)} collective-permute-done((f32[4,128,128]{2,1,0:T(8,128)S(1)}, f32[4,128,128]{2,1,0:T(8,128)S(1)}, u32[]{:S(2)}, u32[]{:S(2)}) %collective-permute-start.1) | collective-permute-done | bytes 262176 | tf_op jit(solution)/shard_map/ppermute | solution.py:50
  22.1 0.5 collective-permute-done.2
  22.6 2.0 %fusion.3 = (f32[4,128,128]{2,1,0:T(8,128)S(1)}, f32[4,128,128]{2,1,0:T(8,128)S(1)}) fusion(f32[4,4,128,128]{3,2,1,0:T(8,128)S(1)} %bitcast_dynamic-update-slice_fusion.9, f32[]{:T(128)} %bitcast.8, f32[]{:T(128)} %bitcast.10, f32[]{:T(128)S(6)} %mul.176, f32[]{:T(128)} %bitcast.12), kind=kLoop, calls=%fused_computation.9 | loop fusion | flops 458752 | bytes 1572880 | tf_op jit(solution)/shard_map/add | solution.py:77
  24.6 4.0 %collective-permute-start.3 = (f32[4,128,128]{2,1,0:T(8,128)S(1)}, f32[4,128,128]{2,1,0:T(8,128)S(1)}, u32[]{:S(2)}, u32[]{:S(2)}) collective-permute-start(f32[4,128,128]{2,1,0:T(8,128)S(1)} %get-tuple-element.34), channel_id=1, source_target_pairs={{0,4},{1,5},{2,6},{3,7},{4,8},{5,9},{6,10},{7,11},{8,12},{9,13},{1... | collective-permute-start | bytes 786440 | tf_op jit(solution)/shard_map/ppermute | solution.py:89
  31.2 3.3 %collective-permute-done.3 = f32[4,128,128]{2,1,0:T(8,128)S(1)} collective-permute-done((f32[4,128,128]{2,1,0:T(8,128)S(1)}, f32[4,128,128]{2,1,0:T(8,128)S(1)}, u32[]{:S(2)}, u32[]{:S(2)}) %collective-permute-start.3) | collective-permute-done | bytes 262176 | tf_op jit(solution)/shard_map/ppermute | solution.py:89
  34.6 5.1 %collective-permute-start.4 = (f32[4,128,128]{2,1,0:T(8,128)S(1)}, f32[4,128,128]{2,1,0:T(8,128)S(1)}, u32[]{:S(2)}, u32[]{:S(2)}) collective-permute-start(f32[4,128,128]{2,1,0:T(8,128)S(1)} %multiply_add_fusion.3), channel_id=1, source_target_pairs={{0,8},{1,9},{2,10},{3,11},{4,12},{5,13},{6,14},{7,15},{16,24},{17,... | collective-permute-start | bytes 786440 | tf_op jit(solution)/shard_map/ppermute | solution.py:89
  39.7 0.6 subtract_reduce_fusion
  40.4 7.7 %shard_map.85 = (bf16[16,384,384]{2,1,0:T(8,128)(2,1)}, f32[384,2048]{1,0:T(8,128)}) custom-call(bf16[384,2048]{1,0:T(8,128)(2,1)} %query_ref.3, bf16[384,2048]{1,0:T(8,128)(2,1)} %key_ref.5, bf16[384,2048]{1,0:T(8,128)(2,1)} %value_ref.5, s32[384,128]{1,0:T(8,128)} %broadcast_in_dim.101.rel_ref), custom_call_target="tpu_custom_call" | custom-call | tf_op jit(solution)/shard_map/pallas_call | solution.py:154
  48.1 1.3 add_bitcast_fusion.4
  49.4 0.7 add_bitcast_fusion.3
  50.4 0.4 collective-permute-start.5
  50.8 1.9 %collective-permute-start.6 = (f32[4,128,128]{2,1,0:T(8,128)S(1)}, f32[4,128,128]{2,1,0:T(8,128)S(1)}, u32[]{:S(2)}, u32[]{:S(2)}) collective-permute-start(f32[4,128,128]{2,1,0:T(8,128)S(1)} %get-tuple-element.91), channel_id=1, source_target_pairs={{0,2},{1,3},{2,0},{3,1},{4,6},{5,7},{6,4},{7,5},{8,10},{9,11},{10,... | collective-permute-start | bytes 786440 | tf_op jit(solution)/shard_map/ppermute | solution.py:50
  52.7 0.2 convert_reduce_fusion
  52.9 3.1 %collective-permute-done.5 = f32[4,128,128]{2,1,0:T(8,128)S(1)} collective-permute-done((f32[4,128,128]{2,1,0:T(8,128)S(1)}, f32[4,128,128]{2,1,0:T(8,128)S(1)}, u32[]{:S(2)}, u32[]{:S(2)}) %collective-permute-start.5) | collective-permute-done | bytes 262176 | tf_op jit(solution)/shard_map/ppermute | solution.py:50
  56.0 8.2 %collective-permute-done.6 = f32[4,128,128]{2,1,0:T(8,128)S(1)} collective-permute-done((f32[4,128,128]{2,1,0:T(8,128)S(1)}, f32[4,128,128]{2,1,0:T(8,128)S(1)}, u32[]{:S(2)}, u32[]{:S(2)}) %collective-permute-start.6) | collective-permute-done | bytes 262176 | tf_op jit(solution)/shard_map/ppermute | solution.py:50
  64.2 0.6 collective-permute-done.7
  64.9 1.0 copy-done
  65.8 7.3 %shard_map.86 = (bf16[384,2048]{1,0:T(8,128)(2,1)}, bf16[384,2048]{1,0:T(8,128)(2,1)}, f32[16,128,128]{2,1,0:T(8,128)}) custom-call(bf16[384,2048]{1,0:T(8,128)(2,1)} %query_ref.3, f32[384,2048]{1,0:T(8,128)} %get-tuple-element.41.inside_ref, f32[16,128,128]{2,1,0:T(8,128)} %bitcast.117, bf16[384,2048]{1,0:T(8,128)(2,1)} %cot_ref.1, ...), custom_call_target="tpu_custom_call" | custom-call | tf_op jit(solution)/shard_map/pallas_call | solution.py:262
  73.3 1.1 copy-done.3
  74.6 0.7 fusion.13
  75.9 0.5 collective-permute-start.10
  76.3 11.6 %shard_map.87 = (bf16[384,2048]{1,0:T(8,128)(2,1)}, f32[384,2048]{1,0:T(8,128)}, f32[384,2048]{1,0:T(8,128)}) custom-call(bf16[384,2048]{1,0:T(8,128)(2,1)} %query_ref.3, bf16[384,2048]{1,0:T(8,128)(2,1)} %key_ref.5, bf16[384,2048]{1,0:T(8,128)(2,1)} %value_ref.5, bf16[384,2048]{1,0:T(8,128)(2,1)} %get-tuple-element.51.grad_ref, ...), custom_call_target="tpu_custom_call" | custom-call | tf_op jit(solution)/shard_map/pallas_call | solution.py:154
  88.0 2.0 %bitcast_add_fusion = (f32[4,128,128]{2,1,0:T(8,128)S(1)}, f32[4,128,128]{2,1,0:T(8,128)S(1)}) fusion(f32[4,4,128,128]{3,2,1,0:T(8,128)S(1)} %bitcast_dynamic-update-slice_fusion.3, f32[]{:T(128)} %bitcast.40, f32[]{:T(128)} %bitcast.34, f32[]{:T(128)S(6)} %mul.198, f32[]{:T(128)} %bitcast.36), kind=kLoop, calls=%fused_computation.13 | loop fusion | flops 458752 | bytes 1572880 | tf_op jit(solution)/shard_map/add | solution.py:77
  90.1 1.3 collective-permute-start.11
  94.0 8.6 %collective-permute-done.11 = f32[4,128,128]{2,1,0:T(8,128)S(1)} collective-permute-done((f32[4,128,128]{2,1,0:T(8,128)S(1)}, f32[4,128,128]{2,1,0:T(8,128)S(1)}, u32[]{:S(2)}, u32[]{:S(2)}) %collective-permute-start.11) | collective-permute-done | bytes 262176 | tf_op jit(solution)/shard_map/ppermute | solution.py:89
  102.6 1.3 collective-permute-start.12
  103.9 0.6 fusion.10
  104.5 13.8 %collective-permute-done.12 = f32[4,128,128]{2,1,0:T(8,128)S(1)} collective-permute-done((f32[4,128,128]{2,1,0:T(8,128)S(1)}, f32[4,128,128]{2,1,0:T(8,128)S(1)}, u32[]{:S(2)}, u32[]{:S(2)}) %collective-permute-start.12) | collective-permute-done | bytes 262176 | tf_op jit(solution)/shard_map/ppermute | solution.py:89
  118.3 1.3 add_bitcast_fusion.1
  119.7 0.7 add_bitcast_fusion
  120.6 3.3 %collective-permute-start.13 = (f32[4,128,128]{2,1,0:T(8,128)S(1)}, f32[4,128,128]{2,1,0:T(8,128)S(1)}, u32[]{:S(2)}, u32[]{:S(2)}) collective-permute-start(f32[4,128,128]{2,1,0:T(8,128)S(1)} %get-tuple-element.84), channel_id=1, source_target_pairs={{0,1},{1,2},{2,3},{3,0},{4,5},{5,6},{6,7},{7,4},{8,9},{9,10},{10,1... | collective-permute-start | bytes 786440 | tf_op jit(solution)/shard_map/ppermute | solution.py:50
  123.9 0.6 compare_reduce_fusion
  125.2 0.5 collective-permute-start.15
  125.7 3.7 %collective-permute-done.13 = f32[4,128,128]{2,1,0:T(8,128)S(1)} collective-permute-done((f32[4,128,128]{2,1,0:T(8,128)S(1)}, f32[4,128,128]{2,1,0:T(8,128)S(1)}, u32[]{:S(2)}, u32[]{:S(2)}) %collective-permute-start.13) | collective-permute-done | bytes 262176 | tf_op jit(solution)/shard_map/ppermute | solution.py:50
  129.4 5.6 %collective-permute-done.14 = f32[4,128,128]{2,1,0:T(8,128)S(1)} collective-permute-done((f32[4,128,128]{2,1,0:T(8,128)S(1)}, f32[4,128,128]{2,1,0:T(8,128)S(1)}, u32[]{:S(2)}, u32[]{:S(2)}) %collective-permute-start.14) | collective-permute-done | bytes 262176 | tf_op jit(solution)/shard_map/ppermute | solution.py:50
  135.0 0.6 collective-permute-done.15
  135.6 0.6 broadcast_in_dim.114.gate_ref
  136.3 0.3 copy-done.1
  136.6 7.0 %shard_map.88 = (bf16[384,2048]{1,0:T(8,128)(2,1)}, bf16[384,2048]{1,0:T(8,128)(2,1)}) custom-call(bf16[384,2048]{1,0:T(8,128)(2,1)} %key_ref.5, bf16[384,2048]{1,0:T(8,128)(2,1)} %value_ref.5, f32[384,2048]{1,0:T(8,128)} %get-tuple-element.59.key_part, f32[384,2048]{1,0:T(8,128)} %get-tuple-element.60.value_part, f32[16,128,128]{2,1,0:T(8,128)} %bitcast.119, ...), custom_call_target="tpu_custom_call" | custom-call | tf_op jit(solution)/shard_map/pallas_call | solution.py:154
  (45 shorter events, 1.5 us)
Async XLA Ops:
  7.0 1.2 copy-start.2
  8.3 8.1 %collective-permute-start = (f32[4,128,128]{2,1,0:T(8,128)S(1)}, f32[4,128,128]{2,1,0:T(8,128)S(1)}, u32[]{:S(2)}, u32[]{:S(2)}) collective-permute-start(f32[4,128,128]{2,1,0:T(8,128)S(1)} %get-tuple-element.96), channel_id=1, source_target_pairs={{0,1},{1,2},{2,3},{3,0},{4,5},{5,6},{6,7},{7,4},{8,9},{9,10},{10,1... | collective-permute-start | bytes 786440 | tf_op jit(solution)/shard_map/ppermute | solution.py:50
  11.0 11.1 %collective-permute-start.1 = (f32[4,128,128]{2,1,0:T(8,128)S(1)}, f32[4,128,128]{2,1,0:T(8,128)S(1)}, u32[]{:S(2)}, u32[]{:S(2)}) collective-permute-start(f32[4,128,128]{2,1,0:T(8,128)S(1)} %get-tuple-element.95), channel_id=1, source_target_pairs={{0,2},{1,3},{2,0},{3,1},{4,6},{5,7},{6,4},{7,5},{8,10},{9,11},{10,... | collective-permute-start | bytes 786440 | tf_op jit(solution)/shard_map/ppermute | solution.py:50
  11.0 11.6 %collective-permute-start.2 = (f32[4,128,128]{2,1,0:T(8,128)S(1)}, f32[4,128,128]{2,1,0:T(8,128)S(1)}, u32[]{:S(2)}, u32[]{:S(2)}) collective-permute-start(f32[4,128,128]{2,1,0:T(8,128)S(1)} %get-tuple-element.94), channel_id=1, source_target_pairs={{0,3},{1,0},{2,1},{3,2},{4,7},{5,4},{6,5},{7,6},{8,11},{9,8},{10,9... | collective-permute-start | bytes 786440 | tf_op jit(solution)/shard_map/ppermute | solution.py:50
  24.6 10.0 %collective-permute-start.3 = (f32[4,128,128]{2,1,0:T(8,128)S(1)}, f32[4,128,128]{2,1,0:T(8,128)S(1)}, u32[]{:S(2)}, u32[]{:S(2)}) collective-permute-start(f32[4,128,128]{2,1,0:T(8,128)S(1)} %get-tuple-element.34), channel_id=1, source_target_pairs={{0,4},{1,5},{2,6},{3,7},{4,8},{5,9},{6,10},{7,11},{8,12},{9,13},{1... | collective-permute-start | bytes 786440 | tf_op jit(solution)/shard_map/ppermute | solution.py:89
  34.6 13.4 %collective-permute-start.4 = (f32[4,128,128]{2,1,0:T(8,128)S(1)}, f32[4,128,128]{2,1,0:T(8,128)S(1)}, u32[]{:S(2)}, u32[]{:S(2)}) collective-permute-start(f32[4,128,128]{2,1,0:T(8,128)S(1)} %multiply_add_fusion.3), channel_id=1, source_target_pairs={{0,8},{1,9},{2,10},{3,11},{4,12},{5,13},{6,14},{7,15},{16,24},{17,... | collective-permute-start | bytes 786440 | tf_op jit(solution)/shard_map/ppermute | solution.py:89
  50.4 5.6 %collective-permute-start.5 = (f32[4,128,128]{2,1,0:T(8,128)S(1)}, f32[4,128,128]{2,1,0:T(8,128)S(1)}, u32[]{:S(2)}, u32[]{:S(2)}) collective-permute-start(f32[4,128,128]{2,1,0:T(8,128)S(1)} %get-tuple-element.92), channel_id=1, source_target_pairs={{0,1},{1,2},{2,3},{3,0},{4,5},{5,6},{6,7},{7,4},{8,9},{9,10},{10,1... | collective-permute-start | bytes 786440 | tf_op jit(solution)/shard_map/ppermute | solution.py:50
  50.8 13.4 %collective-permute-start.6 = (f32[4,128,128]{2,1,0:T(8,128)S(1)}, f32[4,128,128]{2,1,0:T(8,128)S(1)}, u32[]{:S(2)}, u32[]{:S(2)}) collective-permute-start(f32[4,128,128]{2,1,0:T(8,128)S(1)} %get-tuple-element.91), channel_id=1, source_target_pairs={{0,2},{1,3},{2,0},{3,1},{4,6},{5,7},{6,4},{7,5},{8,10},{9,11},{10,... | collective-permute-start | bytes 786440 | tf_op jit(solution)/shard_map/ppermute | solution.py:50
  52.9 12.0 %collective-permute-start.7 = (f32[4,128,128]{2,1,0:T(8,128)S(1)}, f32[4,128,128]{2,1,0:T(8,128)S(1)}, u32[]{:S(2)}, u32[]{:S(2)}) collective-permute-start(f32[4,128,128]{2,1,0:T(8,128)S(1)} %get-tuple-element.90), channel_id=1, source_target_pairs={{0,3},{1,0},{2,1},{3,2},{4,7},{5,4},{6,5},{7,6},{8,11},{9,8},{10,9... | collective-permute-start | bytes 786440 | tf_op jit(solution)/shard_map/ppermute | solution.py:50
  64.9 1.0 copy-start
  73.1 1.2 copy-start.3
  74.4 13.5 %collective-permute-start.8 = (f32[4,128,128]{2,1,0:T(8,128)S(1)}, f32[4,128,128]{2,1,0:T(8,128)S(1)}, u32[]{:S(2)}, u32[]{:S(2)}) collective-permute-start(f32[4,128,128]{2,1,0:T(8,128)S(1)} %get-tuple-element.88), channel_id=1, source_target_pairs={{0,1},{1,2},{2,3},{3,0},{4,5},{5,6},{6,7},{7,4},{8,9},{9,10},{10,1... | collective-permute-start | bytes 786440 | tf_op jit(solution)/shard_map/ppermute | solution.py:50
  74.5 13.4 %collective-permute-start.9 = (f32[4,128,128]{2,1,0:T(8,128)S(1)}, f32[4,128,128]{2,1,0:T(8,128)S(1)}, u32[]{:S(2)}, u32[]{:S(2)}) collective-permute-start(f32[4,128,128]{2,1,0:T(8,128)S(1)} %get-tuple-element.87), channel_id=1, source_target_pairs={{0,2},{1,3},{2,0},{3,1},{4,6},{5,7},{6,4},{7,5},{8,10},{9,11},{10,... | collective-permute-start | bytes 786440 | tf_op jit(solution)/shard_map/ppermute | solution.py:50
  75.9 12.1 %collective-permute-start.10 = (f32[4,128,128]{2,1,0:T(8,128)S(1)}, f32[4,128,128]{2,1,0:T(8,128)S(1)}, u32[]{:S(2)}, u32[]{:S(2)}) collective-permute-start(f32[4,128,128]{2,1,0:T(8,128)S(1)} %get-tuple-element.86), channel_id=1, source_target_pairs={{0,3},{1,0},{2,1},{3,2},{4,7},{5,4},{6,5},{7,6},{8,11},{9,8},{10,9... | collective-permute-start | bytes 786440 | tf_op jit(solution)/shard_map/ppermute | solution.py:50
  90.1 12.5 %collective-permute-start.11 = (f32[4,128,128]{2,1,0:T(8,128)S(1)}, f32[4,128,128]{2,1,0:T(8,128)S(1)}, u32[]{:S(2)}, u32[]{:S(2)}) collective-permute-start(f32[4,128,128]{2,1,0:T(8,128)S(1)} %get-tuple-element.76), channel_id=1, source_target_pairs={{4,0},{5,1},{6,2},{7,3},{8,4},{9,5},{10,6},{11,7},{12,8},{13,9},{1... | collective-permute-start | bytes 786440 | tf_op jit(solution)/shard_map/ppermute | solution.py:89
  102.6 15.7 %collective-permute-start.12 = (f32[4,128,128]{2,1,0:T(8,128)S(1)}, f32[4,128,128]{2,1,0:T(8,128)S(1)}, u32[]{:S(2)}, u32[]{:S(2)}) collective-permute-start(f32[4,128,128]{2,1,0:T(8,128)S(1)} %multiply_add_fusion.1), channel_id=1, source_target_pairs={{8,0},{9,1},{10,2},{11,3},{12,4},{13,5},{14,6},{15,7},{24,16},{25,... | collective-permute-start | bytes 786440 | tf_op jit(solution)/shard_map/ppermute | solution.py:89
  120.6 8.8 %collective-permute-start.13 = (f32[4,128,128]{2,1,0:T(8,128)S(1)}, f32[4,128,128]{2,1,0:T(8,128)S(1)}, u32[]{:S(2)}, u32[]{:S(2)}) collective-permute-start(f32[4,128,128]{2,1,0:T(8,128)S(1)} %get-tuple-element.84), channel_id=1, source_target_pairs={{0,1},{1,2},{2,3},{3,0},{4,5},{5,6},{6,7},{7,4},{8,9},{9,10},{10,1... | collective-permute-start | bytes 786440 | tf_op jit(solution)/shard_map/ppermute | solution.py:50
  123.9 11.1 %collective-permute-start.14 = (f32[4,128,128]{2,1,0:T(8,128)S(1)}, f32[4,128,128]{2,1,0:T(8,128)S(1)}, u32[]{:S(2)}, u32[]{:S(2)}) collective-permute-start(f32[4,128,128]{2,1,0:T(8,128)S(1)} %get-tuple-element.83), channel_id=1, source_target_pairs={{0,2},{1,3},{2,0},{3,1},{4,6},{5,7},{6,4},{7,5},{8,10},{9,11},{10,... | collective-permute-start | bytes 786440 | tf_op jit(solution)/shard_map/ppermute | solution.py:50
  125.2 10.4 %collective-permute-start.15 = (f32[4,128,128]{2,1,0:T(8,128)S(1)}, f32[4,128,128]{2,1,0:T(8,128)S(1)}, u32[]{:S(2)}, u32[]{:S(2)}) collective-permute-start(f32[4,128,128]{2,1,0:T(8,128)S(1)} %get-tuple-element.82), channel_id=1, source_target_pairs={{0,3},{1,0},{2,1},{3,2},{4,7},{5,4},{6,5},{7,6},{8,11},{9,8},{10,9... | collective-permute-start | bytes 786440 | tf_op jit(solution)/shard_map/ppermute | solution.py:50
  135.6 1.0 copy-start.1

commit v15 on v12

--- a/solution.py
+++ b/solution.py
@@ -119,7 +119,7 @@
     return windowed_prefix((state, fallback_flag), direction)[0], filler(*filler_inputs)
 
 
-HEAD_STEP = 4
+HEAD_STEP = 8
 INTERPRET = False
 NN = ((1,), (0,))
 NT = ((1,), (1,))

time: 143 us -> 141 us (0.986)
  Pallas kernels: 38.1 us -> 36.5 us
    pallas_call x4, Pallas kernels: 30.8 us -> 29.2 us  [head_call(): pl.pallas_call(body, grid=(heads // HEAD_STEP,), in_specs=[spec(x.shape)...]
where the time goes in v15:
time: 141 us; the launch traced here: 140 us
  waiting for transfers between devices  56.6 us (40%)
  Pallas kernels  36.5 us (26%)
  starting transfers between devices  20.5 us (15%)
  other arithmetic  11.6 us (8%)
  between operations  8.14 us (6%)
  local copies, waits for them, and re-layouts  7.17 us (5%)
    ppermute x12, waiting for transfers between devices, member_exchange(): got.append(lax.ppermute(piece, axis, pairs))  42.1 us
    pallas_call x4, Pallas kernels, head_call(): pl.pallas_call(body, grid=(heads // HEAD_STEP,), in_specs=[spec(x.shape)...  29.2 us
    ppermute x4, waiting for transfers between devices, shifted(): return lax.ppermute(value, 'seq', pairs)  14.5 us
    ppermute x4, starting transfers between devices, shifted(): return lax.ppermute(value, 'seq', pairs)  11.7 us
    ppermute x12, starting transfers between devices, member_exchange(): got.append(lax.ppermute(piece, axis, pairs))  8.73 us
    pallas_call x1, Pallas kernels, middle_call(): pl.pallas_call(middle_body, grid=(rows // step,), in_specs=[row_block, ro...  7.29 us
    another operation x6, other arithmetic, row_scan(): jnp.stack([inner[index] + inner_keep[index] * entering for index in range...  4.3 us
    add x2, other arithmetic, row_scan(): total = mine[index] + keep_row[index] * total  3.89 us
  transfers between devices with their start and end apart: 16, of which 15 were waited for; matrix products, arithmetic and copies ran while one was open for 3% of the time, Pallas kernels for 14%

profile of v15, /device:TPU:1, one launch (start us, length us, event | category | flops | bytes accessed | tf_op | source)
XLA Modules:
  0.0 140.4 jit_solution(8849621916620285059)
XLA Ops:
  0.7 0.8 select_reduce_fusion.1
  1.6 0.8 broadcast_in_dim.101.rel_ref
  2.4 3.2 %shard_map.84 = f32[16,128,128]{2,1,0:T(8,128)} custom-call(bf16[384,2048]{1,0:T(8,128)(2,1)} %key_ref.5, bf16[384,2048]{1,0:T(8,128)(2,1)} %value_ref.5, s32[384,128]{1,0:T(8,128)} %broadcast_in_dim.101.rel_ref), custom_call_target="tpu_custom_call" | custom-call | tf_op jit(solution)/shard_map/pallas_call | solution.py:144
  5.8 1.1 copy-done.2
  7.0 2.6 %collective-permute-start = (f32[4,128,128]{2,1,0:T(8,128)S(1)}, f32[4,128,128]{2,1,0:T(8,128)S(1)}, u32[]{:S(2)}, u32[]{:S(2)}) collective-permute-start(f32[4,128,128]{2,1,0:T(8,128)S(1)} %get-tuple-element.96), channel_id=1, source_target_pairs={{0,1},{1,2},{2,3},{3,0},{4,5},{5,6},{6,7},{7,4},{8,9},{9,10},{10,1... | collective-permute-start | bytes 786440 | tf_op jit(solution)/shard_map/ppermute | solution.py:50
  9.6 0.5 collective-permute-start.2
  10.4 0.6 fusion.16
  11.6 3.5 %collective-permute-done = f32[4,128,128]{2,1,0:T(8,128)S(1)} collective-permute-done((f32[4,128,128]{2,1,0:T(8,128)S(1)}, f32[4,128,128]{2,1,0:T(8,128)S(1)}, u32[]{:S(2)}, u32[]{:S(2)}) %collective-permute-start) | collective-permute-done | bytes 262176 | tf_op jit(solution)/shard_map/ppermute | solution.py:50
  15.1 5.6 %collective-permute-done.1 = f32[4,128,128]{2,1,0:T(8,128)S(1)} collective-permute-done((f32[4,128,128]{2,1,0:T(8,128)S(1)}, f32[4,128,128]{2,1,0:T(8,128)S(1)}, u32[]{:S(2)}, u32[]{:S(2)}) %collective-permute-start.1) | collective-permute-done | bytes 262176 | tf_op jit(solution)/shard_map/ppermute | solution.py:50
  20.7 0.5 collective-permute-done.2
  21.3 2.0 %fusion.7 = (f32[4,128,128]{2,1,0:T(8,128)S(1)}, f32[4,128,128]{2,1,0:T(8,128)S(1)}) fusion(f32[4,4,128,128]{3,2,1,0:T(8,128)S(1)} %bitcast_dynamic-update-slice_fusion.9, f32[]{:T(128)} %bitcast.8, f32[]{:T(128)} %bitcast.10, f32[]{:T(128)S(6)} %mul.176, f32[]{:T(128)} %bitcast.12), kind=kLoop, calls=%fused_computation.17 | loop fusion | flops 458752 | bytes 1572880 | tf_op jit(solution)/shard_map/add | solution.py:71
  23.3 4.0 %collective-permute-start.3 = (f32[4,128,128]{2,1,0:T(8,128)S(1)}, f32[4,128,128]{2,1,0:T(8,128)S(1)}, u32[]{:S(2)}, u32[]{:S(2)}) collective-permute-start(f32[4,128,128]{2,1,0:T(8,128)S(1)} %get-tuple-element.34), channel_id=1, source_target_pairs={{0,4},{1,5},{2,6},{3,7},{4,8},{5,9},{6,10},{7,11},{8,12},{9,13},{1... | collective-permute-start | bytes 786440 | tf_op jit(solution)/shard_map/ppermute | solution.py:82
  29.9 3.3 %collective-permute-done.3 = f32[4,128,128]{2,1,0:T(8,128)S(1)} collective-permute-done((f32[4,128,128]{2,1,0:T(8,128)S(1)}, f32[4,128,128]{2,1,0:T(8,128)S(1)}, u32[]{:S(2)}, u32[]{:S(2)}) %collective-permute-start.3) | collective-permute-done | bytes 262176 | tf_op jit(solution)/shard_map/ppermute | solution.py:82
  33.3 5.1 %collective-permute-start.4 = (f32[4,128,128]{2,1,0:T(8,128)S(1)}, f32[4,128,128]{2,1,0:T(8,128)S(1)}, u32[]{:S(2)}, u32[]{:S(2)}) collective-permute-start(f32[4,128,128]{2,1,0:T(8,128)S(1)} %multiply_add_fusion.3), channel_id=1, source_target_pairs={{0,8},{1,9},{2,10},{3,11},{4,12},{5,13},{6,14},{7,15},{16,24},{17,... | collective-permute-start | bytes 786440 | tf_op jit(solution)/shard_map/ppermute | solution.py:82
  38.4 0.6 subtract_reduce_fusion
  39.1 7.6 %shard_map.85 = (bf16[16,384,384]{2,1,0:T(8,128)(2,1)}, f32[384,2048]{1,0:T(8,128)}) custom-call(bf16[384,2048]{1,0:T(8,128)(2,1)} %query_ref.3, bf16[384,2048]{1,0:T(8,128)(2,1)} %key_ref.5, bf16[384,2048]{1,0:T(8,128)(2,1)} %value_ref.5, s32[384,128]{1,0:T(8,128)} %broadcast_in_dim.101.rel_ref), custom_call_target="tpu_custom_call" | custom-call | tf_op jit(solution)/shard_map/pallas_call | solution.py:144
  46.7 1.3 add_bitcast_fusion.5
  48.0 0.7 add_bitcast_fusion.4
  49.1 0.4 collective-permute-start.5
  49.4 1.9 %collective-permute-start.6 = (f32[4,128,128]{2,1,0:T(8,128)S(1)}, f32[4,128,128]{2,1,0:T(8,128)S(1)}, u32[]{:S(2)}, u32[]{:S(2)}) collective-permute-start(f32[4,128,128]{2,1,0:T(8,128)S(1)} %get-tuple-element.91), channel_id=1, source_target_pairs={{0,2},{1,3},{2,0},{3,1},{4,6},{5,7},{6,4},{7,5},{8,10},{9,11},{10,... | collective-permute-start | bytes 786440 | tf_op jit(solution)/shard_map/ppermute | solution.py:50
  51.6 3.1 %collective-permute-done.5 = f32[4,128,128]{2,1,0:T(8,128)S(1)} collective-permute-done((f32[4,128,128]{2,1,0:T(8,128)S(1)}, f32[4,128,128]{2,1,0:T(8,128)S(1)}, u32[]{:S(2)}, u32[]{:S(2)}) %collective-permute-start.5) | collective-permute-done | bytes 262176 | tf_op jit(solution)/shard_map/ppermute | solution.py:50
  54.7 8.2 %collective-permute-done.6 = f32[4,128,128]{2,1,0:T(8,128)S(1)} collective-permute-done((f32[4,128,128]{2,1,0:T(8,128)S(1)}, f32[4,128,128]{2,1,0:T(8,128)S(1)}, u32[]{:S(2)}, u32[]{:S(2)}) %collective-permute-start.6) | collective-permute-done | bytes 262176 | tf_op jit(solution)/shard_map/ppermute | solution.py:50
  62.9 0.6 collective-permute-done.7
  63.5 1.0 copy-done
  64.5 7.3 %shard_map.86 = (bf16[384,2048]{1,0:T(8,128)(2,1)}, bf16[384,2048]{1,0:T(8,128)(2,1)}, f32[16,128,128]{2,1,0:T(8,128)}) custom-call(bf16[384,2048]{1,0:T(8,128)(2,1)} %query_ref.3, f32[384,2048]{1,0:T(8,128)} %get-tuple-element.41.inside_ref, f32[16,128,128]{2,1,0:T(8,128)} %bitcast.122, bf16[384,2048]{1,0:T(8,128)(2,1)} %cot_ref.1, ...), custom_call_target="tpu_custom_call" | custom-call | tf_op jit(solution)/shard_map/pallas_call | solution.py:252
  71.9 1.1 copy-done.3
  73.2 0.7 fusion.15
  74.6 0.5 collective-permute-start.10
  75.0 3.5 %collective-permute-done.8 = f32[4,128,128]{2,1,0:T(8,128)S(1)} collective-permute-done((f32[4,128,128]{2,1,0:T(8,128)S(1)}, f32[4,128,128]{2,1,0:T(8,128)S(1)}, u32[]{:S(2)}, u32[]{:S(2)}) %collective-permute-start.8) | collective-permute-done | bytes 262176 | tf_op jit(solution)/shard_map/ppermute | solution.py:50
  78.6 5.6 %collective-permute-done.9 = f32[4,128,128]{2,1,0:T(8,128)S(1)} collective-permute-done((f32[4,128,128]{2,1,0:T(8,128)S(1)}, f32[4,128,128]{2,1,0:T(8,128)S(1)}, u32[]{:S(2)}, u32[]{:S(2)}) %collective-permute-start.9) | collective-permute-done | bytes 262176 | tf_op jit(solution)/shard_map/ppermute | solution.py:50
  84.2 0.7 collective-permute-done.10
  85.0 1.9 %fusion.3 = (f32[4,128,128]{2,1,0:T(8,128)S(1)}, f32[4,128,128]{2,1,0:T(8,128)S(1)}) fusion(f32[4,4,128,128]{3,2,1,0:T(8,128)S(1)} %bitcast_dynamic-update-slice_fusion.3, f32[]{:T(128)} %bitcast.34, f32[]{:T(128)} %bitcast.36, f32[]{:T(128)S(6)} %mul.199, f32[]{:T(128)} %bitcast.38), kind=kLoop, calls=%fused_computation.9 | loop fusion | flops 458752 | bytes 1572880 | tf_op jit(solution)/shard_map/add | solution.py:71
  86.8 1.3 collective-permute-start.11
  90.6 9.5 %collective-permute-done.11 = f32[4,128,128]{2,1,0:T(8,128)S(1)} collective-permute-done((f32[4,128,128]{2,1,0:T(8,128)S(1)}, f32[4,128,128]{2,1,0:T(8,128)S(1)}, u32[]{:S(2)}, u32[]{:S(2)}) %collective-permute-start.11) | collective-permute-done | bytes 262176 | tf_op jit(solution)/shard_map/ppermute | solution.py:82
  100.2 1.3 collective-permute-start.12
  101.5 0.7 fusion.12
  102.2 12.2 %shard_map.87 = (bf16[384,2048]{1,0:T(8,128)(2,1)}, f32[384,2048]{1,0:T(8,128)}, f32[384,2048]{1,0:T(8,128)}) custom-call(bf16[384,2048]{1,0:T(8,128)(2,1)} %query_ref.3, bf16[384,2048]{1,0:T(8,128)(2,1)} %key_ref.5, bf16[384,2048]{1,0:T(8,128)(2,1)} %value_ref.5, bf16[384,2048]{1,0:T(8,128)(2,1)} %get-tuple-element.51.grad_ref, ...), custom_call_target="tpu_custom_call" | custom-call | tf_op jit(solution)/shard_map/pallas_call | solution.py:144
  114.3 1.7 %collective-permute-done.12 = f32[4,128,128]{2,1,0:T(8,128)S(1)} collective-permute-done((f32[4,128,128]{2,1,0:T(8,128)S(1)}, f32[4,128,128]{2,1,0:T(8,128)S(1)}, u32[]{:S(2)}, u32[]{:S(2)}) %collective-permute-start.12) | collective-permute-done | bytes 262176 | tf_op jit(solution)/shard_map/ppermute | solution.py:82
  116.0 1.3 add_bitcast_fusion.2
  117.4 0.7 add_bitcast_fusion.1
  118.4 1.4 collective-permute-start.13
  119.8 1.3 collective-permute-start.14
  121.1 0.6 compare_reduce_fusion
  122.4 2.8 %collective-permute-done.13 = f32[4,128,128]{2,1,0:T(8,128)S(1)} collective-permute-done((f32[4,128,128]{2,1,0:T(8,128)S(1)}, f32[4,128,128]{2,1,0:T(8,128)S(1)}, u32[]{:S(2)}, u32[]{:S(2)}) %collective-permute-start.13) | collective-permute-done | bytes 262176 | tf_op jit(solution)/shard_map/ppermute | solution.py:50
  125.3 7.3 %collective-permute-done.14 = f32[4,128,128]{2,1,0:T(8,128)S(1)} collective-permute-done((f32[4,128,128]{2,1,0:T(8,128)S(1)}, f32[4,128,128]{2,1,0:T(8,128)S(1)}, u32[]{:S(2)}, u32[]{:S(2)}) %collective-permute-start.14) | collective-permute-done | bytes 262176 | tf_op jit(solution)/shard_map/ppermute | solution.py:50
  132.6 0.6 collective-permute-done.15
  133.3 0.6 broadcast_in_dim.114.gate_ref
  134.2 6.2 %shard_map.88 = (bf16[384,2048]{1,0:T(8,128)(2,1)}, bf16[384,2048]{1,0:T(8,128)(2,1)}) custom-call(bf16[384,2048]{1,0:T(8,128)(2,1)} %key_ref.5, bf16[384,2048]{1,0:T(8,128)(2,1)} %value_ref.5, f32[384,2048]{1,0:T(8,128)} %get-tuple-element.59.key_part, f32[384,2048]{1,0:T(8,128)} %get-tuple-element.60.value_part, f32[16,128,128]{2,1,0:T(8,128)} %bitcast.124, ...), custom_call_target="tpu_custom_call" | custom-call | tf_op jit(solution)/shard_map/pallas_call | solution.py:144
  (45 shorter events, 2.3 us)
Async XLA Ops:
  5.7 1.2 copy-start.2
  7.0 8.1 %collective-permute-start = (f32[4,128,128]{2,1,0:T(8,128)S(1)}, f32[4,128,128]{2,1,0:T(8,128)S(1)}, u32[]{:S(2)}, u32[]{:S(2)}) collective-permute-start(f32[4,128,128]{2,1,0:T(8,128)S(1)} %get-tuple-element.96), channel_id=1, source_target_pairs={{0,1},{1,2},{2,3},{3,0},{4,5},{5,6},{6,7},{7,4},{8,9},{9,10},{10,1... | collective-permute-start | bytes 786440 | tf_op jit(solution)/shard_map/ppermute | solution.py:50
  9.6 11.1 %collective-permute-start.1 = (f32[4,128,128]{2,1,0:T(8,128)S(1)}, f32[4,128,128]{2,1,0:T(8,128)S(1)}, u32[]{:S(2)}, u32[]{:S(2)}) collective-permute-start(f32[4,128,128]{2,1,0:T(8,128)S(1)} %get-tuple-element.95), channel_id=1, source_target_pairs={{0,2},{1,3},{2,0},{3,1},{4,6},{5,7},{6,4},{7,5},{8,10},{9,11},{10,... | collective-permute-start | bytes 786440 | tf_op jit(solution)/shard_map/ppermute | solution.py:50
  9.6 11.6 %collective-permute-start.2 = (f32[4,128,128]{2,1,0:T(8,128)S(1)}, f32[4,128,128]{2,1,0:T(8,128)S(1)}, u32[]{:S(2)}, u32[]{:S(2)}) collective-permute-start(f32[4,128,128]{2,1,0:T(8,128)S(1)} %get-tuple-element.94), channel_id=1, source_target_pairs={{0,3},{1,0},{2,1},{3,2},{4,7},{5,4},{6,5},{7,6},{8,11},{9,8},{10,9... | collective-permute-start | bytes 786440 | tf_op jit(solution)/shard_map/ppermute | solution.py:50
  23.3 10.0 %collective-permute-start.3 = (f32[4,128,128]{2,1,0:T(8,128)S(1)}, f32[4,128,128]{2,1,0:T(8,128)S(1)}, u32[]{:S(2)}, u32[]{:S(2)}) collective-permute-start(f32[4,128,128]{2,1,0:T(8,128)S(1)} %get-tuple-element.34), channel_id=1, source_target_pairs={{0,4},{1,5},{2,6},{3,7},{4,8},{5,9},{6,10},{7,11},{8,12},{9,13},{1... | collective-permute-start | bytes 786440 | tf_op jit(solution)/shard_map/ppermute | solution.py:82
  33.3 13.4 %collective-permute-start.4 = (f32[4,128,128]{2,1,0:T(8,128)S(1)}, f32[4,128,128]{2,1,0:T(8,128)S(1)}, u32[]{:S(2)}, u32[]{:S(2)}) collective-permute-start(f32[4,128,128]{2,1,0:T(8,128)S(1)} %multiply_add_fusion.3), channel_id=1, source_target_pairs={{0,8},{1,9},{2,10},{3,11},{4,12},{5,13},{6,14},{7,15},{16,24},{17,... | collective-permute-start | bytes 786440 | tf_op jit(solution)/shard_map/ppermute | solution.py:82
  49.1 5.6 %collective-permute-start.5 = (f32[4,128,128]{2,1,0:T(8,128)S(1)}, f32[4,128,128]{2,1,0:T(8,128)S(1)}, u32[]{:S(2)}, u32[]{:S(2)}) collective-permute-start(f32[4,128,128]{2,1,0:T(8,128)S(1)} %get-tuple-element.92), channel_id=1, source_target_pairs={{0,1},{1,2},{2,3},{3,0},{4,5},{5,6},{6,7},{7,4},{8,9},{9,10},{10,1... | collective-permute-start | bytes 786440 | tf_op jit(solution)/shard_map/ppermute | solution.py:50
  49.4 13.4 %collective-permute-start.6 = (f32[4,128,128]{2,1,0:T(8,128)S(1)}, f32[4,128,128]{2,1,0:T(8,128)S(1)}, u32[]{:S(2)}, u32[]{:S(2)}) collective-permute-start(f32[4,128,128]{2,1,0:T(8,128)S(1)} %get-tuple-element.91), channel_id=1, source_target_pairs={{0,2},{1,3},{2,0},{3,1},{4,6},{5,7},{6,4},{7,5},{8,10},{9,11},{10,... | collective-permute-start | bytes 786440 | tf_op jit(solution)/shard_map/ppermute | solution.py:50
  51.5 12.0 %collective-permute-start.7 = (f32[4,128,128]{2,1,0:T(8,128)S(1)}, f32[4,128,128]{2,1,0:T(8,128)S(1)}, u32[]{:S(2)}, u32[]{:S(2)}) collective-permute-start(f32[4,128,128]{2,1,0:T(8,128)S(1)} %get-tuple-element.90), channel_id=1, source_target_pairs={{0,3},{1,0},{2,1},{3,2},{4,7},{5,4},{6,5},{7,6},{8,11},{9,8},{10,9... | collective-permute-start | bytes 786440 | tf_op jit(solution)/shard_map/ppermute | solution.py:50
  63.5 1.0 copy-start
  71.8 1.2 copy-start.3
  73.1 5.5 %collective-permute-start.8 = (f32[4,128,128]{2,1,0:T(8,128)S(1)}, f32[4,128,128]{2,1,0:T(8,128)S(1)}, u32[]{:S(2)}, u32[]{:S(2)}) collective-permute-start(f32[4,128,128]{2,1,0:T(8,128)S(1)} %get-tuple-element.88), channel_id=1, source_target_pairs={{0,1},{1,2},{2,3},{3,0},{4,5},{5,6},{6,7},{7,4},{8,9},{9,10},{10,1... | collective-permute-start | bytes 786440 | tf_op jit(solution)/shard_map/ppermute | solution.py:50
  73.2 11.0 %collective-permute-start.9 = (f32[4,128,128]{2,1,0:T(8,128)S(1)}, f32[4,128,128]{2,1,0:T(8,128)S(1)}, u32[]{:S(2)}, u32[]{:S(2)}) collective-permute-start(f32[4,128,128]{2,1,0:T(8,128)S(1)} %get-tuple-element.87), channel_id=1, source_target_pairs={{0,2},{1,3},{2,0},{3,1},{4,6},{5,7},{6,4},{7,5},{8,10},{9,11},{10,... | collective-permute-start | bytes 786440 | tf_op jit(solution)/shard_map/ppermute | solution.py:50
  74.6 10.4 %collective-permute-start.10 = (f32[4,128,128]{2,1,0:T(8,128)S(1)}, f32[4,128,128]{2,1,0:T(8,128)S(1)}, u32[]{:S(2)}, u32[]{:S(2)}) collective-permute-start(f32[4,128,128]{2,1,0:T(8,128)S(1)} %get-tuple-element.86), channel_id=1, source_target_pairs={{0,3},{1,0},{2,1},{3,2},{4,7},{5,4},{6,5},{7,6},{8,11},{9,8},{10,9... | collective-permute-start | bytes 786440 | tf_op jit(solution)/shard_map/ppermute | solution.py:50
  86.8 13.3 %collective-permute-start.11 = (f32[4,128,128]{2,1,0:T(8,128)S(1)}, f32[4,128,128]{2,1,0:T(8,128)S(1)}, u32[]{:S(2)}, u32[]{:S(2)}) collective-permute-start(f32[4,128,128]{2,1,0:T(8,128)S(1)} %get-tuple-element.47), channel_id=1, source_target_pairs={{4,0},{5,1},{6,2},{7,3},{8,4},{9,5},{10,6},{11,7},{12,8},{13,9},{1... | collective-permute-start | bytes 786440 | tf_op jit(solution)/shard_map/ppermute | solution.py:82
  100.2 15.9 %collective-permute-start.12 = (f32[4,128,128]{2,1,0:T(8,128)S(1)}, f32[4,128,128]{2,1,0:T(8,128)S(1)}, u32[]{:S(2)}, u32[]{:S(2)}) collective-permute-start(f32[4,128,128]{2,1,0:T(8,128)S(1)} %multiply_add_fusion.1), channel_id=1, source_target_pairs={{8,0},{9,1},{10,2},{11,3},{12,4},{13,5},{14,6},{15,7},{24,16},{25,... | collective-permute-start | bytes 786440 | tf_op jit(solution)/shard_map/ppermute | solution.py:82
  118.4 6.9 %collective-permute-start.13 = (f32[4,128,128]{2,1,0:T(8,128)S(1)}, f32[4,128,128]{2,1,0:T(8,128)S(1)}, u32[]{:S(2)}, u32[]{:S(2)}) collective-permute-start(f32[4,128,128]{2,1,0:T(8,128)S(1)} %get-tuple-element.84), channel_id=1, source_target_pairs={{0,1},{1,2},{2,3},{3,0},{4,5},{5,6},{6,7},{7,4},{8,9},{9,10},{10,1... | collective-permute-start | bytes 786440 | tf_op jit(solution)/shard_map/ppermute | solution.py:50
  119.8 12.8 %collective-permute-start.14 = (f32[4,128,128]{2,1,0:T(8,128)S(1)}, f32[4,128,128]{2,1,0:T(8,128)S(1)}, u32[]{:S(2)}, u32[]{:S(2)}) collective-permute-start(f32[4,128,128]{2,1,0:T(8,128)S(1)} %get-tuple-element.83), channel_id=1, source_target_pairs={{0,2},{1,3},{2,0},{3,1},{4,6},{5,7},{6,4},{7,5},{8,10},{9,11},{10,... | collective-permute-start | bytes 786440 | tf_op jit(solution)/shard_map/ppermute | solution.py:50
  122.4 10.9 %collective-permute-start.15 = (f32[4,128,128]{2,1,0:T(8,128)S(1)}, f32[4,128,128]{2,1,0:T(8,128)S(1)}, u32[]{:S(2)}, u32[]{:S(2)}) collective-permute-start(f32[4,128,128]{2,1,0:T(8,128)S(1)} %get-tuple-element.82), channel_id=1, source_target_pairs={{0,3},{1,0},{2,1},{3,2},{4,7},{5,4},{6,5},{7,6},{8,11},{9,8},{10,9... | collective-permute-start | bytes 786440 | tf_op jit(solution)/shard_map/ppermute | solution.py:50
  133.3 1.0 copy-start.1

commit v16 on v15

--- a/solution.py
+++ b/solution.py
@@ -119,7 +119,7 @@
     return windowed_prefix((state, fallback_flag), direction)[0], filler(*filler_inputs)
 
 
-HEAD_STEP = 8
+HEAD_STEP = 16
 INTERPRET = False
 NN = ((1,), (0,))
 NT = ((1,), (1,))

time: 141 us -> 143 us (1.014)
  Pallas kernels: 36.5 us -> 41.7 us
  waiting for transfers between devices: 56.6 us -> 53.7 us
    pallas_call x4, Pallas kernels: 29.2 us -> 34.4 us  [head_call(): pl.pallas_call(body, grid=(heads // HEAD_STEP,), in_specs=[spec(x.shape)...]
    ppermute x4, waiting for transfers between devices: 14.5 us -> 11.6 us  [shifted(): return lax.ppermute(value, 'seq', pairs)]
  transfers between devices with their start and end apart: 16 -> 16, of which waited for: 15 -> 14; matrix products, arithmetic and copies ran while one was open for 3% -> 3% of each run, Pallas kernels for 14% -> 17%
where the time goes in v16:
time: 143 us; the launch traced here: 142 us
  waiting for transfers between devices  53.7 us (38%)
  Pallas kernels  41.7 us (29%)
  starting transfers between devices  19.8 us (14%)
  other arithmetic  11.6 us (8%)
  between operations  8.14 us (6%)
  local copies, waits for them, and re-layouts  7.17 us (5%)
    ppermute x12, waiting for transfers between devices, member_exchange(): got.append(lax.ppermute(piece, axis, pairs))  42.1 us
    pallas_call x4, Pallas kernels, head_call(): pl.pallas_call(body, grid=(heads // HEAD_STEP,), in_specs=[spec(x.shape)...  34.4 us
    ppermute x4, starting transfers between devices, shifted(): return lax.ppermute(value, 'seq', pairs)  11.9 us
    ppermute x4, waiting for transfers between devices, shifted(): return lax.ppermute(value, 'seq', pairs)  11.6 us
    ppermute x12, starting transfers between devices, member_exchange(): got.append(lax.ppermute(piece, axis, pairs))  7.84 us
    pallas_call x1, Pallas kernels, middle_call(): pl.pallas_call(middle_body, grid=(rows // step,), in_specs=[row_block, ro...  7.29 us
    another operation x6, other arithmetic, row_scan(): jnp.stack([inner[index] + inner_keep[index] * entering for index in range...  4.3 us
    add x2, other arithmetic, row_scan(): total = mine[index] + keep_row[index] * total  3.89 us
  transfers between devices with their start and end apart: 16, of which 14 were waited for; matrix products, arithmetic and copies ran while one was open for 3% of the time, Pallas kernels for 17%

profile of v16, /device:TPU:1, one launch (start us, length us, event | category | flops | bytes accessed | tf_op | source)
XLA Modules:
  0.0 142.0 jit_solution(10242832318312946217)
XLA Ops:
  0.7 0.8 select_reduce_fusion.1
  1.6 0.8 broadcast_in_dim.101.rel_ref
  2.4 3.6 %shard_map.84 = f32[16,128,128]{2,1,0:T(8,128)} custom-call(bf16[384,2048]{1,0:T(8,128)(2,1)} %key_ref.5, bf16[384,2048]{1,0:T(8,128)(2,1)} %value_ref.5, s32[384,128]{1,0:T(8,128)} %broadcast_in_dim.101.rel_ref), custom_call_target="tpu_custom_call" | custom-call | tf_op jit(solution)/shard_map/pallas_call | solution.py:144
  6.1 1.1 copy-done.2
  7.3 2.6 %collective-permute-start = (f32[4,128,128]{2,1,0:T(8,128)S(1)}, f32[4,128,128]{2,1,0:T(8,128)S(1)}, u32[]{:S(2)}, u32[]{:S(2)}) collective-permute-start(f32[4,128,128]{2,1,0:T(8,128)S(1)} %get-tuple-element.96), channel_id=1, source_target_pairs={{0,1},{1,2},{2,3},{3,0},{4,5},{5,6},{6,7},{7,4},{8,9},{9,10},{10,1... | collective-permute-start | bytes 786440 | tf_op jit(solution)/shard_map/ppermute | solution.py:50
  10.0 0.5 collective-permute-start.2
  10.7 0.6 fusion.16
  12.0 3.5 %collective-permute-done = f32[4,128,128]{2,1,0:T(8,128)S(1)} collective-permute-done((f32[4,128,128]{2,1,0:T(8,128)S(1)}, f32[4,128,128]{2,1,0:T(8,128)S(1)}, u32[]{:S(2)}, u32[]{:S(2)}) %collective-permute-start) | collective-permute-done | bytes 262176 | tf_op jit(solution)/shard_map/ppermute | solution.py:50
  15.5 5.6 %collective-permute-done.1 = f32[4,128,128]{2,1,0:T(8,128)S(1)} collective-permute-done((f32[4,128,128]{2,1,0:T(8,128)S(1)}, f32[4,128,128]{2,1,0:T(8,128)S(1)}, u32[]{:S(2)}, u32[]{:S(2)}) %collective-permute-start.1) | collective-permute-done | bytes 262176 | tf_op jit(solution)/shard_map/ppermute | solution.py:50
  21.1 0.5 collective-permute-done.2
  21.6 2.0 %fusion.7 = (f32[4,128,128]{2,1,0:T(8,128)S(1)}, f32[4,128,128]{2,1,0:T(8,128)S(1)}) fusion(f32[4,4,128,128]{3,2,1,0:T(8,128)S(1)} %bitcast_dynamic-update-slice_fusion.9, f32[]{:T(128)} %bitcast.8, f32[]{:T(128)} %bitcast.10, f32[]{:T(128)S(6)} %mul.176, f32[]{:T(128)} %bitcast.12), kind=kLoop, calls=%fused_computation.17 | loop fusion | flops 458752 | bytes 1572880 | tf_op jit(solution)/shard_map/add | solution.py:71
  23.6 4.0 %collective-permute-start.3 = (f32[4,128,128]{2,1,0:T(8,128)S(1)}, f32[4,128,128]{2,1,0:T(8,128)S(1)}, u32[]{:S(2)}, u32[]{:S(2)}) collective-permute-start(f32[4,128,128]{2,1,0:T(8,128)S(1)} %get-tuple-element.34), channel_id=1, source_target_pairs={{0,4},{1,5},{2,6},{3,7},{4,8},{5,9},{6,10},{7,11},{8,12},{9,13},{1... | collective-permute-start | bytes 786440 | tf_op jit(solution)/shard_map/ppermute | solution.py:82
  30.3 3.3 %collective-permute-done.3 = f32[4,128,128]{2,1,0:T(8,128)S(1)} collective-permute-done((f32[4,128,128]{2,1,0:T(8,128)S(1)}, f32[4,128,128]{2,1,0:T(8,128)S(1)}, u32[]{:S(2)}, u32[]{:S(2)}) %collective-permute-start.3) | collective-permute-done | bytes 262176 | tf_op jit(solution)/shard_map/ppermute | solution.py:82
  33.6 5.1 %collective-permute-start.4 = (f32[4,128,128]{2,1,0:T(8,128)S(1)}, f32[4,128,128]{2,1,0:T(8,128)S(1)}, u32[]{:S(2)}, u32[]{:S(2)}) collective-permute-start(f32[4,128,128]{2,1,0:T(8,128)S(1)} %multiply_add_fusion.3), channel_id=1, source_target_pairs={{0,8},{1,9},{2,10},{3,11},{4,12},{5,13},{6,14},{7,15},{16,24},{17,... | collective-permute-start | bytes 786440 | tf_op jit(solution)/shard_map/ppermute | solution.py:82
  38.8 0.6 subtract_reduce_fusion
  39.4 8.9 %shard_map.85 = (bf16[16,384,384]{2,1,0:T(8,128)(2,1)}, f32[384,2048]{1,0:T(8,128)}) custom-call(bf16[384,2048]{1,0:T(8,128)(2,1)} %query_ref.3, bf16[384,2048]{1,0:T(8,128)(2,1)} %key_ref.5, bf16[384,2048]{1,0:T(8,128)(2,1)} %value_ref.5, s32[384,128]{1,0:T(8,128)} %broadcast_in_dim.101.rel_ref), custom_call_target="tpu_custom_call" | custom-call | tf_op jit(solution)/shard_map/pallas_call | solution.py:144
  48.3 1.3 add_bitcast_fusion.5
  49.7 0.7 add_bitcast_fusion.4
  50.7 0.4 collective-permute-start.5
  51.1 1.8 %collective-permute-start.6 = (f32[4,128,128]{2,1,0:T(8,128)S(1)}, f32[4,128,128]{2,1,0:T(8,128)S(1)}, u32[]{:S(2)}, u32[]{:S(2)}) collective-permute-start(f32[4,128,128]{2,1,0:T(8,128)S(1)} %get-tuple-element.91), channel_id=1, source_target_pairs={{0,2},{1,3},{2,0},{3,1},{4,6},{5,7},{6,4},{7,5},{8,10},{9,11},{10,... | collective-permute-start | bytes 786440 | tf_op jit(solution)/shard_map/ppermute | solution.py:50
  53.2 3.1 %collective-permute-done.5 = f32[4,128,128]{2,1,0:T(8,128)S(1)} collective-permute-done((f32[4,128,128]{2,1,0:T(8,128)S(1)}, f32[4,128,128]{2,1,0:T(8,128)S(1)}, u32[]{:S(2)}, u32[]{:S(2)}) %collective-permute-start.5) | collective-permute-done | bytes 262176 | tf_op jit(solution)/shard_map/ppermute | solution.py:50
  56.3 8.1 %collective-permute-done.6 = f32[4,128,128]{2,1,0:T(8,128)S(1)} collective-permute-done((f32[4,128,128]{2,1,0:T(8,128)S(1)}, f32[4,128,128]{2,1,0:T(8,128)S(1)}, u32[]{:S(2)}, u32[]{:S(2)}) %collective-permute-start.6) | collective-permute-done | bytes 262176 | tf_op jit(solution)/shard_map/ppermute | solution.py:50
  64.5 0.6 collective-permute-done.7
  65.1 1.0 copy-done
  66.1 7.3 %shard_map.86 = (bf16[384,2048]{1,0:T(8,128)(2,1)}, bf16[384,2048]{1,0:T(8,128)(2,1)}, f32[16,128,128]{2,1,0:T(8,128)}) custom-call(bf16[384,2048]{1,0:T(8,128)(2,1)} %query_ref.3, f32[384,2048]{1,0:T(8,128)} %get-tuple-element.41.inside_ref, f32[16,128,128]{2,1,0:T(8,128)} %bitcast.122, bf16[384,2048]{1,0:T(8,128)(2,1)} %cot_ref.1, ...), custom_call_target="tpu_custom_call" | custom-call | tf_op jit(solution)/shard_map/pallas_call | solution.py:252
  73.5 1.1 copy-done.3
  74.8 0.7 fusion.15
  76.2 0.5 collective-permute-start.10
  76.6 3.5 %collective-permute-done.8 = f32[4,128,128]{2,1,0:T(8,128)S(1)} collective-permute-done((f32[4,128,128]{2,1,0:T(8,128)S(1)}, f32[4,128,128]{2,1,0:T(8,128)S(1)}, u32[]{:S(2)}, u32[]{:S(2)}) %collective-permute-start.8) | collective-permute-done | bytes 262176 | tf_op jit(solution)/shard_map/ppermute | solution.py:50
  80.2 5.6 %collective-permute-done.9 = f32[4,128,128]{2,1,0:T(8,128)S(1)} collective-permute-done((f32[4,128,128]{2,1,0:T(8,128)S(1)}, f32[4,128,128]{2,1,0:T(8,128)S(1)}, u32[]{:S(2)}, u32[]{:S(2)}) %collective-permute-start.9) | collective-permute-done | bytes 262176 | tf_op jit(solution)/shard_map/ppermute | solution.py:50
  85.8 0.7 collective-permute-done.10
  86.6 1.9 %fusion.3 = (f32[4,128,128]{2,1,0:T(8,128)S(1)}, f32[4,128,128]{2,1,0:T(8,128)S(1)}) fusion(f32[4,4,128,128]{3,2,1,0:T(8,128)S(1)} %bitcast_dynamic-update-slice_fusion.3, f32[]{:T(128)} %bitcast.34, f32[]{:T(128)} %bitcast.36, f32[]{:T(128)S(6)} %mul.199, f32[]{:T(128)} %bitcast.38), kind=kLoop, calls=%fused_computation.9 | loop fusion | flops 458752 | bytes 1572880 | tf_op jit(solution)/shard_map/add | solution.py:71
  88.5 1.3 collective-permute-start.11
  92.2 8.2 %collective-permute-done.11 = f32[4,128,128]{2,1,0:T(8,128)S(1)} collective-permute-done((f32[4,128,128]{2,1,0:T(8,128)S(1)}, f32[4,128,128]{2,1,0:T(8,128)S(1)}, u32[]{:S(2)}, u32[]{:S(2)}) %collective-permute-start.11) | collective-permute-done | bytes 262176 | tf_op jit(solution)/shard_map/ppermute | solution.py:82
  100.5 1.5 %collective-permute-start.12 = (f32[4,128,128]{2,1,0:T(8,128)S(1)}, f32[4,128,128]{2,1,0:T(8,128)S(1)}, u32[]{:S(2)}, u32[]{:S(2)}) collective-permute-start(f32[4,128,128]{2,1,0:T(8,128)S(1)} %multiply_add_fusion.1), channel_id=1, source_target_pairs={{8,0},{9,1},{10,2},{11,3},{12,4},{13,5},{14,6},{15,7},{24,16},{25,... | collective-permute-start | bytes 786440 | tf_op jit(solution)/shard_map/ppermute | solution.py:82
  102.0 0.7 fusion.12
  102.7 14.7 %shard_map.87 = (bf16[384,2048]{1,0:T(8,128)(2,1)}, f32[384,2048]{1,0:T(8,128)}, f32[384,2048]{1,0:T(8,128)}) custom-call(bf16[384,2048]{1,0:T(8,128)(2,1)} %query_ref.3, bf16[384,2048]{1,0:T(8,128)(2,1)} %key_ref.5, bf16[384,2048]{1,0:T(8,128)(2,1)} %value_ref.5, bf16[384,2048]{1,0:T(8,128)(2,1)} %get-tuple-element.51.grad_ref, ...), custom_call_target="tpu_custom_call" | custom-call | tf_op jit(solution)/shard_map/pallas_call | solution.py:144
  117.4 1.3 add_bitcast_fusion.2
  118.7 0.7 add_bitcast_fusion.1
  119.8 0.4 collective-permute-start.13
  120.2 1.4 collective-permute-start.14
  121.6 0.6 compare_reduce_fusion
  122.9 2.5 %collective-permute-done.13 = f32[4,128,128]{2,1,0:T(8,128)S(1)} collective-permute-done((f32[4,128,128]{2,1,0:T(8,128)S(1)}, f32[4,128,128]{2,1,0:T(8,128)S(1)}, u32[]{:S(2)}, u32[]{:S(2)}) %collective-permute-start.13) | collective-permute-done | bytes 262176 | tf_op jit(solution)/shard_map/ppermute | solution.py:50
  125.5 7.6 %collective-permute-done.14 = f32[4,128,128]{2,1,0:T(8,128)S(1)} collective-permute-done((f32[4,128,128]{2,1,0:T(8,128)S(1)}, f32[4,128,128]{2,1,0:T(8,128)S(1)}, u32[]{:S(2)}, u32[]{:S(2)}) %collective-permute-start.14) | collective-permute-done | bytes 262176 | tf_op jit(solution)/shard_map/ppermute | solution.py:50
  133.1 0.7 collective-permute-done.15
  133.8 0.6 broadcast_in_dim.114.gate_ref
  134.4 0.3 copy-done.1
  134.8 7.3 %shard_map.88 = (bf16[384,2048]{1,0:T(8,128)(2,1)}, bf16[384,2048]{1,0:T(8,128)(2,1)}) custom-call(bf16[384,2048]{1,0:T(8,128)(2,1)} %key_ref.5, bf16[384,2048]{1,0:T(8,128)(2,1)} %value_ref.5, f32[384,2048]{1,0:T(8,128)} %get-tuple-element.59.key_part, f32[384,2048]{1,0:T(8,128)} %get-tuple-element.60.value_part, f32[16,128,128]{2,1,0:T(8,128)} %bitcast.124, ...), custom_call_target="tpu_custom_call" | custom-call | tf_op jit(solution)/shard_map/pallas_call | solution.py:144
  (45 shorter events, 2.0 us)
Async XLA Ops:
  6.0 1.2 copy-start.2
  7.3 8.1 %collective-permute-start = (f32[4,128,128]{2,1,0:T(8,128)S(1)}, f32[4,128,128]{2,1,0:T(8,128)S(1)}, u32[]{:S(2)}, u32[]{:S(2)}) collective-permute-start(f32[4,128,128]{2,1,0:T(8,128)S(1)} %get-tuple-element.96), channel_id=1, source_target_pairs={{0,1},{1,2},{2,3},{3,0},{4,5},{5,6},{6,7},{7,4},{8,9},{9,10},{10,1... | collective-permute-start | bytes 786440 | tf_op jit(solution)/shard_map/ppermute | solution.py:50
  10.0 11.1 %collective-permute-start.1 = (f32[4,128,128]{2,1,0:T(8,128)S(1)}, f32[4,128,128]{2,1,0:T(8,128)S(1)}, u32[]{:S(2)}, u32[]{:S(2)}) collective-permute-start(f32[4,128,128]{2,1,0:T(8,128)S(1)} %get-tuple-element.95), channel_id=1, source_target_pairs={{0,2},{1,3},{2,0},{3,1},{4,6},{5,7},{6,4},{7,5},{8,10},{9,11},{10,... | collective-permute-start | bytes 786440 | tf_op jit(solution)/shard_map/ppermute | solution.py:50
  10.0 11.6 %collective-permute-start.2 = (f32[4,128,128]{2,1,0:T(8,128)S(1)}, f32[4,128,128]{2,1,0:T(8,128)S(1)}, u32[]{:S(2)}, u32[]{:S(2)}) collective-permute-start(f32[4,128,128]{2,1,0:T(8,128)S(1)} %get-tuple-element.94), channel_id=1, source_target_pairs={{0,3},{1,0},{2,1},{3,2},{4,7},{5,4},{6,5},{7,6},{8,11},{9,8},{10,9... | collective-permute-start | bytes 786440 | tf_op jit(solution)/shard_map/ppermute | solution.py:50
  23.6 10.0 %collective-permute-start.3 = (f32[4,128,128]{2,1,0:T(8,128)S(1)}, f32[4,128,128]{2,1,0:T(8,128)S(1)}, u32[]{:S(2)}, u32[]{:S(2)}) collective-permute-start(f32[4,128,128]{2,1,0:T(8,128)S(1)} %get-tuple-element.34), channel_id=1, source_target_pairs={{0,4},{1,5},{2,6},{3,7},{4,8},{5,9},{6,10},{7,11},{8,12},{9,13},{1... | collective-permute-start | bytes 786440 | tf_op jit(solution)/shard_map/ppermute | solution.py:82
  33.6 14.7 %collective-permute-start.4 = (f32[4,128,128]{2,1,0:T(8,128)S(1)}, f32[4,128,128]{2,1,0:T(8,128)S(1)}, u32[]{:S(2)}, u32[]{:S(2)}) collective-permute-start(f32[4,128,128]{2,1,0:T(8,128)S(1)} %multiply_add_fusion.3), channel_id=1, source_target_pairs={{0,8},{1,9},{2,10},{3,11},{4,12},{5,13},{6,14},{7,15},{16,24},{17,... | collective-permute-start | bytes 786440 | tf_op jit(solution)/shard_map/ppermute | solution.py:82
  50.7 5.6 %collective-permute-start.5 = (f32[4,128,128]{2,1,0:T(8,128)S(1)}, f32[4,128,128]{2,1,0:T(8,128)S(1)}, u32[]{:S(2)}, u32[]{:S(2)}) collective-permute-start(f32[4,128,128]{2,1,0:T(8,128)S(1)} %get-tuple-element.92), channel_id=1, source_target_pairs={{0,1},{1,2},{2,3},{3,0},{4,5},{5,6},{6,7},{7,4},{8,9},{9,10},{10,1... | collective-permute-start | bytes 786440 | tf_op jit(solution)/shard_map/ppermute | solution.py:50
  51.1 13.4 %collective-permute-start.6 = (f32[4,128,128]{2,1,0:T(8,128)S(1)}, f32[4,128,128]{2,1,0:T(8,128)S(1)}, u32[]{:S(2)}, u32[]{:S(2)}) collective-permute-start(f32[4,128,128]{2,1,0:T(8,128)S(1)} %get-tuple-element.91), channel_id=1, source_target_pairs={{0,2},{1,3},{2,0},{3,1},{4,6},{5,7},{6,4},{7,5},{8,10},{9,11},{10,... | collective-permute-start | bytes 786440 | tf_op jit(solution)/shard_map/ppermute | solution.py:50
  53.1 12.0 %collective-permute-start.7 = (f32[4,128,128]{2,1,0:T(8,128)S(1)}, f32[4,128,128]{2,1,0:T(8,128)S(1)}, u32[]{:S(2)}, u32[]{:S(2)}) collective-permute-start(f32[4,128,128]{2,1,0:T(8,128)S(1)} %get-tuple-element.90), channel_id=1, source_target_pairs={{0,3},{1,0},{2,1},{3,2},{4,7},{5,4},{6,5},{7,6},{8,11},{9,8},{10,9... | collective-permute-start | bytes 786440 | tf_op jit(solution)/shard_map/ppermute | solution.py:50
  65.1 1.0 copy-start
  73.4 1.2 copy-start.3
  74.7 5.5 %collective-permute-start.8 = (f32[4,128,128]{2,1,0:T(8,128)S(1)}, f32[4,128,128]{2,1,0:T(8,128)S(1)}, u32[]{:S(2)}, u32[]{:S(2)}) collective-permute-start(f32[4,128,128]{2,1,0:T(8,128)S(1)} %get-tuple-element.88), channel_id=1, source_target_pairs={{0,1},{1,2},{2,3},{3,0},{4,5},{5,6},{6,7},{7,4},{8,9},{9,10},{10,1... | collective-permute-start | bytes 786440 | tf_op jit(solution)/shard_map/ppermute | solution.py:50
  74.8 11.0 %collective-permute-start.9 = (f32[4,128,128]{2,1,0:T(8,128)S(1)}, f32[4,128,128]{2,1,0:T(8,128)S(1)}, u32[]{:S(2)}, u32[]{:S(2)}) collective-permute-start(f32[4,128,128]{2,1,0:T(8,128)S(1)} %get-tuple-element.87), channel_id=1, source_target_pairs={{0,2},{1,3},{2,0},{3,1},{4,6},{5,7},{6,4},{7,5},{8,10},{9,11},{10,... | collective-permute-start | bytes 786440 | tf_op jit(solution)/shard_map/ppermute | solution.py:50
  76.2 10.4 %collective-permute-start.10 = (f32[4,128,128]{2,1,0:T(8,128)S(1)}, f32[4,128,128]{2,1,0:T(8,128)S(1)}, u32[]{:S(2)}, u32[]{:S(2)}) collective-permute-start(f32[4,128,128]{2,1,0:T(8,128)S(1)} %get-tuple-element.86), channel_id=1, source_target_pairs={{0,3},{1,0},{2,1},{3,2},{4,7},{5,4},{6,5},{7,6},{8,11},{9,8},{10,9... | collective-permute-start | bytes 786440 | tf_op jit(solution)/shard_map/ppermute | solution.py:50
  88.5 12.0 %collective-permute-start.11 = (f32[4,128,128]{2,1,0:T(8,128)S(1)}, f32[4,128,128]{2,1,0:T(8,128)S(1)}, u32[]{:S(2)}, u32[]{:S(2)}) collective-permute-start(f32[4,128,128]{2,1,0:T(8,128)S(1)} %get-tuple-element.47), channel_id=1, source_target_pairs={{4,0},{5,1},{6,2},{7,3},{8,4},{9,5},{10,6},{11,7},{12,8},{13,9},{1... | collective-permute-start | bytes 786440 | tf_op jit(solution)/shard_map/ppermute | solution.py:82
  100.5 16.9 %collective-permute-start.12 = (f32[4,128,128]{2,1,0:T(8,128)S(1)}, f32[4,128,128]{2,1,0:T(8,128)S(1)}, u32[]{:S(2)}, u32[]{:S(2)}) collective-permute-start(f32[4,128,128]{2,1,0:T(8,128)S(1)} %multiply_add_fusion.1), channel_id=1, source_target_pairs={{8,0},{9,1},{10,2},{11,3},{12,4},{13,5},{14,6},{15,7},{24,16},{25,... | collective-permute-start | bytes 786440 | tf_op jit(solution)/shard_map/ppermute | solution.py:82
  119.8 5.7 %collective-permute-start.13 = (f32[4,128,128]{2,1,0:T(8,128)S(1)}, f32[4,128,128]{2,1,0:T(8,128)S(1)}, u32[]{:S(2)}, u32[]{:S(2)}) collective-permute-start(f32[4,128,128]{2,1,0:T(8,128)S(1)} %get-tuple-element.84), channel_id=1, source_target_pairs={{0,1},{1,2},{2,3},{3,0},{4,5},{5,6},{6,7},{7,4},{8,9},{9,10},{10,1... | collective-permute-start | bytes 786440 | tf_op jit(solution)/shard_map/ppermute | solution.py:50
  120.2 12.9 %collective-permute-start.14 = (f32[4,128,128]{2,1,0:T(8,128)S(1)}, f32[4,128,128]{2,1,0:T(8,128)S(1)}, u32[]{:S(2)}, u32[]{:S(2)}) collective-permute-start(f32[4,128,128]{2,1,0:T(8,128)S(1)} %get-tuple-element.83), channel_id=1, source_target_pairs={{0,2},{1,3},{2,0},{3,1},{4,6},{5,7},{6,4},{7,5},{8,10},{9,11},{10,... | collective-permute-start | bytes 786440 | tf_op jit(solution)/shard_map/ppermute | solution.py:50
  122.9 10.9 %collective-permute-start.15 = (f32[4,128,128]{2,1,0:T(8,128)S(1)}, f32[4,128,128]{2,1,0:T(8,128)S(1)}, u32[]{:S(2)}, u32[]{:S(2)}) collective-permute-start(f32[4,128,128]{2,1,0:T(8,128)S(1)} %get-tuple-element.82), channel_id=1, source_target_pairs={{0,3},{1,0},{2,1},{3,2},{4,7},{5,4},{6,5},{7,6},{8,11},{9,8},{10,9... | collective-permute-start | bytes 786440 | tf_op jit(solution)/shard_map/ppermute | solution.py:50
  133.8 1.0 copy-start.1

commit v17 on v15

--- a/solution.py
+++ b/solution.py
@@ -217,7 +217,7 @@
         value_out[:, columns(i)] = (value_part[:, columns(i)] + value_carry).astype(jnp.bfloat16)
 
 
-MIDDLE_ROWS = 128
+MIDDLE_ROWS = 96
 
 
 def middle_body(query_ref, inside_ref, prefix_ref, cot_ref, rel_ref, attn_ref, grad_ref, local_ref, mixed_ref):

time: 141 us -> 141 us (level)
  no operation moved by 1% of the time
where the time goes in v17:
time: 141 us
  waiting for transfers between devices  56.6 us (40%)
  Pallas kernels  36.9 us (26%)
  starting transfers between devices  20.5 us (15%)
  other arithmetic  11.6 us (8%)
  between operations  8.14 us (6%)
  local copies, waits for them, and re-layouts  7.17 us (5%)
    ppermute x12, waiting for transfers between devices, member_exchange(): got.append(lax.ppermute(piece, axis, pairs))  42.1 us
    pallas_call x4, Pallas kernels, head_call(): pl.pallas_call(body, grid=(heads // HEAD_STEP,), in_specs=[spec(x.shape)...  29.2 us
    ppermute x4, waiting for transfers between devices, shifted(): return lax.ppermute(value, 'seq', pairs)  14.5 us
    ppermute x4, starting transfers between devices, shifted(): return lax.ppermute(value, 'seq', pairs)  11.7 us
    ppermute x12, starting transfers between devices, member_exchange(): got.append(lax.ppermute(piece, axis, pairs))  8.73 us
    pallas_call x1, Pallas kernels, middle_call(): pl.pallas_call(middle_body, grid=(rows // step,), in_specs=[row_block, ro...  7.64 us
    another operation x6, other arithmetic, row_scan(): jnp.stack([inner[index] + inner_keep[index] * entering for index in range...  4.3 us
    add x2, other arithmetic, row_scan(): total = mine[index] + keep_row[index] * total  3.89 us
  transfers between devices with their start and end apart: 16, of which 15 were waited for; matrix products, arithmetic and copies ran while one was open for 3% of the time, Pallas kernels for 14%

profile of v17, /device:TPU:1, one launch (start us, length us, event | category | flops | bytes accessed | tf_op | source)
XLA Modules:
  0.0 140.8 jit_solution(6601995418380635358)
XLA Ops:
  0.7 0.8 select_reduce_fusion.1
  1.6 0.8 broadcast_in_dim.101.rel_ref
  2.4 3.2 %shard_map.84 = f32[16,128,128]{2,1,0:T(8,128)} custom-call(bf16[384,2048]{1,0:T(8,128)(2,1)} %key_ref.5, bf16[384,2048]{1,0:T(8,128)(2,1)} %value_ref.5, s32[384,128]{1,0:T(8,128)} %broadcast_in_dim.101.rel_ref), custom_call_target="tpu_custom_call" | custom-call | tf_op jit(solution)/shard_map/pallas_call | solution.py:144
  5.8 1.1 copy-done.2
  7.0 2.6 %collective-permute-start = (f32[4,128,128]{2,1,0:T(8,128)S(1)}, f32[4,128,128]{2,1,0:T(8,128)S(1)}, u32[]{:S(2)}, u32[]{:S(2)}) collective-permute-start(f32[4,128,128]{2,1,0:T(8,128)S(1)} %get-tuple-element.96), channel_id=1, source_target_pairs={{0,1},{1,2},{2,3},{3,0},{4,5},{5,6},{6,7},{7,4},{8,9},{9,10},{10,1... | collective-permute-start | bytes 786440 | tf_op jit(solution)/shard_map/ppermute | solution.py:50
  9.6 0.5 collective-permute-start.2
  10.4 0.6 fusion.16
  11.6 3.5 %collective-permute-done = f32[4,128,128]{2,1,0:T(8,128)S(1)} collective-permute-done((f32[4,128,128]{2,1,0:T(8,128)S(1)}, f32[4,128,128]{2,1,0:T(8,128)S(1)}, u32[]{:S(2)}, u32[]{:S(2)}) %collective-permute-start) | collective-permute-done | bytes 262176 | tf_op jit(solution)/shard_map/ppermute | solution.py:50
  15.1 5.6 %collective-permute-done.1 = f32[4,128,128]{2,1,0:T(8,128)S(1)} collective-permute-done((f32[4,128,128]{2,1,0:T(8,128)S(1)}, f32[4,128,128]{2,1,0:T(8,128)S(1)}, u32[]{:S(2)}, u32[]{:S(2)}) %collective-permute-start.1) | collective-permute-done | bytes 262176 | tf_op jit(solution)/shard_map/ppermute | solution.py:50
  20.7 0.5 collective-permute-done.2
  21.3 2.0 %fusion.7 = (f32[4,128,128]{2,1,0:T(8,128)S(1)}, f32[4,128,128]{2,1,0:T(8,128)S(1)}) fusion(f32[4,4,128,128]{3,2,1,0:T(8,128)S(1)} %bitcast_dynamic-update-slice_fusion.9, f32[]{:T(128)} %bitcast.8, f32[]{:T(128)} %bitcast.10, f32[]{:T(128)S(6)} %mul.176, f32[]{:T(128)} %bitcast.12), kind=kLoop, calls=%fused_computation.17 | loop fusion | flops 458752 | bytes 1572880 | tf_op jit(solution)/shard_map/add | solution.py:71
  23.3 4.0 %collective-permute-start.3 = (f32[4,128,128]{2,1,0:T(8,128)S(1)}, f32[4,128,128]{2,1,0:T(8,128)S(1)}, u32[]{:S(2)}, u32[]{:S(2)}) collective-permute-start(f32[4,128,128]{2,1,0:T(8,128)S(1)} %get-tuple-element.34), channel_id=1, source_target_pairs={{0,4},{1,5},{2,6},{3,7},{4,8},{5,9},{6,10},{7,11},{8,12},{9,13},{1... | collective-permute-start | bytes 786440 | tf_op jit(solution)/shard_map/ppermute | solution.py:82
  29.9 3.3 %collective-permute-done.3 = f32[4,128,128]{2,1,0:T(8,128)S(1)} collective-permute-done((f32[4,128,128]{2,1,0:T(8,128)S(1)}, f32[4,128,128]{2,1,0:T(8,128)S(1)}, u32[]{:S(2)}, u32[]{:S(2)}) %collective-permute-start.3) | collective-permute-done | bytes 262176 | tf_op jit(solution)/shard_map/ppermute | solution.py:82
  33.3 5.1 %collective-permute-start.4 = (f32[4,128,128]{2,1,0:T(8,128)S(1)}, f32[4,128,128]{2,1,0:T(8,128)S(1)}, u32[]{:S(2)}, u32[]{:S(2)}) collective-permute-start(f32[4,128,128]{2,1,0:T(8,128)S(1)} %multiply_add_fusion.3), channel_id=1, source_target_pairs={{0,8},{1,9},{2,10},{3,11},{4,12},{5,13},{6,14},{7,15},{16,24},{17,... | collective-permute-start | bytes 786440 | tf_op jit(solution)/shard_map/ppermute | solution.py:82
  38.4 0.6 subtract_reduce_fusion
  39.1 7.6 %shard_map.85 = (bf16[16,384,384]{2,1,0:T(8,128)(2,1)}, f32[384,2048]{1,0:T(8,128)}) custom-call(bf16[384,2048]{1,0:T(8,128)(2,1)} %query_ref.3, bf16[384,2048]{1,0:T(8,128)(2,1)} %key_ref.5, bf16[384,2048]{1,0:T(8,128)(2,1)} %value_ref.5, s32[384,128]{1,0:T(8,128)} %broadcast_in_dim.101.rel_ref), custom_call_target="tpu_custom_call" | custom-call | tf_op jit(solution)/shard_map/pallas_call | solution.py:144
  46.7 1.3 add_bitcast_fusion.5
  48.0 0.7 add_bitcast_fusion.4
  49.1 0.4 collective-permute-start.5
  49.4 1.9 %collective-permute-start.6 = (f32[4,128,128]{2,1,0:T(8,128)S(1)}, f32[4,128,128]{2,1,0:T(8,128)S(1)}, u32[]{:S(2)}, u32[]{:S(2)}) collective-permute-start(f32[4,128,128]{2,1,0:T(8,128)S(1)} %get-tuple-element.91), channel_id=1, source_target_pairs={{0,2},{1,3},{2,0},{3,1},{4,6},{5,7},{6,4},{7,5},{8,10},{9,11},{10,... | collective-permute-start | bytes 786440 | tf_op jit(solution)/shard_map/ppermute | solution.py:50
  51.6 3.1 %collective-permute-done.5 = f32[4,128,128]{2,1,0:T(8,128)S(1)} collective-permute-done((f32[4,128,128]{2,1,0:T(8,128)S(1)}, f32[4,128,128]{2,1,0:T(8,128)S(1)}, u32[]{:S(2)}, u32[]{:S(2)}) %collective-permute-start.5) | collective-permute-done | bytes 262176 | tf_op jit(solution)/shard_map/ppermute | solution.py:50
  54.7 8.2 %collective-permute-done.6 = f32[4,128,128]{2,1,0:T(8,128)S(1)} collective-permute-done((f32[4,128,128]{2,1,0:T(8,128)S(1)}, f32[4,128,128]{2,1,0:T(8,128)S(1)}, u32[]{:S(2)}, u32[]{:S(2)}) %collective-permute-start.6) | collective-permute-done | bytes 262176 | tf_op jit(solution)/shard_map/ppermute | solution.py:50
  62.9 0.6 collective-permute-done.7
  63.5 1.0 copy-done
  64.5 7.6 %shard_map.86 = (bf16[384,2048]{1,0:T(8,128)(2,1)}, bf16[384,2048]{1,0:T(8,128)(2,1)}, f32[16,128,128]{2,1,0:T(8,128)}) custom-call(bf16[384,2048]{1,0:T(8,128)(2,1)} %query_ref.3, f32[384,2048]{1,0:T(8,128)} %get-tuple-element.41.inside_ref, f32[16,128,128]{2,1,0:T(8,128)} %bitcast.122, bf16[384,2048]{1,0:T(8,128)(2,1)} %cot_ref.1, ...), custom_call_target="tpu_custom_call" | custom-call | tf_op jit(solution)/shard_map/pallas_call | solution.py:252
  72.2 1.1 copy-done.3
  73.6 0.7 fusion.15
  74.9 0.5 collective-permute-start.10
  75.4 3.5 %collective-permute-done.8 = f32[4,128,128]{2,1,0:T(8,128)S(1)} collective-permute-done((f32[4,128,128]{2,1,0:T(8,128)S(1)}, f32[4,128,128]{2,1,0:T(8,128)S(1)}, u32[]{:S(2)}, u32[]{:S(2)}) %collective-permute-start.8) | collective-permute-done | bytes 262176 | tf_op jit(solution)/shard_map/ppermute | solution.py:50
  78.9 5.6 %collective-permute-done.9 = f32[4,128,128]{2,1,0:T(8,128)S(1)} collective-permute-done((f32[4,128,128]{2,1,0:T(8,128)S(1)}, f32[4,128,128]{2,1,0:T(8,128)S(1)}, u32[]{:S(2)}, u32[]{:S(2)}) %collective-permute-start.9) | collective-permute-done | bytes 262176 | tf_op jit(solution)/shard_map/ppermute | solution.py:50
  84.6 0.7 collective-permute-done.10
  85.3 1.9 %fusion.3 = (f32[4,128,128]{2,1,0:T(8,128)S(1)}, f32[4,128,128]{2,1,0:T(8,128)S(1)}) fusion(f32[4,4,128,128]{3,2,1,0:T(8,128)S(1)} %bitcast_dynamic-update-slice_fusion.3, f32[]{:T(128)} %bitcast.34, f32[]{:T(128)} %bitcast.36, f32[]{:T(128)S(6)} %mul.199, f32[]{:T(128)} %bitcast.38), kind=kLoop, calls=%fused_computation.9 | loop fusion | flops 458752 | bytes 1572880 | tf_op jit(solution)/shard_map/add | solution.py:71
  87.2 1.3 collective-permute-start.11
  91.0 9.5 %collective-permute-done.11 = f32[4,128,128]{2,1,0:T(8,128)S(1)} collective-permute-done((f32[4,128,128]{2,1,0:T(8,128)S(1)}, f32[4,128,128]{2,1,0:T(8,128)S(1)}, u32[]{:S(2)}, u32[]{:S(2)}) %collective-permute-start.11) | collective-permute-done | bytes 262176 | tf_op jit(solution)/shard_map/ppermute | solution.py:82
  100.5 1.3 collective-permute-start.12
  101.8 0.7 fusion.12
  102.5 12.2 %shard_map.87 = (bf16[384,2048]{1,0:T(8,128)(2,1)}, f32[384,2048]{1,0:T(8,128)}, f32[384,2048]{1,0:T(8,128)}) custom-call(bf16[384,2048]{1,0:T(8,128)(2,1)} %query_ref.3, bf16[384,2048]{1,0:T(8,128)(2,1)} %key_ref.5, bf16[384,2048]{1,0:T(8,128)(2,1)} %value_ref.5, bf16[384,2048]{1,0:T(8,128)(2,1)} %get-tuple-element.51.grad_ref, ...), custom_call_target="tpu_custom_call" | custom-call | tf_op jit(solution)/shard_map/pallas_call | solution.py:144
  114.7 1.7 %collective-permute-done.12 = f32[4,128,128]{2,1,0:T(8,128)S(1)} collective-permute-done((f32[4,128,128]{2,1,0:T(8,128)S(1)}, f32[4,128,128]{2,1,0:T(8,128)S(1)}, u32[]{:S(2)}, u32[]{:S(2)}) %collective-permute-start.12) | collective-permute-done | bytes 262176 | tf_op jit(solution)/shard_map/ppermute | solution.py:82
  116.4 1.3 add_bitcast_fusion.2
  117.7 0.7 add_bitcast_fusion.1
  118.8 1.4 collective-permute-start.13
  120.1 1.3 collective-permute-start.14
  121.4 0.6 compare_reduce_fusion
  122.8 2.8 %collective-permute-done.13 = f32[4,128,128]{2,1,0:T(8,128)S(1)} collective-permute-done((f32[4,128,128]{2,1,0:T(8,128)S(1)}, f32[4,128,128]{2,1,0:T(8,128)S(1)}, u32[]{:S(2)}, u32[]{:S(2)}) %collective-permute-start.13) | collective-permute-done | bytes 262176 | tf_op jit(solution)/shard_map/ppermute | solution.py:50
  125.6 7.3 %collective-permute-done.14 = f32[4,128,128]{2,1,0:T(8,128)S(1)} collective-permute-done((f32[4,128,128]{2,1,0:T(8,128)S(1)}, f32[4,128,128]{2,1,0:T(8,128)S(1)}, u32[]{:S(2)}, u32[]{:S(2)}) %collective-permute-start.14) | collective-permute-done | bytes 262176 | tf_op jit(solution)/shard_map/ppermute | solution.py:50
  133.0 0.6 collective-permute-done.15
  133.6 0.6 broadcast_in_dim.114.gate_ref
  134.6 6.2 %shard_map.88 = (bf16[384,2048]{1,0:T(8,128)(2,1)}, bf16[384,2048]{1,0:T(8,128)(2,1)}) custom-call(bf16[384,2048]{1,0:T(8,128)(2,1)} %key_ref.5, bf16[384,2048]{1,0:T(8,128)(2,1)} %value_ref.5, f32[384,2048]{1,0:T(8,128)} %get-tuple-element.59.key_part, f32[384,2048]{1,0:T(8,128)} %get-tuple-element.60.value_part, f32[16,128,128]{2,1,0:T(8,128)} %bitcast.124, ...), custom_call_target="tpu_custom_call" | custom-call | tf_op jit(solution)/shard_map/pallas_call | solution.py:144
  (45 shorter events, 2.3 us)
Async XLA Ops:
  5.7 1.2 copy-start.2
  7.0 8.1 %collective-permute-start = (f32[4,128,128]{2,1,0:T(8,128)S(1)}, f32[4,128,128]{2,1,0:T(8,128)S(1)}, u32[]{:S(2)}, u32[]{:S(2)}) collective-permute-start(f32[4,128,128]{2,1,0:T(8,128)S(1)} %get-tuple-element.96), channel_id=1, source_target_pairs={{0,1},{1,2},{2,3},{3,0},{4,5},{5,6},{6,7},{7,4},{8,9},{9,10},{10,1... | collective-permute-start | bytes 786440 | tf_op jit(solution)/shard_map/ppermute | solution.py:50
  9.6 11.1 %collective-permute-start.1 = (f32[4,128,128]{2,1,0:T(8,128)S(1)}, f32[4,128,128]{2,1,0:T(8,128)S(1)}, u32[]{:S(2)}, u32[]{:S(2)}) collective-permute-start(f32[4,128,128]{2,1,0:T(8,128)S(1)} %get-tuple-element.95), channel_id=1, source_target_pairs={{0,2},{1,3},{2,0},{3,1},{4,6},{5,7},{6,4},{7,5},{8,10},{9,11},{10,... | collective-permute-start | bytes 786440 | tf_op jit(solution)/shard_map/ppermute | solution.py:50
  9.6 11.6 %collective-permute-start.2 = (f32[4,128,128]{2,1,0:T(8,128)S(1)}, f32[4,128,128]{2,1,0:T(8,128)S(1)}, u32[]{:S(2)}, u32[]{:S(2)}) collective-permute-start(f32[4,128,128]{2,1,0:T(8,128)S(1)} %get-tuple-element.94), channel_id=1, source_target_pairs={{0,3},{1,0},{2,1},{3,2},{4,7},{5,4},{6,5},{7,6},{8,11},{9,8},{10,9... | collective-permute-start | bytes 786440 | tf_op jit(solution)/shard_map/ppermute | solution.py:50
  23.3 10.0 %collective-permute-start.3 = (f32[4,128,128]{2,1,0:T(8,128)S(1)}, f32[4,128,128]{2,1,0:T(8,128)S(1)}, u32[]{:S(2)}, u32[]{:S(2)}) collective-permute-start(f32[4,128,128]{2,1,0:T(8,128)S(1)} %get-tuple-element.34), channel_id=1, source_target_pairs={{0,4},{1,5},{2,6},{3,7},{4,8},{5,9},{6,10},{7,11},{8,12},{9,13},{1... | collective-permute-start | bytes 786440 | tf_op jit(solution)/shard_map/ppermute | solution.py:82
  33.3 13.4 %collective-permute-start.4 = (f32[4,128,128]{2,1,0:T(8,128)S(1)}, f32[4,128,128]{2,1,0:T(8,128)S(1)}, u32[]{:S(2)}, u32[]{:S(2)}) collective-permute-start(f32[4,128,128]{2,1,0:T(8,128)S(1)} %multiply_add_fusion.3), channel_id=1, source_target_pairs={{0,8},{1,9},{2,10},{3,11},{4,12},{5,13},{6,14},{7,15},{16,24},{17,... | collective-permute-start | bytes 786440 | tf_op jit(solution)/shard_map/ppermute | solution.py:82
  49.1 5.6 %collective-permute-start.5 = (f32[4,128,128]{2,1,0:T(8,128)S(1)}, f32[4,128,128]{2,1,0:T(8,128)S(1)}, u32[]{:S(2)}, u32[]{:S(2)}) collective-permute-start(f32[4,128,128]{2,1,0:T(8,128)S(1)} %get-tuple-element.92), channel_id=1, source_target_pairs={{0,1},{1,2},{2,3},{3,0},{4,5},{5,6},{6,7},{7,4},{8,9},{9,10},{10,1... | collective-permute-start | bytes 786440 | tf_op jit(solution)/shard_map/ppermute | solution.py:50
  49.4 13.4 %collective-permute-start.6 = (f32[4,128,128]{2,1,0:T(8,128)S(1)}, f32[4,128,128]{2,1,0:T(8,128)S(1)}, u32[]{:S(2)}, u32[]{:S(2)}) collective-permute-start(f32[4,128,128]{2,1,0:T(8,128)S(1)} %get-tuple-element.91), channel_id=1, source_target_pairs={{0,2},{1,3},{2,0},{3,1},{4,6},{5,7},{6,4},{7,5},{8,10},{9,11},{10,... | collective-permute-start | bytes 786440 | tf_op jit(solution)/shard_map/ppermute | solution.py:50
  51.5 12.0 %collective-permute-start.7 = (f32[4,128,128]{2,1,0:T(8,128)S(1)}, f32[4,128,128]{2,1,0:T(8,128)S(1)}, u32[]{:S(2)}, u32[]{:S(2)}) collective-permute-start(f32[4,128,128]{2,1,0:T(8,128)S(1)} %get-tuple-element.90), channel_id=1, source_target_pairs={{0,3},{1,0},{2,1},{3,2},{4,7},{5,4},{6,5},{7,6},{8,11},{9,8},{10,9... | collective-permute-start | bytes 786440 | tf_op jit(solution)/shard_map/ppermute | solution.py:50
  63.5 1.0 copy-start
  72.1 1.2 copy-start.3
  73.4 5.5 %collective-permute-start.8 = (f32[4,128,128]{2,1,0:T(8,128)S(1)}, f32[4,128,128]{2,1,0:T(8,128)S(1)}, u32[]{:S(2)}, u32[]{:S(2)}) collective-permute-start(f32[4,128,128]{2,1,0:T(8,128)S(1)} %get-tuple-element.88), channel_id=1, source_target_pairs={{0,1},{1,2},{2,3},{3,0},{4,5},{5,6},{6,7},{7,4},{8,9},{9,10},{10,1... | collective-permute-start | bytes 786440 | tf_op jit(solution)/shard_map/ppermute | solution.py:50
  73.5 11.0 %collective-permute-start.9 = (f32[4,128,128]{2,1,0:T(8,128)S(1)}, f32[4,128,128]{2,1,0:T(8,128)S(1)}, u32[]{:S(2)}, u32[]{:S(2)}) collective-permute-start(f32[4,128,128]{2,1,0:T(8,128)S(1)} %get-tuple-element.87), channel_id=1, source_target_pairs={{0,2},{1,3},{2,0},{3,1},{4,6},{5,7},{6,4},{7,5},{8,10},{9,11},{10,... | collective-permute-start | bytes 786440 | tf_op jit(solution)/shard_map/ppermute | solution.py:50
  74.9 10.4 %collective-permute-start.10 = (f32[4,128,128]{2,1,0:T(8,128)S(1)}, f32[4,128,128]{2,1,0:T(8,128)S(1)}, u32[]{:S(2)}, u32[]{:S(2)}) collective-permute-start(f32[4,128,128]{2,1,0:T(8,128)S(1)} %get-tuple-element.86), channel_id=1, source_target_pairs={{0,3},{1,0},{2,1},{3,2},{4,7},{5,4},{6,5},{7,6},{8,11},{9,8},{10,9... | collective-permute-start | bytes 786440 | tf_op jit(solution)/shard_map/ppermute | solution.py:50
  87.2 13.3 %collective-permute-start.11 = (f32[4,128,128]{2,1,0:T(8,128)S(1)}, f32[4,128,128]{2,1,0:T(8,128)S(1)}, u32[]{:S(2)}, u32[]{:S(2)}) collective-permute-start(f32[4,128,128]{2,1,0:T(8,128)S(1)} %get-tuple-element.47), channel_id=1, source_target_pairs={{4,0},{5,1},{6,2},{7,3},{8,4},{9,5},{10,6},{11,7},{12,8},{13,9},{1... | collective-permute-start | bytes 786440 | tf_op jit(solution)/shard_map/ppermute | solution.py:82
  100.5 15.9 %collective-permute-start.12 = (f32[4,128,128]{2,1,0:T(8,128)S(1)}, f32[4,128,128]{2,1,0:T(8,128)S(1)}, u32[]{:S(2)}, u32[]{:S(2)}) collective-permute-start(f32[4,128,128]{2,1,0:T(8,128)S(1)} %multiply_add_fusion.1), channel_id=1, source_target_pairs={{8,0},{9,1},{10,2},{11,3},{12,4},{13,5},{14,6},{15,7},{24,16},{25,... | collective-permute-start | bytes 786440 | tf_op jit(solution)/shard_map/ppermute | solution.py:82
  118.8 6.9 %collective-permute-start.13 = (f32[4,128,128]{2,1,0:T(8,128)S(1)}, f32[4,128,128]{2,1,0:T(8,128)S(1)}, u32[]{:S(2)}, u32[]{:S(2)}) collective-permute-start(f32[4,128,128]{2,1,0:T(8,128)S(1)} %get-tuple-element.84), channel_id=1, source_target_pairs={{0,1},{1,2},{2,3},{3,0},{4,5},{5,6},{6,7},{7,4},{8,9},{9,10},{10,1... | collective-permute-start | bytes 786440 | tf_op jit(solution)/shard_map/ppermute | solution.py:50
  120.1 12.8 %collective-permute-start.14 = (f32[4,128,128]{2,1,0:T(8,128)S(1)}, f32[4,128,128]{2,1,0:T(8,128)S(1)}, u32[]{:S(2)}, u32[]{:S(2)}) collective-permute-start(f32[4,128,128]{2,1,0:T(8,128)S(1)} %get-tuple-element.83), channel_id=1, source_target_pairs={{0,2},{1,3},{2,0},{3,1},{4,6},{5,7},{6,4},{7,5},{8,10},{9,11},{10,... | collective-permute-start | bytes 786440 | tf_op jit(solution)/shard_map/ppermute | solution.py:50
  122.7 10.9 %collective-permute-start.15 = (f32[4,128,128]{2,1,0:T(8,128)S(1)}, f32[4,128,128]{2,1,0:T(8,128)S(1)}, u32[]{:S(2)}, u32[]{:S(2)}) collective-permute-start(f32[4,128,128]{2,1,0:T(8,128)S(1)} %get-tuple-element.82), channel_id=1, source_target_pairs={{0,3},{1,0},{2,1},{3,2},{4,7},{5,4},{6,5},{7,6},{8,11},{9,8},{10,9... | collective-permute-start | bytes 786440 | tf_op jit(solution)/shard_map/ppermute | solution.py:50
  133.6 1.0 copy-start.1
